TPU v7x, 128 devices: a whole 4x4x4 slice. The times are simulated.
128 devices in a mesh: blk: 32 (over x, z_hi, y), rep: 4 (over z_lo, core).
Axes of the slice: x: 4, y: 4, z: 4 (z_hi: 2, z_lo: 2; z = z_hi * 2 + z_lo), core: 2. Of those that a mesh axis runs over, the one named last changes fastest.
Arguments:
- queries: bfloat16 [32768, 4096], P(('blk', 'rep')), as said below
- query_group: int32 [32768, 1], P(('blk', 'rep')), may hold values from 0 to 3; in each aligned block of 256 rows (0 to 255, 256 to 511, ...) at most 128 rows name the same one
- query_bin: int32 [32768], P(('blk', 'rep')), may hold values from 0 to 63
- query_shift: int32 [32768], P(('blk', 'rep')), may hold values from 1 to 2
- library: bfloat16 [4, 1024, 4096], P('rep', 'blk'), as said below
- library_bin: int32 [4, 1024], P('rep', 'blk'), may hold values from 0 to 63
Outputs:
- best_scores: float32 [32768, 8], P(('blk', 'rep'))
Inputs may be any that keep to these rules, and one draw needn't show every extreme that they name: `query_group`: among the 256 queries of one device at most 128 name the same group, and on every draw some device has a group named by exactly 128 of its queries. `queries`: intensities are nonnegative and every spectrum has peaks. `library`: intensities are nonnegative and every spectrum has peaks.
All inputs are finite; a program needn't handle non-finite values.
Results may differ from a plain program's by a relative error of at most 0.0021.
Values may be sent and summed in bfloat16 or wider, within the bound.
No kernel may reach another device: no remote copies, remote signals or barrier semaphores. Data moves between devices by JAX's collectives and lax.ppermute only.
A program may use at most 192 MiB of HBM per device.

v0:
```python
import jax
import jax.numpy as jnp
from jax import lax
from jax.sharding import Mesh
from jax.sharding import PartitionSpec as P

W = 4096
K = 8
NSHIFT = 2
SHIFT_BINS = 16
WIN = 16
CAP = 128
BLK = ("blk_0", "blk_1", "blk_2")
BLK_REP = ("blk_0", "blk_1", "blk_2", "rep")


def gathered_by_axis(x, axes, dim):
    for axis in reversed(axes):
        x = lax.all_gather(x, axis, axis=dim, tiled=True)
    return x


def unit_rows(raw):
    values = jnp.sqrt(raw.astype(jnp.float32))
    total = jnp.sum(values * values, axis=-1, keepdims=True)
    return (values * lax.rsqrt(total + 1e-06)).astype(jnp.bfloat16)


def lower_bins(rows, amount):
    tail = jnp.zeros(rows.shape[:-1] + (amount,), rows.dtype)
    return jnp.concatenate([rows[..., amount:], tail], axis=-1)


def slot_index(group, groups, capacity):
    labels = jnp.arange(groups, dtype=jnp.int32)
    onehot = (group[:, None] == labels[None, :]).astype(jnp.int32)
    before = jnp.cumsum(onehot, axis=0) - onehot
    place = jnp.sum(before * onehot, axis=1)
    return group * capacity + place


def stop_scores(plain, shifted, query_bins, lib_bins):
    near = jnp.abs(lib_bins[:, None] - query_bins[None, :]) <= WIN
    return jnp.where(near, jnp.maximum(plain, shifted), 0.0)


def keep_best(best, scores):
    joined = jnp.concatenate([best, scores], axis=0)
    height = joined.shape[0]
    position = lax.broadcasted_iota(jnp.int32, joined.shape, 0)
    picked = []
    for step in range(K):
        top = jnp.max(joined, axis=0)
        first = jnp.min(jnp.where(joined == top[None, :], position, height), axis=0)
        picked.append(top)
        joined = jnp.where(position == first[None, :], -3e38, joined)
    return jnp.stack(picked, axis=0)


def on_device(queries, query_group, query_bin, query_shift, library, library_bin):
    groups = lax.axis_size("rep")
    lib_rows = library.shape[1]
    slots = groups * CAP
    unit_q = unit_rows(queries)
    group = query_group[:, 0]
    slot = slot_index(group, groups, CAP)
    slot_ids = jnp.arange(slots, dtype=jnp.int32)
    placed = slot[:, None] == slot_ids[None, :]
    placed_bf = placed.astype(jnp.bfloat16)
    placed_int = placed.astype(jnp.int32)
    send_q = lax.dot_general(
        placed_bf, unit_q, (((0,), (0,)), ((), ())), preferred_element_type=jnp.float32
    )
    send_q = send_q.astype(jnp.bfloat16).reshape(groups, CAP, W)
    send_bin = jnp.sum(placed_int * query_bin[:, None], axis=0).reshape(groups, CAP)
    send_shift = jnp.sum(placed_int * query_shift[:, None], axis=0).reshape(groups, CAP)
    unit_lib = unit_rows(library)
    bin_row = jnp.pad(library_bin.astype(jnp.bfloat16), ((0, 0), (0, W - lib_rows)))[:, None, :]
    packed_lib = jnp.concatenate([unit_lib, bin_row], axis=1)
    rows = lax.all_to_all(send_q, "rep", split_axis=0, concat_axis=0, tiled=True)
    rbin = lax.all_to_all(send_bin, "rep", split_axis=0, concat_axis=0, tiled=True)
    rshift = lax.all_to_all(send_shift, "rep", split_axis=0, concat_axis=0, tiled=True)
    items = rows.shape[1]
    flat = rows.reshape(-1, W)
    flat_bin = rbin.reshape(-1)
    flat_shift = rshift.reshape(-1)
    total = flat.shape[0]
    start_best = jnp.full((K, total), -1.0, jnp.float32)
    moved = jnp.zeros_like(flat)
    for s in range(1, NSHIFT + 1):
        moved = jnp.where((flat_shift == s)[:, None], lower_bins(flat, s * SHIFT_BINS), moved)
    both = jnp.concatenate([flat, moved], axis=0)
    split = gathered_by_axis(packed_lib, ("blk_2", "blk_0", "blk_1"), 1).reshape(
        -1, lib_rows + 1, W
    )
    blocks = split[:, :lib_rows].reshape(-1, W)
    lib_bins = split[:, lib_rows, :lib_rows].reshape(-1).astype(jnp.int32)
    prod = lax.dot_general(
        blocks, both, (((1,), (1,)), ((), ())), preferred_element_type=jnp.float32
    )
    best = keep_best(start_best, stop_scores(prod[:, :total], prod[:, total:], flat_bin, lib_bins))
    results = best.reshape(K, groups, items).transpose(1, 2, 0)
    home = lax.all_to_all(results, "rep", split_axis=0, concat_axis=0, tiled=True)
    back = placed.astype(jnp.float32)
    return jnp.dot(
        back,
        home.reshape(slots, K),
        preferred_element_type=jnp.float32,
        precision=lax.Precision.HIGHEST,
    )


def solution(mesh):
    split = Mesh(
        mesh.devices.reshape(4, 2, 4, mesh.shape["rep"]), ("blk_0", "blk_1", "blk_2", "rep")
    )
    in_specs = (
        P(BLK_REP, None),
        P(BLK_REP, None),
        P(BLK_REP),
        P(BLK_REP),
        P("rep", BLK, None),
        P("rep", BLK),
    )
    out_specs = P(BLK_REP, None)
    return jax.shard_map(
        on_device, mesh=split, in_specs=in_specs, out_specs=out_specs, check_vma=False
    )
```

profile of v0, /device:TPU:1, one launch (start us, length us, event | category | flops | bytes accessed | tf_op | source)
XLA Modules:
  0.0 232.1 jit_solution(17135073077377979420)
XLA Ops:
  6.5 0.7 convert_element_type.44
  7.2 1.2 multiply_reduce_fusion.1
  8.5 1.1 multiply_convert_fusion.2
  9.6 0.6 copy.27
  10.2 17.2 %all_gather.9 = bf16[1,66,4096]{2,0,1:T(2,128)(2,1)} all-gather(bf16[1,33,4096]{2,0,1:T(2,128)(2,1)S(1)} %copy.27), channel_id=1, replica_groups=mesh['blk_0'=4,'blk_1'=2,'blk_2'=4,'rep'=4] {'blk_1'}, dimensions={1}, use_global_device_ids=true | all-gather | bytes 811008 | tf_op jit(solution)/shard_map/all_gather | solution.py:19
  27.4 0.0 all-gather.5.cloned.1.call-start
  27.4 51.8 %all-gather.3.cloned.1.call-done = bf16[1,264,4096]{2,0,1:T(2,128)(2,1)} async-done(((bf16[1,66,4096]{2,0,1:T(2,128)(2,1)}), bf16[1,264,4096]{2,0,1:T(2,128)(2,1)}) %all-gather.3.cloned.1.call-update) | async-done | bytes 2162704 | tf_op jit(solution)/shard_map/all_gather | solution.py:19
  79.2 6.0 %copy.28 = bf16[1,264,4096]{2,1,0:T(8,128)(2,1)} copy(bf16[1,264,4096]{2,0,1:T(2,128)(2,1)} %all-gather.3.cloned.1.call-done) | data formatting | bytes 4325376 | tf_op jit(solution)/shard_map/all_gather | solution.py:19
  85.2 0.6 copy-done.2
  85.9 1.2 reduce-window.6
  87.1 0.1 slice.32
  87.2 0.1 copy.25
  87.3 0.1 copy.26
  87.4 0.1 add_bitcast_fusion
  87.5 0.8 select_reduce_fusion.9
  88.3 3.8 %all-to-all-start.2 = ((s32[4,1,128]{2,1,0:T(1,128)}), s32[4,1,128]{2,1,0:T(1,128)S(1)}, u32[]{:S(2)}, u32[]{:S(2)}) async-start(s32[4,1,128]{2,1,0:T(1,128)} %bitcast.12), calls=%async_computation.2 | async-start | bytes 4096 | tf_op jit(solution)/shard_map/all_to_all | solution.py:82
  92.1 1.4 multiply_reduce_fusion
  93.5 4.1 %convolution_convert_fusion = bf16[512,4096]{1,0:T(8,128)(2,1)} fusion(bf16[256,4096]{1,0:T(8,128)(2,1)S(1)} %copy-done, f32[256]{0:T(256)S(1)} %add_rsqrt_fusion, s32[256]{0:T(256)S(1)} %bitcast.57), kind=kOutput, calls=%fused_computation.4 | convolution fusion | flops 1079115776 | bytes 6293504 | tf_op jit(solution)/shard_map/dot_general | solution.py:71
  97.6 5.0 %all-to-all-start.1 = ((bf16[4,128,4096]{2,1,0:T(8,128)(2,1)}), bf16[4,128,4096]{2,1,0:T(8,128)(2,1)}, u32[]{:S(2)}, u32[]{:S(2)}) async-start(bf16[4,128,4096]{2,1,0:T(8,128)(2,1)} %bitcast.46), calls=%async_computation.1 | async-start | bytes 8388608 | tf_op jit(solution)/shard_map/all_to_all | solution.py:80
  102.6 47.4 %all-to-all-done.1 = bf16[4,128,4096]{2,1,0:T(8,128)(2,1)} async-done(((bf16[4,128,4096]{2,1,0:T(8,128)(2,1)}), bf16[4,128,4096]{2,1,0:T(8,128)(2,1)}, u32[]{:S(2)}, u32[]{:S(2)}) %all-to-all-start.1) | async-done | bytes 4194336 | tf_op jit(solution)/shard_map/all_to_all | solution.py:80
  150.0 4.1 %all-to-all-start = ((s32[4,1,128]{2,1,0:T(1,128)}), s32[4,1,128]{2,1,0:T(1,128)S(1)}, u32[]{:S(2)}, u32[]{:S(2)}) async-start(s32[4,1,128]{2,1,0:T(1,128)} %bitcast.7), calls=%async_computation | async-start | bytes 4096 | tf_op jit(solution)/shard_map/all_to_all | solution.py:81
  154.0 5.4 %slice.36 = bf16[512,4080]{1,0:T(8,128)(2,1)S(1)} slice(bf16[512,4096]{1,0:T(8,128)(2,1)} %bitcast.11), slice={[0:512], [16:4096]} | slice | bytes 8355840 | tf_op jit(solution)/shard_map/slice | solution.py:31
  159.5 5.4 %slice.35 = bf16[512,4064]{1,0:T(8,128)(2,1)S(1)} slice(bf16[512,4096]{1,0:T(8,128)(2,1)} %bitcast.11), slice={[0:512], [32:4096]} | slice | bytes 8323072 | tf_op jit(solution)/shard_map/slice | solution.py:31
  164.9 4.2 %select_select_fusion = bf16[512,4096]{1,0:T(8,128)(2,1)} fusion(bf16[512,4080]{1,0:T(8,128)(2,1)S(1)} %slice.36, bf16[512,4064]{1,0:T(8,128)(2,1)S(1)} %slice.35, pred[512]{0:T(512)(128)(4,1)S(1)} %bitcast.66, pred[512]{0:T(512)(128)(4,1)S(1)} %bitcast.65), kind=kLoop, calls=%fused_computation.5 | loop fusion | flops 4194304 | bytes 12534784 | tf_op jit(solution)/shard_map/jit(_where)/select_n | solution.py:91
  169.1 2.0 all-gather.5.cloned.1.call-done
  171.1 8.7 %reshape.117 = bf16[32,33,4096]{2,1,0:T(8,128)(2,1)} reshape(bf16[1,1056,4096]{2,1,0:T(8,128)(2,1)} %all-gather.5.cloned.1.call-done) | data formatting | bytes 17301504 | tf_op jit(solution)/shard_map/reshape | solution.py:93
  179.8 8.0 %slice.34 = bf16[32,32,4096]{2,1,0:T(8,128)(2,1)} slice(bf16[32,33,4096]{2,1,0:T(8,128)(2,1)} %reshape.117), slice={[0:32], [0:32], [0:4096]} | slice | bytes 16777216 | tf_op jit(solution)/shard_map/slice | solution.py:96
  187.8 14.0 %fusion = f32[1024,1024]{1,0:T(8,128)} fusion(bf16[1024,4096]{1,0:T(8,128)(2,1)} %bitcast.47, bf16[512,4096]{1,0:T(8,128)(2,1)S(1)} %copy-done.1, bf16[512,4096]{1,0:T(8,128)(2,1)} %bitcast.11), kind=kOutput, calls=%fused_computation | convolution fusion | flops 8606711808 | bytes 20971520 | tf_op jit(solution)/shard_map/dot_general | solution.py:98
  201.8 0.9 fusion.20
  202.7 0.1 reshape.122
  202.7 2.8 %fusion.10 = f32[1024,512]{1,0:T(8,128)S(1)} fusion(f32[1024,1024]{1,0:T(8,128)} %fusion, s32[512]{0:T(512)S(1)} %bitcast.61, s32[1024]{0:T(1024)S(1)} %reshape.122), kind=kLoop, calls=%fused_computation.31 | loop fusion | flops 2621440 | bytes 6297600 | tf_op jit(solution)/shard_map/jit(_where)/select_n | solution.py:44
  205.5 0.2 pad_reduce_fusion
  205.7 0.4 select_reduce_fusion.7
  206.1 0.4 fusion.15
  206.5 0.5 select_reduce_fusion.6
  207.0 0.5 fusion.14
  207.5 0.7 select_reduce_fusion.5
  208.2 0.7 fusion.26
  208.9 0.9 select_reduce_fusion.4
  209.8 0.8 fusion.13
  210.6 1.1 select_reduce_fusion.3
  211.7 1.0 fusion.19
  212.7 1.2 select_reduce_fusion.2
  213.9 1.2 fusion.12
  215.1 1.4 select_reduce_fusion.1
  216.5 1.3 select_reduce_fusion
  217.9 6.4 %all_to_all.28 = f32[4,128,8]{1,2,0:T(8,128)S(1)} all-to-all(f32[4,128,8]{1,2,0:T(8,128)S(1)} %bitcast.48), channel_id=1, replica_groups=mesh['blk_0'=4,'blk_1'=2,'blk_2'=4,'rep'=4] {'rep'}, dimensions={0} | all-to-all | bytes 32768 | tf_op jit(solution)/shard_map/all_to_all | solution.py:103
  224.3 1.0 fusion.16
  (25 shorter events, 0.3 us)
Async XLA Ops:
  6.5 72.7 %all-gather.3.cloned.1.call-start = ((), (), s32[]{:S(2)}) async-start(), calls=%async_computation.4 | async-start | bytes 5406720 | tf_op jit(solution)/shard_map/all_gather | solution.py:19
  27.4 143.7 %all-gather.5.cloned.1.call-start = ((), (), s32[]{:S(2)}) async-start(), calls=%async_computation.5 | async-start | bytes 10813440 | tf_op jit(solution)/shard_map/all_gather | solution.py:19
  85.2 0.7 copy-start.2
  85.2 2.3 copy-start.3
  85.2 2.3 %copy-start.4 = (s32[256]{0:T(256)S(1)}, s32[256]{0:T(256)}, u32[]{:S(2)}) copy-start(s32[256]{0:T(256)} %param.9) | copy-start | bytes 3076
  85.2 6.9 %copy-start = (bf16[256,4096]{1,0:T(8,128)(2,1)S(1)}, bf16[256,4096]{1,0:T(8,128)(2,1)}, u32[]{:S(2)}) copy-start(bf16[256,4096]{1,0:T(8,128)(2,1)} %param.6) | copy-start | bytes 6291460
  88.3 9.3 %all-to-all-start.2 = ((s32[4,1,128]{2,1,0:T(1,128)}), s32[4,1,128]{2,1,0:T(1,128)S(1)}, u32[]{:S(2)}, u32[]{:S(2)}) async-start(s32[4,1,128]{2,1,0:T(1,128)} %bitcast.12), calls=%async_computation.2 | async-start | bytes 4096 | tf_op jit(solution)/shard_map/all_to_all | solution.py:82
  97.6 52.4 %all-to-all-start.1 = ((bf16[4,128,4096]{2,1,0:T(8,128)(2,1)}), bf16[4,128,4096]{2,1,0:T(8,128)(2,1)}, u32[]{:S(2)}, u32[]{:S(2)}) async-start(bf16[4,128,4096]{2,1,0:T(8,128)(2,1)} %bitcast.46), calls=%async_computation.1 | async-start | bytes 8388608 | tf_op jit(solution)/shard_map/all_to_all | solution.py:80
  150.0 52.8 %all-to-all-start = ((s32[4,1,128]{2,1,0:T(1,128)}), s32[4,1,128]{2,1,0:T(1,128)S(1)}, u32[]{:S(2)}, u32[]{:S(2)}) async-start(s32[4,1,128]{2,1,0:T(1,128)} %bitcast.7), calls=%async_computation | async-start | bytes 4096 | tf_op jit(solution)/shard_map/all_to_all | solution.py:81
  179.8 8.0 %copy-start.1 = (bf16[512,4096]{1,0:T(8,128)(2,1)S(1)}, bf16[512,4096]{1,0:T(8,128)(2,1)}, u32[]{:S(2)}) copy-start(bf16[512,4096]{1,0:T(8,128)(2,1)} %select_select_fusion) | copy-start | bytes 12582916
Sparse Core Ops, SparseCore 0:
  27.5 51.6 all-gather.2
  85.3 85.6 all-gather.4
where the time goes:
time: 233 us; the launch traced here: 232 us
  waiting for transfers between devices  101 us (43%)
  local copies, waits for them, and re-layouts  35.1 us (15%)
  other arithmetic  26.8 us (12%)
  blocking collectives  23.6 us (10%)
  matrix products  19 us (8%)
  between operations  13.5 us (6%)
  starting transfers between devices  12.9 us (6%)
    all_gather x2, waiting for transfers between devices, gathered_by_axis(): x = lax.all_gather(x, axis, axis=dim, tiled=True)  53.8 us
    all_to_all x1, waiting for transfers between devices, on_device(): lax.all_to_all(send_q, 'rep', split_axis=0, concat_axis=0, tiled=True)  47.4 us
    all_gather x1, blocking collectives, gathered_by_axis(): x = lax.all_gather(x, axis, axis=dim, tiled=True)  17.2 us
    dot_general x1, matrix products, on_device(): lax.dot_general(blocks, both, (((1,), (1,)), ((), ())), preferred_element...  14 us
    slice x2, local copies, waits for them, and re-layouts, lower_bins(): return jnp.concatenate([rows[..., amount:], tail], axis=-1)  10.8 us
    reshape x1, local copies, waits for them, and re-layouts, on_device(): gathered_by_axis(packed_lib, ('blk_2', 'blk_0', 'blk_1'), 1)  8.74 us
    slice x1, local copies, waits for them, and re-layouts, on_device(): blocks = split[:, :lib_rows].reshape(-1, W)  7.98 us
    all_to_all x1, blocking collectives, on_device(): lax.all_to_all(results, 'rep', split_axis=0, concat_axis=0, tiled=True)  6.42 us
  transfers between devices with their start and end apart: 5, of which 3 were waited for; matrix products, arithmetic and copies ran while one was open for 24% of the time, Pallas kernels for 0%

commit v1 on v0

v1 whole, which is shorter than its diff:
```python
import jax
import jax.numpy as jnp
from jax import lax
from jax.sharding import Mesh
from jax.sharding import PartitionSpec as P

W = 4096
K = 8
NSHIFT = 2
SHIFT_BINS = 16
WIN = 16
CAP = 128
BLK = ("blk_0", "blk_1", "blk_2")
BLK_REP = ("blk_0", "blk_1", "blk_2", "rep")
ZRING = ("blk_1", "rep")


def ring_index(z, core):
    return (z // 2) * 4 + (z % 2) * 2 + core


UP = [(ring_index(z, 0), ring_index((z + 1) % 4, 0)) for z in range(4)] + [
    (ring_index(z, 1), ring_index((z + 3) % 4, 1)) for z in range(4)
]
CROSS = [(ring_index(z, 1), ring_index((z + 1) % 4, 0)) for z in range(4)] + [
    (ring_index(z, 0), ring_index((z + 3) % 4, 1)) for z in range(4)
]
SIBLING = [(ring_index(z, c), ring_index(z, 1 - c)) for z in range(4) for c in range(2)]


def inverse(perm):
    return [(b, a) for a, b in perm]


def unit_rows(raw):
    values = jnp.sqrt(raw.astype(jnp.float32))
    total = jnp.sum(values * values, axis=-1, keepdims=True)
    return (values * lax.rsqrt(total + 1e-06)).astype(jnp.bfloat16)


def lower_bins(rows, amount):
    tail = jnp.zeros(rows.shape[:-1] + (amount,), rows.dtype)
    return jnp.concatenate([rows[..., amount:], tail], axis=-1)


def slot_index(role, roles, capacity):
    labels = jnp.arange(roles, dtype=jnp.int32)
    onehot = (role[:, None] == labels[None, :]).astype(jnp.int32)
    before = jnp.cumsum(onehot, axis=0) - onehot
    place = jnp.sum(before * onehot, axis=1)
    return role * capacity + place


def top_rows(scores):
    height = scores.shape[0]
    position = lax.broadcasted_iota(jnp.int32, scores.shape, 0)
    picked = []
    for step in range(K):
        top = jnp.max(scores, axis=0)
        first = jnp.min(jnp.where(scores == top[None, :], position, height), axis=0)
        picked.append(top)
        scores = jnp.where(position == first[None, :], -3e38, scores)
    return jnp.stack(picked, axis=1)


def route(blocks, perms):
    return [blocks[0]] + [lax.ppermute(b, ZRING, p) for b, p in zip(blocks[1:], perms)]


def on_device(queries, query_group, query_bin, query_shift, library, library_bin):
    lib_rows = library.shape[1]
    z_lo = lax.axis_index("rep") // 2
    core = lax.axis_index("rep") % 2
    roles = 4
    slots = roles * CAP

    unit_lib = unit_rows(library[0])
    bin_row = jnp.pad(library_bin.astype(jnp.bfloat16), ((0, 0), (0, W - lib_rows)))
    packed_lib = jnp.concatenate([unit_lib, bin_row], axis=0)
    half = lax.all_gather(packed_lib, "blk_1", axis=0, tiled=True)
    full = lax.all_gather(half, ("blk_0", "blk_2"), axis=0, tiled=True)
    stride = lib_rows + 1
    blocks_n = full.shape[0] // stride
    lib_bins = full.reshape(blocks_n, stride, W)[:, lib_rows, :stride].reshape(-1)
    lib_bins = lib_bins.astype(jnp.int32)
    valid = (jnp.arange(full.shape[0], dtype=jnp.int32) % stride) != lib_rows

    unit_q = unit_rows(queries)
    group = query_group[:, 0]
    role = ((group // 2) != z_lo).astype(jnp.int32) * 2 + ((group % 2) != core).astype(jnp.int32)
    slot = slot_index(role, roles, CAP)
    slot_ids = jnp.arange(slots, dtype=jnp.int32)
    placed = slot[:, None] == slot_ids[None, :]
    placed_int = placed.astype(jnp.int32)
    send_q = lax.dot_general(
        placed.astype(jnp.bfloat16), unit_q, (((0,), (0,)), ((), ())),
        preferred_element_type=jnp.float32,
    ).astype(jnp.bfloat16).reshape(roles, CAP, W)
    send_bin = jnp.sum(placed_int * query_bin[:, None], axis=0).reshape(roles, CAP)
    send_shift = jnp.sum(placed_int * query_shift[:, None], axis=0).reshape(roles, CAP)
    send_meta = jnp.stack([send_bin, send_shift], axis=1)

    perms = (SIBLING, UP, CROSS)
    rows = jnp.concatenate(route([send_q[i] for i in range(roles)], perms), axis=0)
    meta = jnp.stack(route([send_meta[i] for i in range(roles)], perms), axis=0)
    flat_bin = meta[:, 0].reshape(-1)
    flat_shift = meta[:, 1].reshape(-1)
    total = rows.shape[0]

    moved = jnp.zeros_like(rows)
    for s in range(1, NSHIFT + 1):
        moved = jnp.where((flat_shift == s)[:, None], lower_bins(rows, s * SHIFT_BINS), moved)
    both = jnp.concatenate([rows, moved], axis=0)
    prod = lax.dot_general(full, both, (((1,), (1,)), ((), ())), preferred_element_type=jnp.float32)
    near = (jnp.abs(lib_bins[:, None] - flat_bin[None, :]) <= WIN) & valid[:, None]
    scores = jnp.where(near, jnp.maximum(prod[:, :total], prod[:, total:]), 0.0)
    scores = jnp.where(valid[:, None], scores, -1.0)
    best = top_rows(scores).reshape(roles, CAP, K)

    home = route([best[i] for i in range(roles)], tuple(inverse(p) for p in perms))
    home = jnp.concatenate(home, axis=0)
    return jnp.take(home, slot, axis=0)


def solution(mesh):
    split = Mesh(
        mesh.devices.reshape(4, 2, 4, mesh.shape["rep"]), ("blk_0", "blk_1", "blk_2", "rep")
    )
    in_specs = (
        P(BLK_REP, None),
        P(BLK_REP, None),
        P(BLK_REP),
        P(BLK_REP),
        P("rep", BLK, None),
        P("rep", BLK),
    )
    out_specs = P(BLK_REP, None)
    return jax.shard_map(
        on_device, mesh=split, in_specs=in_specs, out_specs=out_specs, check_vma=False
    )
```

time: 233 us -> 166 us (0.71)
  waiting for transfers between devices: 101 us -> 52.4 us
  blocking collectives: 23.6 us -> 12.5 us
  matrix products: 19 us -> 14.9 us
  starting transfers between devices: 12.9 us -> 9.28 us
    all_to_all x3 -> x0, waiting for transfers between devices: 47.4 us -> none  [the longest x1 47.4 us: on_device(): lax.all_to_all(send_q, 'rep', split_axis=0, concat_axis=0, tiled=True)]
    all_gather x2 -> x1, waiting for transfers between devices: 53.8 us -> 30.2 us  [on_device(): full = lax.all_gather(half, ('blk_0', 'blk_2'), axis=0, tiled=True)]
    ppermute x0 -> x9, waiting for transfers between devices: none -> 22.3 us  [route(): lax.ppermute(b, ZRING, p)]
    all_to_all x3 -> x0, starting transfers between devices: 12.8 us -> none  [the longest x1 4.97 us: on_device(): lax.all_to_all(send_q, 'rep', split_axis=0, concat_axis=0, tiled=True)]
    unnamed x10 -> x13, local copies, waits for them, and re-layouts: 0.66 us -> 12.3 us
    ppermute x0 -> x9, starting transfers between devices: none -> 9.27 us  [route(): lax.ppermute(b, ZRING, p)]
    select_n x2 -> x1, other arithmetic: 6.97 us -> 0.1 us  [on_device(): return jnp.take(home, slot, axis=0)]
    all_to_all x1 -> x0, blocking collectives: 6.42 us -> none  [on_device(): lax.all_to_all(results, 'rep', split_axis=0, concat_axis=0, tiled=True)]
  transfers between devices with their start and end apart: 5 -> 10, of which waited for: 3 -> 5; matrix products, arithmetic and copies ran while one was open for 24% -> 13% of each run, Pallas kernels for 0% -> 0%
where the time goes in v1:
time: 166 us; the launch traced here: 164 us
  waiting for transfers between devices  52.4 us (32%)
  local copies, waits for them, and re-layouts  35.5 us (21%)
  other arithmetic  25.8 us (16%)
  matrix products  14.9 us (9%)
  between operations  13.6 us (8%)
  blocking collectives  12.5 us (8%)
  starting transfers between devices  9.28 us (6%)
    all_gather x1, waiting for transfers between devices, on_device(): full = lax.all_gather(half, ('blk_0', 'blk_2'), axis=0, tiled=True)  30.2 us
    ppermute x9, waiting for transfers between devices, route(): lax.ppermute(b, ZRING, p)  22.3 us
    reshape x1, local copies, waits for them, and re-layouts, on_device(): full.reshape(blocks_n, stride, W)[:, lib_rows, :stride].reshape(-1)  13.2 us
    dot_general x1, matrix products, on_device(): lax.dot_general(full, both, (((1,), (1,)), ((), ())), preferred_element_t...  13 us
    all_gather x1, blocking collectives, on_device(): half = lax.all_gather(packed_lib, 'blk_1', axis=0, tiled=True)  12.5 us
    unnamed x13, local copies, waits for them, and re-layouts  12.3 us
    ppermute x9, starting transfers between devices, route(): lax.ppermute(b, ZRING, p)  9.27 us
    reduce_max x8, other arithmetic, top_rows(): top = jnp.max(scores, axis=0)  7.39 us
  transfers between devices with their start and end apart: 10, of which 5 were waited for; matrix products, arithmetic and copies ran while one was open for 13% of the time, Pallas kernels for 0%

profile of v1, /device:TPU:1, one launch (start us, length us, event | category | flops | bytes accessed | tf_op | source)
XLA Modules:
  0.0 164.1 jit_solution(16801492224332433308)
XLA Ops:
  6.5 1.4 fusion.15
  7.9 1.1 fusion.16
  9.1 0.7 convert_element_type.53
  9.7 12.5 %all-gather = bf16[2,33,4096]{2,1,0:T(8,128)(2,1)S(1)} all-gather(bf16[1,33,4096]{2,1,0:T(8,128)(2,1)S(1)} %fusion.18), channel_id=1, replica_groups=mesh['blk_0'=4,'blk_1'=2,'blk_2'=4,'rep'=4] {'blk_1'}, dimensions={0}, use_global_device_ids=true | all-gather | bytes 811008 | tf_op jit(solution)/shard_map/all_gather | solution.py:80
  22.3 0.9 reshape.119
  23.3 1.2 reduce-window.6
  24.9 1.4 multiply_reduce_fusion
  26.4 2.0 %convolution_convert_fusion = bf16[512,4096]{1,0:T(8,128)(2,1)S(1)} fusion(bf16[256,4096]{1,0:T(8,128)(2,1)S(1)} %copy-done, f32[256]{0:T(256)S(1)} %add_rsqrt_fusion, s32[256]{0:T(256)S(1)} %bitcast.72), kind=kOutput, calls=%fused_computation.1 | convolution fusion | flops 1079115776 | bytes 6293504 | tf_op jit(solution)/shard_map/dot_general | solution.py:95
  28.4 1.7 %fusion.39 = (bf16[128,4096]{1,0:T(8,128)(2,1)S(1)}, bf16[1024,4096]{1,0:T(8,128)(2,1)}, bf16[128,4096]{1,0:T(8,128)(2,1)S(1)}, bf16[128,4096]{1,0:T(8,128)(2,1)S(1)}, bf16[128,4096]{1,0:T(8,128)(2,1)S(1)}) fusion(bf16[512,4096]{1,0:T(8,128)(2,1)S(1)} %convolution_convert_fusion), kind=kLoop, calls=%fused_computation.106 | loop fusion | bytes 9437184 | tf_op jit(solution)/shard_map/slice | solution.py:104
  30.1 1.3 collective-permute-start.3
  31.3 3.1 %collective-permute-start.4 = (bf16[128,4096]{1,0:T(8,128)(2,1)S(1)}, bf16[128,4096]{1,0:T(8,128)(2,1)S(1)}, u32[]{:S(2)}, u32[]{:S(2)}) collective-permute-start(bf16[128,4096]{1,0:T(8,128)(2,1)S(1)} %get-tuple-element.15), channel_id=1, source_target_pairs={{0,2},{2,16},{16,18},{18,0},{1,19},{3,1},{17,3},{19,17},{4,6},{6,2... | collective-permute-start | bytes 3145736 | tf_op jit(solution)/shard_map/ppermute | solution.py:67
  34.7 0.6 collective-permute-start
  35.6 0.5 collective-permute-done
  36.1 1.5 collective-permute-start.2
  37.6 19.1 %collective-permute-done.1 = s32[2,128]{1,0:T(2,128)S(1)} collective-permute-done((s32[2,128]{1,0:T(2,128)S(1)}, s32[2,128]{1,0:T(2,128)S(1)}, u32[]{:S(2)}, u32[]{:S(2)}) %collective-permute-start.1) | collective-permute-done | bytes 1056 | tf_op jit(solution)/shard_map/ppermute | solution.py:67
  56.9 0.5 pad_maximum_fusion
  57.4 3.2 %slice.108 = bf16[512,4064]{1,0:T(8,128)(2,1)S(1)} slice(bf16[512,4096]{1,0:T(8,128)(2,1)S(1)} %pad_maximum_fusion), slice={[0:512], [32:4096]} | slice | bytes 8323072 | tf_op jit(solution)/shard_map/slice | solution.py:43
  60.6 3.2 %slice.109 = bf16[512,4080]{1,0:T(8,128)(2,1)S(1)} slice(bf16[512,4096]{1,0:T(8,128)(2,1)S(1)} %pad_maximum_fusion), slice={[0:512], [16:4096]} | slice | bytes 8355840 | tf_op jit(solution)/shard_map/slice | solution.py:43
  63.8 1.1 constant_dynamic-update-slice_fusion.2
  64.9 1.1 constant_dynamic-update-slice_fusion.1
  66.0 1.1 constant_dynamic-update-slice_fusion
  67.0 4.1 %select_dynamic-update-slice_fusion = bf16[1024,4096]{1,0:T(8,128)(2,1)} fusion(bf16[1024,4096]{1,0:T(8,128)(2,1)} %constant_dynamic-update-slice_fusion, bf16[512,4080]{1,0:T(8,128)(2,1)S(1)} %slice.109, bf16[512,4064]{1,0:T(8,128)(2,1)S(1)} %slice.108, pred[512]{0:T(512)(128)(4,1)S(1)} %get-tuple-element.22, pred[512]{0:T(512)(128)(4,1)S(1)} %get-tuple-element.21), kind=kLoop, calls=%fused_computation.3 | loop fusion | flops 4194304 | bytes 12534784 | tf_op jit(solution)/shard_map/concatenate | solution.py:113
  71.2 30.2 %all-gather.4.cloned.1.call-done = bf16[16,66,4096]{2,1,0:T(8,128)(2,1)} async-done(((bf16[1,66,4096]{2,1,0:T(8,128)(2,1)}), bf16[16,66,4096]{2,1,0:T(8,128)(2,1)}) %all-gather.4.cloned.1.call-update) | async-done | bytes 8650768 | tf_op jit(solution)/shard_map/all_gather | solution.py:81
  101.3 13.2 %reshape.107 = bf16[32,33,4096]{2,1,0:T(8,128)(2,1)} reshape(bf16[16,66,4096]{2,1,0:T(8,128)(2,1)} %all-gather.4.cloned.1.call-done) | data formatting | bytes 17301504 | tf_op jit(solution)/shard_map/reshape | solution.py:84
  114.5 0.9 fusion.21
  115.5 8.2 %reshape.120 = bf16[1056,4096]{1,0:T(8,128)(2,1)} reshape(bf16[16,66,4096]{2,1,0:T(8,128)(2,1)} %all-gather.4.cloned.1.call-done) | data formatting | bytes 17301504
  123.6 13.0 %fusion.41 = f32[1056,1024]{1,0:T(8,128)S(1)} fusion(bf16[1056,4096]{1,0:T(8,128)(2,1)} %reshape.120, bf16[1024,4096]{1,0:T(8,128)(2,1)} %select_dynamic-update-slice_fusion), kind=kOutput, calls=%fused_computation.108 | convolution fusion | flops 8858370048 | bytes 21364736 | tf_op jit(solution)/shard_map/dot_general | solution.py:114
  136.6 1.4 fusion.37
  138.0 0.4 select_reduce_fusion.7
  138.8 0.5 select_reduce_fusion.6
  139.3 0.5 fusion.12
  139.8 0.8 select_reduce_fusion.5
  140.6 0.7 fusion.36
  141.3 0.9 select_reduce_fusion.4
  142.2 0.8 fusion.11
  143.0 1.1 select_reduce_fusion.3
  144.2 1.0 fusion.20
  145.2 1.3 select_reduce_fusion.2
  146.5 1.2 fusion.10
  147.7 1.5 select_reduce_fusion.1
  149.2 1.4 select_reduce_fusion
  150.6 0.8 collective-permute-start.6
  151.4 1.3 collective-permute-start.7
  152.6 0.4 collective-permute-start.8
  153.1 1.9 %collective-permute-done.7 = f32[128,8]{0,1:T(8,128)S(1)} collective-permute-done((f32[128,8]{0,1:T(8,128)S(1)}, f32[128,8]{0,1:T(8,128)S(1)}, u32[]{:S(2)}, u32[]{:S(2)}) %collective-permute-start.7) | collective-permute-done | bytes 4128 | tf_op jit(solution)/shard_map/ppermute | solution.py:67
  155.0 0.6 collective-permute-done.8
  155.8 0.7 gather_fusion
  156.6 0.7 copy.37
  (44 shorter events, 1.8 us)
Async XLA Ops:
  6.5 16.7 %copy-start.1 = (s32[256,1]{0,1:T(1,128)S(1)}, s32[256,1]{0,1:T(1,128)}, u32[]{:S(2)}) copy-start(s32[256,1]{0,1:T(1,128)} %param.7) | copy-start | bytes 3076
  6.5 18.4 %copy-start = (bf16[256,4096]{1,0:T(8,128)(2,1)S(1)}, bf16[256,4096]{1,0:T(8,128)(2,1)}, u32[]{:S(2)}) copy-start(bf16[256,4096]{1,0:T(8,128)(2,1)} %param.6) | copy-start | bytes 6291460
  6.5 94.8 %all-gather.4.cloned.1.call-start = ((), (), s32[]{:S(2)}) async-start(), calls=%async_computation | async-start | bytes 10027008 | tf_op jit(solution)/shard_map/all_gather | solution.py:81
  28.4 6.1 %copy-start.2 = (s32[256]{0:T(256)S(1)}, s32[256]{0:T(256)}, u32[]{:S(2)}) copy-start(s32[256]{0:T(256)} %param.8) | copy-start | bytes 3076
  28.4 6.1 %copy-start.3 = (s32[256]{0:T(256)S(1)}, s32[256]{0:T(256)}, u32[]{:S(2)}) copy-start(s32[256]{0:T(256)} %param.9) | copy-start | bytes 3076
  30.1 26.7 %collective-permute-start.3 = (bf16[128,4096]{1,0:T(8,128)(2,1)S(1)}, bf16[128,4096]{1,0:T(8,128)(2,1)S(1)}, u32[]{:S(2)}, u32[]{:S(2)}) collective-permute-start(bf16[128,4096]{1,0:T(8,128)(2,1)S(1)} %get-tuple-element.16), channel_id=1, source_target_pairs={{0,1},{1,0},{2,3},{3,2},{16,17},{17,16},{18,19},{19,18},{4,5},{5,4... | collective-permute-start | bytes 3145736 | tf_op jit(solution)/shard_map/ppermute | solution.py:67
  31.3 25.5 %collective-permute-start.4 = (bf16[128,4096]{1,0:T(8,128)(2,1)S(1)}, bf16[128,4096]{1,0:T(8,128)(2,1)S(1)}, u32[]{:S(2)}, u32[]{:S(2)}) collective-permute-start(bf16[128,4096]{1,0:T(8,128)(2,1)S(1)} %get-tuple-element.15), channel_id=1, source_target_pairs={{0,2},{2,16},{16,18},{18,0},{1,19},{3,1},{17,3},{19,17},{4,6},{6,2... | collective-permute-start | bytes 3145736 | tf_op jit(solution)/shard_map/ppermute | solution.py:67
  34.5 22.4 %collective-permute-start.5 = (bf16[128,4096]{1,0:T(8,128)(2,1)S(1)}, bf16[128,4096]{1,0:T(8,128)(2,1)S(1)}, u32[]{:S(2)}, u32[]{:S(2)}) collective-permute-start(bf16[128,4096]{1,0:T(8,128)(2,1)S(1)} %get-tuple-element.14), channel_id=1, source_target_pairs={{1,2},{3,16},{17,18},{19,0},{0,19},{2,1},{16,3},{18,17},{5,6},{7,2... | collective-permute-start | bytes 3145736 | tf_op jit(solution)/shard_map/ppermute | solution.py:67
  34.7 1.4 collective-permute-start
  35.3 21.5 %collective-permute-start.1 = (s32[2,128]{1,0:T(2,128)S(1)}, s32[2,128]{1,0:T(2,128)S(1)}, u32[]{:S(2)}, u32[]{:S(2)}) collective-permute-start(s32[2,128]{1,0:T(2,128)S(1)} %get-tuple-element.26), channel_id=1, source_target_pairs={{0,2},{2,16},{16,18},{18,0},{1,19},{3,1},{17,3},{19,17},{4,6},{6,2... | collective-permute-start | bytes 3080 | tf_op jit(solution)/shard_map/ppermute | solution.py:67
  36.1 20.7 %collective-permute-start.2 = (s32[2,128]{1,0:T(2,128)S(1)}, s32[2,128]{1,0:T(2,128)S(1)}, u32[]{:S(2)}, u32[]{:S(2)}) collective-permute-start(s32[2,128]{1,0:T(2,128)S(1)} %get-tuple-element.25), channel_id=1, source_target_pairs={{1,2},{3,16},{17,18},{19,0},{0,19},{2,1},{16,3},{18,17},{5,6},{7,2... | collective-permute-start | bytes 3080 | tf_op jit(solution)/shard_map/ppermute | solution.py:67
  150.6 2.5 %collective-permute-start.6 = (f32[128,8]{0,1:T(8,128)S(1)}, f32[128,8]{0,1:T(8,128)S(1)}, u32[]{:S(2)}, u32[]{:S(2)}) collective-permute-start(f32[128,8]{0,1:T(8,128)S(1)} %get-tuple-element.20), channel_id=1, source_target_pairs={{1,0},{0,1},{3,2},{2,3},{17,16},{16,17},{19,18},{18,19},{5,4},{4,5... | collective-permute-start | bytes 12296 | tf_op jit(solution)/shard_map/ppermute | solution.py:67
  151.4 3.7 %collective-permute-start.7 = (f32[128,8]{0,1:T(8,128)S(1)}, f32[128,8]{0,1:T(8,128)S(1)}, u32[]{:S(2)}, u32[]{:S(2)}) collective-permute-start(f32[128,8]{0,1:T(8,128)S(1)} %get-tuple-element.19), channel_id=1, source_target_pairs={{2,0},{16,2},{18,16},{0,18},{19,1},{1,3},{3,17},{17,19},{6,4},{20,... | collective-permute-start | bytes 12296 | tf_op jit(solution)/shard_map/ppermute | solution.py:67
  152.6 3.0 %collective-permute-start.8 = (f32[128,8]{0,1:T(8,128)S(1)}, f32[128,8]{0,1:T(8,128)S(1)}, u32[]{:S(2)}, u32[]{:S(2)}) collective-permute-start(f32[128,8]{0,1:T(8,128)S(1)} %get-tuple-element.18), channel_id=1, source_target_pairs={{2,1},{16,3},{18,17},{0,19},{19,0},{1,2},{3,16},{17,18},{6,5},{20,... | collective-permute-start | bytes 12296 | tf_op jit(solution)/shard_map/ppermute | solution.py:67
Sparse Core Ops, SparseCore 0:
  23.4 77.9 all-gather.3

commit v2 on v1

--- a/solution.py
+++ b/solution.py
@@ -51,16 +51,34 @@
     return role * capacity + place
 
 
+SORT8 = (
+    ((0, 1), (2, 3), (4, 5), (6, 7)),
+    ((0, 2), (1, 3), (4, 6), (5, 7)),
+    ((1, 2), (5, 6)),
+    ((0, 4), (1, 5), (2, 6), (3, 7)),
+    ((2, 4), (3, 5)),
+    ((1, 2), (3, 4), (5, 6)),
+)
+
+
+def exchange(lists, i, j):
+    lists[i], lists[j] = jnp.maximum(lists[i], lists[j]), jnp.minimum(lists[i], lists[j])
+
+
 def top_rows(scores):
-    height = scores.shape[0]
-    position = lax.broadcasted_iota(jnp.int32, scores.shape, 0)
-    picked = []
-    for step in range(K):
-        top = jnp.max(scores, axis=0)
-        first = jnp.min(jnp.where(scores == top[None, :], position, height), axis=0)
-        picked.append(top)
-        scores = jnp.where(position == first[None, :], -3e38, scores)
-    return jnp.stack(picked, axis=1)
+    depth = scores.shape[0] // K
+    lists = [scores[k * depth:(k + 1) * depth] for k in range(K)]
+    for stage in SORT8:
+        for i, j in stage:
+            exchange(lists, i, j)
+    while depth > 1:
+        depth //= 2
+        lists = [jnp.maximum(lists[i][:depth], lists[K - 1 - i][depth:]) for i in range(K)]
+        for step in (4, 2, 1):
+            for i in range(K):
+                if (i // step) % 2 == 0:
+                    exchange(lists, i, i + step)
+    return jnp.concatenate(lists, axis=0).T
 
 
 def route(blocks, perms):
@@ -74,16 +92,13 @@
     roles = 4
     slots = roles * CAP
 
+    z_hi = lax.axis_index("blk_1")
     unit_lib = unit_rows(library[0])
-    bin_row = jnp.pad(library_bin.astype(jnp.bfloat16), ((0, 0), (0, W - lib_rows)))
-    packed_lib = jnp.concatenate([unit_lib, bin_row], axis=0)
-    half = lax.all_gather(packed_lib, "blk_1", axis=0, tiled=True)
-    full = lax.all_gather(half, ("blk_0", "blk_2"), axis=0, tiled=True)
-    stride = lib_rows + 1
-    blocks_n = full.shape[0] // stride
-    lib_bins = full.reshape(blocks_n, stride, W)[:, lib_rows, :stride].reshape(-1)
-    lib_bins = lib_bins.astype(jnp.int32)
-    valid = (jnp.arange(full.shape[0], dtype=jnp.int32) % stride) != lib_rows
+    partner = lax.ppermute(unit_lib, "blk_1", [(0, 1), (1, 0)])
+    pair = jnp.where(z_hi == 0, jnp.concatenate([unit_lib, partner], axis=0),
+                     jnp.concatenate([partner, unit_lib], axis=0))
+    full = lax.all_gather(pair, ("blk_0", "blk_2"), axis=0, tiled=True)
+    lib_bins = lax.all_gather(library_bin[0], ("blk_0", "blk_2", "blk_1"), axis=0, tiled=True)
 
     unit_q = unit_rows(queries)
     group = query_group[:, 0]
@@ -112,9 +127,8 @@
         moved = jnp.where((flat_shift == s)[:, None], lower_bins(rows, s * SHIFT_BINS), moved)
     both = jnp.concatenate([rows, moved], axis=0)
     prod = lax.dot_general(full, both, (((1,), (1,)), ((), ())), preferred_element_type=jnp.float32)
-    near = (jnp.abs(lib_bins[:, None] - flat_bin[None, :]) <= WIN) & valid[:, None]
+    near = jnp.abs(lib_bins[:, None] - flat_bin[None, :]) <= WIN
     scores = jnp.where(near, jnp.maximum(prod[:, :total], prod[:, total:]), 0.0)
-    scores = jnp.where(valid[:, None], scores, -1.0)
     best = top_rows(scores).reshape(roles, CAP, K)
 
     home = route([best[i] for i in range(roles)], tuple(inverse(p) for p in perms))

time: 166 us -> 125 us (0.75)
  waiting for transfers between devices: 52.4 us -> 14 us
  blocking collectives: 12.5 us -> 33.5 us
  local copies, waits for them, and re-layouts: 35.5 us -> 15.8 us
  other arithmetic: 25.8 us -> 17.4 us
  starting transfers between devices: 9.28 us -> 13.3 us
    unnamed x0 -> x1, blocking collectives: none -> 33.5 us
    all_gather x1, waiting for transfers between devices: 30.2 us -> 5.33 us  [on_device(): full = lax.all_gather(pair, ('blk_0', 'blk_2'), axis=0, tiled=True)]
    ppermute x9, waiting for transfers between devices: 22.3 us -> 2.6 us  [route(): lax.ppermute(b, ZRING, p)]
    reshape x1 -> x0, local copies, waits for them, and re-layouts: 13.2 us -> none  [on_device(): full.reshape(blocks_n, stride, W)[:, lib_rows, :stride].reshape(-1)]
    all_gather x1 -> x0, blocking collectives: 12.5 us -> none  [on_device(): half = lax.all_gather(packed_lib, 'blk_1', axis=0, tiled=True)]
    reduce_max x8 -> x0, other arithmetic: 7.39 us -> none  [top_rows(): top = jnp.max(scores, axis=0)]
    unnamed x13 -> x18, local copies, waits for them, and re-layouts: 12.3 us -> 5.16 us
    reduce_min x7 -> x0, other arithmetic: 6.51 us -> none  [top_rows(): first = jnp.min(jnp.where(scores == top[None, :], position, height), axis=0)]
  transfers between devices with their start and end apart: 10 -> 11, of which waited for: 5 -> 4; matrix products, arithmetic and copies ran while one was open for 13% -> 22% of each run, Pallas kernels for 0% -> 0%
where the time goes in v2:
time: 125 us; the launch traced here: 123 us
  blocking collectives  33.5 us (27%)
  other arithmetic  17.4 us (14%)
  local copies, waits for them, and re-layouts  15.8 us (13%)
  matrix products  14.9 us (12%)
  between operations  14.5 us (12%)
  waiting for transfers between devices  14 us (11%)
  starting transfers between devices  13.3 us (11%)
    unnamed x1, blocking collectives  33.5 us
    dot_general x1, matrix products, on_device(): lax.dot_general(full, both, (((1,), (1,)), ((), ())), preferred_element_t...  12.9 us
    ppermute x9, starting transfers between devices, route(): lax.ppermute(b, ZRING, p)  8.8 us
    slice x2, local copies, waits for them, and re-layouts, lower_bins(): return jnp.concatenate([rows[..., amount:], tail], axis=-1)  6.43 us
    ppermute x1, waiting for transfers between devices, on_device(): partner = lax.ppermute(unit_lib, 'blk_1', [(0, 1), (1, 0)])  6.03 us
    all_gather x1, waiting for transfers between devices, on_device(): full = lax.all_gather(pair, ('blk_0', 'blk_2'), axis=0, tiled=True)  5.33 us
    unnamed x18, local copies, waits for them, and re-layouts  5.16 us
    ppermute x1, starting transfers between devices, on_device(): partner = lax.ppermute(unit_lib, 'blk_1', [(0, 1), (1, 0)])  4.51 us
  transfers between devices with their start and end apart: 11, of which 4 were waited for; matrix products, arithmetic and copies ran while one was open for 22% of the time, Pallas kernels for 0%

profile of v2, /device:TPU:1, one launch (start us, length us, event | category | flops | bytes accessed | tf_op | source)
XLA Modules:
  0.0 123.4 jit_solution(3923577876884454957)
XLA Ops:
  6.5 1.4 %fusion.2 = f32[32]{0:T(128)S(1)} fusion(bf16[1,32,4096]{2,1,0:T(8,128)(2,1)} %param.10), kind=kLoop, calls=%fused_computation.14 | loop fusion | flops 393184 | bytes 262272 | tf_op jit(solution)/shard_map/reduce_sum | solution.py:37
  7.9 1.1 fusion.3
  9.1 4.5 %collective-permute-start.3 = (bf16[32,4096]{1,0:T(8,128)(2,1)S(1)}, bf16[32,4096]{1,0:T(8,128)(2,1)S(1)}, u32[]{:S(2)}, u32[]{:S(2)}) collective-permute-start(bf16[32,4096]{1,0:T(8,128)(2,1)S(1)} %fusion.3), channel_id=1, source_target_pairs={{0,16},{16,0},{1,17},{17,1},{2,18},{18,2},{3,19},{19,3},{4,20},{20... | collective-permute-start | bytes 786440 | tf_op jit(solution)/shard_map/ppermute | solution.py:97
  13.6 6.0 %collective-permute-done.3 = bf16[32,4096]{1,0:T(8,128)(2,1)S(1)} collective-permute-done((bf16[32,4096]{1,0:T(8,128)(2,1)S(1)}, bf16[32,4096]{1,0:T(8,128)(2,1)S(1)}, u32[]{:S(2)}, u32[]{:S(2)}) %collective-permute-start.3) | collective-permute-done | bytes 262176 | tf_op jit(solution)/shard_map/ppermute | solution.py:97
  19.6 0.9 maximum_select_fusion
  20.5 0.7 fusion.51
  21.3 1.2 reduce-window.6
  22.5 0.1 slice.570
  22.6 0.1 copy.18
  22.7 0.1 copy.19
  22.9 3.0 %multiply_reduce_fusion = f32[256]{0:T(256)S(1)} fusion(bf16[256,4096]{1,0:T(8,128)(2,1)} %param.6), kind=kLoop, calls=%fused_computation.5 | loop fusion | flops 3145472 | bytes 2098176 | tf_op jit(solution)/shard_map/reduce_sum | solution.py:37
  26.0 2.0 %convolution_convert_fusion = bf16[512,4096]{1,0:T(8,128)(2,1)S(1)} fusion(bf16[256,4096]{1,0:T(8,128)(2,1)S(1)} %copy-done, f32[256]{0:T(256)S(1)} %add_rsqrt_fusion, s32[256]{0:T(256)S(1)} %bitcast.60), kind=kOutput, calls=%fused_computation.1 | convolution fusion | flops 1079115776 | bytes 6293504 | tf_op jit(solution)/shard_map/dot_general | solution.py:110
  28.0 2.3 %fusion.127 = (bf16[128,4096]{1,0:T(8,128)(2,1)S(1)}, bf16[1024,4096]{1,0:T(8,128)(2,1)}, bf16[128,4096]{1,0:T(8,128)(2,1)}, bf16[128,4096]{1,0:T(8,128)(2,1)}, bf16[128,4096]{1,0:T(8,128)(2,1)}) fusion(bf16[512,4096]{1,0:T(8,128)(2,1)S(1)} %convolution_convert_fusion), kind=kLoop, calls=%fused_computation.256 | loop fusion | bytes 9437184 | tf_op jit(solution)/shard_map/slice | solution.py:119
  30.4 1.2 collective-permute-start.4
  31.6 3.1 %collective-permute-start.5 = (bf16[128,4096]{1,0:T(8,128)(2,1)}, bf16[128,4096]{1,0:T(8,128)(2,1)S(1)}, u32[]{:S(2)}, u32[]{:S(2)}) collective-permute-start(bf16[128,4096]{1,0:T(8,128)(2,1)} %get-tuple-element.102), channel_id=1, source_target_pairs={{0,2},{2,16},{16,18},{18,0},{1,19},{3,1},{17,3},{19,17},{4,6},{6,2... | collective-permute-start | bytes 3145736 | tf_op jit(solution)/shard_map/ppermute | solution.py:85
  34.7 0.2 select_reduce_fusion.1
  34.9 0.6 collective-permute-start
  35.5 0.3 collective-permute-start.1
  35.8 0.6 dynamic-slice
  37.1 0.1 bitcast_dynamic-update-slice_fusion
  37.2 1.1 collective-permute-start.2
  38.3 33.5 %all-reduce.2 = s32[1024]{0:T(1024)S(1)} all-reduce(s32[1024]{0:T(1024)S(1)} %bitcast_dynamic-update-slice_fusion), channel_id=2, replica_groups=mesh['blk_0'=4,'blk_1'=2,'blk_2'=4,'rep'=4] {'blk_0','blk_2','blk_1'}, use_global_device_ids=true, to_apply=%add.2 | all-reduce | flops 1024 | bytes 8192
  71.9 1.6 %pad_maximum_fusion = bf16[512,4096]{1,0:T(8,128)(2,1)S(1)} fusion(bf16[128,4096]{1,0:T(8,128)(2,1)} %collective-permute-done.6, bf16[128,4096]{1,0:T(8,128)(2,1)S(1)} %collective-permute-done.5, bf16[128,4096]{1,0:T(8,128)(2,1)S(1)} %collective-permute-done.4, bf16[128,4096]{1,0:T(8,128)(2,1)S(1)} %get-tuple-element.99), kind=kLoop, calls=%fused_computation.2 | loop fusion | flops 16777216 | bytes 8388608 | tf_op jit(solution)/shard_map/concatenate | solution.py:119
  73.5 3.2 %slice.583 = bf16[512,4064]{1,0:T(8,128)(2,1)S(1)} slice(bf16[512,4096]{1,0:T(8,128)(2,1)S(1)} %pad_maximum_fusion), slice={[0:512], [32:4096]} | slice | bytes 8323072 | tf_op jit(solution)/shard_map/slice | solution.py:43
  76.8 3.2 %slice.584 = bf16[512,4080]{1,0:T(8,128)(2,1)S(1)} slice(bf16[512,4096]{1,0:T(8,128)(2,1)S(1)} %pad_maximum_fusion), slice={[0:512], [16:4096]} | slice | bytes 8355840 | tf_op jit(solution)/shard_map/slice | solution.py:43
  80.0 1.1 constant_dynamic-update-slice_fusion.2
  81.1 1.0 constant_dynamic-update-slice_fusion.1
  82.1 2.3 %constant_dynamic-update-slice_fusion = bf16[1024,4096]{1,0:T(8,128)(2,1)} fusion(bf16[1024,4096]{1,0:T(8,128)(2,1)} %constant_dynamic-update-slice_fusion.1, bf16[128,4096]{1,0:T(8,128)(2,1)} %collective-permute-done.6), kind=kLoop, calls=%fused_computation.125 | loop fusion | bytes 2097152
  84.4 4.1 %select_dynamic-update-slice_fusion = bf16[1024,4096]{1,0:T(8,128)(2,1)} fusion(bf16[1024,4096]{1,0:T(8,128)(2,1)} %constant_dynamic-update-slice_fusion, bf16[512,4080]{1,0:T(8,128)(2,1)S(1)} %slice.584, bf16[512,4064]{1,0:T(8,128)(2,1)S(1)} %slice.583, pred[512]{0:T(512)(128)(4,1)S(1)} %get-tuple-element.161, pred[512]{0:T(512)(128)(4,1)S(1)} %get-tuple-element.160), kind=kLoop, calls=%fused_computation.3 | loop fusion | flops 4194304 | bytes 12534784 | tf_op jit(solution)/shard_map/concatenate | solution.py:128
  88.5 5.3 %all-gather.3.cloned.1.call-done = bf16[1024,4096]{1,0:T(8,128)(2,1)} async-done(((bf16[64,4096]{1,0:T(8,128)(2,1)}), bf16[1024,4096]{1,0:T(8,128)(2,1)}) %all-gather.3.cloned.1.call-update) | async-done | bytes 8388624 | tf_op jit(solution)/shard_map/all_gather | solution.py:100
  93.9 12.9 %fusion.129 = f32[1024,1024]{1,0:T(8,128)S(1)} fusion(bf16[1024,4096]{1,0:T(8,128)(2,1)} %all-gather.3.cloned.1.call-done, bf16[1024,4096]{1,0:T(8,128)(2,1)} %select_dynamic-update-slice_fusion), kind=kOutput, calls=%fused_computation.258 | convolution fusion | flops 8589934592 | bytes 20971520 | tf_op jit(solution)/shard_map/dot_general | solution.py:129
  106.8 0.5 fusion
  107.3 0.3 minimum_minimum_fusion.4
  107.7 0.4 minimum_maximum_fusion.1
  108.1 0.3 minimum_maximum_fusion
  108.4 0.2 minimum_minimum_fusion.6
  108.6 0.2 maximum_maximum_fusion.3
  109.0 0.1 minimum_minimum_fusion.8
  109.1 0.1 maximum_maximum_fusion.5
  109.9 0.7 collective-permute-start.7
  110.6 1.3 %collective-permute-start.8 = (f32[128,8]{0,1:T(8,128)S(1)}, f32[128,8]{0,1:T(8,128)S(1)}, u32[]{:S(2)}, u32[]{:S(2)}) collective-permute-start(f32[128,8]{0,1:T(8,128)S(1)} %get-tuple-element.146), channel_id=1, source_target_pairs={{2,0},{16,2},{18,16},{0,18},{19,1},{1,3},{3,17},{17,19},{6,4},{20,... | collective-permute-start | bytes 12296 | tf_op jit(solution)/shard_map/ppermute | solution.py:85
  111.9 0.4 collective-permute-start.9
  112.3 1.9 %collective-permute-done.8 = f32[128,8]{0,1:T(8,128)S(1)} collective-permute-done((f32[128,8]{0,1:T(8,128)S(1)}, f32[128,8]{0,1:T(8,128)S(1)}, u32[]{:S(2)}, u32[]{:S(2)}) %collective-permute-start.8) | collective-permute-done | bytes 4128 | tf_op jit(solution)/shard_map/ppermute | solution.py:85
  114.3 0.6 collective-permute-done.9
  114.9 0.1 copy.23
  115.0 0.7 gather_fusion
  115.8 0.1 broadcast_select_fusion
  115.9 0.7 copy.24
  (63 shorter events, 0.9 us)
Async XLA Ops:
  6.5 19.4 %copy-start.1 = (s32[256,1]{0,1:T(1,128)S(1)}, s32[256,1]{0,1:T(1,128)}, u32[]{:S(2)}) copy-start(s32[256,1]{0,1:T(1,128)} %param.7) | copy-start | bytes 3076
  6.5 19.4 %copy-start = (bf16[256,4096]{1,0:T(8,128)(2,1)S(1)}, bf16[256,4096]{1,0:T(8,128)(2,1)}, u32[]{:S(2)}) copy-start(bf16[256,4096]{1,0:T(8,128)(2,1)} %param.6) | copy-start | bytes 6291460
  6.5 87.3 %all-gather.3.cloned.1.call-start = ((), (), s32[]{:S(2)}) async-start(), calls=%async_computation | async-start | bytes 8912896 | tf_op jit(solution)/shard_map/all_gather | solution.py:100
  9.1 10.5 %collective-permute-start.3 = (bf16[32,4096]{1,0:T(8,128)(2,1)S(1)}, bf16[32,4096]{1,0:T(8,128)(2,1)S(1)}, u32[]{:S(2)}, u32[]{:S(2)}) collective-permute-start(bf16[32,4096]{1,0:T(8,128)(2,1)S(1)} %fusion.3), channel_id=1, source_target_pairs={{0,16},{16,0},{1,17},{17,1},{2,18},{18,2},{3,19},{19,3},{4,20},{20... | collective-permute-start | bytes 786440 | tf_op jit(solution)/shard_map/ppermute | solution.py:97
  28.0 6.7 %copy-start.2 = (s32[256]{0:T(256)S(1)}, s32[256]{0:T(256)}, u32[]{:S(2)}) copy-start(s32[256]{0:T(256)} %param.8) | copy-start | bytes 3076
  28.0 6.7 %copy-start.3 = (s32[256]{0:T(256)S(1)}, s32[256]{0:T(256)}, u32[]{:S(2)}) copy-start(s32[256]{0:T(256)} %param.9) | copy-start | bytes 3076
  28.0 7.8 %copy-start.5 = (u32[128]{0:T(128)S(1)}, u32[128]{0:T(128)}, u32[]{:S(2)}) copy-start(u32[128]{0:T(128)} %constant.98) | copy-start | bytes 1540
  28.0 9.0 %copy-start.4 = (s32[1,32]{1,0:T(1,128)S(1)}, s32[1,32]{1,0:T(1,128)}, u32[]{:S(2)}) copy-start(s32[1,32]{1,0:T(1,128)} %param.11) | copy-start | bytes 388
  30.4 41.5 %collective-permute-start.4 = (bf16[128,4096]{1,0:T(8,128)(2,1)}, bf16[128,4096]{1,0:T(8,128)(2,1)S(1)}, u32[]{:S(2)}, u32[]{:S(2)}) collective-permute-start(bf16[128,4096]{1,0:T(8,128)(2,1)} %get-tuple-element.103), channel_id=1, source_target_pairs={{0,1},{1,0},{2,3},{3,2},{16,17},{17,16},{18,19},{19,18},{4,5},{5,4... | collective-permute-start | bytes 3145736 | tf_op jit(solution)/shard_map/ppermute | solution.py:85
  31.6 40.3 %collective-permute-start.5 = (bf16[128,4096]{1,0:T(8,128)(2,1)}, bf16[128,4096]{1,0:T(8,128)(2,1)S(1)}, u32[]{:S(2)}, u32[]{:S(2)}) collective-permute-start(bf16[128,4096]{1,0:T(8,128)(2,1)} %get-tuple-element.102), channel_id=1, source_target_pairs={{0,2},{2,16},{16,18},{18,0},{1,19},{3,1},{17,3},{19,17},{4,6},{6,2... | collective-permute-start | bytes 3145736 | tf_op jit(solution)/shard_map/ppermute | solution.py:85
  34.7 37.2 %collective-permute-start.6 = (bf16[128,4096]{1,0:T(8,128)(2,1)}, bf16[128,4096]{1,0:T(8,128)(2,1)}, u32[]{:S(2)}, u32[]{:S(2)}) collective-permute-start(bf16[128,4096]{1,0:T(8,128)(2,1)} %get-tuple-element.101), channel_id=1, source_target_pairs={{1,2},{3,16},{17,18},{19,0},{0,19},{2,1},{16,3},{18,17},{5,6},{7,2... | collective-permute-start | bytes 3145736 | tf_op jit(solution)/shard_map/ppermute | solution.py:85
  34.9 2.3 %collective-permute-start = (s32[2,128]{1,0:T(2,128)S(1)}, s32[2,128]{1,0:T(2,128)S(1)}, u32[]{:S(2)}, u32[]{:S(2)}) collective-permute-start(s32[2,128]{1,0:T(2,128)S(1)} %get-tuple-element.163), channel_id=1, source_target_pairs={{0,1},{1,0},{2,3},{3,2},{16,17},{17,16},{18,19},{19,18},{4,5},{5,4... | collective-permute-start | bytes 3080 | tf_op jit(solution)/shard_map/ppermute | solution.py:85
  35.5 36.3 %collective-permute-start.1 = (s32[2,128]{1,0:T(2,128)S(1)}, s32[2,128]{1,0:T(2,128)S(1)}, u32[]{:S(2)}, u32[]{:S(2)}) collective-permute-start(s32[2,128]{1,0:T(2,128)S(1)} %get-tuple-element.165), channel_id=1, source_target_pairs={{0,2},{2,16},{16,18},{18,0},{1,19},{3,1},{17,3},{19,17},{4,6},{6,2... | collective-permute-start | bytes 3080 | tf_op jit(solution)/shard_map/ppermute | solution.py:85
  37.2 34.6 %collective-permute-start.2 = (s32[2,128]{1,0:T(2,128)S(1)}, s32[2,128]{1,0:T(2,128)S(1)}, u32[]{:S(2)}, u32[]{:S(2)}) collective-permute-start(s32[2,128]{1,0:T(2,128)S(1)} %get-tuple-element.164), channel_id=1, source_target_pairs={{1,2},{3,16},{17,18},{19,0},{0,19},{2,1},{16,3},{18,17},{5,6},{7,2... | collective-permute-start | bytes 3080 | tf_op jit(solution)/shard_map/ppermute | solution.py:85
  109.9 2.5 %collective-permute-start.7 = (f32[128,8]{0,1:T(8,128)S(1)}, f32[128,8]{0,1:T(8,128)S(1)}, u32[]{:S(2)}, u32[]{:S(2)}) collective-permute-start(f32[128,8]{0,1:T(8,128)S(1)} %get-tuple-element.147), channel_id=1, source_target_pairs={{1,0},{0,1},{3,2},{2,3},{17,16},{16,17},{19,18},{18,19},{5,4},{4,5... | collective-permute-start | bytes 12296 | tf_op jit(solution)/shard_map/ppermute | solution.py:85
  110.6 3.7 %collective-permute-start.8 = (f32[128,8]{0,1:T(8,128)S(1)}, f32[128,8]{0,1:T(8,128)S(1)}, u32[]{:S(2)}, u32[]{:S(2)}) collective-permute-start(f32[128,8]{0,1:T(8,128)S(1)} %get-tuple-element.146), channel_id=1, source_target_pairs={{2,0},{16,2},{18,16},{0,18},{19,1},{1,3},{3,17},{17,19},{6,4},{20,... | collective-permute-start | bytes 12296 | tf_op jit(solution)/shard_map/ppermute | solution.py:85
  111.9 3.0 %collective-permute-start.9 = (f32[128,8]{0,1:T(8,128)S(1)}, f32[128,8]{0,1:T(8,128)S(1)}, u32[]{:S(2)}, u32[]{:S(2)}) collective-permute-start(f32[128,8]{0,1:T(8,128)S(1)} %get-tuple-element.145), channel_id=1, source_target_pairs={{2,1},{16,3},{18,17},{0,19},{19,0},{1,2},{3,16},{17,18},{6,5},{20,... | collective-permute-start | bytes 12296 | tf_op jit(solution)/shard_map/ppermute | solution.py:85
Sparse Core Ops, SparseCore 0:
  20.6 73.1 all-gather.2

commit v3 on v2

--- a/solution.py
+++ b/solution.py
@@ -10,6 +10,7 @@
 SHIFT_BINS = 16
 WIN = 16
 CAP = 128
+LANE = 128
 BLK = ("blk_0", "blk_1", "blk_2")
 BLK_REP = ("blk_0", "blk_1", "blk_2", "rep")
 ZRING = ("blk_1", "rep")
@@ -65,6 +66,15 @@
     lists[i], lists[j] = jnp.maximum(lists[i], lists[j]), jnp.minimum(lists[i], lists[j])
 
 
+def bitonic_merge(first, second, depth):
+    lists = [jnp.maximum(first[i][:depth], second[K - 1 - i][:depth]) for i in range(K)]
+    for step in (4, 2, 1):
+        for i in range(K):
+            if (i // step) % 2 == 0:
+                exchange(lists, i, i + step)
+    return lists
+
+
 def top_rows(scores):
     depth = scores.shape[0] // K
     lists = [scores[k * depth:(k + 1) * depth] for k in range(K)]
@@ -73,12 +83,8 @@
             exchange(lists, i, j)
     while depth > 1:
         depth //= 2
-        lists = [jnp.maximum(lists[i][:depth], lists[K - 1 - i][depth:]) for i in range(K)]
-        for step in (4, 2, 1):
-            for i in range(K):
-                if (i // step) % 2 == 0:
-                    exchange(lists, i, i + step)
-    return jnp.concatenate(lists, axis=0).T
+        lists = bitonic_merge(lists, [a[depth:] for a in lists], depth)
+    return lists
 
 
 def route(blocks, perms):
@@ -86,19 +92,17 @@
 
 
 def on_device(queries, query_group, query_bin, query_shift, library, library_bin):
-    lib_rows = library.shape[1]
     z_lo = lax.axis_index("rep") // 2
     core = lax.axis_index("rep") % 2
     roles = 4
     slots = roles * CAP
 
-    z_hi = lax.axis_index("blk_1")
     unit_lib = unit_rows(library[0])
-    partner = lax.ppermute(unit_lib, "blk_1", [(0, 1), (1, 0)])
-    pair = jnp.where(z_hi == 0, jnp.concatenate([unit_lib, partner], axis=0),
-                     jnp.concatenate([partner, unit_lib], axis=0))
-    full = lax.all_gather(pair, ("blk_0", "blk_2"), axis=0, tiled=True)
-    lib_bins = lax.all_gather(library_bin[0], ("blk_0", "blk_2", "blk_1"), axis=0, tiled=True)
+    bin_cols = jnp.pad(library_bin[0].astype(jnp.bfloat16)[:, None], ((0, 0), (0, LANE - 1)))
+    packed = jnp.concatenate([unit_lib, bin_cols], axis=1)
+    partner = lax.ppermute(packed, "blk_1", [(0, 1), (1, 0)])
+    near_lib = lax.all_gather(packed, ("blk_0", "blk_2"), axis=0, tiled=True)
+    far_lib = lax.all_gather(partner, ("blk_0", "blk_2"), axis=0, tiled=True)
 
     unit_q = unit_rows(queries)
     group = query_group[:, 0]
@@ -125,11 +129,16 @@
     moved = jnp.zeros_like(rows)
     for s in range(1, NSHIFT + 1):
         moved = jnp.where((flat_shift == s)[:, None], lower_bins(rows, s * SHIFT_BINS), moved)
-    both = jnp.concatenate([rows, moved], axis=0)
-    prod = lax.dot_general(full, both, (((1,), (1,)), ((), ())), preferred_element_type=jnp.float32)
-    near = jnp.abs(lib_bins[:, None] - flat_bin[None, :]) <= WIN
-    scores = jnp.where(near, jnp.maximum(prod[:, :total], prod[:, total:]), 0.0)
-    best = top_rows(scores).reshape(roles, CAP, K)
+    both = jnp.pad(jnp.concatenate([rows, moved], axis=0), ((0, 0), (0, LANE)))
+
+    def best_of(lib):
+        prod = lax.dot_general(lib, both, (((1,), (1,)), ((), ())), preferred_element_type=jnp.float32)
+        lib_bins = lib[:, W].astype(jnp.int32)
+        near = jnp.abs(lib_bins[:, None] - flat_bin[None, :]) <= WIN
+        return top_rows(jnp.where(near, jnp.maximum(prod[:, :total], prod[:, total:]), 0.0))
+
+    best = bitonic_merge(best_of(near_lib), best_of(far_lib), 1)
+    best = jnp.concatenate(best, axis=0).T.reshape(roles, CAP, K)
 
     home = route([best[i] for i in range(roles)], tuple(inverse(p) for p in perms))
     home = jnp.concatenate(home, axis=0)

time: 125 us -> 148 us (1.18)
  waiting for transfers between devices: 14 us -> 66.1 us
  blocking collectives: 33.5 us -> 0 us
  matrix products: 14.9 us -> 19.1 us
  other arithmetic: 17.4 us -> 19.6 us
  local copies, waits for them, and re-layouts: 15.8 us -> 13.9 us
    unnamed x1 -> x0, blocking collectives: 33.5 us -> none
    all_gather x1 -> x2, waiting for transfers between devices: 5.33 us -> 37.4 us  [the longest x1 37.3 us: on_device(): far_lib = lax.all_gather(partner, ('blk_0', 'blk_2'), axis=0, tiled=True)]
    ppermute x9, waiting for transfers between devices: 2.6 us -> 22.3 us  [route(): lax.ppermute(b, ZRING, p)]
    dot_general x1 -> x2, matrix products: 12.9 us -> 17.2 us  [best_of(): lax.dot_general(lib, both, (((1,), (1,)), ((), ())), preferred_element_ty...]
    sub x0 -> x2, other arithmetic: none -> 2.1 us  [best_of(): near = jnp.abs(lib_bins[:, None] - flat_bin[None, :]) <= WIN]
    unnamed x18 -> x12, local copies, waits for them, and re-layouts: 5.16 us -> 3.99 us
    concatenate x1 -> x2, other arithmetic: 4.12 us -> 4.92 us  [the longest x1 4.19 us: on_device(): both = jnp.pad(jnp.concatenate([rows, moved], axis=0), ((0, 0), (0, LANE)))]
  transfers between devices with their start and end apart: 11 -> 12, of which waited for: 4 -> 6; matrix products, arithmetic and copies ran while one was open for 22% -> 23% of each run, Pallas kernels for 0% -> 0%
where the time goes in v3:
time: 148 us; the launch traced here: 147 us
  waiting for transfers between devices  66.1 us (45%)
  other arithmetic  19.6 us (13%)
  matrix products  19.1 us (13%)
  between operations  14 us (9%)
  local copies, waits for them, and re-layouts  13.9 us (9%)
  starting transfers between devices  13.8 us (9%)
    all_gather x1, waiting for transfers between devices, on_device(): far_lib = lax.all_gather(partner, ('blk_0', 'blk_2'), axis=0, tiled=True)  37.3 us
    ppermute x9, waiting for transfers between devices, route(): lax.ppermute(b, ZRING, p)  22.3 us
    dot_general x2, matrix products, best_of(): lax.dot_general(lib, both, (((1,), (1,)), ((), ())), preferred_element_ty...  17.2 us
    ppermute x9, starting transfers between devices, route(): lax.ppermute(b, ZRING, p)  9.24 us
    ppermute x1, waiting for transfers between devices, on_device(): partner = lax.ppermute(packed, 'blk_1', [(0, 1), (1, 0)])  6.42 us
    slice x2, local copies, waits for them, and re-layouts, lower_bins(): return jnp.concatenate([rows[..., amount:], tail], axis=-1)  6.41 us
    ppermute x1, starting transfers between devices, on_device(): partner = lax.ppermute(packed, 'blk_1', [(0, 1), (1, 0)])  4.51 us
    reduce_sum x2, other arithmetic, unit_rows(): total = jnp.sum(values * values, axis=-1, keepdims=True)  4.41 us
  transfers between devices with their start and end apart: 12, of which 6 were waited for; matrix products, arithmetic and copies ran while one was open for 23% of the time, Pallas kernels for 0%

profile of v3, /device:TPU:1, one launch (start us, length us, event | category | flops | bytes accessed | tf_op | source)
XLA Modules:
  0.0 146.5 jit_solution(13691740039298247509)
XLA Ops:
  6.5 1.4 fusion.8
  7.9 1.1 fusion.9
  9.1 0.7 convert_bitcast_fusion
  9.7 0.1 copy.28
  9.8 0.7 fusion.10
  10.6 4.5 %collective-permute-start.6 = (bf16[32,4224]{1,0:T(8,128)(2,1)}, bf16[32,4224]{1,0:T(8,128)(2,1)S(1)}, u32[]{:S(2)}, u32[]{:S(2)}) collective-permute-start(bf16[32,4224]{1,0:T(8,128)(2,1)} %fusion.10), channel_id=1, source_target_pairs={{0,16},{16,0},{1,17},{17,1},{2,18},{18,2},{3,19},{19,3},{4,20},{20... | collective-permute-start | bytes 811016 | tf_op jit(solution)/shard_map/ppermute | solution.py:103
  15.1 6.4 %collective-permute-done.6 = bf16[32,4224]{1,0:T(8,128)(2,1)S(1)} collective-permute-done((bf16[32,4224]{1,0:T(8,128)(2,1)}, bf16[32,4224]{1,0:T(8,128)(2,1)S(1)}, u32[]{:S(2)}, u32[]{:S(2)}) %collective-permute-start.6) | collective-permute-done | bytes 270368 | tf_op jit(solution)/shard_map/ppermute | solution.py:103
  21.5 0.7 copy-done.1
  22.3 0.7 fusion.82
  23.0 1.2 reduce-window.6
  24.7 3.0 %multiply_reduce_fusion = f32[256]{0:T(256)S(1)} fusion(bf16[256,4096]{1,0:T(8,128)(2,1)} %param.6), kind=kLoop, calls=%fused_computation.9 | loop fusion | flops 3145472 | bytes 2098176 | tf_op jit(solution)/shard_map/reduce_sum | solution.py:38
  27.7 0.7 and_reduce_fusion
  28.4 2.0 %convolution_convert_fusion = bf16[512,4096]{1,0:T(8,128)(2,1)S(1)} fusion(bf16[256,4096]{1,0:T(8,128)(2,1)S(1)} %copy-done, f32[256]{0:T(256)S(1)} %add_rsqrt_fusion, s32[256]{0:T(256)S(1)} %bitcast.59), kind=kOutput, calls=%fused_computation.5 | convolution fusion | flops 1079115776 | bytes 6293504 | tf_op jit(solution)/shard_map/dot_general | solution.py:114
  30.4 1.6 %fusion.200 = (bf16[128,4096]{1,0:T(8,128)(2,1)S(1)}, bf16[1024,4096]{1,0:T(8,128)(2,1)}, bf16[128,4096]{1,0:T(8,128)(2,1)S(1)}, bf16[128,4096]{1,0:T(8,128)(2,1)S(1)}, bf16[128,4096]{1,0:T(8,128)(2,1)S(1)}) fusion(bf16[512,4096]{1,0:T(8,128)(2,1)S(1)} %convolution_convert_fusion), kind=kLoop, calls=%fused_computation.411 | loop fusion | bytes 9437184 | tf_op jit(solution)/shard_map/slice | solution.py:123
  32.1 1.2 collective-permute-start.3
  33.3 3.1 %collective-permute-start.4 = (bf16[128,4096]{1,0:T(8,128)(2,1)S(1)}, bf16[128,4096]{1,0:T(8,128)(2,1)S(1)}, u32[]{:S(2)}, u32[]{:S(2)}) collective-permute-start(bf16[128,4096]{1,0:T(8,128)(2,1)S(1)} %get-tuple-element.169), channel_id=1, source_target_pairs={{0,2},{2,16},{16,18},{18,0},{1,19},{3,1},{17,3},{19,17},{4,6},{6,2... | collective-permute-start | bytes 3145736 | tf_op jit(solution)/shard_map/ppermute | solution.py:91
  36.4 0.2 select_reduce_fusion.1
  36.6 0.6 collective-permute-start
  37.2 0.3 collective-permute-start.1
  37.5 0.5 collective-permute-done
  38.0 1.6 %collective-permute-start.2 = (s32[2,128]{1,0:T(2,128)S(1)}, s32[2,128]{1,0:T(2,128)S(1)}, u32[]{:S(2)}, u32[]{:S(2)}) collective-permute-start(s32[2,128]{1,0:T(2,128)S(1)} %get-tuple-element.281), channel_id=1, source_target_pairs={{1,2},{3,16},{17,18},{19,0},{0,19},{2,1},{16,3},{18,17},{5,6},{7,2... | collective-permute-start | bytes 3080 | tf_op jit(solution)/shard_map/ppermute | solution.py:91
  39.6 19.2 %collective-permute-done.1 = s32[2,128]{1,0:T(2,128)S(1)} collective-permute-done((s32[2,128]{1,0:T(2,128)S(1)}, s32[2,128]{1,0:T(2,128)S(1)}, u32[]{:S(2)}, u32[]{:S(2)}) %collective-permute-start.1) | collective-permute-done | bytes 1056 | tf_op jit(solution)/shard_map/ppermute | solution.py:91
  58.8 0.5 pad_maximum_fusion
  59.4 3.2 %slice.952 = bf16[512,4064]{1,0:T(8,128)(2,1)S(1)} slice(bf16[512,4096]{1,0:T(8,128)(2,1)S(1)} %pad_maximum_fusion), slice={[0:512], [32:4096]} | slice | bytes 8323072 | tf_op jit(solution)/shard_map/slice | solution.py:44
  62.6 3.2 %slice.953 = bf16[512,4080]{1,0:T(8,128)(2,1)S(1)} slice(bf16[512,4096]{1,0:T(8,128)(2,1)S(1)} %pad_maximum_fusion), slice={[0:512], [16:4096]} | slice | bytes 8355840 | tf_op jit(solution)/shard_map/slice | solution.py:44
  65.8 1.1 constant_dynamic-update-slice_fusion.2
  66.9 1.0 constant_dynamic-update-slice_fusion.1
  67.9 1.1 constant_dynamic-update-slice_fusion
  68.9 4.2 %select_dynamic-update-slice_fusion = bf16[1024,4096]{1,0:T(8,128)(2,1)} fusion(bf16[1024,4096]{1,0:T(8,128)(2,1)} %constant_dynamic-update-slice_fusion, bf16[512,4080]{1,0:T(8,128)(2,1)S(1)} %slice.953, bf16[512,4064]{1,0:T(8,128)(2,1)S(1)} %slice.952, pred[512]{0:T(512)(128)(4,1)S(1)} %get-tuple-element.278, pred[512]{0:T(512)(128)(4,1)S(1)} %get-tuple-element.277), kind=kLoop, calls=%fused_computation.7 | loop fusion | flops 4194304 | bytes 12534784 | tf_op jit(solution)/shard_map/concatenate | solution.py:132
  73.1 1.1 convert_reduce_fusion.1
  74.2 8.5 %fusion.2 = f32[512,1024]{1,0:T(8,128)S(1)} fusion(bf16[512,4224]{1,0:T(8,128)(2,1)} %all-gather.3.cloned.1.call-done, bf16[1024,4096]{1,0:T(8,128)(2,1)} %select_dynamic-update-slice_fusion), kind=kOutput, calls=%fused_computation.3 | convolution fusion | flops 4429185024 | bytes 14811136 | tf_op jit(solution)/shard_map/dot_general | solution.py:135
  82.7 37.3 %all-gather.5.cloned.1.call-done = bf16[512,4224]{1,0:T(8,128)(2,1)} async-done(((bf16[32,4224]{1,0:T(8,128)(2,1)}), bf16[512,4224]{1,0:T(8,128)(2,1)}) %all-gather.5.cloned.1.call-update) | async-done | bytes 4325392 | tf_op jit(solution)/shard_map/all_gather | solution.py:105
  120.0 8.7 %fusion = f32[512,1024]{1,0:T(8,128)S(1)} fusion(bf16[512,4224]{1,0:T(8,128)(2,1)} %all-gather.5.cloned.1.call-done, bf16[1024,4096]{1,0:T(8,128)(2,1)} %select_dynamic-update-slice_fusion), kind=kOutput, calls=%fused_computation.1 | convolution fusion | flops 4429185024 | bytes 14811136 | tf_op jit(solution)/shard_map/dot_general | solution.py:135
  128.7 1.1 convert_reduce_fusion
  129.8 0.5 fusion.6
  130.3 0.1 minimum_minimum_fusion.9
  130.5 0.2 minimum_maximum_fusion.6
  131.5 0.2 minimum_minimum_fusion.4
  131.6 0.2 minimum_maximum_fusion.1
  131.8 0.1 minimum_maximum_fusion
  133.0 0.8 collective-permute-start.7
  133.7 1.3 collective-permute-start.8
  135.0 0.4 collective-permute-start.9
  135.4 1.9 %collective-permute-done.8 = f32[128,8]{0,1:T(8,128)S(1)} collective-permute-done((f32[128,8]{0,1:T(8,128)S(1)}, f32[128,8]{0,1:T(8,128)S(1)}, u32[]{:S(2)}, u32[]{:S(2)}) %collective-permute-start.8) | collective-permute-done | bytes 4128 | tf_op jit(solution)/shard_map/ppermute | solution.py:91
  137.4 0.6 collective-permute-done.9
  138.0 0.1 copy.26
  138.2 0.7 gather_fusion
  139.0 0.7 copy.27
  (86 shorter events, 2.1 us)
Async XLA Ops:
  6.5 21.9 %copy-start = (bf16[256,4096]{1,0:T(8,128)(2,1)S(1)}, bf16[256,4096]{1,0:T(8,128)(2,1)}, u32[]{:S(2)}) copy-start(bf16[256,4096]{1,0:T(8,128)(2,1)} %param.6) | copy-start | bytes 6291460
  6.5 66.6 %all-gather.3.cloned.1.call-start = ((), (), s32[]{:S(2)}) async-start(), calls=%async_computation | async-start | bytes 4595712 | tf_op jit(solution)/shard_map/all_gather | solution.py:104
  10.6 109.5 %all-gather.5.cloned.1.call-start = ((), (), s32[]{:S(2)}) async-start(), calls=%async_computation.1 | async-start | bytes 4595712 | tf_op jit(solution)/shard_map/all_gather | solution.py:105
  10.6 10.9 %collective-permute-start.6 = (bf16[32,4224]{1,0:T(8,128)(2,1)}, bf16[32,4224]{1,0:T(8,128)(2,1)S(1)}, u32[]{:S(2)}, u32[]{:S(2)}) collective-permute-start(bf16[32,4224]{1,0:T(8,128)(2,1)} %fusion.10), channel_id=1, source_target_pairs={{0,16},{16,0},{1,17},{17,1},{2,18},{18,2},{3,19},{19,3},{4,20},{20... | collective-permute-start | bytes 811016 | tf_op jit(solution)/shard_map/ppermute | solution.py:103
  21.5 0.7 copy-start.1
  30.4 6.0 %copy-start.2 = (s32[256]{0:T(256)S(1)}, s32[256]{0:T(256)}, u32[]{:S(2)}) copy-start(s32[256]{0:T(256)} %param.8) | copy-start | bytes 3076
  30.4 6.0 %copy-start.3 = (s32[256]{0:T(256)S(1)}, s32[256]{0:T(256)}, u32[]{:S(2)}) copy-start(s32[256]{0:T(256)} %param.9) | copy-start | bytes 3076
  32.1 26.7 %collective-permute-start.3 = (bf16[128,4096]{1,0:T(8,128)(2,1)S(1)}, bf16[128,4096]{1,0:T(8,128)(2,1)S(1)}, u32[]{:S(2)}, u32[]{:S(2)}) collective-permute-start(bf16[128,4096]{1,0:T(8,128)(2,1)S(1)} %get-tuple-element.170), channel_id=1, source_target_pairs={{0,1},{1,0},{2,3},{3,2},{16,17},{17,16},{18,19},{19,18},{4,5},{5,4... | collective-permute-start | bytes 3145736 | tf_op jit(solution)/shard_map/ppermute | solution.py:91
  33.3 25.5 %collective-permute-start.4 = (bf16[128,4096]{1,0:T(8,128)(2,1)S(1)}, bf16[128,4096]{1,0:T(8,128)(2,1)S(1)}, u32[]{:S(2)}, u32[]{:S(2)}) collective-permute-start(bf16[128,4096]{1,0:T(8,128)(2,1)S(1)} %get-tuple-element.169), channel_id=1, source_target_pairs={{0,2},{2,16},{16,18},{18,0},{1,19},{3,1},{17,3},{19,17},{4,6},{6,2... | collective-permute-start | bytes 3145736 | tf_op jit(solution)/shard_map/ppermute | solution.py:91
  36.4 22.4 %collective-permute-start.5 = (bf16[128,4096]{1,0:T(8,128)(2,1)S(1)}, bf16[128,4096]{1,0:T(8,128)(2,1)S(1)}, u32[]{:S(2)}, u32[]{:S(2)}) collective-permute-start(bf16[128,4096]{1,0:T(8,128)(2,1)S(1)} %get-tuple-element.168), channel_id=1, source_target_pairs={{1,2},{3,16},{17,18},{19,0},{0,19},{2,1},{16,3},{18,17},{5,6},{7,2... | collective-permute-start | bytes 3145736 | tf_op jit(solution)/shard_map/ppermute | solution.py:91
  36.6 1.4 collective-permute-start
  37.2 21.5 %collective-permute-start.1 = (s32[2,128]{1,0:T(2,128)S(1)}, s32[2,128]{1,0:T(2,128)S(1)}, u32[]{:S(2)}, u32[]{:S(2)}) collective-permute-start(s32[2,128]{1,0:T(2,128)S(1)} %get-tuple-element.282), channel_id=1, source_target_pairs={{0,2},{2,16},{16,18},{18,0},{1,19},{3,1},{17,3},{19,17},{4,6},{6,2... | collective-permute-start | bytes 3080 | tf_op jit(solution)/shard_map/ppermute | solution.py:91
  38.0 20.7 %collective-permute-start.2 = (s32[2,128]{1,0:T(2,128)S(1)}, s32[2,128]{1,0:T(2,128)S(1)}, u32[]{:S(2)}, u32[]{:S(2)}) collective-permute-start(s32[2,128]{1,0:T(2,128)S(1)} %get-tuple-element.281), channel_id=1, source_target_pairs={{1,2},{3,16},{17,18},{19,0},{0,19},{2,1},{16,3},{18,17},{5,6},{7,2... | collective-permute-start | bytes 3080 | tf_op jit(solution)/shard_map/ppermute | solution.py:91
  133.0 2.5 %collective-permute-start.7 = (f32[128,8]{0,1:T(8,128)S(1)}, f32[128,8]{0,1:T(8,128)S(1)}, u32[]{:S(2)}, u32[]{:S(2)}) collective-permute-start(f32[128,8]{0,1:T(8,128)S(1)} %get-tuple-element.242), channel_id=1, source_target_pairs={{1,0},{0,1},{3,2},{2,3},{17,16},{16,17},{19,18},{18,19},{5,4},{4,5... | collective-permute-start | bytes 12296 | tf_op jit(solution)/shard_map/ppermute | solution.py:91
  133.7 3.7 %collective-permute-start.8 = (f32[128,8]{0,1:T(8,128)S(1)}, f32[128,8]{0,1:T(8,128)S(1)}, u32[]{:S(2)}, u32[]{:S(2)}) collective-permute-start(f32[128,8]{0,1:T(8,128)S(1)} %get-tuple-element.241), channel_id=1, source_target_pairs={{2,0},{16,2},{18,16},{0,18},{19,1},{1,3},{3,17},{17,19},{6,4},{20,... | collective-permute-start | bytes 12296 | tf_op jit(solution)/shard_map/ppermute | solution.py:91
  135.0 3.0 %collective-permute-start.9 = (f32[128,8]{0,1:T(8,128)S(1)}, f32[128,8]{0,1:T(8,128)S(1)}, u32[]{:S(2)}, u32[]{:S(2)}) collective-permute-start(f32[128,8]{0,1:T(8,128)S(1)} %get-tuple-element.240), channel_id=1, source_target_pairs={{2,1},{16,3},{18,17},{0,19},{19,0},{1,2},{3,16},{17,18},{6,5},{20,... | collective-permute-start | bytes 12296 | tf_op jit(solution)/shard_map/ppermute | solution.py:91
Sparse Core Ops, SparseCore 0:
  10.7 55.3 all-gather.2
  68.3 51.7 all-gather.4

commit v4 on v3

--- a/solution.py
+++ b/solution.py
@@ -87,6 +87,18 @@
     return lists
 
 
+def ring_gather(block, axis):
+    size = 4
+    up = [(i, (i + 1) % size) for i in range(size)]
+    down = [(i, (i - 1) % size) for i in range(size)]
+    below = lax.ppermute(block, axis, up)
+    above = lax.ppermute(block, axis, down)
+    half = block.shape[0] // 2
+    far_low = lax.ppermute(below[:half], axis, up)
+    far_high = lax.ppermute(above[half:], axis, down)
+    return [block, below, above, far_low, far_high]
+
+
 def route(blocks, perms):
     return [blocks[0]] + [lax.ppermute(b, ZRING, p) for b, p in zip(blocks[1:], perms)]
 
@@ -101,8 +113,15 @@
     bin_cols = jnp.pad(library_bin[0].astype(jnp.bfloat16)[:, None], ((0, 0), (0, LANE - 1)))
     packed = jnp.concatenate([unit_lib, bin_cols], axis=1)
     partner = lax.ppermute(packed, "blk_1", [(0, 1), (1, 0)])
-    near_lib = lax.all_gather(packed, ("blk_0", "blk_2"), axis=0, tiled=True)
-    far_lib = lax.all_gather(partner, ("blk_0", "blk_2"), axis=0, tiled=True)
+    chunk = jnp.concatenate([packed, partner], axis=0)
+    half = chunk.shape[0] // 2
+    x_first = ring_gather(chunk[:half], "blk_0")
+    y_first = ring_gather(chunk[half:], "blk_2")
+    x_then_y = ring_gather(jnp.concatenate(x_first, axis=0), "blk_2")
+    y_then_x = ring_gather(jnp.concatenate(y_first, axis=0), "blk_0")
+    early = jnp.concatenate([chunk] + x_first[1:] + y_first[1:], axis=0)
+    middle = jnp.concatenate(x_then_y[1:3] + y_then_x[1:3], axis=0)
+    late = jnp.concatenate(x_then_y[3:] + y_then_x[3:], axis=0)
 
     unit_q = unit_rows(queries)
     group = query_group[:, 0]
@@ -137,7 +156,8 @@
         near = jnp.abs(lib_bins[:, None] - flat_bin[None, :]) <= WIN
         return top_rows(jnp.where(near, jnp.maximum(prod[:, :total], prod[:, total:]), 0.0))
 
-    best = bitonic_merge(best_of(near_lib), best_of(far_lib), 1)
+    best = bitonic_merge(best_of(early), best_of(middle), 1)
+    best = bitonic_merge(best, best_of(late), 1)
     best = jnp.concatenate(best, axis=0).T.reshape(roles, CAP, K)
 
     home = route([best[i] for i in range(roles)], tuple(inverse(p) for p in perms))

time: 148 us -> 135 us (0.912)
  starting transfers between devices: 13.8 us -> 38.3 us
  waiting for transfers between devices: 66.1 us -> 46.9 us
  between operations: 14 us -> 0.98 us
  matrix products: 19.1 us -> 11.6 us
  local copies, waits for them, and re-layouts: 13.9 us -> 17.9 us
    ppermute x0 -> x16, waiting for transfers between devices: none -> 44.4 us  [the longest x4 30.3 us: ring_gather(): far_low = lax.ppermute(below[:half], axis, up)]
    all_gather x2 -> x0, waiting for transfers between devices: 37.4 us -> none  [the longest x1 37.3 us: on_device(): far_lib = lax.all_gather(partner, ('blk_0', 'blk_2'), axis=0, tiled=True)]
    ppermute x9, waiting for transfers between devices: 22.3 us -> 2.42 us  [route(): lax.ppermute(b, ZRING, p)]
    ppermute x0 -> x16, starting transfers between devices: none -> 18.6 us  [the longest x4 6.9 us: ring_gather(): above = lax.ppermute(block, axis, down)]
    dot_general x2 -> x3, matrix products: 17.2 us -> 9.63 us  [best_of(): lax.dot_general(lib, both, (((1,), (1,)), ((), ())), preferred_element_ty...]
    ppermute x1, waiting for transfers between devices: 6.42 us -> 0.01 us  [on_device(): partner = lax.ppermute(packed, 'blk_1', [(0, 1), (1, 0)])]
    ppermute x9, starting transfers between devices: 9.24 us -> 15.3 us  [route(): lax.ppermute(b, ZRING, p)]
    unnamed x12 -> x26, local copies, waits for them, and re-layouts: 3.99 us -> 6.93 us
  transfers between devices with their start and end apart: 12 -> 26, of which waited for: 6 -> 8; matrix products, arithmetic and copies ran while one was open for 23% -> 28% of each run, Pallas kernels for 0% -> 0%
where the time goes in v4:
time: 135 us; the launch traced here: 134 us
  waiting for transfers between devices  46.9 us (35%)
  starting transfers between devices  38.3 us (28%)
  other arithmetic  18.6 us (14%)
  local copies, waits for them, and re-layouts  17.9 us (13%)
  matrix products  11.6 us (9%)
    ppermute x4, waiting for transfers between devices, ring_gather(): far_low = lax.ppermute(below[:half], axis, up)  30.3 us
    ppermute x9, starting transfers between devices, route(): lax.ppermute(b, ZRING, p)  15.3 us
    dot_general x3, matrix products, best_of(): lax.dot_general(lib, both, (((1,), (1,)), ((), ())), preferred_element_ty...  9.63 us
    ppermute x4, waiting for transfers between devices, ring_gather(): above = lax.ppermute(block, axis, down)  8.22 us
    unnamed x26, local copies, waits for them, and re-layouts  6.93 us
    ppermute x4, starting transfers between devices, ring_gather(): above = lax.ppermute(block, axis, down)  6.9 us
    slice x2, local copies, waits for them, and re-layouts, lower_bins(): return jnp.concatenate([rows[..., amount:], tail], axis=-1)  6.4 us
    ppermute x4, starting transfers between devices, ring_gather(): far_high = lax.ppermute(above[half:], axis, down)  6.3 us
  transfers between devices with their start and end apart: 26, of which 8 were waited for; matrix products, arithmetic and copies ran while one was open for 28% of the time, Pallas kernels for 0%

profile of v4, /device:TPU:1, one launch (start us, length us, event | category | flops | bytes accessed | tf_op | source)
XLA Modules:
  0.0 134.3 jit_solution(9005726777235792713)
XLA Ops:
  0.0 0.8 convert_bitcast_fusion
  0.9 1.2 fusion.11
  2.2 1.1 fusion.12
  3.3 0.9 constant_dynamic-update-slice_fusion.9
  4.1 4.4 %collective-permute-start = (bf16[32,4224]{1,0:T(8,128)(2,1)S(1)}, bf16[32,4224]{1,0:T(8,128)(2,1)S(1)}, u32[]{:S(2)}, u32[]{:S(2)}) collective-permute-start(bf16[32,4224]{1,0:T(8,128)(2,1)S(1)} %get-tuple-element.279), channel_id=1, source_target_pairs={{0,16},{16,0},{1,17},{17,1},{2,18},{18,2},{3,19},{19,3},{4,20},{20... | collective-permute-start | bytes 811016 | tf_op jit(solution)/shard_map/ppermute | solution.py:115
  8.6 1.2 collective-permute-start.1
  10.5 1.2 reduce-window.6
  12.8 0.9 select_reduce_fusion.1
  13.7 1.9 %collective-permute-start.11 = (s32[2,128]{1,0:T(2,128)S(1)}, s32[2,128]{1,0:T(2,128)S(1)}, u32[]{:S(2)}, u32[]{:S(2)}) collective-permute-start(s32[2,128]{1,0:T(2,128)S(1)} %get-tuple-element.405), channel_id=1, source_target_pairs={{1,2},{3,16},{17,18},{19,0},{0,19},{2,1},{16,3},{18,17},{5,6},{7,2... | collective-permute-start | bytes 3080 | tf_op jit(solution)/shard_map/ppermute | solution.py:103
  15.7 1.9 %collective-permute-start.10 = (s32[2,128]{1,0:T(2,128)S(1)}, s32[2,128]{1,0:T(2,128)S(1)}, u32[]{:S(2)}, u32[]{:S(2)}) collective-permute-start(s32[2,128]{1,0:T(2,128)S(1)} %get-tuple-element.406), channel_id=1, source_target_pairs={{0,2},{2,16},{16,18},{18,0},{1,19},{3,1},{17,3},{19,17},{4,6},{6,2... | collective-permute-start | bytes 3080 | tf_op jit(solution)/shard_map/ppermute | solution.py:103
  17.6 3.0 %multiply_reduce_fusion = f32[256]{0:T(256)S(1)} fusion(bf16[256,4096]{1,0:T(8,128)(2,1)} %param.6), kind=kLoop, calls=%fused_computation.11 | loop fusion | flops 3145472 | bytes 2098176 | tf_op jit(solution)/shard_map/reduce_sum | solution.py:38
  20.7 2.0 %convolution_convert_fusion = bf16[512,4096]{1,0:T(8,128)(2,1)S(1)} fusion(bf16[256,4096]{1,0:T(8,128)(2,1)S(1)} %copy-done, f32[256]{0:T(256)S(1)} %add_rsqrt_fusion, s32[256]{0:T(256)S(1)} %bitcast.63), kind=kOutput, calls=%fused_computation.7 | convolution fusion | flops 1079115776 | bytes 6293504 | tf_op jit(solution)/shard_map/dot_general | solution.py:133
  22.7 1.6 %fusion.280 = (bf16[128,4096]{1,0:T(8,128)(2,1)S(1)}, bf16[1024,4096]{1,0:T(8,128)(2,1)}, bf16[128,4096]{1,0:T(8,128)(2,1)S(1)}, bf16[128,4096]{1,0:T(8,128)(2,1)S(1)}, bf16[128,4096]{1,0:T(8,128)(2,1)S(1)}) fusion(bf16[512,4096]{1,0:T(8,128)(2,1)S(1)} %convolution_convert_fusion), kind=kLoop, calls=%fused_computation.568 | loop fusion | bytes 9437184 | tf_op jit(solution)/shard_map/slice | solution.py:142
  24.3 1.5 %collective-permute-start.2 = (bf16[32,4224]{1,0:T(8,128)(2,1)S(1)}, bf16[32,4224]{1,0:T(8,128)(2,1)S(1)}, u32[]{:S(2)}, u32[]{:S(2)}) collective-permute-start(bf16[32,4224]{1,0:T(8,128)(2,1)S(1)} %get-tuple-element.279), channel_id=1, source_target_pairs={{0,96},{32,0},{64,32},{96,64},{1,97},{33,1},{65,33},{97,65},{2,98}... | collective-permute-start | bytes 811016 | tf_op jit(solution)/shard_map/ppermute | solution.py:95
  25.8 0.8 collective-permute-start.12
  26.7 5.1 %collective-permute-done.2 = bf16[32,4224]{1,0:T(8,128)(2,1)S(1)} collective-permute-done((bf16[32,4224]{1,0:T(8,128)(2,1)S(1)}, bf16[32,4224]{1,0:T(8,128)(2,1)S(1)}, u32[]{:S(2)}, u32[]{:S(2)}) %collective-permute-start.2) | collective-permute-done | bytes 270368 | tf_op jit(solution)/shard_map/ppermute | solution.py:95
  31.8 1.2 collective-permute-start.3
  33.1 1.5 %collective-permute-start.4 = (bf16[16,4224]{1,0:T(8,128)(2,1)S(1)}, bf16[16,4224]{1,0:T(8,128)(2,1)S(1)}, u32[]{:S(2)}, u32[]{:S(2)}) collective-permute-start(bf16[16,4224]{1,0:T(8,128)(2,1)S(1)} %slice.1272), channel_id=1, source_target_pairs={{0,96},{32,0},{64,32},{96,64},{1,97},{33,1},{65,33},{97,65},{2,98}... | collective-permute-start | bytes 405512 | tf_op jit(solution)/shard_map/ppermute | solution.py:98
  34.6 0.7 constant_dynamic-update-slice_fusion.8
  35.3 0.8 constant_dynamic-update-slice_fusion.7
  36.2 0.9 constant_dynamic-update-slice_fusion.6
  37.2 1.3 collective-permute-start.5
  38.5 0.7 constant_dynamic-update-slice_fusion.5
  39.3 1.4 %collective-permute-start.6 = (bf16[32,4224]{1,0:T(8,128)(2,1)S(1)}, bf16[32,4224]{1,0:T(8,128)(2,1)S(1)}, u32[]{:S(2)}, u32[]{:S(2)}) collective-permute-start(bf16[32,4224]{1,0:T(8,128)(2,1)S(1)} %collective-permute-done), channel_id=1, source_target_pairs={{0,12},{4,0},{8,4},{12,8},{1,13},{5,1},{9,5},{13,9},{2,14},{6,2},{... | collective-permute-start | bytes 811016 | tf_op jit(solution)/shard_map/ppermute | solution.py:95
  40.7 0.7 constant_dynamic-update-slice_fusion.4
  41.4 2.9 %collective-permute-done.5 = bf16[32,4224]{1,0:T(8,128)(2,1)S(1)} collective-permute-done((bf16[32,4224]{1,0:T(8,128)(2,1)S(1)}, bf16[32,4224]{1,0:T(8,128)(2,1)S(1)}, u32[]{:S(2)}, u32[]{:S(2)}) %collective-permute-start.5) | collective-permute-done | bytes 270368 | tf_op jit(solution)/shard_map/ppermute | solution.py:94
  44.3 0.7 constant_dynamic-update-slice_fusion.3
  45.1 1.3 collective-permute-start.7
  46.4 0.7 constant_dynamic-update-slice_fusion.2
  47.1 23.7 %collective-permute-done.7 = bf16[16,4224]{1,0:T(8,128)(2,1)S(1)} collective-permute-done((bf16[16,4224]{1,0:T(8,128)(2,1)S(1)}, bf16[16,4224]{1,0:T(8,128)(2,1)S(1)}, u32[]{:S(2)}, u32[]{:S(2)}) %collective-permute-start.7) | collective-permute-done | bytes 135200 | tf_op jit(solution)/shard_map/ppermute | solution.py:97
  71.7 3.1 %collective-permute-done.8 = bf16[16,4224]{1,0:T(8,128)(2,1)S(1)} collective-permute-done((bf16[16,4224]{1,0:T(8,128)(2,1)S(1)}, bf16[16,4224]{1,0:T(8,128)(2,1)S(1)}, u32[]{:S(2)}, u32[]{:S(2)}) %collective-permute-start.8) | collective-permute-done | bytes 135200 | tf_op jit(solution)/shard_map/ppermute | solution.py:98
  74.8 1.3 collective-permute-start.16
  76.8 1.0 convert_reduce_fusion.2
  77.8 2.7 %collective-permute-start.18 = (bf16[128,4224]{1,0:T(8,128)(2,1)S(1)}, bf16[128,4224]{1,0:T(8,128)(2,1)S(1)}, u32[]{:S(2)}, u32[]{:S(2)}) collective-permute-start(bf16[128,4224]{1,0:T(8,128)(2,1)S(1)} %get-tuple-element.296), channel_id=1, source_target_pairs={{0,96},{32,0},{64,32},{96,64},{1,97},{33,1},{65,33},{97,65},{2,98}... | collective-permute-start | bytes 3244040 | tf_op jit(solution)/shard_map/ppermute | solution.py:95
  81.0 3.2 %slice.1289 = bf16[512,4080]{1,0:T(8,128)(2,1)S(1)} slice(bf16[512,4096]{1,0:T(8,128)(2,1)S(1)} %pad_maximum_fusion), slice={[0:512], [16:4096]} | slice | bytes 8355840 | tf_op jit(solution)/shard_map/slice | solution.py:44
  84.2 3.2 %slice.1288 = bf16[512,4064]{1,0:T(8,128)(2,1)S(1)} slice(bf16[512,4096]{1,0:T(8,128)(2,1)S(1)} %pad_maximum_fusion), slice={[0:512], [32:4096]} | slice | bytes 8323072 | tf_op jit(solution)/shard_map/slice | solution.py:44
  87.8 3.1 %select_dynamic-update-slice_fusion = bf16[1024,4096]{1,0:T(8,128)(2,1)S(1)} fusion(bf16[1024,4096]{1,0:T(8,128)(2,1)S(1)} %constant_dynamic-update-slice_fusion.10, bf16[512,4080]{1,0:T(8,128)(2,1)S(1)} %slice.1289, bf16[512,4064]{1,0:T(8,128)(2,1)S(1)} %slice.1288, pred[512]{0:T(512)(128)(4,1)S(1)} %get-tuple-element.402, ...), kind=kLoop, calls=%fused_computation.9 | loop fusion | flops 4194304 | bytes 12583936 | tf_op jit(solution)/shard_map/concatenate | solution.py:151
  90.9 2.4 %fusion.4 = f32[256,1024]{1,0:T(8,128)S(1)} fusion(bf16[256,4224]{1,0:T(8,128)(2,1)S(1)} %copy-done.1, bf16[1024,4096]{1,0:T(8,128)(2,1)S(1)} %select_dynamic-update-slice_fusion), kind=kOutput, calls=%fused_computation.5 | convolution fusion | flops 2214592512 | bytes 11599872 | tf_op jit(solution)/shard_map/dot_general | solution.py:154
  93.6 3.1 %collective-permute-done.16 = bf16[128,4224]{1,0:T(8,128)(2,1)S(1)} collective-permute-done((bf16[128,4224]{1,0:T(8,128)(2,1)}, bf16[128,4224]{1,0:T(8,128)(2,1)S(1)}, u32[]{:S(2)}, u32[]{:S(2)}) %collective-permute-start.16) | collective-permute-done | bytes 1081376 | tf_op jit(solution)/shard_map/ppermute | solution.py:95
  96.7 1.9 %collective-permute-start.20 = (bf16[64,4224]{1,0:T(8,128)(2,1)S(1)}, bf16[64,4224]{1,0:T(8,128)(2,1)S(1)}, u32[]{:S(2)}, u32[]{:S(2)}) collective-permute-start(bf16[64,4224]{1,0:T(8,128)(2,1)S(1)} %slice.1488), channel_id=1, source_target_pairs={{0,12},{4,0},{8,4},{12,8},{1,13},{5,1},{9,5},{13,9},{2,14},{6,2},{... | collective-permute-start | bytes 1622024 | tf_op jit(solution)/shard_map/ppermute | solution.py:98
  99.2 4.6 %fusion.2 = f32[512,1024]{1,0:T(8,128)S(1)} fusion(bf16[512,4224]{1,0:T(8,128)(2,1)S(1)} %constant_dynamic-update-slice_fusion.24, bf16[1024,4096]{1,0:T(8,128)(2,1)S(1)} %select_dynamic-update-slice_fusion), kind=kOutput, calls=%fused_computation.3 | convolution fusion | flops 4429185024 | bytes 14811136 | tf_op jit(solution)/shard_map/dot_general | solution.py:154
  105.5 2.7 %collective-permute-start.22 = (bf16[64,4224]{1,0:T(8,128)(2,1)S(1)}, bf16[64,4224]{1,0:T(8,128)(2,1)S(1)}, u32[]{:S(2)}, u32[]{:S(2)}) collective-permute-start(bf16[64,4224]{1,0:T(8,128)(2,1)S(1)} %slice.1490), channel_id=1, source_target_pairs={{0,96},{32,0},{64,32},{96,64},{1,97},{33,1},{65,33},{97,65},{2,98}... | collective-permute-start | bytes 1622024 | tf_op jit(solution)/shard_map/ppermute | solution.py:98
  108.5 6.4 %collective-permute-done.21 = bf16[64,4224]{1,0:T(8,128)(2,1)S(1)} collective-permute-done((bf16[64,4224]{1,0:T(8,128)(2,1)S(1)}, bf16[64,4224]{1,0:T(8,128)(2,1)S(1)}, u32[]{:S(2)}, u32[]{:S(2)}) %collective-permute-start.21) | collective-permute-done | bytes 540704 | tf_op jit(solution)/shard_map/ppermute | solution.py:97
  115.0 2.6 %fusion = f32[256,1024]{1,0:T(8,128)S(1)} fusion(bf16[256,4224]{1,0:T(8,128)(2,1)S(1)} %constant_dynamic-update-slice_fusion.28, bf16[1024,4096]{1,0:T(8,128)(2,1)S(1)} %select_dynamic-update-slice_fusion), kind=kOutput, calls=%fused_computation.1 | convolution fusion | flops 2214592512 | bytes 11599872 | tf_op jit(solution)/shard_map/dot_general | solution.py:154
  119.7 8.4 %collective-permute-start.25 = (f32[128,8]{0,1:T(8,128)S(1)}, f32[128,8]{0,1:T(8,128)S(1)}, u32[]{:S(2)}, u32[]{:S(2)}) collective-permute-start(f32[128,8]{0,1:T(8,128)S(1)} %get-tuple-element.366), channel_id=1, source_target_pairs={{2,1},{16,3},{18,17},{0,19},{19,0},{1,2},{3,16},{17,18},{6,5},{20,... | collective-permute-start | bytes 12296 | tf_op jit(solution)/shard_map/ppermute | solution.py:103
  128.4 1.8 %collective-permute-start.23 = (f32[128,8]{0,1:T(8,128)S(1)}, f32[128,8]{0,1:T(8,128)S(1)}, u32[]{:S(2)}, u32[]{:S(2)}) collective-permute-start(f32[128,8]{0,1:T(8,128)S(1)} %get-tuple-element.368), channel_id=1, source_target_pairs={{1,0},{0,1},{3,2},{2,3},{17,16},{16,17},{19,18},{18,19},{5,4},{4,5... | collective-permute-start | bytes 12296 | tf_op jit(solution)/shard_map/ppermute | solution.py:103
  130.2 2.4 %collective-permute-done.24 = f32[128,8]{0,1:T(8,128)S(1)} collective-permute-done((f32[128,8]{0,1:T(8,128)S(1)}, f32[128,8]{0,1:T(8,128)S(1)}, u32[]{:S(2)}, u32[]{:S(2)}) %collective-permute-start.24) | collective-permute-done | bytes 4128 | tf_op jit(solution)/shard_map/ppermute | solution.py:103
  132.8 0.7 gather_fusion
  (156 shorter events, 10.2 us)
Async XLA Ops:
  0.0 20.7 %copy-start = (bf16[256,4096]{1,0:T(8,128)(2,1)S(1)}, bf16[256,4096]{1,0:T(8,128)(2,1)}, u32[]{:S(2)}) copy-start(bf16[256,4096]{1,0:T(8,128)(2,1)} %param.6) | copy-start | bytes 6291460
  4.1 28.9 %collective-permute-start = (bf16[32,4224]{1,0:T(8,128)(2,1)S(1)}, bf16[32,4224]{1,0:T(8,128)(2,1)S(1)}, u32[]{:S(2)}, u32[]{:S(2)}) collective-permute-start(bf16[32,4224]{1,0:T(8,128)(2,1)S(1)} %get-tuple-element.279), channel_id=1, source_target_pairs={{0,16},{16,0},{1,17},{17,1},{2,18},{18,2},{3,19},{19,3},{4,20},{20... | collective-permute-start | bytes 811016 | tf_op jit(solution)/shard_map/ppermute | solution.py:115
  8.6 18.0 %collective-permute-start.1 = (bf16[32,4224]{1,0:T(8,128)(2,1)S(1)}, bf16[32,4224]{1,0:T(8,128)(2,1)S(1)}, u32[]{:S(2)}, u32[]{:S(2)}) collective-permute-start(bf16[32,4224]{1,0:T(8,128)(2,1)S(1)} %get-tuple-element.279), channel_id=1, source_target_pairs={{0,32},{32,64},{64,96},{96,0},{1,33},{33,65},{65,97},{97,1},{2,34}... | collective-permute-start | bytes 811016 | tf_op jit(solution)/shard_map/ppermute | solution.py:94
  13.7 10.6 %collective-permute-start.11 = (s32[2,128]{1,0:T(2,128)S(1)}, s32[2,128]{1,0:T(2,128)S(1)}, u32[]{:S(2)}, u32[]{:S(2)}) collective-permute-start(s32[2,128]{1,0:T(2,128)S(1)} %get-tuple-element.405), channel_id=1, source_target_pairs={{1,2},{3,16},{17,18},{19,0},{0,19},{2,1},{16,3},{18,17},{5,6},{7,2... | collective-permute-start | bytes 3080 | tf_op jit(solution)/shard_map/ppermute | solution.py:103
  15.7 10.1 %collective-permute-start.10 = (s32[2,128]{1,0:T(2,128)S(1)}, s32[2,128]{1,0:T(2,128)S(1)}, u32[]{:S(2)}, u32[]{:S(2)}) collective-permute-start(s32[2,128]{1,0:T(2,128)S(1)} %get-tuple-element.406), channel_id=1, source_target_pairs={{0,2},{2,16},{16,18},{18,0},{1,19},{3,1},{17,3},{19,17},{4,6},{6,2... | collective-permute-start | bytes 3080 | tf_op jit(solution)/shard_map/ppermute | solution.py:103
  17.6 8.9 %collective-permute-start.9 = (s32[2,128]{1,0:T(2,128)S(1)}, s32[2,128]{1,0:T(2,128)S(1)}, u32[]{:S(2)}, u32[]{:S(2)}) collective-permute-start(s32[2,128]{1,0:T(2,128)S(1)} %get-tuple-element.404), channel_id=1, source_target_pairs={{0,1},{1,0},{2,3},{3,2},{16,17},{17,16},{18,19},{19,18},{4,5},{5,4... | collective-permute-start | bytes 3080 | tf_op jit(solution)/shard_map/ppermute | solution.py:103
  24.3 7.5 %collective-permute-start.2 = (bf16[32,4224]{1,0:T(8,128)(2,1)S(1)}, bf16[32,4224]{1,0:T(8,128)(2,1)S(1)}, u32[]{:S(2)}, u32[]{:S(2)}) collective-permute-start(bf16[32,4224]{1,0:T(8,128)(2,1)S(1)} %get-tuple-element.279), channel_id=1, source_target_pairs={{0,96},{32,0},{64,32},{96,64},{1,97},{33,1},{65,33},{97,65},{2,98}... | collective-permute-start | bytes 811016 | tf_op jit(solution)/shard_map/ppermute | solution.py:95
  25.8 52.0 %collective-permute-start.12 = (bf16[128,4096]{1,0:T(8,128)(2,1)S(1)}, bf16[128,4096]{1,0:T(8,128)(2,1)S(1)}, u32[]{:S(2)}, u32[]{:S(2)}) collective-permute-start(bf16[128,4096]{1,0:T(8,128)(2,1)S(1)} %get-tuple-element.247), channel_id=1, source_target_pairs={{0,1},{1,0},{2,3},{3,2},{16,17},{17,16},{18,19},{19,18},{4,5},{5,4... | collective-permute-start | bytes 3145736 | tf_op jit(solution)/shard_map/ppermute | solution.py:103
  26.6 51.3 %collective-permute-start.13 = (bf16[128,4096]{1,0:T(8,128)(2,1)S(1)}, bf16[128,4096]{1,0:T(8,128)(2,1)S(1)}, u32[]{:S(2)}, u32[]{:S(2)}) collective-permute-start(bf16[128,4096]{1,0:T(8,128)(2,1)S(1)} %get-tuple-element.246), channel_id=1, source_target_pairs={{0,2},{2,16},{16,18},{18,0},{1,19},{3,1},{17,3},{19,17},{4,6},{6,2... | collective-permute-start | bytes 3145736 | tf_op jit(solution)/shard_map/ppermute | solution.py:103
  26.6 53.9 %collective-permute-start.14 = (bf16[128,4096]{1,0:T(8,128)(2,1)S(1)}, bf16[128,4096]{1,0:T(8,128)(2,1)S(1)}, u32[]{:S(2)}, u32[]{:S(2)}) collective-permute-start(bf16[128,4096]{1,0:T(8,128)(2,1)S(1)} %get-tuple-element.245), channel_id=1, source_target_pairs={{1,2},{3,16},{17,18},{19,0},{0,19},{2,1},{16,3},{18,17},{5,6},{7,2... | collective-permute-start | bytes 3145736 | tf_op jit(solution)/shard_map/ppermute | solution.py:103
  31.8 5.4 %collective-permute-start.3 = (bf16[16,4224]{1,0:T(8,128)(2,1)S(1)}, bf16[16,4224]{1,0:T(8,128)(2,1)S(1)}, u32[]{:S(2)}, u32[]{:S(2)}) collective-permute-start(bf16[16,4224]{1,0:T(8,128)(2,1)S(1)} %slice.1271), channel_id=1, source_target_pairs={{0,32},{32,64},{64,96},{96,0},{1,33},{33,65},{65,97},{97,1},{2,34}... | collective-permute-start | bytes 405512 | tf_op jit(solution)/shard_map/ppermute | solution.py:97
  33.1 6.2 %collective-permute-start.4 = (bf16[16,4224]{1,0:T(8,128)(2,1)S(1)}, bf16[16,4224]{1,0:T(8,128)(2,1)S(1)}, u32[]{:S(2)}, u32[]{:S(2)}) collective-permute-start(bf16[16,4224]{1,0:T(8,128)(2,1)S(1)} %slice.1272), channel_id=1, source_target_pairs={{0,96},{32,0},{64,32},{96,64},{1,97},{33,1},{65,33},{97,65},{2,98}... | collective-permute-start | bytes 405512 | tf_op jit(solution)/shard_map/ppermute | solution.py:98
  37.2 7.1 %collective-permute-start.5 = (bf16[32,4224]{1,0:T(8,128)(2,1)S(1)}, bf16[32,4224]{1,0:T(8,128)(2,1)S(1)}, u32[]{:S(2)}, u32[]{:S(2)}) collective-permute-start(bf16[32,4224]{1,0:T(8,128)(2,1)S(1)} %collective-permute-done), channel_id=1, source_target_pairs={{0,4},{4,8},{8,12},{12,0},{1,5},{5,9},{9,13},{13,1},{2,6},{6,10},{... | collective-permute-start | bytes 811016 | tf_op jit(solution)/shard_map/ppermute | solution.py:94
  39.3 5.8 %collective-permute-start.6 = (bf16[32,4224]{1,0:T(8,128)(2,1)S(1)}, bf16[32,4224]{1,0:T(8,128)(2,1)S(1)}, u32[]{:S(2)}, u32[]{:S(2)}) collective-permute-start(bf16[32,4224]{1,0:T(8,128)(2,1)S(1)} %collective-permute-done), channel_id=1, source_target_pairs={{0,12},{4,0},{8,4},{12,8},{1,13},{5,1},{9,5},{13,9},{2,14},{6,2},{... | collective-permute-start | bytes 811016 | tf_op jit(solution)/shard_map/ppermute | solution.py:95
  44.3 49.0 %collective-permute-start.15 = (bf16[128,4224]{1,0:T(8,128)(2,1)}, bf16[128,4224]{1,0:T(8,128)(2,1)S(1)}, u32[]{:S(2)}, u32[]{:S(2)}) collective-permute-start(bf16[128,4224]{1,0:T(8,128)(2,1)} %get-tuple-element.300), channel_id=1, source_target_pairs={{0,4},{4,8},{8,12},{12,0},{1,5},{5,9},{9,13},{13,1},{2,6},{6,10},{... | collective-permute-start | bytes 3244040 | tf_op jit(solution)/shard_map/ppermute | solution.py:94
  45.1 25.8 %collective-permute-start.7 = (bf16[16,4224]{1,0:T(8,128)(2,1)S(1)}, bf16[16,4224]{1,0:T(8,128)(2,1)S(1)}, u32[]{:S(2)}, u32[]{:S(2)}) collective-permute-start(bf16[16,4224]{1,0:T(8,128)(2,1)S(1)} %slice.1273), channel_id=1, source_target_pairs={{0,4},{4,8},{8,12},{12,0},{1,5},{5,9},{9,13},{13,1},{2,6},{6,10},{... | collective-permute-start | bytes 405512 | tf_op jit(solution)/shard_map/ppermute | solution.py:97
  70.9 3.9 %collective-permute-start.8 = (bf16[16,4224]{1,0:T(8,128)(2,1)S(1)}, bf16[16,4224]{1,0:T(8,128)(2,1)S(1)}, u32[]{:S(2)}, u32[]{:S(2)}) collective-permute-start(bf16[16,4224]{1,0:T(8,128)(2,1)S(1)} %slice.1274), channel_id=1, source_target_pairs={{0,12},{4,0},{8,4},{12,8},{1,13},{5,1},{9,5},{13,9},{2,14},{6,2},{... | collective-permute-start | bytes 405512 | tf_op jit(solution)/shard_map/ppermute | solution.py:98
  74.8 21.9 %collective-permute-start.16 = (bf16[128,4224]{1,0:T(8,128)(2,1)}, bf16[128,4224]{1,0:T(8,128)(2,1)S(1)}, u32[]{:S(2)}, u32[]{:S(2)}) collective-permute-start(bf16[128,4224]{1,0:T(8,128)(2,1)} %get-tuple-element.300), channel_id=1, source_target_pairs={{0,12},{4,0},{8,4},{12,8},{1,13},{5,1},{9,5},{13,9},{2,14},{6,2},{... | collective-permute-start | bytes 3244040 | tf_op jit(solution)/shard_map/ppermute | solution.py:95
  77.7 21.1 %collective-permute-start.17 = (bf16[128,4224]{1,0:T(8,128)(2,1)S(1)}, bf16[128,4224]{1,0:T(8,128)(2,1)S(1)}, u32[]{:S(2)}, u32[]{:S(2)}) collective-permute-start(bf16[128,4224]{1,0:T(8,128)(2,1)S(1)} %get-tuple-element.296), channel_id=1, source_target_pairs={{0,32},{32,64},{64,96},{96,0},{1,33},{33,65},{65,97},{97,1},{2,34}... | collective-permute-start | bytes 3244040 | tf_op jit(solution)/shard_map/ppermute | solution.py:94
  77.8 21.2 %collective-permute-start.18 = (bf16[128,4224]{1,0:T(8,128)(2,1)S(1)}, bf16[128,4224]{1,0:T(8,128)(2,1)S(1)}, u32[]{:S(2)}, u32[]{:S(2)}) collective-permute-start(bf16[128,4224]{1,0:T(8,128)(2,1)S(1)} %get-tuple-element.296), channel_id=1, source_target_pairs={{0,96},{32,0},{64,32},{96,64},{1,97},{33,1},{65,33},{97,65},{2,98}... | collective-permute-start | bytes 3244040 | tf_op jit(solution)/shard_map/ppermute | solution.py:95
  81.0 6.4 %slice-start = ((s8[8388608]{0:T(1024)(128)(4,1)}), s8[4194304]{0:T(1024)(128)(4,1)S(1)}, s32[]{:S(2)}) async-start(s8[8388608]{0:T(1024)(128)(4,1)} %bitcast.59), calls=%async_computation | async-start | bytes 8388608
  84.2 3.2 %slice-start.1 = ((s8[8388608]{0:T(1024)(128)(4,1)}), s8[4194304]{0:T(1024)(128)(4,1)S(1)}, s32[]{:S(2)}) async-start(s8[8388608]{0:T(1024)(128)(4,1)} %bitcast.59), calls=%async_computation.1 | async-start | bytes 8388608
  87.8 3.1 %copy-start.1 = (bf16[256,4224]{1,0:T(8,128)(2,1)S(1)}, bf16[256,4224]{1,0:T(8,128)(2,1)}, u32[]{:S(2)}) copy-start(bf16[256,4224]{1,0:T(8,128)(2,1)} %get-tuple-element.295) | copy-start | bytes 6488068
  93.4 15.0 %collective-permute-start.19 = (bf16[64,4224]{1,0:T(8,128)(2,1)S(1)}, bf16[64,4224]{1,0:T(8,128)(2,1)S(1)}, u32[]{:S(2)}, u32[]{:S(2)}) collective-permute-start(bf16[64,4224]{1,0:T(8,128)(2,1)S(1)} %slice.1487), channel_id=1, source_target_pairs={{0,4},{4,8},{8,12},{12,0},{1,5},{5,9},{9,13},{13,1},{2,6},{6,10},{... | collective-permute-start | bytes 1622024 | tf_op jit(solution)/shard_map/ppermute | solution.py:97
  96.7 11.7 %collective-permute-start.20 = (bf16[64,4224]{1,0:T(8,128)(2,1)S(1)}, bf16[64,4224]{1,0:T(8,128)(2,1)S(1)}, u32[]{:S(2)}, u32[]{:S(2)}) collective-permute-start(bf16[64,4224]{1,0:T(8,128)(2,1)S(1)} %slice.1488), channel_id=1, source_target_pairs={{0,12},{4,0},{8,4},{12,8},{1,13},{5,1},{9,5},{13,9},{2,14},{6,2},{... | collective-permute-start | bytes 1622024 | tf_op jit(solution)/shard_map/ppermute | solution.py:98
  105.4 9.5 %collective-permute-start.21 = (bf16[64,4224]{1,0:T(8,128)(2,1)S(1)}, bf16[64,4224]{1,0:T(8,128)(2,1)S(1)}, u32[]{:S(2)}, u32[]{:S(2)}) collective-permute-start(bf16[64,4224]{1,0:T(8,128)(2,1)S(1)} %slice.1489), channel_id=1, source_target_pairs={{0,32},{32,64},{64,96},{96,0},{1,33},{33,65},{65,97},{97,1},{2,34}... | collective-permute-start | bytes 1622024 | tf_op jit(solution)/shard_map/ppermute | solution.py:97
  105.5 9.4 %collective-permute-start.22 = (bf16[64,4224]{1,0:T(8,128)(2,1)S(1)}, bf16[64,4224]{1,0:T(8,128)(2,1)S(1)}, u32[]{:S(2)}, u32[]{:S(2)}) collective-permute-start(bf16[64,4224]{1,0:T(8,128)(2,1)S(1)} %slice.1490), channel_id=1, source_target_pairs={{0,96},{32,0},{64,32},{96,64},{1,97},{33,1},{65,33},{97,65},{2,98}... | collective-permute-start | bytes 1622024 | tf_op jit(solution)/shard_map/ppermute | solution.py:98
  119.7 10.6 %collective-permute-start.25 = (f32[128,8]{0,1:T(8,128)S(1)}, f32[128,8]{0,1:T(8,128)S(1)}, u32[]{:S(2)}, u32[]{:S(2)}) collective-permute-start(f32[128,8]{0,1:T(8,128)S(1)} %get-tuple-element.366), channel_id=1, source_target_pairs={{2,1},{16,3},{18,17},{0,19},{19,0},{1,2},{3,16},{17,18},{6,5},{20,... | collective-permute-start | bytes 12296 | tf_op jit(solution)/shard_map/ppermute | solution.py:103
  128.1 4.6 %collective-permute-start.24 = (f32[128,8]{0,1:T(8,128)S(1)}, f32[128,8]{0,1:T(8,128)S(1)}, u32[]{:S(2)}, u32[]{:S(2)}) collective-permute-start(f32[128,8]{0,1:T(8,128)S(1)} %get-tuple-element.367), channel_id=1, source_target_pairs={{2,0},{16,2},{18,16},{0,18},{19,1},{1,3},{3,17},{17,19},{6,4},{20,... | collective-permute-start | bytes 12296 | tf_op jit(solution)/shard_map/ppermute | solution.py:103
  128.4 4.3 %collective-permute-start.23 = (f32[128,8]{0,1:T(8,128)S(1)}, f32[128,8]{0,1:T(8,128)S(1)}, u32[]{:S(2)}, u32[]{:S(2)}) collective-permute-start(f32[128,8]{0,1:T(8,128)S(1)} %get-tuple-element.368), channel_id=1, source_target_pairs={{1,0},{0,1},{3,2},{2,3},{17,16},{16,17},{19,18},{18,19},{5,4},{4,5... | collective-permute-start | bytes 12296 | tf_op jit(solution)/shard_map/ppermute | solution.py:103

commit v5 on v4

--- a/solution.py
+++ b/solution.py
@@ -77,6 +77,7 @@
 
 def top_rows(scores):
     depth = scores.shape[0] // K
+    assert depth & (depth - 1) == 0
     lists = [scores[k * depth:(k + 1) * depth] for k in range(K)]
     for stage in SORT8:
         for i, j in stage:
@@ -115,13 +116,11 @@
     partner = lax.ppermute(packed, "blk_1", [(0, 1), (1, 0)])
     chunk = jnp.concatenate([packed, partner], axis=0)
     half = chunk.shape[0] // 2
-    x_first = ring_gather(chunk[:half], "blk_0")
+    gathered = lax.all_gather(chunk[:half], ("blk_0", "blk_2"), axis=0, tiled=True)
     y_first = ring_gather(chunk[half:], "blk_2")
-    x_then_y = ring_gather(jnp.concatenate(x_first, axis=0), "blk_2")
     y_then_x = ring_gather(jnp.concatenate(y_first, axis=0), "blk_0")
-    early = jnp.concatenate([chunk] + x_first[1:] + y_first[1:], axis=0)
-    middle = jnp.concatenate(x_then_y[1:3] + y_then_x[1:3], axis=0)
-    late = jnp.concatenate(x_then_y[3:] + y_then_x[3:], axis=0)
+    middle = jnp.concatenate(y_then_x[1:3], axis=0)
+    late = jnp.concatenate(y_then_x[3:], axis=0)
 
     unit_q = unit_rows(queries)
     group = query_group[:, 0]
@@ -156,8 +155,9 @@
         near = jnp.abs(lib_bins[:, None] - flat_bin[None, :]) <= WIN
         return top_rows(jnp.where(near, jnp.maximum(prod[:, :total], prod[:, total:]), 0.0))
 
-    best = bitonic_merge(best_of(early), best_of(middle), 1)
+    best = bitonic_merge(best_of(y_then_x[0]), best_of(middle), 1)
     best = bitonic_merge(best, best_of(late), 1)
+    best = bitonic_merge(best, best_of(gathered), 1)
     best = jnp.concatenate(best, axis=0).T.reshape(roles, CAP, K)
 
     home = route([best[i] for i in range(roles)], tuple(inverse(p) for p in perms))

time: 135 us -> 138 us (1.022)
  between operations: 0.98 us -> 14.4 us
  starting transfers between devices: 38.3 us -> 26 us
  local copies, waits for them, and re-layouts: 17.9 us -> 9.49 us
  matrix products: 11.6 us -> 18.4 us
  waiting for transfers between devices: 46.9 us -> 51.2 us
    ppermute x4 -> x2, waiting for transfers between devices: 2.87 us -> 33.2 us  [ring_gather(): below = lax.ppermute(block, axis, up)]
    ppermute x4 -> x2, waiting for transfers between devices: 30.3 us -> 13.6 us  [ring_gather(): far_low = lax.ppermute(below[:half], axis, up)]
    ppermute x4 -> x2, waiting for transfers between devices: 8.22 us -> 0.01 us  [ring_gather(): above = lax.ppermute(block, axis, down)]
    dot_general x3 -> x4, matrix products: 9.63 us -> 16.4 us  [best_of(): lax.dot_general(lib, both, (((1,), (1,)), ((), ())), preferred_element_ty...]
    unnamed x26 -> x16, local copies, waits for them, and re-layouts: 6.93 us -> 0.53 us
    ppermute x9, starting transfers between devices: 15.3 us -> 10.2 us  [route(): lax.ppermute(b, ZRING, p)]
    ppermute x4 -> x2, starting transfers between devices: 6.9 us -> 3.69 us  [ring_gather(): above = lax.ppermute(block, axis, down)]
    ppermute x4 -> x2, waiting for transfers between devices: 3.07 us -> 0.01 us  [ring_gather(): far_high = lax.ppermute(above[half:], axis, down)]
  transfers between devices with their start and end apart: 26 -> 19, of which waited for: 8 -> 7; matrix products, arithmetic and copies ran while one was open for 28% -> 22% of each run, Pallas kernels for 0% -> 0%
where the time goes in v5:
time: 138 us
  waiting for transfers between devices  51.2 us (37%)
  starting transfers between devices  26 us (19%)
  matrix products  18.4 us (13%)
  other arithmetic  18.3 us (13%)
  between operations  14.4 us (10%)
  local copies, waits for them, and re-layouts  9.49 us (7%)
    ppermute x2, waiting for transfers between devices, ring_gather(): below = lax.ppermute(block, axis, up)  33.2 us
    dot_general x4, matrix products, best_of(): lax.dot_general(lib, both, (((1,), (1,)), ((), ())), preferred_element_ty...  16.4 us
    ppermute x2, waiting for transfers between devices, ring_gather(): far_low = lax.ppermute(below[:half], axis, up)  13.6 us
    ppermute x9, starting transfers between devices, route(): lax.ppermute(b, ZRING, p)  10.2 us
    slice x2, local copies, waits for them, and re-layouts, lower_bins(): return jnp.concatenate([rows[..., amount:], tail], axis=-1)  6.37 us
    ppermute x2, starting transfers between devices, ring_gather(): far_high = lax.ppermute(above[half:], axis, down)  4.94 us
    ppermute x1, starting transfers between devices, on_device(): partner = lax.ppermute(packed, 'blk_1', [(0, 1), (1, 0)])  4.51 us
    reduce_sum x2, other arithmetic, unit_rows(): total = jnp.sum(values * values, axis=-1, keepdims=True)  4.4 us
  transfers between devices with their start and end apart: 19, of which 7 were waited for; matrix products, arithmetic and copies ran while one was open for 22% of the time, Pallas kernels for 0%

profile of v5, /device:TPU:1, one launch (start us, length us, event | category | flops | bytes accessed | tf_op | source)
XLA Modules:
  0.0 137.8 jit_solution(13967944251018034325)
XLA Ops:
  6.5 1.4 fusion.12
  7.9 1.1 fusion.13
  9.1 0.7 convert_bitcast_fusion
  9.9 4.5 %collective-permute-start = (bf16[32,4224]{1,0:T(8,128)(2,1)S(1)}, bf16[32,4224]{1,0:T(8,128)(2,1)S(1)}, u32[]{:S(2)}, u32[]{:S(2)}) collective-permute-start(bf16[32,4224]{1,0:T(8,128)(2,1)S(1)} %fusion.14), channel_id=1, source_target_pairs={{0,16},{16,0},{1,17},{17,1},{2,18},{18,2},{3,19},{19,3},{4,20},{20... | collective-permute-start | bytes 811016 | tf_op jit(solution)/shard_map/ppermute | solution.py:116
  14.4 0.7 fusion.112
  15.1 1.2 reduce-window.6
  16.8 0.7 and_reduce_fusion
  17.5 0.9 select_reduce_fusion.1
  18.4 1.0 collective-permute-start.5
  19.4 0.5 collective-permute-start.6
  19.9 0.3 collective-permute-start.7
  20.2 3.0 %multiply_reduce_fusion = f32[256]{0:T(256)S(1)} fusion(bf16[256,4096]{1,0:T(8,128)(2,1)} %param.6), kind=kLoop, calls=%fused_computation.13 | loop fusion | flops 3145472 | bytes 2098176 | tf_op jit(solution)/shard_map/reduce_sum | solution.py:38
  23.2 2.0 %convolution_convert_fusion = bf16[512,4096]{1,0:T(8,128)(2,1)S(1)} fusion(bf16[256,4096]{1,0:T(8,128)(2,1)S(1)} %copy-done.1, f32[256]{0:T(256)S(1)} %add_rsqrt_fusion, s32[256]{0:T(256)S(1)} %bitcast.62), kind=kOutput, calls=%fused_computation.1 | convolution fusion | flops 1079115776 | bytes 6293504 | tf_op jit(solution)/shard_map/dot_general | solution.py:132
  25.2 0.4 fusion.332
  25.7 1.5 %collective-permute-start.10 = (bf16[128,4096]{1,0:T(8,128)(2,1)S(1)}, bf16[128,4096]{1,0:T(8,128)(2,1)S(1)}, u32[]{:S(2)}, u32[]{:S(2)}) collective-permute-start(bf16[128,4096]{1,0:T(8,128)(2,1)S(1)} %get-tuple-element.302), channel_id=1, source_target_pairs={{1,2},{3,16},{17,18},{19,0},{0,19},{2,1},{16,3},{18,17},{5,6},{7,2... | collective-permute-start | bytes 3145736 | tf_op jit(solution)/shard_map/ppermute | solution.py:104
  27.2 1.8 %collective-permute-start.8 = (bf16[128,4096]{1,0:T(8,128)(2,1)S(1)}, bf16[128,4096]{1,0:T(8,128)(2,1)S(1)}, u32[]{:S(2)}, u32[]{:S(2)}) collective-permute-start(bf16[128,4096]{1,0:T(8,128)(2,1)S(1)} %get-tuple-element.304), channel_id=1, source_target_pairs={{0,1},{1,0},{2,3},{3,2},{16,17},{17,16},{18,19},{19,18},{4,5},{5,4... | collective-permute-start | bytes 3145736 | tf_op jit(solution)/shard_map/ppermute | solution.py:104
  29.0 0.7 collective-permute-start.9
  29.8 1.4 collective-permute-start.1
  31.2 1.5 %collective-permute-start.2 = (bf16[32,4224]{1,0:T(8,128)(2,1)S(1)}, bf16[32,4224]{1,0:T(8,128)(2,1)S(1)}, u32[]{:S(2)}, u32[]{:S(2)}) collective-permute-start(bf16[32,4224]{1,0:T(8,128)(2,1)S(1)} %collective-permute-done), channel_id=1, source_target_pairs={{0,12},{4,0},{8,4},{12,8},{1,13},{5,1},{9,5},{13,9},{2,14},{6,2},{... | collective-permute-start | bytes 811016 | tf_op jit(solution)/shard_map/ppermute | solution.py:96
  32.7 9.1 %collective-permute-done.1 = bf16[32,4224]{1,0:T(8,128)(2,1)S(1)} collective-permute-done((bf16[32,4224]{1,0:T(8,128)(2,1)S(1)}, bf16[32,4224]{1,0:T(8,128)(2,1)S(1)}, u32[]{:S(2)}, u32[]{:S(2)}) %collective-permute-start.1) | collective-permute-done | bytes 270368 | tf_op jit(solution)/shard_map/ppermute | solution.py:95
  42.0 2.7 %collective-permute-start.4 = (bf16[16,4224]{1,0:T(8,128)(2,1)S(1)}, bf16[16,4224]{1,0:T(8,128)(2,1)S(1)}, u32[]{:S(2)}, u32[]{:S(2)}) collective-permute-start(bf16[16,4224]{1,0:T(8,128)(2,1)S(1)} %slice.1492), channel_id=1, source_target_pairs={{0,12},{4,0},{8,4},{12,8},{1,13},{5,1},{9,5},{13,9},{2,14},{6,2},{... | collective-permute-start | bytes 405512 | tf_op jit(solution)/shard_map/ppermute | solution.py:99
  44.7 3.2 %collective-permute-done.3 = bf16[16,4224]{1,0:T(8,128)(2,1)S(1)} collective-permute-done((bf16[16,4224]{1,0:T(8,128)(2,1)S(1)}, bf16[16,4224]{1,0:T(8,128)(2,1)S(1)}, u32[]{:S(2)}, u32[]{:S(2)}) %collective-permute-start.3) | collective-permute-done | bytes 135200 | tf_op jit(solution)/shard_map/ppermute | solution.py:98
  47.9 0.6 collective-permute-start.11
  48.5 2.2 %collective-permute-start.12 = (bf16[128,4224]{1,0:T(8,128)(2,1)S(1)}, bf16[128,4224]{1,0:T(8,128)(2,1)S(1)}, u32[]{:S(2)}, u32[]{:S(2)}) collective-permute-start(bf16[128,4224]{1,0:T(8,128)(2,1)S(1)} %constant_dynamic-update-slice_fusion), channel_id=1, source_target_pairs={{0,96},{32,0},{64,32},{96,64},{1,97},{33,1},{65,33},{97,65},{2,98}... | collective-permute-start | bytes 3244040 | tf_op jit(solution)/shard_map/ppermute | solution.py:96
  50.8 1.4 collective-permute-done.9
  52.2 0.3 pad_maximum_fusion
  52.5 3.2 %slice.1506 = bf16[512,4064]{1,0:T(8,128)(2,1)S(1)} slice(bf16[512,4096]{1,0:T(8,128)(2,1)S(1)} %pad_maximum_fusion), slice={[0:512], [32:4096]} | slice | bytes 8323072 | tf_op jit(solution)/shard_map/slice | solution.py:44
  55.7 3.2 %slice.1507 = bf16[512,4080]{1,0:T(8,128)(2,1)S(1)} slice(bf16[512,4096]{1,0:T(8,128)(2,1)S(1)} %pad_maximum_fusion), slice={[0:512], [16:4096]} | slice | bytes 8355840 | tf_op jit(solution)/shard_map/slice | solution.py:44
  59.1 3.4 %select_dynamic-update-slice_fusion = bf16[1024,4096]{1,0:T(8,128)(2,1)S(1)} fusion(bf16[1024,4096]{1,0:T(8,128)(2,1)S(1)} %constant_dynamic-update-slice_fusion.5, bf16[512,4080]{1,0:T(8,128)(2,1)S(1)} %slice.1507, bf16[512,4064]{1,0:T(8,128)(2,1)S(1)} %slice.1506, pred[512]{0:T(512)(128)(4,1)S(1)} %get-tuple-element.466, ...), kind=kLoop, calls=%fused_computation.11 | loop fusion | flops 4194304 | bytes 12583936 | tf_op jit(solution)/shard_map/concatenate | solution.py:150
  62.6 2.6 %fusion.6 = f32[128,1024]{1,0:T(8,128)S(1)} fusion(bf16[128,4224]{1,0:T(8,128)(2,1)S(1)} %constant_dynamic-update-slice_fusion, bf16[1024,4096]{1,0:T(8,128)(2,1)S(1)} %select_dynamic-update-slice_fusion), kind=kOutput, calls=%fused_computation.8 | convolution fusion | flops 1107296256 | bytes 9994240 | tf_op jit(solution)/shard_map/dot_general | solution.py:153
  65.2 24.1 %collective-permute-done.11 = bf16[128,4224]{1,0:T(8,128)(2,1)S(1)} collective-permute-done((bf16[128,4224]{1,0:T(8,128)(2,1)S(1)}, bf16[128,4224]{1,0:T(8,128)(2,1)S(1)}, u32[]{:S(2)}, u32[]{:S(2)}) %collective-permute-start.11) | collective-permute-done | bytes 1081376 | tf_op jit(solution)/shard_map/ppermute | solution.py:95
  89.6 2.4 %fusion.4 = f32[256,1024]{1,0:T(8,128)S(1)} fusion(bf16[256,4224]{1,0:T(8,128)(2,1)S(1)} %constant_dynamic-update-slice_fusion.9, bf16[1024,4096]{1,0:T(8,128)(2,1)S(1)} %select_dynamic-update-slice_fusion), kind=kOutput, calls=%fused_computation.6 | convolution fusion | flops 2214592512 | bytes 11599872 | tf_op jit(solution)/shard_map/dot_general | solution.py:153
  92.1 0.2 fusion.11
  92.9 0.6 collective-permute-start.13
  93.5 2.2 %collective-permute-start.14 = (bf16[64,4224]{1,0:T(8,128)(2,1)S(1)}, bf16[64,4224]{1,0:T(8,128)(2,1)S(1)}, u32[]{:S(2)}, u32[]{:S(2)}) collective-permute-start(bf16[64,4224]{1,0:T(8,128)(2,1)S(1)} %slice.1674), channel_id=1, source_target_pairs={{0,96},{32,0},{64,32},{96,64},{1,97},{33,1},{65,33},{97,65},{2,98}... | collective-permute-start | bytes 1622024 | tf_op jit(solution)/shard_map/ppermute | solution.py:99
  95.9 10.5 %collective-permute-done.13 = bf16[64,4224]{1,0:T(8,128)(2,1)S(1)} collective-permute-done((bf16[64,4224]{1,0:T(8,128)(2,1)S(1)}, bf16[64,4224]{1,0:T(8,128)(2,1)S(1)}, u32[]{:S(2)}, u32[]{:S(2)}) %collective-permute-start.13) | collective-permute-done | bytes 540704 | tf_op jit(solution)/shard_map/ppermute | solution.py:98
  106.4 2.6 %fusion.2 = f32[128,1024]{1,0:T(8,128)S(1)} fusion(bf16[128,4224]{1,0:T(8,128)(2,1)S(1)} %constant_dynamic-update-slice_fusion.11, bf16[1024,4096]{1,0:T(8,128)(2,1)S(1)} %select_dynamic-update-slice_fusion), kind=kOutput, calls=%fused_computation.4 | convolution fusion | flops 1107296256 | bytes 9994240 | tf_op jit(solution)/shard_map/dot_general | solution.py:153
  109.2 0.2 fusion.15
  110.5 8.7 %fusion = f32[512,1024]{1,0:T(8,128)S(1)} fusion(bf16[512,4224]{1,0:T(8,128)(2,1)} %all-gather.2.cloned.1.call-done, bf16[1024,4096]{1,0:T(8,128)(2,1)} %copy-done), kind=kOutput, calls=%fused_computation.2 | convolution fusion | flops 4429185024 | bytes 14811136 | tf_op jit(solution)/shard_map/dot_general | solution.py:153
  119.3 1.1 convert_reduce_fusion
  120.3 0.3 fusion.9
  120.8 0.2 minimum_maximum_fusion.1
  122.0 2.6 %collective-permute-start.15 = (f32[128,8]{0,1:T(8,128)S(1)}, f32[128,8]{0,1:T(8,128)S(1)}, u32[]{:S(2)}, u32[]{:S(2)}) collective-permute-start(f32[128,8]{0,1:T(8,128)S(1)} %get-tuple-element.420), channel_id=1, source_target_pairs={{1,0},{0,1},{3,2},{2,3},{17,16},{16,17},{19,18},{18,19},{5,4},{4,5... | collective-permute-start | bytes 12296 | tf_op jit(solution)/shard_map/ppermute | solution.py:104
  124.7 1.6 %collective-permute-start.16 = (f32[128,8]{0,1:T(8,128)S(1)}, f32[128,8]{0,1:T(8,128)S(1)}, u32[]{:S(2)}, u32[]{:S(2)}) collective-permute-start(f32[128,8]{0,1:T(8,128)S(1)} %get-tuple-element.419), channel_id=1, source_target_pairs={{2,0},{16,2},{18,16},{0,18},{19,1},{1,3},{3,17},{17,19},{6,4},{20,... | collective-permute-start | bytes 12296 | tf_op jit(solution)/shard_map/ppermute | solution.py:104
  126.4 1.9 %collective-permute-done.16 = f32[128,8]{0,1:T(8,128)S(1)} collective-permute-done((f32[128,8]{0,1:T(8,128)S(1)}, f32[128,8]{0,1:T(8,128)S(1)}, u32[]{:S(2)}, u32[]{:S(2)}) %collective-permute-start.16) | collective-permute-done | bytes 4128 | tf_op jit(solution)/shard_map/ppermute | solution.py:104
  128.3 0.9 collective-permute-done.17
  129.4 0.7 gather_fusion
  130.3 0.7 copy.27
  (146 shorter events, 4.5 us)
Async XLA Ops:
  6.5 16.7 %copy-start.1 = (bf16[256,4096]{1,0:T(8,128)(2,1)S(1)}, bf16[256,4096]{1,0:T(8,128)(2,1)}, u32[]{:S(2)}) copy-start(bf16[256,4096]{1,0:T(8,128)(2,1)} %param.6) | copy-start | bytes 6291460
  6.5 104.0 %all-gather.2.cloned.1.call-start = ((), (), s32[]{:S(2)}) async-start(), calls=%async_computation | async-start | bytes 4595712 | tf_op jit(solution)/shard_map/all_gather | solution.py:119
  9.8 4.5 %copy-start.2 = (bf16[32,4224]{1,0:T(8,128)(2,1)}, bf16[32,4224]{1,0:T(8,128)(2,1)S(1)}, u32[]{:S(2)}) copy-start(bf16[32,4224]{1,0:T(8,128)(2,1)S(1)} %fusion.14) | copy-start | bytes 811012
  9.9 19.9 %collective-permute-start = (bf16[32,4224]{1,0:T(8,128)(2,1)S(1)}, bf16[32,4224]{1,0:T(8,128)(2,1)S(1)}, u32[]{:S(2)}, u32[]{:S(2)}) collective-permute-start(bf16[32,4224]{1,0:T(8,128)(2,1)S(1)} %fusion.14), channel_id=1, source_target_pairs={{0,16},{16,0},{1,17},{17,1},{2,18},{18,2},{3,19},{19,3},{4,20},{20... | collective-permute-start | bytes 811016 | tf_op jit(solution)/shard_map/ppermute | solution.py:116
  18.4 8.9 %collective-permute-start.5 = (s32[2,128]{1,0:T(2,128)S(1)}, s32[2,128]{1,0:T(2,128)S(1)}, u32[]{:S(2)}, u32[]{:S(2)}) collective-permute-start(s32[2,128]{1,0:T(2,128)S(1)} %get-tuple-element.468), channel_id=1, source_target_pairs={{0,1},{1,0},{2,3},{3,2},{16,17},{17,16},{18,19},{19,18},{4,5},{5,4... | collective-permute-start | bytes 3080 | tf_op jit(solution)/shard_map/ppermute | solution.py:104
  19.4 9.6 %collective-permute-start.6 = (s32[2,128]{1,0:T(2,128)S(1)}, s32[2,128]{1,0:T(2,128)S(1)}, u32[]{:S(2)}, u32[]{:S(2)}) collective-permute-start(s32[2,128]{1,0:T(2,128)S(1)} %get-tuple-element.470), channel_id=1, source_target_pairs={{0,2},{2,16},{16,18},{18,0},{1,19},{3,1},{17,3},{19,17},{4,6},{6,2... | collective-permute-start | bytes 3080 | tf_op jit(solution)/shard_map/ppermute | solution.py:104
  19.9 9.8 %collective-permute-start.7 = (s32[2,128]{1,0:T(2,128)S(1)}, s32[2,128]{1,0:T(2,128)S(1)}, u32[]{:S(2)}, u32[]{:S(2)}) collective-permute-start(s32[2,128]{1,0:T(2,128)S(1)} %get-tuple-element.469), channel_id=1, source_target_pairs={{1,2},{3,16},{17,18},{19,0},{0,19},{2,1},{16,3},{18,17},{5,6},{7,2... | collective-permute-start | bytes 3080 | tf_op jit(solution)/shard_map/ppermute | solution.py:104
  25.7 25.1 %collective-permute-start.10 = (bf16[128,4096]{1,0:T(8,128)(2,1)S(1)}, bf16[128,4096]{1,0:T(8,128)(2,1)S(1)}, u32[]{:S(2)}, u32[]{:S(2)}) collective-permute-start(bf16[128,4096]{1,0:T(8,128)(2,1)S(1)} %get-tuple-element.302), channel_id=1, source_target_pairs={{1,2},{3,16},{17,18},{19,0},{0,19},{2,1},{16,3},{18,17},{5,6},{7,2... | collective-permute-start | bytes 3145736 | tf_op jit(solution)/shard_map/ppermute | solution.py:104
  27.2 23.6 %collective-permute-start.8 = (bf16[128,4096]{1,0:T(8,128)(2,1)S(1)}, bf16[128,4096]{1,0:T(8,128)(2,1)S(1)}, u32[]{:S(2)}, u32[]{:S(2)}) collective-permute-start(bf16[128,4096]{1,0:T(8,128)(2,1)S(1)} %get-tuple-element.304), channel_id=1, source_target_pairs={{0,1},{1,0},{2,3},{3,2},{16,17},{17,16},{18,19},{19,18},{4,5},{5,4... | collective-permute-start | bytes 3145736 | tf_op jit(solution)/shard_map/ppermute | solution.py:104
  29.0 23.2 %collective-permute-start.9 = (bf16[128,4096]{1,0:T(8,128)(2,1)S(1)}, bf16[128,4096]{1,0:T(8,128)(2,1)S(1)}, u32[]{:S(2)}, u32[]{:S(2)}) collective-permute-start(bf16[128,4096]{1,0:T(8,128)(2,1)S(1)} %get-tuple-element.303), channel_id=1, source_target_pairs={{0,2},{2,16},{16,18},{18,0},{1,19},{3,1},{17,3},{19,17},{4,6},{6,2... | collective-permute-start | bytes 3145736 | tf_op jit(solution)/shard_map/ppermute | solution.py:104
  29.8 12.0 %collective-permute-start.1 = (bf16[32,4224]{1,0:T(8,128)(2,1)S(1)}, bf16[32,4224]{1,0:T(8,128)(2,1)S(1)}, u32[]{:S(2)}, u32[]{:S(2)}) collective-permute-start(bf16[32,4224]{1,0:T(8,128)(2,1)S(1)} %collective-permute-done), channel_id=1, source_target_pairs={{0,4},{4,8},{8,12},{12,0},{1,5},{5,9},{9,13},{13,1},{2,6},{6,10},{... | collective-permute-start | bytes 811016 | tf_op jit(solution)/shard_map/ppermute | solution.py:95
  31.2 10.8 %collective-permute-start.2 = (bf16[32,4224]{1,0:T(8,128)(2,1)S(1)}, bf16[32,4224]{1,0:T(8,128)(2,1)S(1)}, u32[]{:S(2)}, u32[]{:S(2)}) collective-permute-start(bf16[32,4224]{1,0:T(8,128)(2,1)S(1)} %collective-permute-done), channel_id=1, source_target_pairs={{0,12},{4,0},{8,4},{12,8},{1,13},{5,1},{9,5},{13,9},{2,14},{6,2},{... | collective-permute-start | bytes 811016 | tf_op jit(solution)/shard_map/ppermute | solution.py:96
  41.8 6.1 %collective-permute-start.3 = (bf16[16,4224]{1,0:T(8,128)(2,1)S(1)}, bf16[16,4224]{1,0:T(8,128)(2,1)S(1)}, u32[]{:S(2)}, u32[]{:S(2)}) collective-permute-start(bf16[16,4224]{1,0:T(8,128)(2,1)S(1)} %slice.1491), channel_id=1, source_target_pairs={{0,4},{4,8},{8,12},{12,0},{1,5},{5,9},{9,13},{13,1},{2,6},{6,10},{... | collective-permute-start | bytes 405512 | tf_op jit(solution)/shard_map/ppermute | solution.py:98
  42.0 6.0 %collective-permute-start.4 = (bf16[16,4224]{1,0:T(8,128)(2,1)S(1)}, bf16[16,4224]{1,0:T(8,128)(2,1)S(1)}, u32[]{:S(2)}, u32[]{:S(2)}) collective-permute-start(bf16[16,4224]{1,0:T(8,128)(2,1)S(1)} %slice.1492), channel_id=1, source_target_pairs={{0,12},{4,0},{8,4},{12,8},{1,13},{5,1},{9,5},{13,9},{2,14},{6,2},{... | collective-permute-start | bytes 405512 | tf_op jit(solution)/shard_map/ppermute | solution.py:99
  47.9 41.4 %collective-permute-start.11 = (bf16[128,4224]{1,0:T(8,128)(2,1)S(1)}, bf16[128,4224]{1,0:T(8,128)(2,1)S(1)}, u32[]{:S(2)}, u32[]{:S(2)}) collective-permute-start(bf16[128,4224]{1,0:T(8,128)(2,1)S(1)} %constant_dynamic-update-slice_fusion), channel_id=1, source_target_pairs={{0,32},{32,64},{64,96},{96,0},{1,33},{33,65},{65,97},{97,1},{2,34}... | collective-permute-start | bytes 3244040 | tf_op jit(solution)/shard_map/ppermute | solution.py:95
  48.5 40.9 %collective-permute-start.12 = (bf16[128,4224]{1,0:T(8,128)(2,1)S(1)}, bf16[128,4224]{1,0:T(8,128)(2,1)S(1)}, u32[]{:S(2)}, u32[]{:S(2)}) collective-permute-start(bf16[128,4224]{1,0:T(8,128)(2,1)S(1)} %constant_dynamic-update-slice_fusion), channel_id=1, source_target_pairs={{0,96},{32,0},{64,32},{96,64},{1,97},{33,1},{65,33},{97,65},{2,98}... | collective-permute-start | bytes 3244040 | tf_op jit(solution)/shard_map/ppermute | solution.py:96
  62.6 43.9 %copy-start = (bf16[1024,4096]{1,0:T(8,128)(2,1)}, bf16[1024,4096]{1,0:T(8,128)(2,1)S(1)}, u32[]{:S(2)}) copy-start(bf16[1024,4096]{1,0:T(8,128)(2,1)S(1)} %select_dynamic-update-slice_fusion) | copy-start | bytes 25165828
  92.9 13.4 %collective-permute-start.13 = (bf16[64,4224]{1,0:T(8,128)(2,1)S(1)}, bf16[64,4224]{1,0:T(8,128)(2,1)S(1)}, u32[]{:S(2)}, u32[]{:S(2)}) collective-permute-start(bf16[64,4224]{1,0:T(8,128)(2,1)S(1)} %slice.1673), channel_id=1, source_target_pairs={{0,32},{32,64},{64,96},{96,0},{1,33},{33,65},{65,97},{97,1},{2,34}... | collective-permute-start | bytes 1622024 | tf_op jit(solution)/shard_map/ppermute | solution.py:98
  93.5 12.9 %collective-permute-start.14 = (bf16[64,4224]{1,0:T(8,128)(2,1)S(1)}, bf16[64,4224]{1,0:T(8,128)(2,1)S(1)}, u32[]{:S(2)}, u32[]{:S(2)}) collective-permute-start(bf16[64,4224]{1,0:T(8,128)(2,1)S(1)} %slice.1674), channel_id=1, source_target_pairs={{0,96},{32,0},{64,32},{96,64},{1,97},{33,1},{65,33},{97,65},{2,98}... | collective-permute-start | bytes 1622024 | tf_op jit(solution)/shard_map/ppermute | solution.py:99
  122.0 4.3 %collective-permute-start.15 = (f32[128,8]{0,1:T(8,128)S(1)}, f32[128,8]{0,1:T(8,128)S(1)}, u32[]{:S(2)}, u32[]{:S(2)}) collective-permute-start(f32[128,8]{0,1:T(8,128)S(1)} %get-tuple-element.420), channel_id=1, source_target_pairs={{1,0},{0,1},{3,2},{2,3},{17,16},{16,17},{19,18},{18,19},{5,4},{4,5... | collective-permute-start | bytes 12296 | tf_op jit(solution)/shard_map/ppermute | solution.py:104
  124.7 3.7 %collective-permute-start.16 = (f32[128,8]{0,1:T(8,128)S(1)}, f32[128,8]{0,1:T(8,128)S(1)}, u32[]{:S(2)}, u32[]{:S(2)}) collective-permute-start(f32[128,8]{0,1:T(8,128)S(1)} %get-tuple-element.419), channel_id=1, source_target_pairs={{2,0},{16,2},{18,16},{0,18},{19,1},{1,3},{3,17},{17,19},{6,4},{20,... | collective-permute-start | bytes 12296 | tf_op jit(solution)/shard_map/ppermute | solution.py:104
  126.2 3.0 %collective-permute-start.17 = (f32[128,8]{0,1:T(8,128)S(1)}, f32[128,8]{0,1:T(8,128)S(1)}, u32[]{:S(2)}, u32[]{:S(2)}) collective-permute-start(f32[128,8]{0,1:T(8,128)S(1)} %get-tuple-element.418), channel_id=1, source_target_pairs={{2,1},{16,3},{18,17},{0,19},{19,0},{1,2},{3,16},{17,18},{6,5},{20,... | collective-permute-start | bytes 12296 | tf_op jit(solution)/shard_map/ppermute | solution.py:104
Sparse Core Ops, SparseCore 0:
  14.5 67.0 all-gather.1

commit v6 on v5

--- a/solution.py
+++ b/solution.py
@@ -115,12 +115,7 @@
     packed = jnp.concatenate([unit_lib, bin_cols], axis=1)
     partner = lax.ppermute(packed, "blk_1", [(0, 1), (1, 0)])
     chunk = jnp.concatenate([packed, partner], axis=0)
-    half = chunk.shape[0] // 2
-    gathered = lax.all_gather(chunk[:half], ("blk_0", "blk_2"), axis=0, tiled=True)
-    y_first = ring_gather(chunk[half:], "blk_2")
-    y_then_x = ring_gather(jnp.concatenate(y_first, axis=0), "blk_0")
-    middle = jnp.concatenate(y_then_x[1:3], axis=0)
-    late = jnp.concatenate(y_then_x[3:], axis=0)
+    gathered = lax.all_gather(chunk, ("blk_0", "blk_2"), axis=0, tiled=True)
 
     unit_q = unit_rows(queries)
     group = query_group[:, 0]
@@ -155,9 +150,7 @@
         near = jnp.abs(lib_bins[:, None] - flat_bin[None, :]) <= WIN
         return top_rows(jnp.where(near, jnp.maximum(prod[:, :total], prod[:, total:]), 0.0))
 
-    best = bitonic_merge(best_of(y_then_x[0]), best_of(middle), 1)
-    best = bitonic_merge(best, best_of(late), 1)
-    best = bitonic_merge(best, best_of(gathered), 1)
+    best = best_of(gathered)
     best = jnp.concatenate(best, axis=0).T.reshape(roles, CAP, K)
 
     home = route([best[i] for i in range(roles)], tuple(inverse(p) for p in perms))

time: 138 us -> 130 us (0.942); the launches traced: 138 us -> 128 us
  starting transfers between devices: 26 us -> 13.8 us
  local copies, waits for them, and re-layouts: 9.49 us -> 13.2 us
  matrix products: 18.4 us -> 16.2 us
  waiting for transfers between devices: 51.2 us -> 52.7 us
    ppermute x8 -> x0, waiting for transfers between devices: 46.9 us -> none  [the longest x2 33.2 us: ring_gather(): below = lax.ppermute(block, axis, up)]
    all_gather x1, waiting for transfers between devices: 0.02 us -> 24.2 us  [on_device(): gathered = lax.all_gather(chunk, ('blk_0', 'blk_2'), axis=0, tiled=True)]
    ppermute x9, waiting for transfers between devices: 4.26 us -> 22.3 us  [route(): lax.ppermute(b, ZRING, p)]
    ppermute x8 -> x0, starting transfers between devices: 11.2 us -> none  [the longest x2 4.94 us: ring_gather(): far_high = lax.ppermute(above[half:], axis, down)]
    ppermute x1, waiting for transfers between devices: 0.01 us -> 6.21 us  [on_device(): partner = lax.ppermute(packed, 'blk_1', [(0, 1), (1, 0)])]
    unnamed x16 -> x12, local copies, waits for them, and re-layouts: 0.53 us -> 3.3 us
    dot_general x4 -> x1, matrix products: 16.4 us -> 14.2 us  [best_of(): lax.dot_general(lib, both, (((1,), (1,)), ((), ())), preferred_element_ty...]
  transfers between devices with their start and end apart: 19 -> 11, of which waited for: 7 -> 6; matrix products, arithmetic and copies ran while one was open for 22% -> 18% of each run, Pallas kernels for 0% -> 0%
where the time goes in v6:
time: 130 us; the launch traced here: 128 us
  waiting for transfers between devices  52.7 us (41%)
  other arithmetic  18.1 us (14%)
  matrix products  16.2 us (12%)
  starting transfers between devices  13.8 us (11%)
  between operations  13.8 us (11%)
  local copies, waits for them, and re-layouts  13.2 us (10%)
    all_gather x1, waiting for transfers between devices, on_device(): gathered = lax.all_gather(chunk, ('blk_0', 'blk_2'), axis=0, tiled=True)  24.2 us
    ppermute x9, waiting for transfers between devices, route(): lax.ppermute(b, ZRING, p)  22.3 us
    dot_general x1, matrix products, best_of(): lax.dot_general(lib, both, (((1,), (1,)), ((), ())), preferred_element_ty...  14.2 us
    ppermute x9, starting transfers between devices, route(): lax.ppermute(b, ZRING, p)  9.25 us
    slice x2, local copies, waits for them, and re-layouts, lower_bins(): return jnp.concatenate([rows[..., amount:], tail], axis=-1)  6.41 us
    ppermute x1, waiting for transfers between devices, on_device(): partner = lax.ppermute(packed, 'blk_1', [(0, 1), (1, 0)])  6.21 us
    ppermute x1, starting transfers between devices, on_device(): partner = lax.ppermute(packed, 'blk_1', [(0, 1), (1, 0)])  4.51 us
    reduce_sum x2, other arithmetic, unit_rows(): total = jnp.sum(values * values, axis=-1, keepdims=True)  4.4 us
  transfers between devices with their start and end apart: 11, of which 6 were waited for; matrix products, arithmetic and copies ran while one was open for 18% of the time, Pallas kernels for 0%

profile of v6, /device:TPU:1, one launch (start us, length us, event | category | flops | bytes accessed | tf_op | source)
XLA Modules:
  0.0 127.7 jit_solution(3884566214483193959)
XLA Ops:
  6.5 1.4 %fusion.4 = f32[32]{0:T(128)S(1)} fusion(bf16[1,32,4096]{2,1,0:T(8,128)(2,1)} %param.10), kind=kLoop, calls=%fused_computation.16 | loop fusion | flops 393184 | bytes 262272 | tf_op jit(solution)/shard_map/reduce_sum | solution.py:38
  7.9 1.1 fusion.5
  9.1 0.7 convert_bitcast_fusion
  9.7 0.1 copy.28
  9.9 4.5 %collective-permute-start = (bf16[32,4224]{1,0:T(8,128)(2,1)S(1)}, bf16[32,4224]{1,0:T(8,128)(2,1)S(1)}, u32[]{:S(2)}, u32[]{:S(2)}) collective-permute-start(bf16[32,4224]{1,0:T(8,128)(2,1)S(1)} %pad_maximum_fusion.2), channel_id=1, source_target_pairs={{0,16},{16,0},{1,17},{17,1},{2,18},{18,2},{3,19},{19,3},{4,20},{20... | collective-permute-start | bytes 811016 | tf_op jit(solution)/shard_map/ppermute | solution.py:116
  14.4 6.2 %collective-permute-done = bf16[32,4224]{1,0:T(8,128)(2,1)S(1)} collective-permute-done((bf16[32,4224]{1,0:T(8,128)(2,1)S(1)}, bf16[32,4224]{1,0:T(8,128)(2,1)S(1)}, u32[]{:S(2)}, u32[]{:S(2)}) %collective-permute-start) | collective-permute-done | bytes 270368 | tf_op jit(solution)/shard_map/ppermute | solution.py:116
  20.6 0.8 pad_maximum_fusion.1
  21.5 0.7 fusion.53
  22.2 1.2 reduce-window.6
  23.5 0.1 copy.20
  23.8 3.0 %multiply_reduce_fusion = f32[256]{0:T(256)S(1)} fusion(bf16[256,4096]{1,0:T(8,128)(2,1)} %param.6), kind=kLoop, calls=%fused_computation.7 | loop fusion | flops 3145472 | bytes 2098176 | tf_op jit(solution)/shard_map/reduce_sum | solution.py:38
  26.9 2.0 %convolution_convert_fusion = bf16[512,4096]{1,0:T(8,128)(2,1)S(1)} fusion(bf16[256,4096]{1,0:T(8,128)(2,1)S(1)} %copy-done, f32[256]{0:T(256)S(1)} %add_rsqrt_fusion, s32[256]{0:T(256)S(1)} %bitcast.58), kind=kOutput, calls=%fused_computation.3 | convolution fusion | flops 1079115776 | bytes 6293504 | tf_op jit(solution)/shard_map/dot_general | solution.py:127
  28.9 1.6 %fusion.130 = (bf16[128,4096]{1,0:T(8,128)(2,1)S(1)}, bf16[1024,4096]{1,0:T(8,128)(2,1)}, bf16[128,4096]{1,0:T(8,128)(2,1)S(1)}, bf16[128,4096]{1,0:T(8,128)(2,1)S(1)}, bf16[128,4096]{1,0:T(8,128)(2,1)S(1)}) fusion(bf16[512,4096]{1,0:T(8,128)(2,1)S(1)} %convolution_convert_fusion), kind=kLoop, calls=%fused_computation.261 | loop fusion | bytes 9437184 | tf_op jit(solution)/shard_map/slice | solution.py:136
  30.5 1.2 collective-permute-start.4
  31.7 3.1 %collective-permute-start.5 = (bf16[128,4096]{1,0:T(8,128)(2,1)S(1)}, bf16[128,4096]{1,0:T(8,128)(2,1)S(1)}, u32[]{:S(2)}, u32[]{:S(2)}) collective-permute-start(bf16[128,4096]{1,0:T(8,128)(2,1)S(1)} %get-tuple-element.102), channel_id=1, source_target_pairs={{0,2},{2,16},{16,18},{18,0},{1,19},{3,1},{17,3},{19,17},{4,6},{6,2... | collective-permute-start | bytes 3145736 | tf_op jit(solution)/shard_map/ppermute | solution.py:104
  34.9 0.2 select_reduce_fusion.1
  35.1 0.6 collective-permute-start.1
  35.7 0.3 collective-permute-start.2
  36.0 0.5 collective-permute-done.1
  36.5 1.5 %collective-permute-start.3 = (s32[2,128]{1,0:T(2,128)S(1)}, s32[2,128]{1,0:T(2,128)S(1)}, u32[]{:S(2)}, u32[]{:S(2)}) collective-permute-start(s32[2,128]{1,0:T(2,128)S(1)} %get-tuple-element.164), channel_id=1, source_target_pairs={{1,2},{3,16},{17,18},{19,0},{0,19},{2,1},{16,3},{18,17},{5,6},{7,2... | collective-permute-start | bytes 3080 | tf_op jit(solution)/shard_map/ppermute | solution.py:104
  38.0 19.2 %collective-permute-done.2 = s32[2,128]{1,0:T(2,128)S(1)} collective-permute-done((s32[2,128]{1,0:T(2,128)S(1)}, s32[2,128]{1,0:T(2,128)S(1)}, u32[]{:S(2)}, u32[]{:S(2)}) %collective-permute-start.2) | collective-permute-done | bytes 1056 | tf_op jit(solution)/shard_map/ppermute | solution.py:104
  57.3 0.5 pad_maximum_fusion
  57.8 3.2 %slice.588 = bf16[512,4064]{1,0:T(8,128)(2,1)S(1)} slice(bf16[512,4096]{1,0:T(8,128)(2,1)S(1)} %pad_maximum_fusion), slice={[0:512], [32:4096]} | slice | bytes 8323072 | tf_op jit(solution)/shard_map/slice | solution.py:44
  61.0 3.2 %slice.589 = bf16[512,4080]{1,0:T(8,128)(2,1)S(1)} slice(bf16[512,4096]{1,0:T(8,128)(2,1)S(1)} %pad_maximum_fusion), slice={[0:512], [16:4096]} | slice | bytes 8355840 | tf_op jit(solution)/shard_map/slice | solution.py:44
  64.2 1.1 constant_dynamic-update-slice_fusion.2
  65.3 1.0 constant_dynamic-update-slice_fusion.1
  66.3 1.1 constant_dynamic-update-slice_fusion
  67.4 4.1 %select_dynamic-update-slice_fusion = bf16[1024,4096]{1,0:T(8,128)(2,1)} fusion(bf16[1024,4096]{1,0:T(8,128)(2,1)} %constant_dynamic-update-slice_fusion, bf16[512,4080]{1,0:T(8,128)(2,1)S(1)} %slice.589, bf16[512,4064]{1,0:T(8,128)(2,1)S(1)} %slice.588, pred[512]{0:T(512)(128)(4,1)S(1)} %get-tuple-element.161, pred[512]{0:T(512)(128)(4,1)S(1)} %get-tuple-element.160), kind=kLoop, calls=%fused_computation.5 | loop fusion | flops 4194304 | bytes 12534784 | tf_op jit(solution)/shard_map/concatenate | solution.py:145
  71.5 24.2 %all-gather.2.cloned.1.call-done = bf16[1024,4224]{1,0:T(8,128)(2,1)} async-done(((bf16[64,4224]{1,0:T(8,128)(2,1)}), bf16[1024,4224]{1,0:T(8,128)(2,1)}) %all-gather.2.cloned.1.call-update) | async-done | bytes 8650768 | tf_op jit(solution)/shard_map/all_gather | solution.py:118
  95.7 1.2 convert_reduce_fusion
  96.9 14.2 %fusion = f32[1024,1024]{1,0:T(8,128)S(1)} fusion(bf16[1024,4224]{1,0:T(8,128)(2,1)} %all-gather.2.cloned.1.call-done, bf16[1024,4096]{1,0:T(8,128)(2,1)} %select_dynamic-update-slice_fusion), kind=kOutput, calls=%fused_computation.1 | convolution fusion | flops 8858370048 | bytes 21233664 | tf_op jit(solution)/shard_map/dot_general | solution.py:148
  111.1 0.5 fusion.2
  111.7 0.3 minimum_minimum_fusion.4
  112.0 0.4 minimum_maximum_fusion.1
  112.5 0.3 minimum_maximum_fusion
  112.7 0.2 minimum_minimum_fusion.6
  113.0 0.2 maximum_maximum_fusion.3
  113.3 0.1 minimum_minimum_fusion.8
  113.4 0.1 maximum_maximum_fusion.5
  114.2 0.8 collective-permute-start.7
  114.9 1.3 collective-permute-start.8
  116.2 0.4 collective-permute-start.9
  116.7 1.9 %collective-permute-done.8 = f32[128,8]{0,1:T(8,128)S(1)} collective-permute-done((f32[128,8]{0,1:T(8,128)S(1)}, f32[128,8]{0,1:T(8,128)S(1)}, u32[]{:S(2)}, u32[]{:S(2)}) %collective-permute-start.8) | collective-permute-done | bytes 4128 | tf_op jit(solution)/shard_map/ppermute | solution.py:104
  118.6 0.6 collective-permute-done.9
  119.3 0.1 copy.26
  119.4 0.7 gather_fusion
  120.1 0.1 broadcast_select_fusion
  120.2 0.7 copy.27
  (60 shorter events, 1.1 us)
Async XLA Ops:
  6.5 20.3 %copy-start.1 = (s32[256,1]{0,1:T(1,128)S(1)}, s32[256,1]{0,1:T(1,128)}, u32[]{:S(2)}) copy-start(s32[256,1]{0,1:T(1,128)} %param.7) | copy-start | bytes 3076
  6.5 20.3 %copy-start = (bf16[256,4096]{1,0:T(8,128)(2,1)S(1)}, bf16[256,4096]{1,0:T(8,128)(2,1)}, u32[]{:S(2)}) copy-start(bf16[256,4096]{1,0:T(8,128)(2,1)} %param.6) | copy-start | bytes 6291460
  6.5 89.2 %all-gather.2.cloned.1.call-start = ((), (), s32[]{:S(2)}) async-start(), calls=%async_computation | async-start | bytes 9191424 | tf_op jit(solution)/shard_map/all_gather | solution.py:118
  9.9 10.7 %collective-permute-start = (bf16[32,4224]{1,0:T(8,128)(2,1)S(1)}, bf16[32,4224]{1,0:T(8,128)(2,1)S(1)}, u32[]{:S(2)}, u32[]{:S(2)}) collective-permute-start(bf16[32,4224]{1,0:T(8,128)(2,1)S(1)} %pad_maximum_fusion.2), channel_id=1, source_target_pairs={{0,16},{16,0},{1,17},{17,1},{2,18},{18,2},{3,19},{19,3},{4,20},{20... | collective-permute-start | bytes 811016 | tf_op jit(solution)/shard_map/ppermute | solution.py:116
  28.9 6.0 %copy-start.2 = (s32[256]{0:T(256)S(1)}, s32[256]{0:T(256)}, u32[]{:S(2)}) copy-start(s32[256]{0:T(256)} %param.8) | copy-start | bytes 3076
  28.9 6.0 %copy-start.3 = (s32[256]{0:T(256)S(1)}, s32[256]{0:T(256)}, u32[]{:S(2)}) copy-start(s32[256]{0:T(256)} %param.9) | copy-start | bytes 3076
  30.5 26.7 %collective-permute-start.4 = (bf16[128,4096]{1,0:T(8,128)(2,1)S(1)}, bf16[128,4096]{1,0:T(8,128)(2,1)S(1)}, u32[]{:S(2)}, u32[]{:S(2)}) collective-permute-start(bf16[128,4096]{1,0:T(8,128)(2,1)S(1)} %get-tuple-element.103), channel_id=1, source_target_pairs={{0,1},{1,0},{2,3},{3,2},{16,17},{17,16},{18,19},{19,18},{4,5},{5,4... | collective-permute-start | bytes 3145736 | tf_op jit(solution)/shard_map/ppermute | solution.py:104
  31.7 25.5 %collective-permute-start.5 = (bf16[128,4096]{1,0:T(8,128)(2,1)S(1)}, bf16[128,4096]{1,0:T(8,128)(2,1)S(1)}, u32[]{:S(2)}, u32[]{:S(2)}) collective-permute-start(bf16[128,4096]{1,0:T(8,128)(2,1)S(1)} %get-tuple-element.102), channel_id=1, source_target_pairs={{0,2},{2,16},{16,18},{18,0},{1,19},{3,1},{17,3},{19,17},{4,6},{6,2... | collective-permute-start | bytes 3145736 | tf_op jit(solution)/shard_map/ppermute | solution.py:104
  34.9 22.4 %collective-permute-start.6 = (bf16[128,4096]{1,0:T(8,128)(2,1)S(1)}, bf16[128,4096]{1,0:T(8,128)(2,1)S(1)}, u32[]{:S(2)}, u32[]{:S(2)}) collective-permute-start(bf16[128,4096]{1,0:T(8,128)(2,1)S(1)} %get-tuple-element.101), channel_id=1, source_target_pairs={{1,2},{3,16},{17,18},{19,0},{0,19},{2,1},{16,3},{18,17},{5,6},{7,2... | collective-permute-start | bytes 3145736 | tf_op jit(solution)/shard_map/ppermute | solution.py:104
  35.1 1.4 %collective-permute-start.1 = (s32[2,128]{1,0:T(2,128)S(1)}, s32[2,128]{1,0:T(2,128)S(1)}, u32[]{:S(2)}, u32[]{:S(2)}) collective-permute-start(s32[2,128]{1,0:T(2,128)S(1)} %get-tuple-element.163), channel_id=1, source_target_pairs={{0,1},{1,0},{2,3},{3,2},{16,17},{17,16},{18,19},{19,18},{4,5},{5,4... | collective-permute-start | bytes 3080 | tf_op jit(solution)/shard_map/ppermute | solution.py:104
  35.7 21.5 %collective-permute-start.2 = (s32[2,128]{1,0:T(2,128)S(1)}, s32[2,128]{1,0:T(2,128)S(1)}, u32[]{:S(2)}, u32[]{:S(2)}) collective-permute-start(s32[2,128]{1,0:T(2,128)S(1)} %get-tuple-element.165), channel_id=1, source_target_pairs={{0,2},{2,16},{16,18},{18,0},{1,19},{3,1},{17,3},{19,17},{4,6},{6,2... | collective-permute-start | bytes 3080 | tf_op jit(solution)/shard_map/ppermute | solution.py:104
  36.5 20.7 %collective-permute-start.3 = (s32[2,128]{1,0:T(2,128)S(1)}, s32[2,128]{1,0:T(2,128)S(1)}, u32[]{:S(2)}, u32[]{:S(2)}) collective-permute-start(s32[2,128]{1,0:T(2,128)S(1)} %get-tuple-element.164), channel_id=1, source_target_pairs={{1,2},{3,16},{17,18},{19,0},{0,19},{2,1},{16,3},{18,17},{5,6},{7,2... | collective-permute-start | bytes 3080 | tf_op jit(solution)/shard_map/ppermute | solution.py:104
  114.2 2.5 %collective-permute-start.7 = (f32[128,8]{0,1:T(8,128)S(1)}, f32[128,8]{0,1:T(8,128)S(1)}, u32[]{:S(2)}, u32[]{:S(2)}) collective-permute-start(f32[128,8]{0,1:T(8,128)S(1)} %get-tuple-element.147), channel_id=1, source_target_pairs={{1,0},{0,1},{3,2},{2,3},{17,16},{16,17},{19,18},{18,19},{5,4},{4,5... | collective-permute-start | bytes 12296 | tf_op jit(solution)/shard_map/ppermute | solution.py:104
  114.9 3.7 %collective-permute-start.8 = (f32[128,8]{0,1:T(8,128)S(1)}, f32[128,8]{0,1:T(8,128)S(1)}, u32[]{:S(2)}, u32[]{:S(2)}) collective-permute-start(f32[128,8]{0,1:T(8,128)S(1)} %get-tuple-element.146), channel_id=1, source_target_pairs={{2,0},{16,2},{18,16},{0,18},{19,1},{1,3},{3,17},{17,19},{6,4},{20,... | collective-permute-start | bytes 12296 | tf_op jit(solution)/shard_map/ppermute | solution.py:104
  116.2 3.0 %collective-permute-start.9 = (f32[128,8]{0,1:T(8,128)S(1)}, f32[128,8]{0,1:T(8,128)S(1)}, u32[]{:S(2)}, u32[]{:S(2)}) collective-permute-start(f32[128,8]{0,1:T(8,128)S(1)} %get-tuple-element.145), channel_id=1, source_target_pairs={{2,1},{16,3},{18,17},{0,19},{19,0},{1,2},{3,16},{17,18},{6,5},{20,... | collective-permute-start | bytes 12296 | tf_op jit(solution)/shard_map/ppermute | solution.py:104
Sparse Core Ops, SparseCore 0:
  21.6 74.1 all-gather.1

commit v7 on v2

--- a/solution.py
+++ b/solution.py
@@ -92,13 +92,11 @@
     roles = 4
     slots = roles * CAP
 
-    z_hi = lax.axis_index("blk_1")
-    unit_lib = unit_rows(library[0])
-    partner = lax.ppermute(unit_lib, "blk_1", [(0, 1), (1, 0)])
-    pair = jnp.where(z_hi == 0, jnp.concatenate([unit_lib, partner], axis=0),
-                     jnp.concatenate([partner, unit_lib], axis=0))
-    full = lax.all_gather(pair, ("blk_0", "blk_2"), axis=0, tiled=True)
-    lib_bins = lax.all_gather(library_bin[0], ("blk_0", "blk_2", "blk_1"), axis=0, tiled=True)
+    partner = lax.ppermute(library[0], "blk_1", [(0, 1), (1, 0)])
+    partner_bin = lax.ppermute(library_bin[0], "blk_1", [(0, 1), (1, 0)])
+    chunk = jnp.concatenate([unit_rows(library[0]), unit_rows(partner)], axis=0)
+    chunk_bin = jnp.concatenate([library_bin[0], partner_bin], axis=0)
+    full, lib_bins = lax.all_gather((chunk, chunk_bin), ("blk_0", "blk_2"), axis=0, tiled=True)
 
     unit_q = unit_rows(queries)
     group = query_group[:, 0]

time: 125 us -> 123 us (0.984); the launches traced: 123 us -> 123 us
  blocking collectives: 33.5 us -> 13.8 us
  waiting for transfers between devices: 14 us -> 32.1 us
    unnamed x1, blocking collectives: 33.5 us -> 13.8 us
    ppermute x1 -> x2, waiting for transfers between devices: 6.03 us -> 25.1 us  [the longest x1 21.2 us: on_device(): partner_bin = lax.ppermute(library_bin[0], 'blk_1', [(0, 1), (1, 0)])]
    all_gather x1, waiting for transfers between devices: 5.33 us -> 3.39 us  [on_device(): lax.all_gather((chunk, chunk_bin), ('blk_0', 'blk_2'), axis=0, tiled=True)]
    ppermute x1 -> x2, starting transfers between devices: 4.51 us -> 5.37 us  [the longest x1 4.43 us: on_device(): partner = lax.ppermute(library[0], 'blk_1', [(0, 1), (1, 0)])]
    reduce_sum x2 -> x3, other arithmetic: 4.4 us -> 4.56 us  [unit_rows(): total = jnp.sum(values * values, axis=-1, keepdims=True)]
    unnamed x18 -> x17, local copies, waits for them, and re-layouts: 5.16 us -> 5.04 us
  transfers between devices with their start and end apart: 11 -> 12, of which waited for: 4 -> 5; matrix products, arithmetic and copies ran while one was open for 22% -> 24% of each run, Pallas kernels for 0% -> 0%
where the time goes in v7:
time: 123 us
  waiting for transfers between devices  32.1 us (26%)
  other arithmetic  17.8 us (14%)
  local copies, waits for them, and re-layouts  15.7 us (13%)
  matrix products  14.9 us (12%)
  between operations  14.5 us (12%)
  starting transfers between devices  14.2 us (12%)
  blocking collectives  13.8 us (11%)
    ppermute x1, waiting for transfers between devices, on_device(): partner_bin = lax.ppermute(library_bin[0], 'blk_1', [(0, 1), (1, 0)])  21.2 us
    unnamed x1, blocking collectives  13.8 us
    dot_general x1, matrix products, on_device(): lax.dot_general(full, both, (((1,), (1,)), ((), ())), preferred_element_t...  12.9 us
    ppermute x9, starting transfers between devices, route(): lax.ppermute(b, ZRING, p)  8.81 us
    slice x2, local copies, waits for them, and re-layouts, lower_bins(): return jnp.concatenate([rows[..., amount:], tail], axis=-1)  6.43 us
    unnamed x17, local copies, waits for them, and re-layouts  5.04 us
    reduce_sum x3, other arithmetic, unit_rows(): total = jnp.sum(values * values, axis=-1, keepdims=True)  4.56 us
    ppermute x1, starting transfers between devices, on_device(): partner = lax.ppermute(library[0], 'blk_1', [(0, 1), (1, 0)])  4.43 us
  transfers between devices with their start and end apart: 12, of which 5 were waited for; matrix products, arithmetic and copies ran while one was open for 24% of the time, Pallas kernels for 0%

profile of v7, /device:TPU:1, one launch (start us, length us, event | category | flops | bytes accessed | tf_op | source)
XLA Modules:
  0.0 123.0 jit_solution(11481582203607225934)
XLA Ops:
  6.5 4.4 %collective-permute-start.4 = (bf16[32,4096]{1,0:T(8,128)(2,1)}, bf16[32,4096]{1,0:T(8,128)(2,1)S(1)}, u32[]{:S(2)}, u32[]{:S(2)}) collective-permute-start(bf16[32,4096]{1,0:T(8,128)(2,1)} %bitcast.54), channel_id=1, source_target_pairs={{0,16},{16,0},{1,17},{17,1},{2,18},{18,2},{3,19},{19,3},{4,20},{20... | collective-permute-start | bytes 786440 | tf_op jit(solution)/shard_map/ppermute | solution.py:95
  11.0 1.3 %multiply_reduce_fusion.2 = f32[32]{0:T(128)S(1)} fusion(bf16[1,32,4096]{2,1,0:T(8,128)(2,1)} %param.10), kind=kLoop, calls=%fused_computation.16 | loop fusion | flops 393184 | bytes 262272 | tf_op jit(solution)/shard_map/reduce_sum | solution.py:37
  12.2 1.1 multiply_convert_fusion.3
  13.4 3.8 %collective-permute-done.4 = bf16[32,4096]{1,0:T(8,128)(2,1)S(1)} collective-permute-done((bf16[32,4096]{1,0:T(8,128)(2,1)}, bf16[32,4096]{1,0:T(8,128)(2,1)S(1)}, u32[]{:S(2)}, u32[]{:S(2)}) %collective-permute-start.4) | collective-permute-done | bytes 262176 | tf_op jit(solution)/shard_map/ppermute | solution.py:95
  17.2 0.3 multiply_reduce_fusion.1
  17.5 0.2 multiply_convert_fusion.2
  17.7 0.8 pad_maximum_fusion.1
  18.6 0.7 fusion.49
  19.3 1.2 reduce-window.6
  20.6 0.1 copy.18
  20.9 3.0 %multiply_reduce_fusion = f32[256]{0:T(256)S(1)} fusion(bf16[256,4096]{1,0:T(8,128)(2,1)} %param.6), kind=kLoop, calls=%fused_computation.5 | loop fusion | flops 3145472 | bytes 2098176 | tf_op jit(solution)/shard_map/reduce_sum | solution.py:37
  24.0 2.0 %convolution_convert_fusion = bf16[512,4096]{1,0:T(8,128)(2,1)S(1)} fusion(bf16[256,4096]{1,0:T(8,128)(2,1)S(1)} %copy-done, f32[256]{0:T(256)S(1)} %add_rsqrt_fusion, s32[256]{0:T(256)S(1)} %bitcast.56), kind=kOutput, calls=%fused_computation.1 | convolution fusion | flops 1079115776 | bytes 6293504 | tf_op jit(solution)/shard_map/dot_general | solution.py:108
  26.1 2.3 %fusion.125 = (bf16[128,4096]{1,0:T(8,128)(2,1)S(1)}, bf16[1024,4096]{1,0:T(8,128)(2,1)}, bf16[128,4096]{1,0:T(8,128)(2,1)}, bf16[128,4096]{1,0:T(8,128)(2,1)}, bf16[128,4096]{1,0:T(8,128)(2,1)}) fusion(bf16[512,4096]{1,0:T(8,128)(2,1)S(1)} %convolution_convert_fusion), kind=kLoop, calls=%fused_computation.258 | loop fusion | bytes 9437184 | tf_op jit(solution)/shard_map/slice | solution.py:117
  28.4 1.2 collective-permute-start.5
  29.6 3.1 %collective-permute-start.6 = (bf16[128,4096]{1,0:T(8,128)(2,1)}, bf16[128,4096]{1,0:T(8,128)(2,1)S(1)}, u32[]{:S(2)}, u32[]{:S(2)}) collective-permute-start(bf16[128,4096]{1,0:T(8,128)(2,1)} %get-tuple-element.102), channel_id=1, source_target_pairs={{0,2},{2,16},{16,18},{18,0},{1,19},{3,1},{17,3},{19,17},{4,6},{6,2... | collective-permute-start | bytes 3145736 | tf_op jit(solution)/shard_map/ppermute | solution.py:85
  32.8 0.2 select_reduce_fusion.1
  33.0 0.6 collective-permute-start.1
  33.6 0.9 collective-permute-start
  34.5 0.6 dynamic-slice
  35.8 21.2 %collective-permute-done = s32[32]{0:T(128)S(1)} collective-permute-done((s32[32]{0:T(128)S(1)}, s32[32]{0:T(128)S(1)}, u32[]{:S(2)}, u32[]{:S(2)}) %collective-permute-start) | collective-permute-done | bytes 160 | tf_op jit(solution)/shard_map/ppermute | solution.py:96
  57.0 0.2 add_dynamic-update-slice_fusion
  57.2 0.7 collective-permute-start.3
  57.8 13.8 %all-reduce.2 = s32[1024]{0:T(1024)S(1)} all-reduce(s32[1024]{0:T(1024)S(1)} %add_dynamic-update-slice_fusion), channel_id=1, replica_groups=mesh['blk_0'=4,'blk_1'=2,'blk_2'=4,'rep'=4] {'blk_0','blk_2'}, use_global_device_ids=true, to_apply=%add.2 | all-reduce | flops 1024 | bytes 8192
  71.7 1.6 %pad_maximum_fusion = bf16[512,4096]{1,0:T(8,128)(2,1)S(1)} fusion(bf16[128,4096]{1,0:T(8,128)(2,1)} %collective-permute-done.7, bf16[128,4096]{1,0:T(8,128)(2,1)S(1)} %collective-permute-done.6, bf16[128,4096]{1,0:T(8,128)(2,1)S(1)} %collective-permute-done.5, bf16[128,4096]{1,0:T(8,128)(2,1)S(1)} %get-tuple-element.99), kind=kLoop, calls=%fused_computation.2 | loop fusion | flops 16777216 | bytes 8388608 | tf_op jit(solution)/shard_map/concatenate | solution.py:117
  73.3 3.2 %slice.583 = bf16[512,4064]{1,0:T(8,128)(2,1)S(1)} slice(bf16[512,4096]{1,0:T(8,128)(2,1)S(1)} %pad_maximum_fusion), slice={[0:512], [32:4096]} | slice | bytes 8323072 | tf_op jit(solution)/shard_map/slice | solution.py:43
  76.5 3.2 %slice.584 = bf16[512,4080]{1,0:T(8,128)(2,1)S(1)} slice(bf16[512,4096]{1,0:T(8,128)(2,1)S(1)} %pad_maximum_fusion), slice={[0:512], [16:4096]} | slice | bytes 8355840 | tf_op jit(solution)/shard_map/slice | solution.py:43
  79.8 1.1 constant_dynamic-update-slice_fusion.2
  80.8 1.0 constant_dynamic-update-slice_fusion.1
  81.9 2.3 %constant_dynamic-update-slice_fusion = bf16[1024,4096]{1,0:T(8,128)(2,1)} fusion(bf16[1024,4096]{1,0:T(8,128)(2,1)} %constant_dynamic-update-slice_fusion.1, bf16[128,4096]{1,0:T(8,128)(2,1)} %collective-permute-done.7), kind=kLoop, calls=%fused_computation.126 | loop fusion | bytes 2097152
  84.2 4.1 %select_dynamic-update-slice_fusion = bf16[1024,4096]{1,0:T(8,128)(2,1)} fusion(bf16[1024,4096]{1,0:T(8,128)(2,1)} %constant_dynamic-update-slice_fusion, bf16[512,4080]{1,0:T(8,128)(2,1)S(1)} %slice.584, bf16[512,4064]{1,0:T(8,128)(2,1)S(1)} %slice.583, pred[512]{0:T(512)(128)(4,1)S(1)} %get-tuple-element.161, pred[512]{0:T(512)(128)(4,1)S(1)} %get-tuple-element.160), kind=kLoop, calls=%fused_computation.3 | loop fusion | flops 4194304 | bytes 12534784 | tf_op jit(solution)/shard_map/concatenate | solution.py:126
  88.3 3.4 %all-gather.2.cloned.1.call-done = bf16[1024,4096]{1,0:T(8,128)(2,1)} async-done(((bf16[64,4096]{1,0:T(8,128)(2,1)}), bf16[1024,4096]{1,0:T(8,128)(2,1)}) %all-gather.2.cloned.1.call-update) | async-done | bytes 8388624 | tf_op jit(solution)/shard_map/all_gather | solution.py:99
  91.7 12.9 %fusion.127 = f32[1024,1024]{1,0:T(8,128)S(1)} fusion(bf16[1024,4096]{1,0:T(8,128)(2,1)} %all-gather.2.cloned.1.call-done, bf16[1024,4096]{1,0:T(8,128)(2,1)} %select_dynamic-update-slice_fusion), kind=kOutput, calls=%fused_computation.260 | convolution fusion | flops 8589934592 | bytes 20971520 | tf_op jit(solution)/shard_map/dot_general | solution.py:127
  104.6 0.5 fusion
  105.2 0.3 minimum_minimum_fusion.4
  105.5 0.4 minimum_maximum_fusion.1
  106.0 0.3 minimum_maximum_fusion
  106.2 0.2 minimum_minimum_fusion.6
  106.5 0.2 maximum_maximum_fusion.3
  106.8 0.1 minimum_minimum_fusion.8
  106.9 0.1 maximum_maximum_fusion.5
  107.7 1.9 %collective-permute-start.10 = (f32[128,8]{0,1:T(8,128)S(1)}, f32[128,8]{0,1:T(8,128)S(1)}, u32[]{:S(2)}, u32[]{:S(2)}) collective-permute-start(f32[128,8]{0,1:T(8,128)S(1)} %get-tuple-element.145), channel_id=1, source_target_pairs={{2,1},{16,3},{18,17},{0,19},{19,0},{1,2},{3,16},{17,18},{6,5},{20,... | collective-permute-start | bytes 12296 | tf_op jit(solution)/shard_map/ppermute | solution.py:85
  109.6 1.2 %collective-permute-start.8 = (f32[128,8]{0,1:T(8,128)S(1)}, f32[128,8]{0,1:T(8,128)S(1)}, u32[]{:S(2)}, u32[]{:S(2)}) collective-permute-start(f32[128,8]{0,1:T(8,128)S(1)} %get-tuple-element.147), channel_id=1, source_target_pairs={{1,0},{0,1},{3,2},{2,3},{17,16},{16,17},{19,18},{18,19},{5,4},{4,5... | collective-permute-start | bytes 12296 | tf_op jit(solution)/shard_map/ppermute | solution.py:85
  110.9 0.8 collective-permute-done.8
  111.7 2.8 %collective-permute-done.9 = f32[128,8]{0,1:T(8,128)S(1)} collective-permute-done((f32[128,8]{0,1:T(8,128)S(1)}, f32[128,8]{0,1:T(8,128)S(1)}, u32[]{:S(2)}, u32[]{:S(2)}) %collective-permute-start.9) | collective-permute-done | bytes 4128 | tf_op jit(solution)/shard_map/ppermute | solution.py:85
  114.5 0.1 copy.23
  114.7 0.7 gather_fusion
  115.4 0.1 broadcast_select_fusion
  115.5 0.7 copy.24
  (68 shorter events, 1.1 us)
Async XLA Ops:
  6.5 17.4 %copy-start.1 = (s32[256,1]{0,1:T(1,128)S(1)}, s32[256,1]{0,1:T(1,128)}, u32[]{:S(2)}) copy-start(s32[256,1]{0,1:T(1,128)} %param.7) | copy-start | bytes 3076
  6.5 17.5 %copy-start = (bf16[256,4096]{1,0:T(8,128)(2,1)S(1)}, bf16[256,4096]{1,0:T(8,128)(2,1)}, u32[]{:S(2)}) copy-start(bf16[256,4096]{1,0:T(8,128)(2,1)} %param.6) | copy-start | bytes 6291460
  6.5 85.2 %all-gather.2.cloned.1.call-start = ((), (), s32[]{:S(2)}) async-start(), calls=%async_computation | async-start | bytes 8912896 | tf_op jit(solution)/shard_map/all_gather | solution.py:99
  6.5 10.7 %collective-permute-start.4 = (bf16[32,4096]{1,0:T(8,128)(2,1)}, bf16[32,4096]{1,0:T(8,128)(2,1)S(1)}, u32[]{:S(2)}, u32[]{:S(2)}) collective-permute-start(bf16[32,4096]{1,0:T(8,128)(2,1)} %bitcast.54), channel_id=1, source_target_pairs={{0,16},{16,0},{1,17},{17,1},{2,18},{18,2},{3,19},{19,3},{4,20},{20... | collective-permute-start | bytes 786440 | tf_op jit(solution)/shard_map/ppermute | solution.py:95
  26.0 6.7 %copy-start.2 = (s32[256]{0:T(256)S(1)}, s32[256]{0:T(256)}, u32[]{:S(2)}) copy-start(s32[256]{0:T(256)} %param.8) | copy-start | bytes 3076
  26.0 6.7 %copy-start.3 = (s32[256]{0:T(256)S(1)}, s32[256]{0:T(256)}, u32[]{:S(2)}) copy-start(s32[256]{0:T(256)} %param.9) | copy-start | bytes 3076
  26.0 7.5 %copy-start.4 = (s32[1,32]{1,0:T(1,128)S(1)}, s32[1,32]{1,0:T(1,128)}, u32[]{:S(2)}) copy-start(s32[1,32]{1,0:T(1,128)} %param.11) | copy-start | bytes 388
  26.0 8.5 %copy-start.5 = (u32[128]{0:T(128)S(1)}, u32[128]{0:T(128)}, u32[]{:S(2)}) copy-start(u32[128]{0:T(128)} %constant.92) | copy-start | bytes 1540
  28.4 43.3 %collective-permute-start.5 = (bf16[128,4096]{1,0:T(8,128)(2,1)}, bf16[128,4096]{1,0:T(8,128)(2,1)S(1)}, u32[]{:S(2)}, u32[]{:S(2)}) collective-permute-start(bf16[128,4096]{1,0:T(8,128)(2,1)} %get-tuple-element.103), channel_id=1, source_target_pairs={{0,1},{1,0},{2,3},{3,2},{16,17},{17,16},{18,19},{19,18},{4,5},{5,4... | collective-permute-start | bytes 3145736 | tf_op jit(solution)/shard_map/ppermute | solution.py:85
  29.6 42.1 %collective-permute-start.6 = (bf16[128,4096]{1,0:T(8,128)(2,1)}, bf16[128,4096]{1,0:T(8,128)(2,1)S(1)}, u32[]{:S(2)}, u32[]{:S(2)}) collective-permute-start(bf16[128,4096]{1,0:T(8,128)(2,1)} %get-tuple-element.102), channel_id=1, source_target_pairs={{0,2},{2,16},{16,18},{18,0},{1,19},{3,1},{17,3},{19,17},{4,6},{6,2... | collective-permute-start | bytes 3145736 | tf_op jit(solution)/shard_map/ppermute | solution.py:85
  32.8 39.0 %collective-permute-start.7 = (bf16[128,4096]{1,0:T(8,128)(2,1)}, bf16[128,4096]{1,0:T(8,128)(2,1)}, u32[]{:S(2)}, u32[]{:S(2)}) collective-permute-start(bf16[128,4096]{1,0:T(8,128)(2,1)} %get-tuple-element.101), channel_id=1, source_target_pairs={{1,2},{3,16},{17,18},{19,0},{0,19},{2,1},{16,3},{18,17},{5,6},{7,2... | collective-permute-start | bytes 3145736 | tf_op jit(solution)/shard_map/ppermute | solution.py:85
  33.0 24.2 %collective-permute-start.1 = (s32[2,128]{1,0:T(2,128)S(1)}, s32[2,128]{1,0:T(2,128)S(1)}, u32[]{:S(2)}, u32[]{:S(2)}) collective-permute-start(s32[2,128]{1,0:T(2,128)S(1)} %get-tuple-element.163), channel_id=1, source_target_pairs={{0,1},{1,0},{2,3},{3,2},{16,17},{17,16},{18,19},{19,18},{4,5},{5,4... | collective-permute-start | bytes 3080 | tf_op jit(solution)/shard_map/ppermute | solution.py:85
  33.6 23.4 %collective-permute-start = (s32[32]{0:T(128)S(1)}, s32[32]{0:T(128)S(1)}, u32[]{:S(2)}, u32[]{:S(2)}) collective-permute-start(s32[32]{0:T(128)S(1)} %bitcast.69), channel_id=1, source_target_pairs={{0,16},{16,0},{1,17},{17,1},{2,18},{18,2},{3,19},{19,3},{4,20},{20... | collective-permute-start | bytes 392 | tf_op jit(solution)/shard_map/ppermute | solution.py:96
  57.0 14.7 %collective-permute-start.2 = (s32[2,128]{1,0:T(2,128)S(1)}, s32[2,128]{1,0:T(2,128)S(1)}, u32[]{:S(2)}, u32[]{:S(2)}) collective-permute-start(s32[2,128]{1,0:T(2,128)S(1)} %get-tuple-element.165), channel_id=1, source_target_pairs={{0,2},{2,16},{16,18},{18,0},{1,19},{3,1},{17,3},{19,17},{4,6},{6,2... | collective-permute-start | bytes 3080 | tf_op jit(solution)/shard_map/ppermute | solution.py:85
  57.2 14.5 %collective-permute-start.3 = (s32[2,128]{1,0:T(2,128)S(1)}, s32[2,128]{1,0:T(2,128)S(1)}, u32[]{:S(2)}, u32[]{:S(2)}) collective-permute-start(s32[2,128]{1,0:T(2,128)S(1)} %get-tuple-element.164), channel_id=1, source_target_pairs={{1,2},{3,16},{17,18},{19,0},{0,19},{2,1},{16,3},{18,17},{5,6},{7,2... | collective-permute-start | bytes 3080 | tf_op jit(solution)/shard_map/ppermute | solution.py:85
  107.7 3.2 %collective-permute-start.10 = (f32[128,8]{0,1:T(8,128)S(1)}, f32[128,8]{0,1:T(8,128)S(1)}, u32[]{:S(2)}, u32[]{:S(2)}) collective-permute-start(f32[128,8]{0,1:T(8,128)S(1)} %get-tuple-element.145), channel_id=1, source_target_pairs={{2,1},{16,3},{18,17},{0,19},{19,0},{1,2},{3,16},{17,18},{6,5},{20,... | collective-permute-start | bytes 12296 | tf_op jit(solution)/shard_map/ppermute | solution.py:85
  109.6 2.1 %collective-permute-start.8 = (f32[128,8]{0,1:T(8,128)S(1)}, f32[128,8]{0,1:T(8,128)S(1)}, u32[]{:S(2)}, u32[]{:S(2)}) collective-permute-start(f32[128,8]{0,1:T(8,128)S(1)} %get-tuple-element.147), channel_id=1, source_target_pairs={{1,0},{0,1},{3,2},{2,3},{17,16},{16,17},{19,18},{18,19},{5,4},{4,5... | collective-permute-start | bytes 12296 | tf_op jit(solution)/shard_map/ppermute | solution.py:85
  110.9 3.7 %collective-permute-start.9 = (f32[128,8]{0,1:T(8,128)S(1)}, f32[128,8]{0,1:T(8,128)S(1)}, u32[]{:S(2)}, u32[]{:S(2)}) collective-permute-start(f32[128,8]{0,1:T(8,128)S(1)} %get-tuple-element.146), channel_id=1, source_target_pairs={{2,0},{16,2},{18,16},{0,18},{19,1},{1,3},{3,17},{17,19},{6,4},{20,... | collective-permute-start | bytes 12296 | tf_op jit(solution)/shard_map/ppermute | solution.py:85
Sparse Core Ops, SparseCore 0:
  18.7 73.0 all-gather.1

commit v8 on v6

--- a/solution.py
+++ b/solution.py
@@ -77,7 +77,6 @@
 
 def top_rows(scores):
     depth = scores.shape[0] // K
-    assert depth & (depth - 1) == 0
     lists = [scores[k * depth:(k + 1) * depth] for k in range(K)]
     for stage in SORT8:
         for i, j in stage:
@@ -110,33 +109,40 @@
     roles = 4
     slots = roles * CAP
 
-    unit_lib = unit_rows(library[0])
     bin_cols = jnp.pad(library_bin[0].astype(jnp.bfloat16)[:, None], ((0, 0), (0, LANE - 1)))
-    packed = jnp.concatenate([unit_lib, bin_cols], axis=1)
-    partner = lax.ppermute(packed, "blk_1", [(0, 1), (1, 0)])
-    chunk = jnp.concatenate([packed, partner], axis=0)
-    gathered = lax.all_gather(chunk, ("blk_0", "blk_2"), axis=0, tiled=True)
+    partner = lax.ppermute(jnp.concatenate([library[0], bin_cols], axis=1), "blk_1", [(0, 1), (1, 0)])
+    own = jnp.concatenate([unit_rows(library[0]), bin_cols], axis=1)
+    partner = jnp.concatenate([unit_rows(partner[:, :W]), partner[:, W:]], axis=1)
+    half = own.shape[0]
+    x_first = ring_gather(own, "blk_0")
+    y_first = ring_gather(partner, "blk_2")
 
     unit_q = unit_rows(queries)
+    meta_cols = jnp.stack([query_bin, query_shift], axis=1).astype(jnp.bfloat16)
+    unit_q = jnp.concatenate([unit_q, jnp.pad(meta_cols, ((0, 0), (0, LANE - 2)))], axis=1)
     group = query_group[:, 0]
     role = ((group // 2) != z_lo).astype(jnp.int32) * 2 + ((group % 2) != core).astype(jnp.int32)
     slot = slot_index(role, roles, CAP)
     slot_ids = jnp.arange(slots, dtype=jnp.int32)
     placed = slot[:, None] == slot_ids[None, :]
-    placed_int = placed.astype(jnp.int32)
     send_q = lax.dot_general(
         placed.astype(jnp.bfloat16), unit_q, (((0,), (0,)), ((), ())),
         preferred_element_type=jnp.float32,
-    ).astype(jnp.bfloat16).reshape(roles, CAP, W)
-    send_bin = jnp.sum(placed_int * query_bin[:, None], axis=0).reshape(roles, CAP)
-    send_shift = jnp.sum(placed_int * query_shift[:, None], axis=0).reshape(roles, CAP)
-    send_meta = jnp.stack([send_bin, send_shift], axis=1)
+    ).astype(jnp.bfloat16).reshape(roles, CAP, W + LANE)
 
     perms = (SIBLING, UP, CROSS)
-    rows = jnp.concatenate(route([send_q[i] for i in range(roles)], perms), axis=0)
-    meta = jnp.stack(route([send_meta[i] for i in range(roles)], perms), axis=0)
-    flat_bin = meta[:, 0].reshape(-1)
-    flat_shift = meta[:, 1].reshape(-1)
+    received = jnp.concatenate(route([send_q[i] for i in range(roles)], perms), axis=0)
+    x_block, y_block, received = lax.optimization_barrier(
+        (jnp.concatenate(x_first, axis=0), jnp.concatenate(y_first, axis=0), received))
+    x_then_y = ring_gather(x_block, "blk_2")
+    y_then_x = ring_gather(y_block, "blk_0")
+    early = jnp.concatenate([own, partner] + x_first[1:] + y_first[1:], axis=0)
+    middle = jnp.concatenate(x_then_y[1:3] + y_then_x[1:3], axis=0)
+    late = jnp.concatenate(x_then_y[3:] + y_then_x[3:], axis=0)
+
+    rows = received[:, :W]
+    flat_bin = received[:, W].astype(jnp.int32)
+    flat_shift = received[:, W + 1].astype(jnp.int32)
     total = rows.shape[0]
 
     moved = jnp.zeros_like(rows)
@@ -150,7 +156,8 @@
         near = jnp.abs(lib_bins[:, None] - flat_bin[None, :]) <= WIN
         return top_rows(jnp.where(near, jnp.maximum(prod[:, :total], prod[:, total:]), 0.0))
 
-    best = best_of(gathered)
+    best = bitonic_merge(best_of(early), best_of(middle), 1)
+    best = bitonic_merge(best, best_of(late), 1)
     best = jnp.concatenate(best, axis=0).T.reshape(roles, CAP, K)
 
     home = route([best[i] for i in range(roles)], tuple(inverse(p) for p in perms))

time: 130 us -> 127 us (0.977); the launches traced: 128 us -> 127 us
  waiting for transfers between devices: 52.7 us -> 15.4 us
  starting transfers between devices: 13.8 us -> 38.7 us
  other arithmetic: 18.1 us -> 34.4 us
  between operations: 13.8 us -> 0.94 us
  local copies, waits for them, and re-layouts: 13.2 us -> 20.1 us
    all_gather x1 -> x0, waiting for transfers between devices: 24.2 us -> none  [on_device(): gathered = lax.all_gather(chunk, ('blk_0', 'blk_2'), axis=0, tiled=True)]
    ppermute x1 -> x17, starting transfers between devices: 4.51 us -> 27 us  [the longest x4 11.4 us: ring_gather(): far_high = lax.ppermute(above[half:], axis, down)]
    ppermute x9 -> x6, waiting for transfers between devices: 22.3 us -> 2.84 us  [route(): lax.ppermute(b, ZRING, p)]
    ppermute x1 -> x17, waiting for transfers between devices: 6.21 us -> 12.5 us  [the longest x4 7.95 us: ring_gather(): far_low = lax.ppermute(below[:half], axis, up)]
    concatenate x1, other arithmetic: 0.51 us -> 5.31 us  [on_device(): jnp.concatenate(route([send_q[i] for i in range(roles)], perms), axis=0)]
    unnamed x12 -> x31, local copies, waits for them, and re-layouts: 3.3 us -> 7.76 us
    select_n x0 -> x1, other arithmetic: none -> 4.14 us  [on_device(): jnp.where((flat_shift == s)[:, None], lower_bins(rows, s * SHIFT_BINS), m...]
    slice x2 -> x12, local copies, waits for them, and re-layouts: 0.18 us -> 3.94 us  [the longest x1 2.52 us: on_device(): rows = received[:, :W]]
  transfers between devices with their start and end apart: 11 -> 23, of which waited for: 6 -> 8; matrix products, arithmetic and copies ran while one was open for 18% -> 31% of each run, Pallas kernels for 0% -> 0%
where the time goes in v8:
time: 127 us
  starting transfers between devices  38.7 us (30%)
  other arithmetic  34.4 us (27%)
  local copies, waits for them, and re-layouts  20.1 us (16%)
  matrix products  17.1 us (13%)
  waiting for transfers between devices  15.4 us (12%)
    dot_general x3, matrix products, best_of(): lax.dot_general(lib, both, (((1,), (1,)), ((), ())), preferred_element_ty...  14 us
    ppermute x6, starting transfers between devices, route(): lax.ppermute(b, ZRING, p)  11.8 us
    ppermute x4, starting transfers between devices, ring_gather(): far_high = lax.ppermute(above[half:], axis, down)  11.4 us
    ppermute x4, waiting for transfers between devices, ring_gather(): far_low = lax.ppermute(below[:half], axis, up)  7.95 us
    unnamed x31, local copies, waits for them, and re-layouts  7.76 us
    concatenate x1, other arithmetic, on_device(): both = jnp.pad(jnp.concatenate([rows, moved], axis=0), ((0, 0), (0, LANE)))  7.61 us
    ppermute x4, starting transfers between devices, ring_gather(): above = lax.ppermute(block, axis, down)  6.83 us
    slice x2, local copies, waits for them, and re-layouts, lower_bins(): return jnp.concatenate([rows[..., amount:], tail], axis=-1)  5.52 us
  transfers between devices with their start and end apart: 23, of which 8 were waited for; matrix products, arithmetic and copies ran while one was open for 31% of the time, Pallas kernels for 0%

profile of v8, /device:TPU:1, one launch (start us, length us, event | category | flops | bytes accessed | tf_op | source)
XLA Modules:
  0.0 126.7 jit_solution(3841950271943394413)
XLA Ops:
  0.0 0.8 convert_bitcast_fusion
  0.9 1.2 multiply_reduce_fusion.2
  2.2 1.1 multiply_convert_fusion.2
  3.3 1.8 %constant_dynamic-update-slice_fusion.9 = (bf16[256,4224]{1,0:T(8,128)(2,1)}, bf16[128,4224]{1,0:T(8,128)(2,1)}, bf16[32,4224]{1,0:T(8,128)(2,1)S(1)}, bf16[32,4224]{1,0:T(8,128)(2,1)S(1)}) fusion(bf16[32,1]{1,0:T(8,128)(2,1)S(1)} %copy.20, bf16[32,4096]{1,0:T(8,128)(2,1)S(1)} %multiply_convert_fusion.2, bf16[32,4096]{1,0:T(8,128)(2,1)} %bitcast.38), kind=kLoop, calls=%fused_computation.104 | loop fusion | flops 1216510 | bytes 1605696
  5.1 2.0 %collective-permute-start.1 = (bf16[32,4224]{1,0:T(8,128)(2,1)S(1)}, bf16[32,4224]{1,0:T(8,128)(2,1)S(1)}, u32[]{:S(2)}, u32[]{:S(2)}) collective-permute-start(bf16[32,4224]{1,0:T(8,128)(2,1)S(1)} %get-tuple-element.285), channel_id=1, source_target_pairs={{0,32},{32,64},{64,96},{96,0},{1,33},{33,65},{65,97},{97,1},{2,34}... | collective-permute-start | bytes 811016 | tf_op jit(solution)/shard_map/ppermute | solution.py:94
  7.2 1.3 %collective-permute-start.2 = (bf16[32,4224]{1,0:T(8,128)(2,1)S(1)}, bf16[32,4224]{1,0:T(8,128)(2,1)S(1)}, u32[]{:S(2)}, u32[]{:S(2)}) collective-permute-start(bf16[32,4224]{1,0:T(8,128)(2,1)S(1)} %get-tuple-element.285), channel_id=1, source_target_pairs={{0,96},{32,0},{64,32},{96,64},{1,97},{33,1},{65,33},{97,65},{2,98}... | collective-permute-start | bytes 811016 | tf_op jit(solution)/shard_map/ppermute | solution.py:95
  8.4 3.8 %collective-permute-start = (bf16[32,4224]{1,0:T(8,128)(2,1)S(1)}, bf16[32,4224]{1,0:T(8,128)(2,1)S(1)}, u32[]{:S(2)}, u32[]{:S(2)}) collective-permute-start(bf16[32,4224]{1,0:T(8,128)(2,1)S(1)} %get-tuple-element.407), channel_id=1, source_target_pairs={{0,16},{16,0},{1,17},{17,1},{2,18},{18,2},{3,19},{19,3},{4,20},{20... | collective-permute-start | bytes 811016 | tf_op jit(solution)/shard_map/ppermute | solution.py:113
  12.4 1.4 %multiply_reduce_fusion = f32[256]{0:T(256)S(1)} fusion(bf16[256,4096]{1,0:T(8,128)(2,1)S(1)} %copy-done.1), kind=kLoop, calls=%fused_computation.11 | loop fusion | flops 3145472 | bytes 2098176 | tf_op jit(solution)/shard_map/reduce_sum | solution.py:38
  13.9 2.6 %multiply_convert_fusion = bf16[256,4096]{1,0:T(8,128)(2,1)} fusion(bf16[256,4096]{1,0:T(8,128)(2,1)S(1)} %copy-done.1, f32[256]{0:T(256)S(1)} %add_rsqrt_fusion), kind=kLoop, calls=%fused_computation.10 | loop fusion | flops 3145728 | bytes 4195328 | tf_op jit(solution)/shard_map/convert_element_type | solution.py:39
  16.5 1.2 reduce-window.6
  18.2 3.1 %convolution_convert_fusion = bf16[512,4224]{1,0:T(8,128)(2,1)S(1)} fusion(bf16[256,2]{1,0:T(8,128)(2,1)S(1)} %copy.21, bf16[256,4096]{1,0:T(8,128)(2,1)} %multiply_convert_fusion, s32[256]{0:T(256)S(1)} %bitcast.45), kind=kOutput, calls=%fused_computation.5 | convolution fusion | flops 1116078080 | bytes 6424576 | tf_op jit(solution)/shard_map/dot_general | solution.py:128
  21.6 2.2 %collective-permute-start.11 = (bf16[128,4224]{1,0:T(8,128)(2,1)S(1)}, bf16[128,4224]{1,0:T(8,128)(2,1)S(1)}, u32[]{:S(2)}, u32[]{:S(2)}) collective-permute-start(bf16[128,4224]{1,0:T(8,128)(2,1)S(1)} %get-tuple-element.250), channel_id=1, source_target_pairs={{1,2},{3,16},{17,18},{19,0},{0,19},{2,1},{16,3},{18,17},{5,6},{7,2... | collective-permute-start | bytes 3244040 | tf_op jit(solution)/shard_map/ppermute | solution.py:103
  23.8 1.9 %collective-permute-start.10 = (bf16[128,4224]{1,0:T(8,128)(2,1)S(1)}, bf16[128,4224]{1,0:T(8,128)(2,1)S(1)}, u32[]{:S(2)}, u32[]{:S(2)}) collective-permute-start(bf16[128,4224]{1,0:T(8,128)(2,1)S(1)} %get-tuple-element.251), channel_id=1, source_target_pairs={{0,2},{2,16},{16,18},{18,0},{1,19},{3,1},{17,3},{19,17},{4,6},{6,2... | collective-permute-start | bytes 3244040 | tf_op jit(solution)/shard_map/ppermute | solution.py:103
  26.2 2.7 %collective-permute-start.4 = (bf16[16,4224]{1,0:T(8,128)(2,1)S(1)}, bf16[16,4224]{1,0:T(8,128)(2,1)S(1)}, u32[]{:S(2)}, u32[]{:S(2)}) collective-permute-start(bf16[16,4224]{1,0:T(8,128)(2,1)S(1)} %slice.1272), channel_id=1, source_target_pairs={{0,96},{32,0},{64,32},{96,64},{1,97},{33,1},{65,33},{97,65},{2,98}... | collective-permute-start | bytes 405512 | tf_op jit(solution)/shard_map/ppermute | solution.py:98
  29.1 0.9 constant_dynamic-update-slice_fusion.8
  29.9 0.9 constant_dynamic-update-slice_fusion.7
  30.8 0.9 constant_dynamic-update-slice_fusion.6
  31.7 1.3 %collective-permute-start.5 = (bf16[32,4224]{1,0:T(8,128)(2,1)S(1)}, bf16[32,4224]{1,0:T(8,128)(2,1)S(1)}, u32[]{:S(2)}, u32[]{:S(2)}) collective-permute-start(bf16[32,4224]{1,0:T(8,128)(2,1)S(1)} %get-tuple-element.282), channel_id=1, source_target_pairs={{0,4},{4,8},{8,12},{12,0},{1,5},{5,9},{9,13},{13,1},{2,6},{6,10},{... | collective-permute-start | bytes 811016 | tf_op jit(solution)/shard_map/ppermute | solution.py:94
  33.0 0.8 constant_dynamic-update-slice_fusion.5
  33.8 1.4 %collective-permute-start.6 = (bf16[32,4224]{1,0:T(8,128)(2,1)S(1)}, bf16[32,4224]{1,0:T(8,128)(2,1)S(1)}, u32[]{:S(2)}, u32[]{:S(2)}) collective-permute-start(bf16[32,4224]{1,0:T(8,128)(2,1)S(1)} %get-tuple-element.282), channel_id=1, source_target_pairs={{0,12},{4,0},{8,4},{12,8},{1,13},{5,1},{9,5},{13,9},{2,14},{6,2},{... | collective-permute-start | bytes 811016 | tf_op jit(solution)/shard_map/ppermute | solution.py:95
  35.9 3.7 %collective-permute-done.5 = bf16[32,4224]{1,0:T(8,128)(2,1)S(1)} collective-permute-done((bf16[32,4224]{1,0:T(8,128)(2,1)S(1)}, bf16[32,4224]{1,0:T(8,128)(2,1)S(1)}, u32[]{:S(2)}, u32[]{:S(2)}) %collective-permute-start.5) | collective-permute-done | bytes 270368 | tf_op jit(solution)/shard_map/ppermute | solution.py:94
  40.1 3.0 %collective-permute-start.8 = (bf16[16,4224]{1,0:T(8,128)(2,1)S(1)}, bf16[16,4224]{1,0:T(8,128)(2,1)S(1)}, u32[]{:S(2)}, u32[]{:S(2)}) collective-permute-start(bf16[16,4224]{1,0:T(8,128)(2,1)S(1)} %slice.1274), channel_id=1, source_target_pairs={{0,12},{4,0},{8,4},{12,8},{1,13},{5,1},{9,5},{13,9},{2,14},{6,2},{... | collective-permute-start | bytes 405512 | tf_op jit(solution)/shard_map/ppermute | solution.py:98
  43.1 0.9 constant_dynamic-update-slice_fusion.3
  44.0 0.9 constant_dynamic-update-slice_fusion.2
  46.6 1.0 convert_reduce_fusion.3
  47.6 0.9 collective-permute-done.10
  48.5 5.3 %pad_maximum_fusion = bf16[512,4224]{1,0:T(8,128)(2,1)S(1)} fusion(bf16[128,4224]{1,0:T(8,128)(2,1)S(1)} %collective-permute-done.11, bf16[128,4224]{1,0:T(8,128)(2,1)S(1)} %collective-permute-done.10, bf16[128,4224]{1,0:T(8,128)(2,1)S(1)} %collective-permute-done.9, bf16[128,4224]{1,0:T(8,128)(2,1)S(1)} %get-tuple-element.249), kind=kLoop, calls=%fused_computation.7 | loop fusion | flops 17301504 | bytes 8650752 | tf_op jit(solution)/shard_map/concatenate | solution.py:134
  53.8 2.8 %slice.969 = bf16[512,4080]{1,0:T(8,128)(2,1)S(1)} slice(bf16[512,4224]{1,0:T(8,128)(2,1)S(1)} %pad_maximum_fusion), slice={[0:512], [16:4096]} | slice | bytes 8355840 | tf_op jit(solution)/shard_map/slice | solution.py:44
  56.6 2.8 %slice.968 = bf16[512,4064]{1,0:T(8,128)(2,1)S(1)} slice(bf16[512,4224]{1,0:T(8,128)(2,1)S(1)} %pad_maximum_fusion), slice={[0:512], [32:4096]} | slice | bytes 8323072 | tf_op jit(solution)/shard_map/slice | solution.py:44
  59.7 2.5 %slice.966 = bf16[512,4096]{1,0:T(8,128)(2,1)} slice(bf16[512,4224]{1,0:T(8,128)(2,1)S(1)} %pad_maximum_fusion), slice={[0:512], [0:4096]} | slice | bytes 8388608 | tf_op jit(solution)/shard_map/slice | solution.py:143
  62.2 1.3 %collective-permute-start.12 = (bf16[128,4224]{1,0:T(8,128)(2,1)}, bf16[128,4224]{1,0:T(8,128)(2,1)}, u32[]{:S(2)}, u32[]{:S(2)}) collective-permute-start(bf16[128,4224]{1,0:T(8,128)(2,1)} %get-tuple-element.9), channel_id=1, source_target_pairs={{0,4},{4,8},{8,12},{12,0},{1,5},{5,9},{9,13},{13,1},{2,6},{6,10},{... | collective-permute-start | bytes 3244040 | tf_op jit(solution)/shard_map/ppermute | solution.py:94
  63.5 1.4 %collective-permute-start.13 = (bf16[128,4224]{1,0:T(8,128)(2,1)}, bf16[128,4224]{1,0:T(8,128)(2,1)S(1)}, u32[]{:S(2)}, u32[]{:S(2)}) collective-permute-start(bf16[128,4224]{1,0:T(8,128)(2,1)} %get-tuple-element.9), channel_id=1, source_target_pairs={{0,12},{4,0},{8,4},{12,8},{1,13},{5,1},{9,5},{13,9},{2,14},{6,2},{... | collective-permute-start | bytes 3244040 | tf_op jit(solution)/shard_map/ppermute | solution.py:95
  64.9 2.7 %collective-permute-start.15 = (bf16[128,4224]{1,0:T(8,128)(2,1)}, bf16[128,4224]{1,0:T(8,128)(2,1)S(1)}, u32[]{:S(2)}, u32[]{:S(2)}) collective-permute-start(bf16[128,4224]{1,0:T(8,128)(2,1)} %get-tuple-element.10), channel_id=1, source_target_pairs={{0,96},{32,0},{64,32},{96,64},{1,97},{33,1},{65,33},{97,65},{2,98}... | collective-permute-start | bytes 3244040 | tf_op jit(solution)/shard_map/ppermute | solution.py:95
  67.6 4.1 %select_select_fusion = bf16[512,4096]{1,0:T(8,128)(2,1)} fusion(bf16[512,4080]{1,0:T(8,128)(2,1)S(1)} %slice.969, bf16[512,4064]{1,0:T(8,128)(2,1)S(1)} %slice.968, pred[512]{0:T(512)(128)(4,1)S(1)} %get-tuple-element.12, pred[512]{0:T(512)(128)(4,1)S(1)} %get-tuple-element.11), kind=kLoop, calls=%fused_computation.9 | loop fusion | flops 4194304 | bytes 12534784 | tf_op jit(solution)/shard_map/jit(_where)/select_n | solution.py:150
  71.8 7.6 %fusion.2 = bf16[1024,4224]{1,0:T(8,128)(2,1)} fusion(bf16[512,4096]{1,0:T(8,128)(2,1)} %select_select_fusion, bf16[512,4096]{1,0:T(8,128)(2,1)} %slice.966), kind=kLoop, calls=%fused_computation.4 | loop fusion | flops 30277632 | bytes 17039360 | tf_op jit(solution)/shard_map/concatenate | solution.py:151
  79.4 1.1 convert_reduce_fusion.1
  80.4 6.7 %fusion.280 = f32[256,1024]{1,0:T(8,128)S(1)} fusion(bf16[256,4224]{1,0:T(8,128)(2,1)} %get-tuple-element.301, bf16[1024,4224]{1,0:T(8,128)(2,1)} %fusion.2), kind=kOutput, calls=%fused_computation.561 | convolution fusion | flops 2214592512 | bytes 11862016 | tf_op jit(solution)/shard_map/dot_general | solution.py:154
  87.2 1.4 %constant_dynamic-update-slice_fusion.23 = bf16[512,4224]{1,0:T(8,128)(2,1)S(1)} fusion(bf16[128,4224]{1,0:T(8,128)(2,1)} %collective-permute-done.12), kind=kLoop, calls=%fused_computation.118 | loop fusion | bytes 2162688
  89.5 4.8 %fusion.281 = f32[512,1024]{1,0:T(8,128)S(1)} fusion(bf16[512,4224]{1,0:T(8,128)(2,1)S(1)} %constant_dynamic-update-slice_fusion.20, bf16[1024,4224]{1,0:T(8,128)(2,1)S(1)} %bitcast.37), kind=kOutput, calls=%fused_computation.562 | convolution fusion | flops 4429185024 | bytes 15073280 | tf_op jit(solution)/shard_map/dot_general | solution.py:154
  95.8 1.1 slice.1477
  97.0 2.7 %collective-permute-start.17 = (bf16[64,4224]{1,0:T(8,128)(2,1)S(1)}, bf16[64,4224]{1,0:T(8,128)(2,1)S(1)}, u32[]{:S(2)}, u32[]{:S(2)}) collective-permute-start(bf16[64,4224]{1,0:T(8,128)(2,1)S(1)} %slice.1478), channel_id=1, source_target_pairs={{0,12},{4,0},{8,4},{12,8},{1,13},{5,1},{9,5},{13,9},{2,14},{6,2},{... | collective-permute-start | bytes 1622024 | tf_op jit(solution)/shard_map/ppermute | solution.py:98
  99.9 3.0 %collective-permute-start.19 = (bf16[64,4224]{1,0:T(8,128)(2,1)S(1)}, bf16[64,4224]{1,0:T(8,128)(2,1)S(1)}, u32[]{:S(2)}, u32[]{:S(2)}) collective-permute-start(bf16[64,4224]{1,0:T(8,128)(2,1)S(1)} %slice.1480), channel_id=1, source_target_pairs={{0,96},{32,0},{64,32},{96,64},{1,97},{33,1},{65,33},{97,65},{2,98}... | collective-permute-start | bytes 1622024 | tf_op jit(solution)/shard_map/ppermute | solution.py:98
  103.0 5.4 %collective-permute-done.16 = bf16[64,4224]{1,0:T(8,128)(2,1)S(1)} collective-permute-done((bf16[64,4224]{1,0:T(8,128)(2,1)S(1)}, bf16[64,4224]{1,0:T(8,128)(2,1)S(1)}, u32[]{:S(2)}, u32[]{:S(2)}) %collective-permute-start.16) | collective-permute-done | bytes 540704 | tf_op jit(solution)/shard_map/ppermute | solution.py:97
  108.6 2.2 %collective-permute-done.18 = bf16[64,4224]{1,0:T(8,128)(2,1)S(1)} collective-permute-done((bf16[64,4224]{1,0:T(8,128)(2,1)S(1)}, bf16[64,4224]{1,0:T(8,128)(2,1)S(1)}, u32[]{:S(2)}, u32[]{:S(2)}) %collective-permute-start.18) | collective-permute-done | bytes 540704 | tf_op jit(solution)/shard_map/ppermute | solution.py:97
  110.9 2.5 %fusion.282 = f32[256,1024]{1,0:T(8,128)S(1)} fusion(bf16[256,4224]{1,0:T(8,128)(2,1)S(1)} %constant_dynamic-update-slice_fusion.24, bf16[1024,4224]{1,0:T(8,128)(2,1)S(1)} %bitcast.37), kind=kOutput, calls=%fused_computation.563 | convolution fusion | flops 2214592512 | bytes 11862016 | tf_op jit(solution)/shard_map/dot_general | solution.py:154
  115.5 5.8 %collective-permute-start.22 = (f32[128,8]{0,1:T(8,128)S(1)}, f32[128,8]{0,1:T(8,128)S(1)}, u32[]{:S(2)}, u32[]{:S(2)}) collective-permute-start(f32[128,8]{0,1:T(8,128)S(1)} %get-tuple-element.372), channel_id=1, source_target_pairs={{2,1},{16,3},{18,17},{0,19},{19,0},{1,2},{3,16},{17,18},{6,5},{20,... | collective-permute-start | bytes 12296 | tf_op jit(solution)/shard_map/ppermute | solution.py:103
  121.4 1.8 %collective-permute-start.20 = (f32[128,8]{0,1:T(8,128)S(1)}, f32[128,8]{0,1:T(8,128)S(1)}, u32[]{:S(2)}, u32[]{:S(2)}) collective-permute-start(f32[128,8]{0,1:T(8,128)S(1)} %get-tuple-element.374), channel_id=1, source_target_pairs={{1,0},{0,1},{3,2},{2,3},{17,16},{16,17},{19,18},{18,19},{5,4},{4,5... | collective-permute-start | bytes 12296 | tf_op jit(solution)/shard_map/ppermute | solution.py:103
  123.1 1.9 %collective-permute-done.21 = f32[128,8]{0,1:T(8,128)S(1)} collective-permute-done((f32[128,8]{0,1:T(8,128)S(1)}, f32[128,8]{0,1:T(8,128)S(1)}, u32[]{:S(2)}, u32[]{:S(2)}) %collective-permute-start.21) | collective-permute-done | bytes 4128 | tf_op jit(solution)/shard_map/ppermute | solution.py:103
  (165 shorter events, 11.1 us)
Async XLA Ops:
  0.0 12.2 %copy-start.3 = (s32[256]{0:T(256)S(1)}, s32[256]{0:T(256)}, u32[]{:S(2)}) copy-start(s32[256]{0:T(256)} %param.9) | copy-start | bytes 3076
  0.0 12.2 %copy-start.4 = (s32[256]{0:T(256)S(1)}, s32[256]{0:T(256)}, u32[]{:S(2)}) copy-start(s32[256]{0:T(256)} %param.8) | copy-start | bytes 3076
  0.0 12.4 %copy-start.1 = (bf16[256,4096]{1,0:T(8,128)(2,1)S(1)}, bf16[256,4096]{1,0:T(8,128)(2,1)}, u32[]{:S(2)}) copy-start(bf16[256,4096]{1,0:T(8,128)(2,1)} %param.6) | copy-start | bytes 6291460
  5.1 20.6 %collective-permute-start.1 = (bf16[32,4224]{1,0:T(8,128)(2,1)S(1)}, bf16[32,4224]{1,0:T(8,128)(2,1)S(1)}, u32[]{:S(2)}, u32[]{:S(2)}) collective-permute-start(bf16[32,4224]{1,0:T(8,128)(2,1)S(1)} %get-tuple-element.285), channel_id=1, source_target_pairs={{0,32},{32,64},{64,96},{96,0},{1,33},{33,65},{65,97},{97,1},{2,34}... | collective-permute-start | bytes 811016 | tf_op jit(solution)/shard_map/ppermute | solution.py:94
  7.2 19.0 %collective-permute-start.2 = (bf16[32,4224]{1,0:T(8,128)(2,1)S(1)}, bf16[32,4224]{1,0:T(8,128)(2,1)S(1)}, u32[]{:S(2)}, u32[]{:S(2)}) collective-permute-start(bf16[32,4224]{1,0:T(8,128)(2,1)S(1)} %get-tuple-element.285), channel_id=1, source_target_pairs={{0,96},{32,0},{64,32},{96,64},{1,97},{33,1},{65,33},{97,65},{2,98}... | collective-permute-start | bytes 811016 | tf_op jit(solution)/shard_map/ppermute | solution.py:95
  8.4 17.3 %collective-permute-start = (bf16[32,4224]{1,0:T(8,128)(2,1)S(1)}, bf16[32,4224]{1,0:T(8,128)(2,1)S(1)}, u32[]{:S(2)}, u32[]{:S(2)}) collective-permute-start(bf16[32,4224]{1,0:T(8,128)(2,1)S(1)} %get-tuple-element.407), channel_id=1, source_target_pairs={{0,16},{16,0},{1,17},{17,1},{2,18},{18,2},{3,19},{19,3},{4,20},{20... | collective-permute-start | bytes 811016 | tf_op jit(solution)/shard_map/ppermute | solution.py:113
  13.9 2.6 %copy-start.2 = (s32[256,1]{0,1:T(1,128)S(1)}, s32[256,1]{0,1:T(1,128)}, u32[]{:S(2)}) copy-start(s32[256,1]{0,1:T(1,128)} %param.7) | copy-start | bytes 3076
  21.6 26.0 %collective-permute-start.11 = (bf16[128,4224]{1,0:T(8,128)(2,1)S(1)}, bf16[128,4224]{1,0:T(8,128)(2,1)S(1)}, u32[]{:S(2)}, u32[]{:S(2)}) collective-permute-start(bf16[128,4224]{1,0:T(8,128)(2,1)S(1)} %get-tuple-element.250), channel_id=1, source_target_pairs={{1,2},{3,16},{17,18},{19,0},{0,19},{2,1},{16,3},{18,17},{5,6},{7,2... | collective-permute-start | bytes 3244040 | tf_op jit(solution)/shard_map/ppermute | solution.py:103
  23.8 24.7 %collective-permute-start.10 = (bf16[128,4224]{1,0:T(8,128)(2,1)S(1)}, bf16[128,4224]{1,0:T(8,128)(2,1)S(1)}, u32[]{:S(2)}, u32[]{:S(2)}) collective-permute-start(bf16[128,4224]{1,0:T(8,128)(2,1)S(1)} %get-tuple-element.251), channel_id=1, source_target_pairs={{0,2},{2,16},{16,18},{18,0},{1,19},{3,1},{17,3},{19,17},{4,6},{6,2... | collective-permute-start | bytes 3244040 | tf_op jit(solution)/shard_map/ppermute | solution.py:103
  25.7 22.8 %collective-permute-start.9 = (bf16[128,4224]{1,0:T(8,128)(2,1)S(1)}, bf16[128,4224]{1,0:T(8,128)(2,1)S(1)}, u32[]{:S(2)}, u32[]{:S(2)}) collective-permute-start(bf16[128,4224]{1,0:T(8,128)(2,1)S(1)} %get-tuple-element.252), channel_id=1, source_target_pairs={{0,1},{1,0},{2,3},{3,2},{16,17},{17,16},{18,19},{19,18},{4,5},{5,4... | collective-permute-start | bytes 3244040 | tf_op jit(solution)/shard_map/ppermute | solution.py:103
  25.8 5.9 %collective-permute-start.3 = (bf16[16,4224]{1,0:T(8,128)(2,1)S(1)}, bf16[16,4224]{1,0:T(8,128)(2,1)S(1)}, u32[]{:S(2)}, u32[]{:S(2)}) collective-permute-start(bf16[16,4224]{1,0:T(8,128)(2,1)S(1)} %slice.1271), channel_id=1, source_target_pairs={{0,32},{32,64},{64,96},{96,0},{1,33},{33,65},{65,97},{97,1},{2,34}... | collective-permute-start | bytes 405512 | tf_op jit(solution)/shard_map/ppermute | solution.py:97
  26.2 7.6 %collective-permute-start.4 = (bf16[16,4224]{1,0:T(8,128)(2,1)S(1)}, bf16[16,4224]{1,0:T(8,128)(2,1)S(1)}, u32[]{:S(2)}, u32[]{:S(2)}) collective-permute-start(bf16[16,4224]{1,0:T(8,128)(2,1)S(1)} %slice.1272), channel_id=1, source_target_pairs={{0,96},{32,0},{64,32},{96,64},{1,97},{33,1},{65,33},{97,65},{2,98}... | collective-permute-start | bytes 405512 | tf_op jit(solution)/shard_map/ppermute | solution.py:98
  31.7 8.0 %collective-permute-start.5 = (bf16[32,4224]{1,0:T(8,128)(2,1)S(1)}, bf16[32,4224]{1,0:T(8,128)(2,1)S(1)}, u32[]{:S(2)}, u32[]{:S(2)}) collective-permute-start(bf16[32,4224]{1,0:T(8,128)(2,1)S(1)} %get-tuple-element.282), channel_id=1, source_target_pairs={{0,4},{4,8},{8,12},{12,0},{1,5},{5,9},{9,13},{13,1},{2,6},{6,10},{... | collective-permute-start | bytes 811016 | tf_op jit(solution)/shard_map/ppermute | solution.py:94
  33.8 6.4 %collective-permute-start.6 = (bf16[32,4224]{1,0:T(8,128)(2,1)S(1)}, bf16[32,4224]{1,0:T(8,128)(2,1)S(1)}, u32[]{:S(2)}, u32[]{:S(2)}) collective-permute-start(bf16[32,4224]{1,0:T(8,128)(2,1)S(1)} %get-tuple-element.282), channel_id=1, source_target_pairs={{0,12},{4,0},{8,4},{12,8},{1,13},{5,1},{9,5},{13,9},{2,14},{6,2},{... | collective-permute-start | bytes 811016 | tf_op jit(solution)/shard_map/ppermute | solution.py:95
  39.7 5.4 %collective-permute-start.7 = (bf16[16,4224]{1,0:T(8,128)(2,1)S(1)}, bf16[16,4224]{1,0:T(8,128)(2,1)S(1)}, u32[]{:S(2)}, u32[]{:S(2)}) collective-permute-start(bf16[16,4224]{1,0:T(8,128)(2,1)S(1)} %slice.1273), channel_id=1, source_target_pairs={{0,4},{4,8},{8,12},{12,0},{1,5},{5,9},{9,13},{13,1},{2,6},{6,10},{... | collective-permute-start | bytes 405512 | tf_op jit(solution)/shard_map/ppermute | solution.py:97
  40.1 5.7 %collective-permute-start.8 = (bf16[16,4224]{1,0:T(8,128)(2,1)S(1)}, bf16[16,4224]{1,0:T(8,128)(2,1)S(1)}, u32[]{:S(2)}, u32[]{:S(2)}) collective-permute-start(bf16[16,4224]{1,0:T(8,128)(2,1)S(1)} %slice.1274), channel_id=1, source_target_pairs={{0,12},{4,0},{8,4},{12,8},{1,13},{5,1},{9,5},{13,9},{2,14},{6,2},{... | collective-permute-start | bytes 405512 | tf_op jit(solution)/shard_map/ppermute | solution.py:98
  53.8 5.8 %copy-start = (bf16[512,4224]{1,0:T(8,128)(2,1)}, bf16[512,4224]{1,0:T(8,128)(2,1)S(1)}, u32[]{:S(2)}) copy-start(bf16[512,4224]{1,0:T(8,128)(2,1)S(1)} %pad_maximum_fusion) | copy-start | bytes 12976132
  62.2 25.0 %collective-permute-start.12 = (bf16[128,4224]{1,0:T(8,128)(2,1)}, bf16[128,4224]{1,0:T(8,128)(2,1)}, u32[]{:S(2)}, u32[]{:S(2)}) collective-permute-start(bf16[128,4224]{1,0:T(8,128)(2,1)} %get-tuple-element.9), channel_id=1, source_target_pairs={{0,4},{4,8},{8,12},{12,0},{1,5},{5,9},{9,13},{13,1},{2,6},{6,10},{... | collective-permute-start | bytes 3244040 | tf_op jit(solution)/shard_map/ppermute | solution.py:94
  63.5 25.1 %collective-permute-start.13 = (bf16[128,4224]{1,0:T(8,128)(2,1)}, bf16[128,4224]{1,0:T(8,128)(2,1)S(1)}, u32[]{:S(2)}, u32[]{:S(2)}) collective-permute-start(bf16[128,4224]{1,0:T(8,128)(2,1)} %get-tuple-element.9), channel_id=1, source_target_pairs={{0,12},{4,0},{8,4},{12,8},{1,13},{5,1},{9,5},{13,9},{2,14},{6,2},{... | collective-permute-start | bytes 3244040 | tf_op jit(solution)/shard_map/ppermute | solution.py:95
  64.9 24.2 %collective-permute-start.14 = (bf16[128,4224]{1,0:T(8,128)(2,1)}, bf16[128,4224]{1,0:T(8,128)(2,1)S(1)}, u32[]{:S(2)}, u32[]{:S(2)}) collective-permute-start(bf16[128,4224]{1,0:T(8,128)(2,1)} %get-tuple-element.10), channel_id=1, source_target_pairs={{0,32},{32,64},{64,96},{96,0},{1,33},{33,65},{65,97},{97,1},{2,34}... | collective-permute-start | bytes 3244040 | tf_op jit(solution)/shard_map/ppermute | solution.py:94
  64.9 24.4 %collective-permute-start.15 = (bf16[128,4224]{1,0:T(8,128)(2,1)}, bf16[128,4224]{1,0:T(8,128)(2,1)S(1)}, u32[]{:S(2)}, u32[]{:S(2)}) collective-permute-start(bf16[128,4224]{1,0:T(8,128)(2,1)} %get-tuple-element.10), channel_id=1, source_target_pairs={{0,96},{32,0},{64,32},{96,64},{1,97},{33,1},{65,33},{97,65},{2,98}... | collective-permute-start | bytes 3244040 | tf_op jit(solution)/shard_map/ppermute | solution.py:95
  80.4 9.0 %slice-start = ((s8[8650752]{0:T(1024)(128)(4,1)}), s8[4194304]{0:T(1024)(128)(4,1)S(1)}, s32[]{:S(2)}) async-start(s8[8650752]{0:T(1024)(128)(4,1)} %bitcast.36), calls=%async_computation | async-start | bytes 8388608
  80.4 9.0 %slice-start.1 = ((s8[8650752]{0:T(1024)(128)(4,1)}), s8[4194304]{0:T(1024)(128)(4,1)S(1)}, s32[]{:S(2)}) async-start(s8[8650752]{0:T(1024)(128)(4,1)} %bitcast.36), calls=%async_computation.1 | async-start | bytes 8388608
  87.2 2.3 %slice-start.2 = ((s8[8650752]{0:T(1024)(128)(4,1)}), s8[262144]{0:T(1024)(128)(4,1)S(1)}, s32[]{:S(2)}) async-start(s8[8650752]{0:T(1024)(128)(4,1)} %bitcast.36), calls=%async_computation.2 | async-start | bytes 524288
  96.9 11.6 %collective-permute-start.16 = (bf16[64,4224]{1,0:T(8,128)(2,1)S(1)}, bf16[64,4224]{1,0:T(8,128)(2,1)S(1)}, u32[]{:S(2)}, u32[]{:S(2)}) collective-permute-start(bf16[64,4224]{1,0:T(8,128)(2,1)S(1)} %slice.1477), channel_id=1, source_target_pairs={{0,4},{4,8},{8,12},{12,0},{1,5},{5,9},{9,13},{13,1},{2,6},{6,10},{... | collective-permute-start | bytes 1622024 | tf_op jit(solution)/shard_map/ppermute | solution.py:97
  97.0 11.5 %collective-permute-start.17 = (bf16[64,4224]{1,0:T(8,128)(2,1)S(1)}, bf16[64,4224]{1,0:T(8,128)(2,1)S(1)}, u32[]{:S(2)}, u32[]{:S(2)}) collective-permute-start(bf16[64,4224]{1,0:T(8,128)(2,1)S(1)} %slice.1478), channel_id=1, source_target_pairs={{0,12},{4,0},{8,4},{12,8},{1,13},{5,1},{9,5},{13,9},{2,14},{6,2},{... | collective-permute-start | bytes 1622024 | tf_op jit(solution)/shard_map/ppermute | solution.py:98
  99.8 11.0 %collective-permute-start.18 = (bf16[64,4224]{1,0:T(8,128)(2,1)S(1)}, bf16[64,4224]{1,0:T(8,128)(2,1)S(1)}, u32[]{:S(2)}, u32[]{:S(2)}) collective-permute-start(bf16[64,4224]{1,0:T(8,128)(2,1)S(1)} %slice.1479), channel_id=1, source_target_pairs={{0,32},{32,64},{64,96},{96,0},{1,33},{33,65},{65,97},{97,1},{2,34}... | collective-permute-start | bytes 1622024 | tf_op jit(solution)/shard_map/ppermute | solution.py:97
  99.9 10.9 %collective-permute-start.19 = (bf16[64,4224]{1,0:T(8,128)(2,1)S(1)}, bf16[64,4224]{1,0:T(8,128)(2,1)S(1)}, u32[]{:S(2)}, u32[]{:S(2)}) collective-permute-start(bf16[64,4224]{1,0:T(8,128)(2,1)S(1)} %slice.1480), channel_id=1, source_target_pairs={{0,96},{32,0},{64,32},{96,64},{1,97},{33,1},{65,33},{97,65},{2,98}... | collective-permute-start | bytes 1622024 | tf_op jit(solution)/shard_map/ppermute | solution.py:98
  115.5 7.6 %collective-permute-start.22 = (f32[128,8]{0,1:T(8,128)S(1)}, f32[128,8]{0,1:T(8,128)S(1)}, u32[]{:S(2)}, u32[]{:S(2)}) collective-permute-start(f32[128,8]{0,1:T(8,128)S(1)} %get-tuple-element.372), channel_id=1, source_target_pairs={{2,1},{16,3},{18,17},{0,19},{19,0},{1,2},{3,16},{17,18},{6,5},{20,... | collective-permute-start | bytes 12296 | tf_op jit(solution)/shard_map/ppermute | solution.py:103
  121.4 3.7 %collective-permute-start.21 = (f32[128,8]{0,1:T(8,128)S(1)}, f32[128,8]{0,1:T(8,128)S(1)}, u32[]{:S(2)}, u32[]{:S(2)}) collective-permute-start(f32[128,8]{0,1:T(8,128)S(1)} %get-tuple-element.373), channel_id=1, source_target_pairs={{2,0},{16,2},{18,16},{0,18},{19,1},{1,3},{3,17},{17,19},{6,4},{20,... | collective-permute-start | bytes 12296 | tf_op jit(solution)/shard_map/ppermute | solution.py:103
  121.4 3.7 %collective-permute-start.20 = (f32[128,8]{0,1:T(8,128)S(1)}, f32[128,8]{0,1:T(8,128)S(1)}, u32[]{:S(2)}, u32[]{:S(2)}) collective-permute-start(f32[128,8]{0,1:T(8,128)S(1)} %get-tuple-element.374), channel_id=1, source_target_pairs={{1,0},{0,1},{3,2},{2,3},{17,16},{16,17},{19,18},{18,19},{5,4},{4,5... | collective-permute-start | bytes 12296 | tf_op jit(solution)/shard_map/ppermute | solution.py:103

commit v9 on v8

--- a/solution.py
+++ b/solution.py
@@ -132,8 +132,8 @@
 
     perms = (SIBLING, UP, CROSS)
     received = jnp.concatenate(route([send_q[i] for i in range(roles)], perms), axis=0)
-    x_block, y_block, received = lax.optimization_barrier(
-        (jnp.concatenate(x_first, axis=0), jnp.concatenate(y_first, axis=0), received))
+    x_block = jnp.concatenate(x_first, axis=0)
+    y_block = jnp.concatenate(y_first, axis=0)
     x_then_y = ring_gather(x_block, "blk_2")
     y_then_x = ring_gather(y_block, "blk_0")
     early = jnp.concatenate([own, partner] + x_first[1:] + y_first[1:], axis=0)

time: 127 us -> 160 us (1.26)
  waiting for transfers between devices: 15.4 us -> 40.1 us
  local copies, waits for them, and re-layouts: 20.1 us -> 31.1 us
  starting transfers between devices: 38.7 us -> 36.3 us
    ppermute x4, waiting for transfers between devices: 7.95 us -> 29.9 us  [ring_gather(): far_low = lax.ppermute(below[:half], axis, up)]
    unnamed x31 -> x33, local copies, waits for them, and re-layouts: 7.76 us -> 12.5 us
    ppermute x4, waiting for transfers between devices: 0.01 us -> 3.94 us  [ring_gather(): far_high = lax.ppermute(above[half:], axis, down)]
    slice x4, local copies, waits for them, and re-layouts: 0.1 us -> 3.1 us  [ring_gather(): far_high = lax.ppermute(above[half:], axis, down)]
    ppermute x4, starting transfers between devices: 11.4 us -> 8.45 us  [ring_gather(): far_high = lax.ppermute(above[half:], axis, down)]
    slice x4, local copies, waits for them, and re-layouts: 1.14 us -> 3.1 us  [ring_gather(): far_low = lax.ppermute(below[:half], axis, up)]
  transfers between devices with their start and end apart: 23 -> 23, of which waited for: 8 -> 6; matrix products, arithmetic and copies ran while one was open for 31% -> 44% of each run, Pallas kernels for 0% -> 0%
where the time goes in v9:
time: 160 us
  waiting for transfers between devices  40.1 us (25%)
  starting transfers between devices  36.3 us (23%)
  other arithmetic  34.7 us (22%)
  local copies, waits for them, and re-layouts  31.1 us (19%)
  matrix products  16.5 us (10%)
    ppermute x4, waiting for transfers between devices, ring_gather(): far_low = lax.ppermute(below[:half], axis, up)  29.9 us
    dot_general x3, matrix products, best_of(): lax.dot_general(lib, both, (((1,), (1,)), ((), ())), preferred_element_ty...  13.4 us
    unnamed x33, local copies, waits for them, and re-layouts  12.5 us
    ppermute x6, starting transfers between devices, route(): lax.ppermute(b, ZRING, p)  12.3 us
    ppermute x4, starting transfers between devices, ring_gather(): far_high = lax.ppermute(above[half:], axis, down)  8.45 us
    concatenate x1, other arithmetic, on_device(): both = jnp.pad(jnp.concatenate([rows, moved], axis=0), ((0, 0), (0, LANE)))  7.62 us
    ppermute x4, starting transfers between devices, ring_gather(): above = lax.ppermute(block, axis, down)  6.7 us
    slice x2, local copies, waits for them, and re-layouts, lower_bins(): return jnp.concatenate([rows[..., amount:], tail], axis=-1)  5.52 us
  transfers between devices with their start and end apart: 23, of which 6 were waited for; matrix products, arithmetic and copies ran while one was open for 44% of the time, Pallas kernels for 0%

profile of v9, /device:TPU:1, one launch (start us, length us, event | category | flops | bytes accessed | tf_op | source)
XLA Modules:
  0.0 159.6 jit_solution(5923529270408535686)
XLA Ops:
  0.9 1.2 multiply_reduce_fusion.2
  2.2 1.1 multiply_convert_fusion.2
  3.3 2.0 %constant_dynamic-update-slice_fusion.9 = (bf16[256,4224]{1,0:T(8,128)(2,1)}, bf16[128,4224]{1,0:T(8,128)(2,1)}, bf16[32,4224]{1,0:T(8,128)(2,1)}, bf16[32,4224]{1,0:T(8,128)(2,1)}) fusion(bf16[32,1]{1,0:T(8,128)(2,1)S(1)} %copy.20, bf16[32,4096]{1,0:T(8,128)(2,1)S(1)} %multiply_convert_fusion.2, bf16[32,4096]{1,0:T(8,128)(2,1)} %bitcast.38), kind=kLoop, calls=%fused_computation.105 | loop fusion | flops 1216510 | bytes 1605696
  5.3 2.0 %collective-permute-start.1 = (bf16[32,4224]{1,0:T(8,128)(2,1)}, bf16[32,4224]{1,0:T(8,128)(2,1)}, u32[]{:S(2)}, u32[]{:S(2)}) collective-permute-start(bf16[32,4224]{1,0:T(8,128)(2,1)} %get-tuple-element.279), channel_id=1, source_target_pairs={{0,32},{32,64},{64,96},{96,0},{1,33},{33,65},{65,97},{97,1},{2,34}... | collective-permute-start | bytes 811016 | tf_op jit(solution)/shard_map/ppermute | solution.py:94
  7.4 1.3 collective-permute-start.2
  8.7 3.8 %collective-permute-start = (bf16[32,4224]{1,0:T(8,128)(2,1)}, bf16[32,4224]{1,0:T(8,128)(2,1)S(1)}, u32[]{:S(2)}, u32[]{:S(2)}) collective-permute-start(bf16[32,4224]{1,0:T(8,128)(2,1)} %get-tuple-element.401), channel_id=1, source_target_pairs={{0,16},{16,0},{1,17},{17,1},{2,18},{18,2},{3,19},{19,3},{4,20},{20... | collective-permute-start | bytes 811016 | tf_op jit(solution)/shard_map/ppermute | solution.py:113
  12.7 1.4 multiply_reduce_fusion
  14.1 2.6 %multiply_convert_fusion = bf16[256,4096]{1,0:T(8,128)(2,1)} fusion(bf16[256,4096]{1,0:T(8,128)(2,1)S(1)} %copy-done.1, f32[256]{0:T(256)S(1)} %add_rsqrt_fusion), kind=kLoop, calls=%fused_computation.10 | loop fusion | flops 3145728 | bytes 4195328 | tf_op jit(solution)/shard_map/convert_element_type | solution.py:39
  16.7 1.2 reduce-window.6
  18.4 3.1 %convolution_convert_fusion = bf16[512,4224]{1,0:T(8,128)(2,1)S(1)} fusion(bf16[256,2]{1,0:T(8,128)(2,1)S(1)} %copy.21, bf16[256,4096]{1,0:T(8,128)(2,1)} %multiply_convert_fusion, s32[256]{0:T(256)S(1)} %bitcast.45), kind=kOutput, calls=%fused_computation.5 | convolution fusion | flops 1116078080 | bytes 6424576 | tf_op jit(solution)/shard_map/dot_general | solution.py:128
  21.8 2.2 %collective-permute-start.11 = (bf16[128,4224]{1,0:T(8,128)(2,1)S(1)}, bf16[128,4224]{1,0:T(8,128)(2,1)S(1)}, u32[]{:S(2)}, u32[]{:S(2)}) collective-permute-start(bf16[128,4224]{1,0:T(8,128)(2,1)S(1)} %get-tuple-element.244), channel_id=1, source_target_pairs={{1,2},{3,16},{17,18},{19,0},{0,19},{2,1},{16,3},{18,17},{5,6},{7,2... | collective-permute-start | bytes 3244040 | tf_op jit(solution)/shard_map/ppermute | solution.py:103
  24.0 1.9 %collective-permute-start.10 = (bf16[128,4224]{1,0:T(8,128)(2,1)S(1)}, bf16[128,4224]{1,0:T(8,128)(2,1)S(1)}, u32[]{:S(2)}, u32[]{:S(2)}) collective-permute-start(bf16[128,4224]{1,0:T(8,128)(2,1)S(1)} %get-tuple-element.245), channel_id=1, source_target_pairs={{0,2},{2,16},{16,18},{18,0},{1,19},{3,1},{17,3},{19,17},{4,6},{6,2... | collective-permute-start | bytes 3244040 | tf_op jit(solution)/shard_map/ppermute | solution.py:103
  28.2 2.7 %collective-permute-start.4 = (bf16[16,4224]{1,0:T(8,128)(2,1)S(1)}, bf16[16,4224]{1,0:T(8,128)(2,1)S(1)}, u32[]{:S(2)}, u32[]{:S(2)}) collective-permute-start(bf16[16,4224]{1,0:T(8,128)(2,1)S(1)} %slice.1272), channel_id=1, source_target_pairs={{0,96},{32,0},{64,32},{96,64},{1,97},{33,1},{65,33},{97,65},{2,98}... | collective-permute-start | bytes 405512 | tf_op jit(solution)/shard_map/ppermute | solution.py:98
  32.0 1.8 %constant_dynamic-update-slice_fusion.7 = (bf16[256,4224]{1,0:T(8,128)(2,1)}, bf16[128,4224]{1,0:T(8,128)(2,1)}) fusion(bf16[256,4224]{1,0:T(8,128)(2,1)} %get-tuple-element.274, bf16[32,4224]{1,0:T(8,128)(2,1)} %collective-permute-done.1, bf16[128,4224]{1,0:T(8,128)(2,1)} %get-tuple-element.278), kind=kLoop, calls=%fused_computation.103 | loop fusion | bytes 811008
  33.8 1.8 %constant_dynamic-update-slice_fusion.6 = (bf16[256,4224]{1,0:T(8,128)(2,1)}, bf16[128,4224]{1,0:T(8,128)(2,1)}) fusion(bf16[256,4224]{1,0:T(8,128)(2,1)} %get-tuple-element.272, bf16[32,4224]{1,0:T(8,128)(2,1)} %collective-permute-done.2, bf16[128,4224]{1,0:T(8,128)(2,1)} %get-tuple-element.273), kind=kLoop, calls=%fused_computation.102 | loop fusion | bytes 811008
  35.6 1.3 collective-permute-start.5
  37.6 1.4 collective-permute-start.6
  39.8 4.0 %collective-permute-done.5 = bf16[32,4224]{1,0:T(8,128)(2,1)S(1)} collective-permute-done((bf16[32,4224]{1,0:T(8,128)(2,1)S(1)}, bf16[32,4224]{1,0:T(8,128)(2,1)S(1)}, u32[]{:S(2)}, u32[]{:S(2)}) %collective-permute-start.5) | collective-permute-done | bytes 270368 | tf_op jit(solution)/shard_map/ppermute | solution.py:94
  44.7 1.3 collective-permute-start.7
  46.9 24.8 %collective-permute-done.7 = bf16[16,4224]{1,0:T(8,128)(2,1)S(1)} collective-permute-done((bf16[16,4224]{1,0:T(8,128)(2,1)S(1)}, bf16[16,4224]{1,0:T(8,128)(2,1)S(1)}, u32[]{:S(2)}, u32[]{:S(2)}) %collective-permute-start.7) | collective-permute-done | bytes 135200 | tf_op jit(solution)/shard_map/ppermute | solution.py:97
  72.6 3.0 %collective-permute-done.8 = bf16[16,4224]{1,0:T(8,128)(2,1)S(1)} collective-permute-done((bf16[16,4224]{1,0:T(8,128)(2,1)S(1)}, bf16[16,4224]{1,0:T(8,128)(2,1)S(1)}, u32[]{:S(2)}, u32[]{:S(2)}) %collective-permute-start.8) | collective-permute-done | bytes 135200 | tf_op jit(solution)/shard_map/ppermute | solution.py:98
  75.6 1.3 collective-permute-start.13
  77.6 1.0 convert_reduce_fusion.3
  78.7 2.7 %collective-permute-start.15 = (bf16[128,4224]{1,0:T(8,128)(2,1)}, bf16[128,4224]{1,0:T(8,128)(2,1)}, u32[]{:S(2)}, u32[]{:S(2)}) collective-permute-start(bf16[128,4224]{1,0:T(8,128)(2,1)} %get-tuple-element.296), channel_id=1, source_target_pairs={{0,96},{32,0},{64,32},{96,64},{1,97},{33,1},{65,33},{97,65},{2,98}... | collective-permute-start | bytes 3244040 | tf_op jit(solution)/shard_map/ppermute | solution.py:95
  81.3 5.2 %pad_maximum_fusion = bf16[512,4224]{1,0:T(8,128)(2,1)S(1)} fusion(bf16[128,4224]{1,0:T(8,128)(2,1)S(1)} %collective-permute-done.11, bf16[128,4224]{1,0:T(8,128)(2,1)S(1)} %collective-permute-done.10, bf16[128,4224]{1,0:T(8,128)(2,1)S(1)} %collective-permute-done.9, bf16[128,4224]{1,0:T(8,128)(2,1)S(1)} %get-tuple-element.243), kind=kLoop, calls=%fused_computation.7 | loop fusion | flops 17301504 | bytes 8650752 | tf_op jit(solution)/shard_map/concatenate | solution.py:134
  86.5 2.8 %slice.1282 = bf16[512,4080]{1,0:T(8,128)(2,1)S(1)} slice(bf16[512,4224]{1,0:T(8,128)(2,1)S(1)} %pad_maximum_fusion), slice={[0:512], [16:4096]} | slice | bytes 8355840 | tf_op jit(solution)/shard_map/slice | solution.py:44
  89.3 2.8 %slice.1281 = bf16[512,4064]{1,0:T(8,128)(2,1)S(1)} slice(bf16[512,4224]{1,0:T(8,128)(2,1)S(1)} %pad_maximum_fusion), slice={[0:512], [32:4096]} | slice | bytes 8323072 | tf_op jit(solution)/shard_map/slice | solution.py:44
  92.1 2.5 %slice.1280 = bf16[512,4096]{1,0:T(8,128)(2,1)} slice(bf16[512,4224]{1,0:T(8,128)(2,1)S(1)} %pad_maximum_fusion), slice={[0:512], [0:4096]} | slice | bytes 8388608 | tf_op jit(solution)/shard_map/slice | solution.py:143
  94.9 4.2 %select_select_fusion = bf16[512,4096]{1,0:T(8,128)(2,1)} fusion(bf16[512,4080]{1,0:T(8,128)(2,1)S(1)} %slice.1282, bf16[512,4064]{1,0:T(8,128)(2,1)S(1)} %slice.1281, pred[512]{0:T(512)(128)(4,1)S(1)} %get-tuple-element.6, pred[512]{0:T(512)(128)(4,1)S(1)} %get-tuple-element.5), kind=kLoop, calls=%fused_computation.9 | loop fusion | flops 4194304 | bytes 12534784 | tf_op jit(solution)/shard_map/jit(_where)/select_n | solution.py:150
  99.1 7.6 %fusion.2 = bf16[1024,4224]{1,0:T(8,128)(2,1)} fusion(bf16[512,4096]{1,0:T(8,128)(2,1)} %select_select_fusion, bf16[512,4096]{1,0:T(8,128)(2,1)} %slice.1280), kind=kLoop, calls=%fused_computation.4 | loop fusion | flops 30277632 | bytes 17039360 | tf_op jit(solution)/shard_map/concatenate | solution.py:151
  106.8 1.0 convert_reduce_fusion.1
  108.4 6.1 %fusion.280 = f32[256,1024]{1,0:T(8,128)S(1)} fusion(bf16[256,4224]{1,0:T(8,128)(2,1)S(1)} %copy-done.2, bf16[1024,4224]{1,0:T(8,128)(2,1)} %fusion.2), kind=kOutput, calls=%fused_computation.562 | convolution fusion | flops 2214592512 | bytes 11862016 | tf_op jit(solution)/shard_map/dot_general | solution.py:154
  114.5 1.1 slice.1480
  115.8 1.1 slice.1481
  116.9 2.6 %collective-permute-start.17 = (bf16[64,4224]{1,0:T(8,128)(2,1)S(1)}, bf16[64,4224]{1,0:T(8,128)(2,1)S(1)}, u32[]{:S(2)}, u32[]{:S(2)}) collective-permute-start(bf16[64,4224]{1,0:T(8,128)(2,1)S(1)} %slice.1481), channel_id=1, source_target_pairs={{0,12},{4,0},{8,4},{12,8},{1,13},{5,1},{9,5},{13,9},{2,14},{6,2},{... | collective-permute-start | bytes 1622024 | tf_op jit(solution)/shard_map/ppermute | solution.py:98
  119.5 1.3 constant_dynamic-update-slice_fusion.23
  120.8 1.4 constant_dynamic-update-slice_fusion.22
  122.2 1.4 constant_dynamic-update-slice_fusion.21
  123.6 1.4 constant_dynamic-update-slice_fusion.20
  125.0 4.8 %fusion.281 = f32[512,1024]{1,0:T(8,128)S(1)} fusion(bf16[512,4224]{1,0:T(8,128)(2,1)S(1)} %constant_dynamic-update-slice_fusion.20, bf16[1024,4224]{1,0:T(8,128)(2,1)S(1)} %bitcast.37), kind=kOutput, calls=%fused_computation.563 | convolution fusion | flops 4429185024 | bytes 15073280 | tf_op jit(solution)/shard_map/dot_general | solution.py:154
  131.3 1.1 slice.1482
  132.5 1.1 slice.1483
  133.5 3.0 %collective-permute-start.19 = (bf16[64,4224]{1,0:T(8,128)(2,1)S(1)}, bf16[64,4224]{1,0:T(8,128)(2,1)S(1)}, u32[]{:S(2)}, u32[]{:S(2)}) collective-permute-start(bf16[64,4224]{1,0:T(8,128)(2,1)S(1)} %slice.1483), channel_id=1, source_target_pairs={{0,96},{32,0},{64,32},{96,64},{1,97},{33,1},{65,33},{97,65},{2,98}... | collective-permute-start | bytes 1622024 | tf_op jit(solution)/shard_map/ppermute | solution.py:98
  136.8 5.1 %collective-permute-done.18 = bf16[64,4224]{1,0:T(8,128)(2,1)S(1)} collective-permute-done((bf16[64,4224]{1,0:T(8,128)(2,1)S(1)}, bf16[64,4224]{1,0:T(8,128)(2,1)S(1)}, u32[]{:S(2)}, u32[]{:S(2)}) %collective-permute-start.18) | collective-permute-done | bytes 540704 | tf_op jit(solution)/shard_map/ppermute | solution.py:97
  142.9 2.5 %fusion.282 = f32[256,1024]{1,0:T(8,128)S(1)} fusion(bf16[256,4224]{1,0:T(8,128)(2,1)S(1)} %constant_dynamic-update-slice_fusion.24, bf16[1024,4224]{1,0:T(8,128)(2,1)S(1)} %bitcast.37), kind=kOutput, calls=%fused_computation.564 | convolution fusion | flops 2214592512 | bytes 11862016 | tf_op jit(solution)/shard_map/dot_general | solution.py:154
  147.5 6.0 %collective-permute-start.22 = (f32[128,8]{0,1:T(8,128)S(1)}, f32[128,8]{0,1:T(8,128)S(1)}, u32[]{:S(2)}, u32[]{:S(2)}) collective-permute-start(f32[128,8]{0,1:T(8,128)S(1)} %get-tuple-element.366), channel_id=1, source_target_pairs={{2,1},{16,3},{18,17},{0,19},{19,0},{1,2},{3,16},{17,18},{6,5},{20,... | collective-permute-start | bytes 12296 | tf_op jit(solution)/shard_map/ppermute | solution.py:103
  153.8 1.9 %collective-permute-start.20 = (f32[128,8]{0,1:T(8,128)S(1)}, f32[128,8]{0,1:T(8,128)S(1)}, u32[]{:S(2)}, u32[]{:S(2)}) collective-permute-start(f32[128,8]{0,1:T(8,128)S(1)} %get-tuple-element.368), channel_id=1, source_target_pairs={{1,0},{0,1},{3,2},{2,3},{17,16},{16,17},{19,18},{18,19},{5,4},{4,5... | collective-permute-start | bytes 12296 | tf_op jit(solution)/shard_map/ppermute | solution.py:103
  155.7 2.2 %collective-permute-done.21 = f32[128,8]{0,1:T(8,128)S(1)} collective-permute-done((f32[128,8]{0,1:T(8,128)S(1)}, f32[128,8]{0,1:T(8,128)S(1)}, u32[]{:S(2)}, u32[]{:S(2)}) %collective-permute-start.21) | collective-permute-done | bytes 4128 | tf_op jit(solution)/shard_map/ppermute | solution.py:103
  (167 shorter events, 17.5 us)
Async XLA Ops:
  0.0 12.4 %copy-start.4 = (s32[256]{0:T(256)S(1)}, s32[256]{0:T(256)}, u32[]{:S(2)}) copy-start(s32[256]{0:T(256)} %param.9) | copy-start | bytes 3076
  0.0 12.5 %copy-start.5 = (s32[256]{0:T(256)S(1)}, s32[256]{0:T(256)}, u32[]{:S(2)}) copy-start(s32[256]{0:T(256)} %param.8) | copy-start | bytes 3076
  0.0 12.6 %copy-start.1 = (bf16[256,4096]{1,0:T(8,128)(2,1)S(1)}, bf16[256,4096]{1,0:T(8,128)(2,1)}, u32[]{:S(2)}) copy-start(bf16[256,4096]{1,0:T(8,128)(2,1)} %param.6) | copy-start | bytes 6291460
  5.3 20.6 %collective-permute-start.1 = (bf16[32,4224]{1,0:T(8,128)(2,1)}, bf16[32,4224]{1,0:T(8,128)(2,1)}, u32[]{:S(2)}, u32[]{:S(2)}) collective-permute-start(bf16[32,4224]{1,0:T(8,128)(2,1)} %get-tuple-element.279), channel_id=1, source_target_pairs={{0,32},{32,64},{64,96},{96,0},{1,33},{33,65},{65,97},{97,1},{2,34}... | collective-permute-start | bytes 811016 | tf_op jit(solution)/shard_map/ppermute | solution.py:94
  7.4 19.9 %collective-permute-start.2 = (bf16[32,4224]{1,0:T(8,128)(2,1)}, bf16[32,4224]{1,0:T(8,128)(2,1)}, u32[]{:S(2)}, u32[]{:S(2)}) collective-permute-start(bf16[32,4224]{1,0:T(8,128)(2,1)} %get-tuple-element.279), channel_id=1, source_target_pairs={{0,96},{32,0},{64,32},{96,64},{1,97},{33,1},{65,33},{97,65},{2,98}... | collective-permute-start | bytes 811016 | tf_op jit(solution)/shard_map/ppermute | solution.py:95
  8.7 18.2 %collective-permute-start = (bf16[32,4224]{1,0:T(8,128)(2,1)}, bf16[32,4224]{1,0:T(8,128)(2,1)S(1)}, u32[]{:S(2)}, u32[]{:S(2)}) collective-permute-start(bf16[32,4224]{1,0:T(8,128)(2,1)} %get-tuple-element.401), channel_id=1, source_target_pairs={{0,16},{16,0},{1,17},{17,1},{2,18},{18,2},{3,19},{19,3},{4,20},{20... | collective-permute-start | bytes 811016 | tf_op jit(solution)/shard_map/ppermute | solution.py:113
  14.1 2.6 %copy-start.3 = (s32[256,1]{0,1:T(1,128)S(1)}, s32[256,1]{0,1:T(1,128)}, u32[]{:S(2)}) copy-start(s32[256,1]{0,1:T(1,128)} %param.7) | copy-start | bytes 3076
  21.8 56.8 %collective-permute-start.11 = (bf16[128,4224]{1,0:T(8,128)(2,1)S(1)}, bf16[128,4224]{1,0:T(8,128)(2,1)S(1)}, u32[]{:S(2)}, u32[]{:S(2)}) collective-permute-start(bf16[128,4224]{1,0:T(8,128)(2,1)S(1)} %get-tuple-element.244), channel_id=1, source_target_pairs={{1,2},{3,16},{17,18},{19,0},{0,19},{2,1},{16,3},{18,17},{5,6},{7,2... | collective-permute-start | bytes 3244040 | tf_op jit(solution)/shard_map/ppermute | solution.py:103
  24.0 54.7 %collective-permute-start.10 = (bf16[128,4224]{1,0:T(8,128)(2,1)S(1)}, bf16[128,4224]{1,0:T(8,128)(2,1)S(1)}, u32[]{:S(2)}, u32[]{:S(2)}) collective-permute-start(bf16[128,4224]{1,0:T(8,128)(2,1)S(1)} %get-tuple-element.245), channel_id=1, source_target_pairs={{0,2},{2,16},{16,18},{18,0},{1,19},{3,1},{17,3},{19,17},{4,6},{6,2... | collective-permute-start | bytes 3244040 | tf_op jit(solution)/shard_map/ppermute | solution.py:103
  26.0 55.4 %collective-permute-start.9 = (bf16[128,4224]{1,0:T(8,128)(2,1)S(1)}, bf16[128,4224]{1,0:T(8,128)(2,1)S(1)}, u32[]{:S(2)}, u32[]{:S(2)}) collective-permute-start(bf16[128,4224]{1,0:T(8,128)(2,1)S(1)} %get-tuple-element.246), channel_id=1, source_target_pairs={{0,1},{1,0},{2,3},{3,2},{16,17},{17,16},{18,19},{19,18},{4,5},{5,4... | collective-permute-start | bytes 3244040 | tf_op jit(solution)/shard_map/ppermute | solution.py:103
  26.9 8.7 %collective-permute-start.3 = (bf16[16,4224]{1,0:T(8,128)(2,1)S(1)}, bf16[16,4224]{1,0:T(8,128)(2,1)S(1)}, u32[]{:S(2)}, u32[]{:S(2)}) collective-permute-start(bf16[16,4224]{1,0:T(8,128)(2,1)S(1)} %slice.1271), channel_id=1, source_target_pairs={{0,32},{32,64},{64,96},{96,0},{1,33},{33,65},{65,97},{97,1},{2,34}... | collective-permute-start | bytes 405512 | tf_op jit(solution)/shard_map/ppermute | solution.py:97
  28.2 9.4 %collective-permute-start.4 = (bf16[16,4224]{1,0:T(8,128)(2,1)S(1)}, bf16[16,4224]{1,0:T(8,128)(2,1)S(1)}, u32[]{:S(2)}, u32[]{:S(2)}) collective-permute-start(bf16[16,4224]{1,0:T(8,128)(2,1)S(1)} %slice.1272), channel_id=1, source_target_pairs={{0,96},{32,0},{64,32},{96,64},{1,97},{33,1},{65,33},{97,65},{2,98}... | collective-permute-start | bytes 405512 | tf_op jit(solution)/shard_map/ppermute | solution.py:98
  35.6 8.2 %collective-permute-start.5 = (bf16[32,4224]{1,0:T(8,128)(2,1)S(1)}, bf16[32,4224]{1,0:T(8,128)(2,1)S(1)}, u32[]{:S(2)}, u32[]{:S(2)}) collective-permute-start(bf16[32,4224]{1,0:T(8,128)(2,1)S(1)} %get-tuple-element.276), channel_id=1, source_target_pairs={{0,4},{4,8},{8,12},{12,0},{1,5},{5,9},{9,13},{13,1},{2,6},{6,10},{... | collective-permute-start | bytes 811016 | tf_op jit(solution)/shard_map/ppermute | solution.py:94
  37.6 7.1 %collective-permute-start.6 = (bf16[32,4224]{1,0:T(8,128)(2,1)S(1)}, bf16[32,4224]{1,0:T(8,128)(2,1)S(1)}, u32[]{:S(2)}, u32[]{:S(2)}) collective-permute-start(bf16[32,4224]{1,0:T(8,128)(2,1)S(1)} %get-tuple-element.276), channel_id=1, source_target_pairs={{0,12},{4,0},{8,4},{12,8},{1,13},{5,1},{9,5},{13,9},{2,14},{6,2},{... | collective-permute-start | bytes 811016 | tf_op jit(solution)/shard_map/ppermute | solution.py:95
  43.9 70.7 %collective-permute-start.12 = (bf16[128,4224]{1,0:T(8,128)(2,1)}, bf16[128,4224]{1,0:T(8,128)(2,1)}, u32[]{:S(2)}, u32[]{:S(2)}) collective-permute-start(bf16[128,4224]{1,0:T(8,128)(2,1)} %get-tuple-element.300), channel_id=1, source_target_pairs={{0,4},{4,8},{8,12},{12,0},{1,5},{5,9},{9,13},{13,1},{2,6},{6,10},{... | collective-permute-start | bytes 3244040 | tf_op jit(solution)/shard_map/ppermute | solution.py:94
  44.7 27.0 %collective-permute-start.7 = (bf16[16,4224]{1,0:T(8,128)(2,1)S(1)}, bf16[16,4224]{1,0:T(8,128)(2,1)S(1)}, u32[]{:S(2)}, u32[]{:S(2)}) collective-permute-start(bf16[16,4224]{1,0:T(8,128)(2,1)S(1)} %slice.1273), channel_id=1, source_target_pairs={{0,4},{4,8},{8,12},{12,0},{1,5},{5,9},{9,13},{13,1},{2,6},{6,10},{... | collective-permute-start | bytes 405512 | tf_op jit(solution)/shard_map/ppermute | solution.py:97
  71.7 3.9 %collective-permute-start.8 = (bf16[16,4224]{1,0:T(8,128)(2,1)S(1)}, bf16[16,4224]{1,0:T(8,128)(2,1)S(1)}, u32[]{:S(2)}, u32[]{:S(2)}) collective-permute-start(bf16[16,4224]{1,0:T(8,128)(2,1)S(1)} %slice.1274), channel_id=1, source_target_pairs={{0,12},{4,0},{8,4},{12,8},{1,13},{5,1},{9,5},{13,9},{2,14},{6,2},{... | collective-permute-start | bytes 405512 | tf_op jit(solution)/shard_map/ppermute | solution.py:98
  75.6 40.2 %collective-permute-start.13 = (bf16[128,4224]{1,0:T(8,128)(2,1)}, bf16[128,4224]{1,0:T(8,128)(2,1)}, u32[]{:S(2)}, u32[]{:S(2)}) collective-permute-start(bf16[128,4224]{1,0:T(8,128)(2,1)} %get-tuple-element.300), channel_id=1, source_target_pairs={{0,12},{4,0},{8,4},{12,8},{1,13},{5,1},{9,5},{13,9},{2,14},{6,2},{... | collective-permute-start | bytes 3244040 | tf_op jit(solution)/shard_map/ppermute | solution.py:95
  78.6 43.6 %collective-permute-start.14 = (bf16[128,4224]{1,0:T(8,128)(2,1)}, bf16[128,4224]{1,0:T(8,128)(2,1)}, u32[]{:S(2)}, u32[]{:S(2)}) collective-permute-start(bf16[128,4224]{1,0:T(8,128)(2,1)} %get-tuple-element.296), channel_id=1, source_target_pairs={{0,32},{32,64},{64,96},{96,0},{1,33},{33,65},{65,97},{97,1},{2,34}... | collective-permute-start | bytes 3244040 | tf_op jit(solution)/shard_map/ppermute | solution.py:94
  78.7 44.9 %collective-permute-start.15 = (bf16[128,4224]{1,0:T(8,128)(2,1)}, bf16[128,4224]{1,0:T(8,128)(2,1)}, u32[]{:S(2)}, u32[]{:S(2)}) collective-permute-start(bf16[128,4224]{1,0:T(8,128)(2,1)} %get-tuple-element.296), channel_id=1, source_target_pairs={{0,96},{32,0},{64,32},{96,64},{1,97},{33,1},{65,33},{97,65},{2,98}... | collective-permute-start | bytes 3244040 | tf_op jit(solution)/shard_map/ppermute | solution.py:95
  81.3 13.3 %copy-start = (bf16[128,4224]{1,0:T(8,128)(2,1)}, bf16[128,4224]{1,0:T(8,128)(2,1)S(1)}, u32[]{:S(2)}) copy-start(bf16[128,4224]{1,0:T(8,128)(2,1)S(1)} %collective-permute-done.9) | copy-start | bytes 3244036
  106.8 1.6 %copy-start.2 = (bf16[256,4224]{1,0:T(8,128)(2,1)S(1)}, bf16[256,4224]{1,0:T(8,128)(2,1)}, u32[]{:S(2)}) copy-start(bf16[256,4224]{1,0:T(8,128)(2,1)} %get-tuple-element.295) | copy-start | bytes 6488068
  108.4 16.6 %slice-start = ((s8[8650752]{0:T(1024)(128)(4,1)}), s8[4194304]{0:T(1024)(128)(4,1)S(1)}, s32[]{:S(2)}) async-start(s8[8650752]{0:T(1024)(128)(4,1)} %bitcast.36), calls=%async_computation | async-start | bytes 8388608
  108.4 16.6 %slice-start.1 = ((s8[8650752]{0:T(1024)(128)(4,1)}), s8[4194304]{0:T(1024)(128)(4,1)S(1)}, s32[]{:S(2)}) async-start(s8[8650752]{0:T(1024)(128)(4,1)} %bitcast.36), calls=%async_computation.1 | async-start | bytes 8388608
  115.6 9.4 %slice-start.2 = ((s8[8650752]{0:T(1024)(128)(4,1)}), s8[262144]{0:T(1024)(128)(4,1)S(1)}, s32[]{:S(2)}) async-start(s8[8650752]{0:T(1024)(128)(4,1)} %bitcast.36), calls=%async_computation.2 | async-start | bytes 524288
  115.6 21.1 %collective-permute-start.16 = (bf16[64,4224]{1,0:T(8,128)(2,1)S(1)}, bf16[64,4224]{1,0:T(8,128)(2,1)S(1)}, u32[]{:S(2)}, u32[]{:S(2)}) collective-permute-start(bf16[64,4224]{1,0:T(8,128)(2,1)S(1)} %slice.1480), channel_id=1, source_target_pairs={{0,4},{4,8},{8,12},{12,0},{1,5},{5,9},{9,13},{13,1},{2,6},{6,10},{... | collective-permute-start | bytes 1622024 | tf_op jit(solution)/shard_map/ppermute | solution.py:97
  116.9 19.8 %collective-permute-start.17 = (bf16[64,4224]{1,0:T(8,128)(2,1)S(1)}, bf16[64,4224]{1,0:T(8,128)(2,1)S(1)}, u32[]{:S(2)}, u32[]{:S(2)}) collective-permute-start(bf16[64,4224]{1,0:T(8,128)(2,1)S(1)} %slice.1481), channel_id=1, source_target_pairs={{0,12},{4,0},{8,4},{12,8},{1,13},{5,1},{9,5},{13,9},{2,14},{6,2},{... | collective-permute-start | bytes 1622024 | tf_op jit(solution)/shard_map/ppermute | solution.py:98
  132.4 9.5 %collective-permute-start.18 = (bf16[64,4224]{1,0:T(8,128)(2,1)S(1)}, bf16[64,4224]{1,0:T(8,128)(2,1)S(1)}, u32[]{:S(2)}, u32[]{:S(2)}) collective-permute-start(bf16[64,4224]{1,0:T(8,128)(2,1)S(1)} %slice.1482), channel_id=1, source_target_pairs={{0,32},{32,64},{64,96},{96,0},{1,33},{33,65},{65,97},{97,1},{2,34}... | collective-permute-start | bytes 1622024 | tf_op jit(solution)/shard_map/ppermute | solution.py:97
  133.5 9.3 %collective-permute-start.19 = (bf16[64,4224]{1,0:T(8,128)(2,1)S(1)}, bf16[64,4224]{1,0:T(8,128)(2,1)S(1)}, u32[]{:S(2)}, u32[]{:S(2)}) collective-permute-start(bf16[64,4224]{1,0:T(8,128)(2,1)S(1)} %slice.1483), channel_id=1, source_target_pairs={{0,96},{32,0},{64,32},{96,64},{1,97},{33,1},{65,33},{97,65},{2,98}... | collective-permute-start | bytes 1622024 | tf_op jit(solution)/shard_map/ppermute | solution.py:98
  147.5 8.2 %collective-permute-start.22 = (f32[128,8]{0,1:T(8,128)S(1)}, f32[128,8]{0,1:T(8,128)S(1)}, u32[]{:S(2)}, u32[]{:S(2)}) collective-permute-start(f32[128,8]{0,1:T(8,128)S(1)} %get-tuple-element.366), channel_id=1, source_target_pairs={{2,1},{16,3},{18,17},{0,19},{19,0},{1,2},{3,16},{17,18},{6,5},{20,... | collective-permute-start | bytes 12296 | tf_op jit(solution)/shard_map/ppermute | solution.py:103
  153.5 4.4 %collective-permute-start.21 = (f32[128,8]{0,1:T(8,128)S(1)}, f32[128,8]{0,1:T(8,128)S(1)}, u32[]{:S(2)}, u32[]{:S(2)}) collective-permute-start(f32[128,8]{0,1:T(8,128)S(1)} %get-tuple-element.367), channel_id=1, source_target_pairs={{2,0},{16,2},{18,16},{0,18},{19,1},{1,3},{3,17},{17,19},{6,4},{20,... | collective-permute-start | bytes 12296 | tf_op jit(solution)/shard_map/ppermute | solution.py:103
  153.8 4.1 %collective-permute-start.20 = (f32[128,8]{0,1:T(8,128)S(1)}, f32[128,8]{0,1:T(8,128)S(1)}, u32[]{:S(2)}, u32[]{:S(2)}) collective-permute-start(f32[128,8]{0,1:T(8,128)S(1)} %get-tuple-element.368), channel_id=1, source_target_pairs={{1,0},{0,1},{3,2},{2,3},{17,16},{16,17},{19,18},{18,19},{5,4},{4,5... | collective-permute-start | bytes 12296 | tf_op jit(solution)/shard_map/ppermute | solution.py:103

commit v10 on v7

--- a/solution.py
+++ b/solution.py
@@ -123,14 +123,21 @@
     moved = jnp.zeros_like(rows)
     for s in range(1, NSHIFT + 1):
         moved = jnp.where((flat_shift == s)[:, None], lower_bins(rows, s * SHIFT_BINS), moved)
-    both = jnp.concatenate([rows, moved], axis=0)
-    prod = lax.dot_general(full, both, (((1,), (1,)), ((), ())), preferred_element_type=jnp.float32)
-    near = jnp.abs(lib_bins[:, None] - flat_bin[None, :]) <= WIN
-    scores = jnp.where(near, jnp.maximum(prod[:, :total], prod[:, total:]), 0.0)
-    best = top_rows(scores).reshape(roles, CAP, K)
 
-    home = route([best[i] for i in range(roles)], tuple(inverse(p) for p in perms))
-    home = jnp.concatenate(home, axis=0)
+    def best_for(first, count):
+        part = slice(first, first + count)
+        both = jnp.concatenate([rows[part], moved[part]], axis=0)
+        prod = lax.dot_general(full, both, (((1,), (1,)), ((), ())), preferred_element_type=jnp.float32)
+        near = jnp.abs(lib_bins[:, None] - flat_bin[None, part]) <= WIN
+        scores = jnp.where(near, jnp.maximum(prod[:, :count], prod[:, count:]), 0.0)
+        return top_rows(scores).reshape(count // CAP, CAP, K)
+
+    far = best_for(2 * CAP, 2 * CAP)
+    back_up = lax.ppermute(far[0], ZRING, inverse(UP))
+    back_cross = lax.ppermute(far[1], ZRING, inverse(CROSS))
+    local = best_for(0, 2 * CAP)
+    back_sibling = lax.ppermute(local[1], ZRING, inverse(SIBLING))
+    home = jnp.concatenate([local[0], back_sibling, back_up, back_cross], axis=0)
     return jnp.take(home, slot, axis=0)
 
 

time: 123 us -> 124 us (level)
  starting transfers between devices: 14.2 us -> 19.1 us
  local copies, waits for them, and re-layouts: 15.7 us -> 12.3 us
  waiting for transfers between devices: 32.1 us -> 30 us
  matrix products: 14.9 us -> 16.2 us
    unnamed x17 -> x22, local copies, waits for them, and re-layouts: 5.04 us -> 0.63 us
    concatenate x2 -> x1, other arithmetic: 4.14 us -> 0.01 us  [on_device(): jnp.concatenate([local[0], back_sibling, back_up, back_cross], axis=0)]
    ppermute x0 -> x3, starting transfers between devices: none -> 3.31 us  [the longest x1 1.29 us: on_device(): back_up = lax.ppermute(far[0], ZRING, inverse(UP))]
    select_n x1 -> x2, other arithmetic: 0.55 us -> 3.39 us  [the longest x1 2.85 us: on_device(): jnp.where((flat_shift == s)[:, None], lower_bins(rows, s * SHIFT_BINS), m...]
    ppermute x9 -> x6, waiting for transfers between devices: 3.64 us -> 0.82 us  [route(): lax.ppermute(b, ZRING, p)]
    ppermute x0 -> x3, waiting for transfers between devices: none -> 2.37 us  [the longest x1 1.82 us: on_device(): back_up = lax.ppermute(far[0], ZRING, inverse(UP))]
    slice x3 -> x5, local copies, waits for them, and re-layouts: 0.18 us -> 1.89 us  [the longest x1 1.71 us: best_for(): both = jnp.concatenate([rows[part], moved[part]], axis=0)]
    ppermute x1, waiting for transfers between devices: 21.2 us -> 19.9 us  [on_device(): partner_bin = lax.ppermute(library_bin[0], 'blk_1', [(0, 1), (1, 0)])]
  transfers between devices with their start and end apart: 12 -> 12, of which waited for: 5 -> 6; matrix products, arithmetic and copies ran while one was open for 24% -> 21% of each run, Pallas kernels for 0% -> 0%
where the time goes in v10:
time: 124 us; the launch traced here: 123 us
  waiting for transfers between devices  30 us (24%)
  starting transfers between devices  19.1 us (15%)
  other arithmetic  16.8 us (14%)
  matrix products  16.2 us (13%)
  between operations  14.7 us (12%)
  blocking collectives  13.8 us (11%)
  local copies, waits for them, and re-layouts  12.3 us (10%)
    ppermute x1, waiting for transfers between devices, on_device(): partner_bin = lax.ppermute(library_bin[0], 'blk_1', [(0, 1), (1, 0)])  19.9 us
    dot_general x2, matrix products, best_for(): lax.dot_general(full, both, (((1,), (1,)), ((), ())), preferred_element_t...  14.2 us
    unnamed x1, blocking collectives  13.8 us
    ppermute x6, starting transfers between devices, route(): lax.ppermute(b, ZRING, p)  9.27 us
    slice x2, local copies, waits for them, and re-layouts, lower_bins(): return jnp.concatenate([rows[..., amount:], tail], axis=-1)  6.43 us
    reduce_sum x3, other arithmetic, unit_rows(): total = jnp.sum(values * values, axis=-1, keepdims=True)  4.56 us
    ppermute x1, starting transfers between devices, on_device(): partner = lax.ppermute(library[0], 'blk_1', [(0, 1), (1, 0)])  4.43 us
    ppermute x1, waiting for transfers between devices, on_device(): partner = lax.ppermute(library[0], 'blk_1', [(0, 1), (1, 0)])  3.84 us
  transfers between devices with their start and end apart: 12, of which 6 were waited for; matrix products, arithmetic and copies ran while one was open for 21% of the time, Pallas kernels for 0%

profile of v10, /device:TPU:1, one launch (start us, length us, event | category | flops | bytes accessed | tf_op | source)
XLA Modules:
  0.0 123.0 jit_solution(12525589550022628394)
XLA Ops:
  6.5 4.4 %collective-permute-start.2 = (bf16[32,4096]{1,0:T(8,128)(2,1)}, bf16[32,4096]{1,0:T(8,128)(2,1)S(1)}, u32[]{:S(2)}, u32[]{:S(2)}) collective-permute-start(bf16[32,4096]{1,0:T(8,128)(2,1)} %bitcast.54), channel_id=1, source_target_pairs={{0,16},{16,0},{1,17},{17,1},{2,18},{18,2},{3,19},{19,3},{4,20},{20... | collective-permute-start | bytes 786440 | tf_op jit(solution)/shard_map/ppermute | solution.py:95
  11.0 1.3 %multiply_reduce_fusion.2 = f32[32]{0:T(128)S(1)} fusion(bf16[1,32,4096]{2,1,0:T(8,128)(2,1)} %param.10), kind=kLoop, calls=%fused_computation.29 | loop fusion | flops 393184 | bytes 262272 | tf_op jit(solution)/shard_map/reduce_sum | solution.py:37
  12.2 1.1 multiply_convert_fusion.3
  13.4 3.8 %collective-permute-done.2 = bf16[32,4096]{1,0:T(8,128)(2,1)S(1)} collective-permute-done((bf16[32,4096]{1,0:T(8,128)(2,1)}, bf16[32,4096]{1,0:T(8,128)(2,1)S(1)}, u32[]{:S(2)}, u32[]{:S(2)}) %collective-permute-start.2) | collective-permute-done | bytes 262176 | tf_op jit(solution)/shard_map/ppermute | solution.py:95
  17.2 0.3 multiply_reduce_fusion.1
  17.5 0.2 multiply_convert_fusion.2
  17.7 0.9 pad_maximum_fusion.3
  18.6 0.7 fusion.83
  19.3 1.2 reduce-window.6
  20.6 0.1 copy.17
  20.7 0.1 copy.18
  20.9 3.0 %multiply_reduce_fusion = f32[256]{0:T(256)S(1)} fusion(bf16[256,4096]{1,0:T(8,128)(2,1)} %param.6), kind=kLoop, calls=%fused_computation.15 | loop fusion | flops 3145472 | bytes 2098176 | tf_op jit(solution)/shard_map/reduce_sum | solution.py:37
  24.0 2.0 %convolution_convert_fusion = bf16[512,4096]{1,0:T(8,128)(2,1)S(1)} fusion(bf16[256,4096]{1,0:T(8,128)(2,1)S(1)} %copy-done, f32[256]{0:T(256)S(1)} %add_rsqrt_fusion, s32[256]{0:T(256)S(1)} %bitcast.57), kind=kOutput, calls=%fused_computation.1 | convolution fusion | flops 1079115776 | bytes 6293504 | tf_op jit(solution)/shard_map/dot_general | solution.py:108
  26.1 1.7 %fusion.251 = (bf16[128,4096]{1,0:T(8,128)(2,1)S(1)}, bf16[128,4096]{1,0:T(8,128)(2,1)}, bf16[128,4096]{1,0:T(8,128)(2,1)}, bf16[128,4096]{1,0:T(8,128)(2,1)}) fusion(bf16[512,4096]{1,0:T(8,128)(2,1)S(1)} %convolution_convert_fusion), kind=kLoop, calls=%fused_computation.464 | loop fusion | bytes 8388608 | tf_op jit(solution)/shard_map/slice | solution.py:117
  27.8 1.2 collective-permute-start.3
  29.0 3.1 %collective-permute-start.6 = (bf16[128,4096]{1,0:T(8,128)(2,1)}, bf16[128,4096]{1,0:T(8,128)(2,1)S(1)}, u32[]{:S(2)}, u32[]{:S(2)}) collective-permute-start(bf16[128,4096]{1,0:T(8,128)(2,1)} %get-tuple-element.192), channel_id=1, source_target_pairs={{0,2},{2,16},{16,18},{18,0},{1,19},{3,1},{17,3},{19,17},{4,6},{6,2... | collective-permute-start | bytes 3145736 | tf_op jit(solution)/shard_map/ppermute | solution.py:85
  32.1 0.2 select_reduce_fusion.1
  32.3 0.8 collective-permute-start.4
  33.1 2.1 %collective-permute-start = (s32[32]{0:T(128)S(1)}, s32[32]{0:T(128)S(1)}, u32[]{:S(2)}, u32[]{:S(2)}) collective-permute-start(s32[32]{0:T(128)S(1)} %bitcast.74), channel_id=1, source_target_pairs={{0,16},{16,0},{1,17},{17,1},{2,18},{18,2},{3,19},{19,3},{4,20},{20... | collective-permute-start | bytes 392 | tf_op jit(solution)/shard_map/ppermute | solution.py:96
  35.2 0.6 dynamic-slice
  36.5 19.9 %collective-permute-done = s32[32]{0:T(128)S(1)} collective-permute-done((s32[32]{0:T(128)S(1)}, s32[32]{0:T(128)S(1)}, u32[]{:S(2)}, u32[]{:S(2)}) %collective-permute-start) | collective-permute-done | bytes 160 | tf_op jit(solution)/shard_map/ppermute | solution.py:96
  56.4 0.7 collective-permute-start.5
  57.0 0.2 add_dynamic-update-slice_fusion
  57.2 13.8 %all-reduce.2 = s32[1024]{0:T(1024)S(1)} all-reduce(s32[1024]{0:T(1024)S(1)} %add_dynamic-update-slice_fusion), channel_id=1, replica_groups=mesh['blk_0'=4,'blk_1'=2,'blk_2'=4,'rep'=4] {'blk_0','blk_2'}, use_global_device_ids=true, to_apply=%add.2 | all-reduce | flops 1024 | bytes 8192
  71.0 3.5 %collective-permute-start.1 = (s32[2,128]{1,0:T(2,128)S(1)}, s32[2,128]{1,0:T(2,128)S(1)}, u32[]{:S(2)}, u32[]{:S(2)}) collective-permute-start(s32[2,128]{1,0:T(2,128)S(1)} %get-tuple-element.307), channel_id=1, source_target_pairs={{0,1},{1,0},{2,3},{3,2},{16,17},{17,16},{18,19},{19,18},{4,5},{5,4... | collective-permute-start | bytes 3080 | tf_op jit(solution)/shard_map/ppermute | solution.py:85
  74.5 0.8 collective-permute-done.1
  75.4 2.2 %pad_maximum_fusion = bf16[512,4096]{1,0:T(8,128)(2,1)S(1)} fusion(bf16[128,4096]{1,0:T(8,128)(2,1)} %collective-permute-done.7, bf16[128,4096]{1,0:T(8,128)(2,1)S(1)} %collective-permute-done.6, bf16[128,4096]{1,0:T(8,128)(2,1)S(1)} %collective-permute-done.3, bf16[128,4096]{1,0:T(8,128)(2,1)S(1)} %get-tuple-element.190), kind=kLoop, calls=%fused_computation.2 | loop fusion | flops 16777216 | bytes 8388608 | tf_op jit(solution)/shard_map/concatenate | solution.py:117
  77.6 3.2 %slice.1092 = bf16[512,4064]{1,0:T(8,128)(2,1)S(1)} slice(bf16[512,4096]{1,0:T(8,128)(2,1)S(1)} %pad_maximum_fusion), slice={[0:512], [32:4096]} | slice | bytes 8323072 | tf_op jit(solution)/shard_map/slice | solution.py:43
  80.9 3.2 %slice.1093 = bf16[512,4080]{1,0:T(8,128)(2,1)S(1)} slice(bf16[512,4096]{1,0:T(8,128)(2,1)S(1)} %pad_maximum_fusion), slice={[0:512], [16:4096]} | slice | bytes 8355840 | tf_op jit(solution)/shard_map/slice | solution.py:43
  84.1 2.9 %select_select_fusion = bf16[512,4096]{1,0:T(8,128)(2,1)S(1)} fusion(bf16[512,4080]{1,0:T(8,128)(2,1)S(1)} %slice.1093, bf16[512,4064]{1,0:T(8,128)(2,1)S(1)} %slice.1092, pred[512]{0:T(512)(128)(4,1)S(1)} %get-tuple-element.305, pred[512]{0:T(512)(128)(4,1)S(1)} %get-tuple-element.304), kind=kLoop, calls=%fused_computation.13 | loop fusion | flops 4194304 | bytes 12534784 | tf_op jit(solution)/shard_map/jit(_where)/select_n | solution.py:125
  86.9 1.7 %fusion.250 = (bf16[256,4096]{1,0:T(8,128)(2,1)S(1)}, bf16[256,4096]{1,0:T(8,128)(2,1)}) fusion(bf16[512,4096]{1,0:T(8,128)(2,1)S(1)} %select_select_fusion), kind=kLoop, calls=%fused_computation.463 | loop fusion | bytes 8388608 | tf_op jit(solution)/shard_map/slice | solution.py:129
  88.7 3.1 %all-gather.2.cloned.1.call-done = bf16[1024,4096]{1,0:T(8,128)(2,1)} async-done(((bf16[64,4096]{1,0:T(8,128)(2,1)}), bf16[1024,4096]{1,0:T(8,128)(2,1)}) %all-gather.2.cloned.1.call-update) | async-done | bytes 8388624 | tf_op jit(solution)/shard_map/all_gather | solution.py:99
  91.7 9.6 %fusion.3 = f32[1024,512]{1,0:T(8,128)S(1)} fusion(bf16[1024,4096]{1,0:T(8,128)(2,1)} %all-gather.2.cloned.1.call-done, bf16[256,4096]{1,0:T(8,128)(2,1)} %get-tuple-element.189, bf16[128,4096]{1,0:T(8,128)(2,1)} %collective-permute-done.7, bf16[128,4096]{1,0:T(8,128)(2,1)} %copy-done.3), kind=kOutput, calls=%fused_computation.7 | convolution fusion | flops 4307550208 | bytes 14680064 | tf_op jit(solution)/shard_map/dot_general | solution.py:130
  101.4 4.6 %fusion = f32[1024,512]{1,0:T(8,128)S(1)} fusion(bf16[1024,4096]{1,0:T(8,128)(2,1)S(1)} %copy-done.8, bf16[256,4096]{1,0:T(8,128)(2,1)S(1)} %get-tuple-element.188, bf16[128,4096]{1,0:T(8,128)(2,1)S(1)} %copy-done.2, bf16[128,4096]{1,0:T(8,128)(2,1)S(1)} %get-tuple-element.190), kind=kOutput, calls=%fused_computation.3 | convolution fusion | flops 4307550208 | bytes 14680064 | tf_op jit(solution)/shard_map/dot_general | solution.py:130
  106.0 0.5 fusion.11
  106.5 0.1 minimum_minimum_fusion.9
  106.6 0.1 minimum_maximum_fusion.6
  107.6 0.1 minimum_minimum_fusion.4
  107.7 0.1 minimum_maximum_fusion.1
  108.8 0.8 collective-permute-start.8
  109.6 1.3 %collective-permute-start.10 = (f32[128,8]{0,1:T(8,128)S(1)}, f32[128,8]{0,1:T(8,128)S(1)}, u32[]{:S(2)}, u32[]{:S(2)}) collective-permute-start(f32[128,8]{0,1:T(8,128)S(1)} %get-tuple-element.283), channel_id=1, source_target_pairs={{2,1},{16,3},{18,17},{0,19},{19,0},{1,2},{3,16},{17,18},{6,5},{20,... | collective-permute-start | bytes 12296 | tf_op jit(solution)/shard_map/ppermute | solution.py:137
  110.9 1.3 %collective-permute-start.9 = (f32[128,8]{0,1:T(8,128)S(1)}, f32[128,8]{0,1:T(8,128)S(1)}, u32[]{:S(2)}, u32[]{:S(2)}) collective-permute-start(f32[128,8]{0,1:T(8,128)S(1)} %get-tuple-element.282), channel_id=1, source_target_pairs={{2,0},{16,2},{18,16},{0,18},{19,1},{1,3},{3,17},{17,19},{6,4},{20,... | collective-permute-start | bytes 12296 | tf_op jit(solution)/shard_map/ppermute | solution.py:136
  112.2 0.5 collective-permute-done.10
  112.7 1.8 %collective-permute-done.9 = f32[128,8]{0,1:T(8,128)S(1)} collective-permute-done((f32[128,8]{0,1:T(8,128)S(1)}, f32[128,8]{0,1:T(8,128)S(1)}, u32[]{:S(2)}, u32[]{:S(2)}) %collective-permute-start.9) | collective-permute-done | bytes 4128 | tf_op jit(solution)/shard_map/ppermute | solution.py:136
  114.5 0.1 copy.21
  114.7 0.7 gather_fusion
  115.4 0.1 broadcast_select_fusion
  115.5 0.7 copy.22
  (108 shorter events, 1.8 us)
Async XLA Ops:
  6.5 17.4 %copy-start.4 = (s32[256,1]{0,1:T(1,128)S(1)}, s32[256,1]{0,1:T(1,128)}, u32[]{:S(2)}) copy-start(s32[256,1]{0,1:T(1,128)} %param.7) | copy-start | bytes 3076
  6.5 17.5 %copy-start = (bf16[256,4096]{1,0:T(8,128)(2,1)S(1)}, bf16[256,4096]{1,0:T(8,128)(2,1)}, u32[]{:S(2)}) copy-start(bf16[256,4096]{1,0:T(8,128)(2,1)} %param.6) | copy-start | bytes 6291460
  6.5 85.2 %all-gather.2.cloned.1.call-start = ((), (), s32[]{:S(2)}) async-start(), calls=%async_computation | async-start | bytes 8912896 | tf_op jit(solution)/shard_map/all_gather | solution.py:99
  6.5 10.7 %collective-permute-start.2 = (bf16[32,4096]{1,0:T(8,128)(2,1)}, bf16[32,4096]{1,0:T(8,128)(2,1)S(1)}, u32[]{:S(2)}, u32[]{:S(2)}) collective-permute-start(bf16[32,4096]{1,0:T(8,128)(2,1)} %bitcast.54), channel_id=1, source_target_pairs={{0,16},{16,0},{1,17},{17,1},{2,18},{18,2},{3,19},{19,3},{4,20},{20... | collective-permute-start | bytes 786440 | tf_op jit(solution)/shard_map/ppermute | solution.py:95
  26.0 6.1 %copy-start.5 = (s32[256]{0:T(256)S(1)}, s32[256]{0:T(256)}, u32[]{:S(2)}) copy-start(s32[256]{0:T(256)} %param.8) | copy-start | bytes 3076
  26.0 6.1 %copy-start.6 = (s32[256]{0:T(256)S(1)}, s32[256]{0:T(256)}, u32[]{:S(2)}) copy-start(s32[256]{0:T(256)} %param.9) | copy-start | bytes 3076
  26.1 7.1 %copy-start.7 = (s32[1,32]{1,0:T(1,128)S(1)}, s32[1,32]{1,0:T(1,128)}, u32[]{:S(2)}) copy-start(s32[1,32]{1,0:T(1,128)} %param.11) | copy-start | bytes 388
  26.1 9.2 %copy-start.9 = (u32[128]{0:T(128)S(1)}, u32[128]{0:T(128)}, u32[]{:S(2)}) copy-start(u32[128]{0:T(128)} %constant.92) | copy-start | bytes 1540
  27.8 47.6 %collective-permute-start.3 = (bf16[128,4096]{1,0:T(8,128)(2,1)}, bf16[128,4096]{1,0:T(8,128)(2,1)S(1)}, u32[]{:S(2)}, u32[]{:S(2)}) collective-permute-start(bf16[128,4096]{1,0:T(8,128)(2,1)} %get-tuple-element.193), channel_id=1, source_target_pairs={{0,1},{1,0},{2,3},{3,2},{16,17},{17,16},{18,19},{19,18},{4,5},{5,4... | collective-permute-start | bytes 3145736 | tf_op jit(solution)/shard_map/ppermute | solution.py:85
  29.0 46.4 %collective-permute-start.6 = (bf16[128,4096]{1,0:T(8,128)(2,1)}, bf16[128,4096]{1,0:T(8,128)(2,1)S(1)}, u32[]{:S(2)}, u32[]{:S(2)}) collective-permute-start(bf16[128,4096]{1,0:T(8,128)(2,1)} %get-tuple-element.192), channel_id=1, source_target_pairs={{0,2},{2,16},{16,18},{18,0},{1,19},{3,1},{17,3},{19,17},{4,6},{6,2... | collective-permute-start | bytes 3145736 | tf_op jit(solution)/shard_map/ppermute | solution.py:85
  32.1 43.2 %collective-permute-start.7 = (bf16[128,4096]{1,0:T(8,128)(2,1)}, bf16[128,4096]{1,0:T(8,128)(2,1)}, u32[]{:S(2)}, u32[]{:S(2)}) collective-permute-start(bf16[128,4096]{1,0:T(8,128)(2,1)} %get-tuple-element.191), channel_id=1, source_target_pairs={{1,2},{3,16},{17,18},{19,0},{0,19},{2,1},{16,3},{18,17},{5,6},{7,2... | collective-permute-start | bytes 3145736 | tf_op jit(solution)/shard_map/ppermute | solution.py:85
  32.3 38.7 %collective-permute-start.4 = (s32[2,128]{1,0:T(2,128)S(1)}, s32[2,128]{1,0:T(2,128)S(1)}, u32[]{:S(2)}, u32[]{:S(2)}) collective-permute-start(s32[2,128]{1,0:T(2,128)S(1)} %get-tuple-element.309), channel_id=1, source_target_pairs={{0,2},{2,16},{16,18},{18,0},{1,19},{3,1},{17,3},{19,17},{4,6},{6,2... | collective-permute-start | bytes 3080 | tf_op jit(solution)/shard_map/ppermute | solution.py:85
  33.1 23.2 %collective-permute-start = (s32[32]{0:T(128)S(1)}, s32[32]{0:T(128)S(1)}, u32[]{:S(2)}, u32[]{:S(2)}) collective-permute-start(s32[32]{0:T(128)S(1)} %bitcast.74), channel_id=1, source_target_pairs={{0,16},{16,0},{1,17},{17,1},{2,18},{18,2},{3,19},{19,3},{4,20},{20... | collective-permute-start | bytes 392 | tf_op jit(solution)/shard_map/ppermute | solution.py:96
  56.4 18.1 %collective-permute-start.5 = (s32[2,128]{1,0:T(2,128)S(1)}, s32[2,128]{1,0:T(2,128)S(1)}, u32[]{:S(2)}, u32[]{:S(2)}) collective-permute-start(s32[2,128]{1,0:T(2,128)S(1)} %get-tuple-element.308), channel_id=1, source_target_pairs={{1,2},{3,16},{17,18},{19,0},{0,19},{2,1},{16,3},{18,17},{5,6},{7,2... | collective-permute-start | bytes 3080 | tf_op jit(solution)/shard_map/ppermute | solution.py:85
  71.0 4.3 %collective-permute-start.1 = (s32[2,128]{1,0:T(2,128)S(1)}, s32[2,128]{1,0:T(2,128)S(1)}, u32[]{:S(2)}, u32[]{:S(2)}) collective-permute-start(s32[2,128]{1,0:T(2,128)S(1)} %get-tuple-element.307), channel_id=1, source_target_pairs={{0,1},{1,0},{2,3},{3,2},{16,17},{17,16},{18,19},{19,18},{4,5},{5,4... | collective-permute-start | bytes 3080 | tf_op jit(solution)/shard_map/ppermute | solution.py:85
  75.3 2.3 %copy-start.1 = (bf16[128,4096]{1,0:T(8,128)(2,1)}, bf16[128,4096]{1,0:T(8,128)(2,1)S(1)}, u32[]{:S(2)}) copy-start(bf16[128,4096]{1,0:T(8,128)(2,1)S(1)} %collective-permute-done.3) | copy-start | bytes 3145732
  75.4 2.3 %copy-start.3 = (bf16[128,4096]{1,0:T(8,128)(2,1)}, bf16[128,4096]{1,0:T(8,128)(2,1)S(1)}, u32[]{:S(2)}) copy-start(bf16[128,4096]{1,0:T(8,128)(2,1)S(1)} %collective-permute-done.6) | copy-start | bytes 3145732
  91.7 9.6 %copy-start.2 = (bf16[128,4096]{1,0:T(8,128)(2,1)S(1)}, bf16[128,4096]{1,0:T(8,128)(2,1)}, u32[]{:S(2)}) copy-start(bf16[128,4096]{1,0:T(8,128)(2,1)} %copy-done.1) | copy-start | bytes 3145732
  91.7 9.6 %copy-start.8 = (bf16[1024,4096]{1,0:T(8,128)(2,1)S(1)}, bf16[1024,4096]{1,0:T(8,128)(2,1)}, u32[]{:S(2)}) copy-start(bf16[1024,4096]{1,0:T(8,128)(2,1)} %all-gather.2.cloned.1.call-done) | copy-start | bytes 25165828
  108.8 3.4 %collective-permute-start.8 = (f32[128,8]{0,1:T(8,128)S(1)}, f32[128,8]{0,1:T(8,128)S(1)}, u32[]{:S(2)}, u32[]{:S(2)}) collective-permute-start(f32[128,8]{0,1:T(8,128)S(1)} %get-tuple-element.275), channel_id=1, source_target_pairs={{1,0},{0,1},{3,2},{2,3},{17,16},{16,17},{19,18},{18,19},{5,4},{4,5... | collective-permute-start | bytes 12296 | tf_op jit(solution)/shard_map/ppermute | solution.py:139
  109.6 3.1 %collective-permute-start.10 = (f32[128,8]{0,1:T(8,128)S(1)}, f32[128,8]{0,1:T(8,128)S(1)}, u32[]{:S(2)}, u32[]{:S(2)}) collective-permute-start(f32[128,8]{0,1:T(8,128)S(1)} %get-tuple-element.283), channel_id=1, source_target_pairs={{2,1},{16,3},{18,17},{0,19},{19,0},{1,2},{3,16},{17,18},{6,5},{20,... | collective-permute-start | bytes 12296 | tf_op jit(solution)/shard_map/ppermute | solution.py:137
  110.9 3.7 %collective-permute-start.9 = (f32[128,8]{0,1:T(8,128)S(1)}, f32[128,8]{0,1:T(8,128)S(1)}, u32[]{:S(2)}, u32[]{:S(2)}) collective-permute-start(f32[128,8]{0,1:T(8,128)S(1)} %get-tuple-element.282), channel_id=1, source_target_pairs={{2,0},{16,2},{18,16},{0,18},{19,1},{1,3},{3,17},{17,19},{6,4},{20,... | collective-permute-start | bytes 12296 | tf_op jit(solution)/shard_map/ppermute | solution.py:136
Sparse Core Ops, SparseCore 0:
  18.7 73.0 all-gather.1

commit v11 on v7

--- a/solution.py
+++ b/solution.py
@@ -78,7 +78,7 @@
             for i in range(K):
                 if (i // step) % 2 == 0:
                     exchange(lists, i, i + step)
-    return jnp.concatenate(lists, axis=0).T
+    return jnp.concatenate(lists, axis=0)
 
 
 def route(blocks, perms):
@@ -127,11 +127,10 @@
     prod = lax.dot_general(full, both, (((1,), (1,)), ((), ())), preferred_element_type=jnp.float32)
     near = jnp.abs(lib_bins[:, None] - flat_bin[None, :]) <= WIN
     scores = jnp.where(near, jnp.maximum(prod[:, :total], prod[:, total:]), 0.0)
-    best = top_rows(scores).reshape(roles, CAP, K)
-
-    home = route([best[i] for i in range(roles)], tuple(inverse(p) for p in perms))
-    home = jnp.concatenate(home, axis=0)
-    return jnp.take(home, slot, axis=0)
+    best = top_rows(scores)
+    home = route([best[:, i * CAP:(i + 1) * CAP] for i in range(roles)], tuple(inverse(p) for p in perms))
+    home = jnp.concatenate(home, axis=1)
+    return jnp.take(home, slot, axis=1).T
 
 
 def solution(mesh):

time: 123 us -> 123 us (level)
  no operation moved by 1% of the time
where the time goes in v11:
time: 123 us
  waiting for transfers between devices  32.3 us (26%)
  other arithmetic  17.7 us (14%)
  local copies, waits for them, and re-layouts  15.5 us (13%)
  matrix products  14.9 us (12%)
  between operations  14.5 us (12%)
  starting transfers between devices  14.2 us (12%)
  blocking collectives  13.8 us (11%)
    ppermute x1, waiting for transfers between devices, on_device(): partner_bin = lax.ppermute(library_bin[0], 'blk_1', [(0, 1), (1, 0)])  21.2 us
    unnamed x1, blocking collectives  13.8 us
    dot_general x1, matrix products, on_device(): lax.dot_general(full, both, (((1,), (1,)), ((), ())), preferred_element_t...  12.9 us
    ppermute x9, starting transfers between devices, route(): lax.ppermute(b, ZRING, p)  8.8 us
    slice x2, local copies, waits for them, and re-layouts, lower_bins(): return jnp.concatenate([rows[..., amount:], tail], axis=-1)  6.37 us
    unnamed x17, local copies, waits for them, and re-layouts  5.07 us
    reduce_sum x3, other arithmetic, unit_rows(): total = jnp.sum(values * values, axis=-1, keepdims=True)  4.56 us
    ppermute x1, starting transfers between devices, on_device(): partner = lax.ppermute(library[0], 'blk_1', [(0, 1), (1, 0)])  4.43 us
  transfers between devices with their start and end apart: 12, of which 5 were waited for; matrix products, arithmetic and copies ran while one was open for 24% of the time, Pallas kernels for 0%

profile of v11, /device:TPU:1, one launch (start us, length us, event | category | flops | bytes accessed | tf_op | source)
XLA Modules:
  0.0 123.0 jit_solution(16209774910901547618)
XLA Ops:
  6.5 4.4 %collective-permute-start.4 = (bf16[32,4096]{1,0:T(8,128)(2,1)}, bf16[32,4096]{1,0:T(8,128)(2,1)S(1)}, u32[]{:S(2)}, u32[]{:S(2)}) collective-permute-start(bf16[32,4096]{1,0:T(8,128)(2,1)} %bitcast.53), channel_id=1, source_target_pairs={{0,16},{16,0},{1,17},{17,1},{2,18},{18,2},{3,19},{19,3},{4,20},{20... | collective-permute-start | bytes 786440 | tf_op jit(solution)/shard_map/ppermute | solution.py:95
  11.0 1.3 %multiply_reduce_fusion.2 = f32[32]{0:T(128)S(1)} fusion(bf16[1,32,4096]{2,1,0:T(8,128)(2,1)} %param.10), kind=kLoop, calls=%fused_computation.16 | loop fusion | flops 393184 | bytes 262272 | tf_op jit(solution)/shard_map/reduce_sum | solution.py:37
  12.2 1.1 multiply_convert_fusion.3
  13.4 3.8 %collective-permute-done.4 = bf16[32,4096]{1,0:T(8,128)(2,1)S(1)} collective-permute-done((bf16[32,4096]{1,0:T(8,128)(2,1)}, bf16[32,4096]{1,0:T(8,128)(2,1)S(1)}, u32[]{:S(2)}, u32[]{:S(2)}) %collective-permute-start.4) | collective-permute-done | bytes 262176 | tf_op jit(solution)/shard_map/ppermute | solution.py:95
  17.2 0.3 multiply_reduce_fusion.1
  17.5 0.2 multiply_convert_fusion.2
  17.7 0.8 pad_maximum_fusion.1
  18.6 0.7 fusion.49
  19.3 1.2 reduce-window.6
  20.6 0.1 copy.18
  20.9 3.0 %multiply_reduce_fusion = f32[256]{0:T(256)S(1)} fusion(bf16[256,4096]{1,0:T(8,128)(2,1)} %param.6), kind=kLoop, calls=%fused_computation.5 | loop fusion | flops 3145472 | bytes 2098176 | tf_op jit(solution)/shard_map/reduce_sum | solution.py:37
  24.0 2.0 %convolution_convert_fusion = bf16[512,4096]{1,0:T(8,128)(2,1)S(1)} fusion(bf16[256,4096]{1,0:T(8,128)(2,1)S(1)} %copy-done, f32[256]{0:T(256)S(1)} %add_rsqrt_fusion, s32[256]{0:T(256)S(1)} %bitcast.54), kind=kOutput, calls=%fused_computation.1 | convolution fusion | flops 1079115776 | bytes 6293504 | tf_op jit(solution)/shard_map/dot_general | solution.py:108
  26.1 2.2 %fusion.125 = (bf16[128,4096]{1,0:T(8,128)(2,1)S(1)}, bf16[1024,4096]{1,0:T(8,128)(2,1)}, bf16[128,4096]{1,0:T(8,128)(2,1)}, bf16[128,4096]{1,0:T(8,128)(2,1)}, bf16[128,4096]{1,0:T(8,128)(2,1)}) fusion(bf16[512,4096]{1,0:T(8,128)(2,1)S(1)} %convolution_convert_fusion), kind=kLoop, calls=%fused_computation.258 | loop fusion | bytes 9437184 | tf_op jit(solution)/shard_map/slice | solution.py:117
  28.3 1.2 %collective-permute-start.5 = (bf16[128,4096]{1,0:T(8,128)(2,1)}, bf16[128,4096]{1,0:T(8,128)(2,1)S(1)}, u32[]{:S(2)}, u32[]{:S(2)}) collective-permute-start(bf16[128,4096]{1,0:T(8,128)(2,1)} %get-tuple-element.103), channel_id=1, source_target_pairs={{0,1},{1,0},{2,3},{3,2},{16,17},{17,16},{18,19},{19,18},{4,5},{5,4... | collective-permute-start | bytes 3145736 | tf_op jit(solution)/shard_map/ppermute | solution.py:85
  29.5 3.1 %collective-permute-start.6 = (bf16[128,4096]{1,0:T(8,128)(2,1)}, bf16[128,4096]{1,0:T(8,128)(2,1)S(1)}, u32[]{:S(2)}, u32[]{:S(2)}) collective-permute-start(bf16[128,4096]{1,0:T(8,128)(2,1)} %get-tuple-element.102), channel_id=1, source_target_pairs={{0,2},{2,16},{16,18},{18,0},{1,19},{3,1},{17,3},{19,17},{4,6},{6,2... | collective-permute-start | bytes 3145736 | tf_op jit(solution)/shard_map/ppermute | solution.py:85
  32.7 0.2 select_reduce_fusion.1
  32.9 0.6 collective-permute-start.1
  33.5 1.0 collective-permute-start
  34.4 0.6 dynamic-slice
  35.7 21.2 %collective-permute-done = s32[32]{0:T(128)S(1)} collective-permute-done((s32[32]{0:T(128)S(1)}, s32[32]{0:T(128)S(1)}, u32[]{:S(2)}, u32[]{:S(2)}) %collective-permute-start) | collective-permute-done | bytes 160 | tf_op jit(solution)/shard_map/ppermute | solution.py:96
  56.9 0.2 add_dynamic-update-slice_fusion
  57.1 0.7 collective-permute-start.3
  57.7 13.8 %all-reduce.2 = s32[1024]{0:T(1024)S(1)} all-reduce(s32[1024]{0:T(1024)S(1)} %add_dynamic-update-slice_fusion), channel_id=1, replica_groups=mesh['blk_0'=4,'blk_1'=2,'blk_2'=4,'rep'=4] {'blk_0','blk_2'}, use_global_device_ids=true, to_apply=%add.2 | all-reduce | flops 1024 | bytes 8192
  71.6 1.5 %pad_maximum_fusion = bf16[512,4096]{1,0:T(8,128)(2,1)S(1)} fusion(bf16[128,4096]{1,0:T(8,128)(2,1)} %collective-permute-done.7, bf16[128,4096]{1,0:T(8,128)(2,1)S(1)} %collective-permute-done.6, bf16[128,4096]{1,0:T(8,128)(2,1)S(1)} %collective-permute-done.5, bf16[128,4096]{1,0:T(8,128)(2,1)S(1)} %get-tuple-element.99), kind=kLoop, calls=%fused_computation.2 | loop fusion | flops 16777216 | bytes 8388608 | tf_op jit(solution)/shard_map/concatenate | solution.py:117
  73.1 3.2 %slice.579 = bf16[512,4064]{1,0:T(8,128)(2,1)S(1)} slice(bf16[512,4096]{1,0:T(8,128)(2,1)S(1)} %pad_maximum_fusion), slice={[0:512], [32:4096]} | slice | bytes 8323072 | tf_op jit(solution)/shard_map/slice | solution.py:43
  76.3 3.2 %slice.580 = bf16[512,4080]{1,0:T(8,128)(2,1)S(1)} slice(bf16[512,4096]{1,0:T(8,128)(2,1)S(1)} %pad_maximum_fusion), slice={[0:512], [16:4096]} | slice | bytes 8355840 | tf_op jit(solution)/shard_map/slice | solution.py:43
  79.5 1.1 constant_dynamic-update-slice_fusion.2
  80.6 1.0 constant_dynamic-update-slice_fusion.1
  81.7 2.3 %constant_dynamic-update-slice_fusion = bf16[1024,4096]{1,0:T(8,128)(2,1)} fusion(bf16[1024,4096]{1,0:T(8,128)(2,1)} %constant_dynamic-update-slice_fusion.1, bf16[128,4096]{1,0:T(8,128)(2,1)} %collective-permute-done.7), kind=kLoop, calls=%fused_computation.126 | loop fusion | bytes 2097152
  84.0 4.1 %select_dynamic-update-slice_fusion = bf16[1024,4096]{1,0:T(8,128)(2,1)} fusion(bf16[1024,4096]{1,0:T(8,128)(2,1)} %constant_dynamic-update-slice_fusion, bf16[512,4080]{1,0:T(8,128)(2,1)S(1)} %slice.580, bf16[512,4064]{1,0:T(8,128)(2,1)S(1)} %slice.579, pred[512]{0:T(512)(128)(4,1)S(1)} %get-tuple-element.161, pred[512]{0:T(512)(128)(4,1)S(1)} %get-tuple-element.160), kind=kLoop, calls=%fused_computation.3 | loop fusion | flops 4194304 | bytes 12534784 | tf_op jit(solution)/shard_map/concatenate | solution.py:126
  88.1 3.6 %all-gather.2.cloned.1.call-done = bf16[1024,4096]{1,0:T(8,128)(2,1)} async-done(((bf16[64,4096]{1,0:T(8,128)(2,1)}), bf16[1024,4096]{1,0:T(8,128)(2,1)}) %all-gather.2.cloned.1.call-update) | async-done | bytes 8388624 | tf_op jit(solution)/shard_map/all_gather | solution.py:99
  91.7 12.9 %fusion.127 = f32[1024,1024]{1,0:T(8,128)S(1)} fusion(bf16[1024,4096]{1,0:T(8,128)(2,1)} %all-gather.2.cloned.1.call-done, bf16[1024,4096]{1,0:T(8,128)(2,1)} %select_dynamic-update-slice_fusion), kind=kOutput, calls=%fused_computation.260 | convolution fusion | flops 8589934592 | bytes 20971520 | tf_op jit(solution)/shard_map/dot_general | solution.py:127
  104.6 0.5 fusion
  105.2 0.3 minimum_minimum_fusion.4
  105.5 0.4 minimum_maximum_fusion.1
  106.0 0.3 minimum_maximum_fusion
  106.2 0.2 minimum_minimum_fusion.6
  106.5 0.2 maximum_maximum_fusion.3
  106.8 0.1 minimum_minimum_fusion.8
  106.9 0.1 maximum_maximum_fusion.5
  107.7 1.9 %collective-permute-start.10 = (f32[8,128]{1,0:T(8,128)S(1)}, f32[8,128]{1,0:T(8,128)S(1)}, u32[]{:S(2)}, u32[]{:S(2)}) collective-permute-start(f32[8,128]{1,0:T(8,128)S(1)} %get-tuple-element.145), channel_id=1, source_target_pairs={{2,1},{16,3},{18,17},{0,19},{19,0},{1,2},{3,16},{17,18},{6,5},{20,... | collective-permute-start | bytes 12296 | tf_op jit(solution)/shard_map/ppermute | solution.py:85
  109.6 1.2 %collective-permute-start.8 = (f32[8,128]{1,0:T(8,128)S(1)}, f32[8,128]{1,0:T(8,128)S(1)}, u32[]{:S(2)}, u32[]{:S(2)}) collective-permute-start(f32[8,128]{1,0:T(8,128)S(1)} %get-tuple-element.147), channel_id=1, source_target_pairs={{1,0},{0,1},{3,2},{2,3},{17,16},{16,17},{19,18},{18,19},{5,4},{4,5... | collective-permute-start | bytes 12296 | tf_op jit(solution)/shard_map/ppermute | solution.py:85
  110.9 0.8 collective-permute-done.8
  111.7 2.8 %collective-permute-done.9 = f32[8,128]{1,0:T(8,128)S(1)} collective-permute-done((f32[8,128]{1,0:T(8,128)S(1)}, f32[8,128]{1,0:T(8,128)S(1)}, u32[]{:S(2)}, u32[]{:S(2)}) %collective-permute-start.9) | collective-permute-done | bytes 4128 | tf_op jit(solution)/shard_map/ppermute | solution.py:85
  114.5 0.1 copy.23
  114.7 0.7 gather_fusion
  115.4 0.1 broadcast_select_fusion
  115.5 0.7 copy.24
  (68 shorter events, 1.1 us)
Async XLA Ops:
  6.5 17.4 %copy-start.1 = (s32[256,1]{0,1:T(1,128)S(1)}, s32[256,1]{0,1:T(1,128)}, u32[]{:S(2)}) copy-start(s32[256,1]{0,1:T(1,128)} %param.7) | copy-start | bytes 3076
  6.5 17.5 %copy-start = (bf16[256,4096]{1,0:T(8,128)(2,1)S(1)}, bf16[256,4096]{1,0:T(8,128)(2,1)}, u32[]{:S(2)}) copy-start(bf16[256,4096]{1,0:T(8,128)(2,1)} %param.6) | copy-start | bytes 6291460
  6.5 85.2 %all-gather.2.cloned.1.call-start = ((), (), s32[]{:S(2)}) async-start(), calls=%async_computation | async-start | bytes 8912896 | tf_op jit(solution)/shard_map/all_gather | solution.py:99
  6.5 10.7 %collective-permute-start.4 = (bf16[32,4096]{1,0:T(8,128)(2,1)}, bf16[32,4096]{1,0:T(8,128)(2,1)S(1)}, u32[]{:S(2)}, u32[]{:S(2)}) collective-permute-start(bf16[32,4096]{1,0:T(8,128)(2,1)} %bitcast.53), channel_id=1, source_target_pairs={{0,16},{16,0},{1,17},{17,1},{2,18},{18,2},{3,19},{19,3},{4,20},{20... | collective-permute-start | bytes 786440 | tf_op jit(solution)/shard_map/ppermute | solution.py:95
  26.0 6.7 %copy-start.2 = (s32[256]{0:T(256)S(1)}, s32[256]{0:T(256)}, u32[]{:S(2)}) copy-start(s32[256]{0:T(256)} %param.8) | copy-start | bytes 3076
  26.0 6.6 %copy-start.3 = (s32[256]{0:T(256)S(1)}, s32[256]{0:T(256)}, u32[]{:S(2)}) copy-start(s32[256]{0:T(256)} %param.9) | copy-start | bytes 3076
  26.0 7.4 %copy-start.4 = (s32[1,32]{1,0:T(1,128)S(1)}, s32[1,32]{1,0:T(1,128)}, u32[]{:S(2)}) copy-start(s32[1,32]{1,0:T(1,128)} %param.11) | copy-start | bytes 388
  26.0 8.4 %copy-start.5 = (u32[128]{0:T(128)S(1)}, u32[128]{0:T(128)}, u32[]{:S(2)}) copy-start(u32[128]{0:T(128)} %constant.92) | copy-start | bytes 1540
  28.3 43.3 %collective-permute-start.5 = (bf16[128,4096]{1,0:T(8,128)(2,1)}, bf16[128,4096]{1,0:T(8,128)(2,1)S(1)}, u32[]{:S(2)}, u32[]{:S(2)}) collective-permute-start(bf16[128,4096]{1,0:T(8,128)(2,1)} %get-tuple-element.103), channel_id=1, source_target_pairs={{0,1},{1,0},{2,3},{3,2},{16,17},{17,16},{18,19},{19,18},{4,5},{5,4... | collective-permute-start | bytes 3145736 | tf_op jit(solution)/shard_map/ppermute | solution.py:85
  29.5 42.1 %collective-permute-start.6 = (bf16[128,4096]{1,0:T(8,128)(2,1)}, bf16[128,4096]{1,0:T(8,128)(2,1)S(1)}, u32[]{:S(2)}, u32[]{:S(2)}) collective-permute-start(bf16[128,4096]{1,0:T(8,128)(2,1)} %get-tuple-element.102), channel_id=1, source_target_pairs={{0,2},{2,16},{16,18},{18,0},{1,19},{3,1},{17,3},{19,17},{4,6},{6,2... | collective-permute-start | bytes 3145736 | tf_op jit(solution)/shard_map/ppermute | solution.py:85
  32.7 39.0 %collective-permute-start.7 = (bf16[128,4096]{1,0:T(8,128)(2,1)}, bf16[128,4096]{1,0:T(8,128)(2,1)}, u32[]{:S(2)}, u32[]{:S(2)}) collective-permute-start(bf16[128,4096]{1,0:T(8,128)(2,1)} %get-tuple-element.101), channel_id=1, source_target_pairs={{1,2},{3,16},{17,18},{19,0},{0,19},{2,1},{16,3},{18,17},{5,6},{7,2... | collective-permute-start | bytes 3145736 | tf_op jit(solution)/shard_map/ppermute | solution.py:85
  32.9 24.2 %collective-permute-start.1 = (s32[2,128]{1,0:T(2,128)S(1)}, s32[2,128]{1,0:T(2,128)S(1)}, u32[]{:S(2)}, u32[]{:S(2)}) collective-permute-start(s32[2,128]{1,0:T(2,128)S(1)} %get-tuple-element.163), channel_id=1, source_target_pairs={{0,1},{1,0},{2,3},{3,2},{16,17},{17,16},{18,19},{19,18},{4,5},{5,4... | collective-permute-start | bytes 3080 | tf_op jit(solution)/shard_map/ppermute | solution.py:85
  33.5 23.4 %collective-permute-start = (s32[32]{0:T(128)S(1)}, s32[32]{0:T(128)S(1)}, u32[]{:S(2)}, u32[]{:S(2)}) collective-permute-start(s32[32]{0:T(128)S(1)} %bitcast.67), channel_id=1, source_target_pairs={{0,16},{16,0},{1,17},{17,1},{2,18},{18,2},{3,19},{19,3},{4,20},{20... | collective-permute-start | bytes 392 | tf_op jit(solution)/shard_map/ppermute | solution.py:96
  56.9 14.7 %collective-permute-start.2 = (s32[2,128]{1,0:T(2,128)S(1)}, s32[2,128]{1,0:T(2,128)S(1)}, u32[]{:S(2)}, u32[]{:S(2)}) collective-permute-start(s32[2,128]{1,0:T(2,128)S(1)} %get-tuple-element.165), channel_id=1, source_target_pairs={{0,2},{2,16},{16,18},{18,0},{1,19},{3,1},{17,3},{19,17},{4,6},{6,2... | collective-permute-start | bytes 3080 | tf_op jit(solution)/shard_map/ppermute | solution.py:85
  57.1 14.5 %collective-permute-start.3 = (s32[2,128]{1,0:T(2,128)S(1)}, s32[2,128]{1,0:T(2,128)S(1)}, u32[]{:S(2)}, u32[]{:S(2)}) collective-permute-start(s32[2,128]{1,0:T(2,128)S(1)} %get-tuple-element.164), channel_id=1, source_target_pairs={{1,2},{3,16},{17,18},{19,0},{0,19},{2,1},{16,3},{18,17},{5,6},{7,2... | collective-permute-start | bytes 3080 | tf_op jit(solution)/shard_map/ppermute | solution.py:85
  107.7 3.2 %collective-permute-start.10 = (f32[8,128]{1,0:T(8,128)S(1)}, f32[8,128]{1,0:T(8,128)S(1)}, u32[]{:S(2)}, u32[]{:S(2)}) collective-permute-start(f32[8,128]{1,0:T(8,128)S(1)} %get-tuple-element.145), channel_id=1, source_target_pairs={{2,1},{16,3},{18,17},{0,19},{19,0},{1,2},{3,16},{17,18},{6,5},{20,... | collective-permute-start | bytes 12296 | tf_op jit(solution)/shard_map/ppermute | solution.py:85
  109.6 2.1 %collective-permute-start.8 = (f32[8,128]{1,0:T(8,128)S(1)}, f32[8,128]{1,0:T(8,128)S(1)}, u32[]{:S(2)}, u32[]{:S(2)}) collective-permute-start(f32[8,128]{1,0:T(8,128)S(1)} %get-tuple-element.147), channel_id=1, source_target_pairs={{1,0},{0,1},{3,2},{2,3},{17,16},{16,17},{19,18},{18,19},{5,4},{4,5... | collective-permute-start | bytes 12296 | tf_op jit(solution)/shard_map/ppermute | solution.py:85
  110.8 3.7 %collective-permute-start.9 = (f32[8,128]{1,0:T(8,128)S(1)}, f32[8,128]{1,0:T(8,128)S(1)}, u32[]{:S(2)}, u32[]{:S(2)}) collective-permute-start(f32[8,128]{1,0:T(8,128)S(1)} %get-tuple-element.146), channel_id=1, source_target_pairs={{2,0},{16,2},{18,16},{0,18},{19,1},{1,3},{3,17},{17,19},{6,4},{20,... | collective-permute-start | bytes 12296 | tf_op jit(solution)/shard_map/ppermute | solution.py:85
Sparse Core Ops, SparseCore 0:
  18.7 73.0 all-gather.1

commit v12 on v11

--- a/solution.py
+++ b/solution.py
@@ -10,6 +10,7 @@
 SHIFT_BINS = 16
 WIN = 16
 CAP = 128
+LANE = 128
 BLK = ("blk_0", "blk_1", "blk_2")
 BLK_REP = ("blk_0", "blk_1", "blk_2", "rep")
 ZRING = ("blk_1", "rep")
@@ -67,18 +68,36 @@
 
 def top_rows(scores):
     depth = scores.shape[0] // K
+    assert depth & (depth - 1) == 0
     lists = [scores[k * depth:(k + 1) * depth] for k in range(K)]
     for stage in SORT8:
         for i, j in stage:
             exchange(lists, i, j)
     while depth > 1:
         depth //= 2
-        lists = [jnp.maximum(lists[i][:depth], lists[K - 1 - i][depth:]) for i in range(K)]
-        for step in (4, 2, 1):
-            for i in range(K):
-                if (i // step) % 2 == 0:
-                    exchange(lists, i, i + step)
-    return jnp.concatenate(lists, axis=0)
+        lists = bitonic_merge([a[:depth] for a in lists], [a[depth:] for a in lists])
+    return lists
+
+
+def ring_gather(block, axis):
+    size = 4
+    up = [(i, (i + 1) % size) for i in range(size)]
+    down = [(i, (i - 1) % size) for i in range(size)]
+    below = lax.ppermute(block, axis, up)
+    above = lax.ppermute(block, axis, down)
+    half = block.shape[0] // 2
+    far_low = lax.ppermute(below[:half], axis, up)
+    far_high = lax.ppermute(above[half:], axis, down)
+    return [block, below, above, far_low, far_high]
+
+
+def bitonic_merge(first, second):
+    lists = [jnp.maximum(first[i], second[K - 1 - i]) for i in range(K)]
+    for step in (4, 2, 1):
+        for i in range(K):
+            if (i // step) % 2 == 0:
+                exchange(lists, i, i + step)
+    return lists
 
 
 def route(blocks, perms):
@@ -94,9 +113,15 @@
 
     partner = lax.ppermute(library[0], "blk_1", [(0, 1), (1, 0)])
     partner_bin = lax.ppermute(library_bin[0], "blk_1", [(0, 1), (1, 0)])
-    chunk = jnp.concatenate([unit_rows(library[0]), unit_rows(partner)], axis=0)
-    chunk_bin = jnp.concatenate([library_bin[0], partner_bin], axis=0)
+    partner = unit_rows(partner)
+    kept = 3 * partner.shape[0] // 2 - library.shape[1]
+    chunk = jnp.concatenate([unit_rows(library[0]), partner[:kept]], axis=0)
+    chunk_bin = jnp.concatenate([library_bin[0], partner_bin[:kept]], axis=0)
     full, lib_bins = lax.all_gather((chunk, chunk_bin), ("blk_0", "blk_2"), axis=0, tiled=True)
+    bin_cols = jnp.pad(partner_bin[kept:].astype(jnp.bfloat16)[:, None], ((0, 0), (0, LANE - 1)))
+    rest = jnp.concatenate([partner[kept:], bin_cols], axis=1)
+    rest = ring_gather(jnp.concatenate(ring_gather(rest, "blk_2"), axis=0), "blk_0")
+    rest = jnp.concatenate(rest, axis=0)
 
     unit_q = unit_rows(queries)
     group = query_group[:, 0]
@@ -124,10 +149,18 @@
     for s in range(1, NSHIFT + 1):
         moved = jnp.where((flat_shift == s)[:, None], lower_bins(rows, s * SHIFT_BINS), moved)
     both = jnp.concatenate([rows, moved], axis=0)
-    prod = lax.dot_general(full, both, (((1,), (1,)), ((), ())), preferred_element_type=jnp.float32)
-    near = jnp.abs(lib_bins[:, None] - flat_bin[None, :]) <= WIN
-    scores = jnp.where(near, jnp.maximum(prod[:, :total], prod[:, total:]), 0.0)
-    best = top_rows(scores)
+
+    def best_of(lib, bins):
+        prod = lax.dot_general(lib, both, (((1,), (1,)), ((), ())), preferred_element_type=jnp.float32)
+        near = jnp.abs(bins[:, None] - flat_bin[None, :]) <= WIN
+        return top_rows(jnp.where(near, jnp.maximum(prod[:, :total], prod[:, total:]), 0.0))
+
+    split_at = full.shape[0] * 2 // 3
+    best = best_of(rest[:, :W], rest[:, W].astype(jnp.int32))
+    best = bitonic_merge(best, best_of(full[:split_at], lib_bins[:split_at]))
+    best = bitonic_merge(best, best_of(full[split_at:], lib_bins[split_at:]))
+    best = jnp.concatenate(best, axis=0)
+
     home = route([best[:, i * CAP:(i + 1) * CAP] for i in range(roles)], tuple(inverse(p) for p in perms))
     home = jnp.concatenate(home, axis=1)
     return jnp.take(home, slot, axis=1).T

time: 123 us -> 153 us (1.24)
  starting transfers between devices: 14.2 us -> 41.3 us
  local copies, waits for them, and re-layouts: 15.5 us -> 22 us
  waiting for transfers between devices: 32.3 us -> 28.1 us
    ppermute x0 -> x8, waiting for transfers between devices: none -> 24.7 us  [the longest x2 9.97 us: ring_gather(): below = lax.ppermute(block, axis, up)]
    ppermute x1, waiting for transfers between devices: 21.2 us -> 2.33 us  [on_device(): partner_bin = lax.ppermute(library_bin[0], 'blk_1', [(0, 1), (1, 0)])]
    ppermute x9, starting transfers between devices: 8.8 us -> 26.3 us  [route(): lax.ppermute(b, ZRING, p)]
    ppermute x0 -> x8, starting transfers between devices: none -> 9.24 us  [the longest x2 3.98 us: ring_gather(): far_high = lax.ppermute(above[half:], axis, down)]
    unnamed x17 -> x40, local copies, waits for them, and re-layouts: 5.07 us -> 10.6 us
    ppermute x1, waiting for transfers between devices: 3.84 us -> 0.01 us  [on_device(): partner = lax.ppermute(library[0], 'blk_1', [(0, 1), (1, 0)])]
    all_gather x1, waiting for transfers between devices: 3.6 us -> 0.02 us  [on_device(): lax.all_gather((chunk, chunk_bin), ('blk_0', 'blk_2'), axis=0, tiled=True)]
    ppermute x9, waiting for transfers between devices: 3.64 us -> 1 us  [route(): lax.ppermute(b, ZRING, p)]
  transfers between devices with their start and end apart: 12 -> 20, of which waited for: 5 -> 6; matrix products, arithmetic and copies ran while one was open for 24% -> 21% of each run, Pallas kernels for 0% -> 0%
where the time goes in v12:
time: 153 us; the launch traced here: 152 us
  starting transfers between devices  41.3 us (27%)
  waiting for transfers between devices  28.1 us (18%)
  local copies, waits for them, and re-layouts  22 us (14%)
  other arithmetic  17.5 us (11%)
  matrix products  15.5 us (10%)
  between operations  15 us (10%)
  blocking collectives  12.9 us (8%)
    ppermute x9, starting transfers between devices, route(): lax.ppermute(b, ZRING, p)  26.3 us
    dot_general x3, matrix products, best_of(): lax.dot_general(lib, both, (((1,), (1,)), ((), ())), preferred_element_ty...  13.5 us
    unnamed x1, blocking collectives  12.9 us
    unnamed x40, local copies, waits for them, and re-layouts  10.6 us
    ppermute x2, waiting for transfers between devices, ring_gather(): below = lax.ppermute(block, axis, up)  9.97 us
    slice x2, local copies, waits for them, and re-layouts, lower_bins(): return jnp.concatenate([rows[..., amount:], tail], axis=-1)  6.32 us
    ppermute x2, waiting for transfers between devices, ring_gather(): above = lax.ppermute(block, axis, down)  6.14 us
    ppermute x2, waiting for transfers between devices, ring_gather(): far_low = lax.ppermute(below[:half], axis, up)  5.43 us
  transfers between devices with their start and end apart: 20, of which 6 were waited for; matrix products, arithmetic and copies ran while one was open for 21% of the time, Pallas kernels for 0%

profile of v12, /device:TPU:1, one launch (start us, length us, event | category | flops | bytes accessed | tf_op | source)
XLA Modules:
  0.0 152.4 jit_solution(753857571645726541)
XLA Ops:
  6.5 4.4 %collective-permute-start = (bf16[32,4096]{1,0:T(8,128)(2,1)}, bf16[32,4096]{1,0:T(8,128)(2,1)S(1)}, u32[]{:S(2)}, u32[]{:S(2)}) collective-permute-start(bf16[32,4096]{1,0:T(8,128)(2,1)} %bitcast.57), channel_id=1, source_target_pairs={{0,16},{16,0},{1,17},{17,1},{2,18},{18,2},{3,19},{19,3},{4,20},{20... | collective-permute-start | bytes 786440 | tf_op jit(solution)/shard_map/ppermute | solution.py:114
  11.0 1.3 multiply_reduce_fusion.1
  12.2 0.7 fusion.99
  13.0 1.2 reduce-window.6
  14.6 0.7 and_reduce_fusion
  15.3 1.1 multiply_convert_fusion.2
  16.4 3.0 %multiply_reduce_fusion = f32[256]{0:T(256)S(1)} fusion(bf16[256,4096]{1,0:T(8,128)(2,1)} %param.6), kind=kLoop, calls=%fused_computation.7 | loop fusion | flops 3145472 | bytes 2098176 | tf_op jit(solution)/shard_map/reduce_sum | solution.py:38
  20.0 0.8 pad_maximum_fusion.1
  20.8 2.0 %convolution_convert_fusion = bf16[512,4096]{1,0:T(8,128)(2,1)S(1)} fusion(bf16[256,4096]{1,0:T(8,128)(2,1)S(1)} %copy-done, f32[256]{0:T(256)S(1)} %add_rsqrt_fusion, s32[256]{0:T(256)S(1)} %bitcast.62), kind=kOutput, calls=%fused_computation.1 | convolution fusion | flops 1079115776 | bytes 6293504 | tf_op jit(solution)/shard_map/dot_general | solution.py:133
  22.8 2.3 %fusion.275 = (bf16[128,4096]{1,0:T(8,128)(2,1)S(1)}, bf16[1024,4096]{1,0:T(8,128)(2,1)}, bf16[128,4096]{1,0:T(8,128)(2,1)}, bf16[128,4096]{1,0:T(8,128)(2,1)}, bf16[128,4096]{1,0:T(8,128)(2,1)}) fusion(bf16[512,4096]{1,0:T(8,128)(2,1)S(1)} %convolution_convert_fusion), kind=kLoop, calls=%fused_computation.553 | loop fusion | bytes 9437184 | tf_op jit(solution)/shard_map/slice | solution.py:142
  25.2 1.0 collective-permute-start.13
  26.1 1.1 collective-permute-start.14
  27.3 1.4 collective-permute-start.1
  28.8 2.3 %collective-permute-done.1 = s32[32]{0:T(128)S(1)} collective-permute-done((s32[32]{0:T(128)S(1)}, s32[32]{0:T(128)S(1)}, u32[]{:S(2)}, u32[]{:S(2)}) %collective-permute-start.1) | collective-permute-done | bytes 160 | tf_op jit(solution)/shard_map/ppermute | solution.py:115
  31.4 0.7 constant_dynamic-update-slice_fusion.4
  32.1 1.3 collective-permute-start.2
  33.4 1.2 collective-permute-start.12
  34.6 12.5 %collective-permute-start.11 = (s32[2,128]{1,0:T(2,128)S(1)}, s32[2,128]{1,0:T(2,128)S(1)}, u32[]{:S(2)}, u32[]{:S(2)}) collective-permute-start(s32[2,128]{1,0:T(2,128)S(1)} %get-tuple-element.398), channel_id=1, source_target_pairs={{0,2},{2,16},{16,18},{18,0},{1,19},{3,1},{17,3},{19,17},{4,6},{6,2... | collective-permute-start | bytes 3080 | tf_op jit(solution)/shard_map/ppermute | solution.py:104
  48.5 12.9 %all-reduce.3 = s32[768]{0:T(1024)S(1)} all-reduce(s32[768]{0:T(1024)S(1)} %add_dynamic-update-slice_fusion), channel_id=1, replica_groups=mesh['blk_0'=4,'blk_1'=2,'blk_2'=4,'rep'=4] {'blk_0','blk_2'}, use_global_device_ids=true, to_apply=%add.3 | all-reduce | flops 768 | bytes 6144
  61.4 1.1 collective-permute-start.3
  62.6 0.8 constant_dynamic-update-slice_fusion.3
  63.3 6.1 %collective-permute-done.3 = bf16[16,4224]{1,0:T(8,128)(2,1)S(1)} collective-permute-done((bf16[16,4224]{1,0:T(8,128)(2,1)S(1)}, bf16[16,4224]{1,0:T(8,128)(2,1)S(1)}, u32[]{:S(2)}, u32[]{:S(2)}) %collective-permute-start.3) | collective-permute-done | bytes 135200 | tf_op jit(solution)/shard_map/ppermute | solution.py:87
  69.5 0.7 constant_dynamic-update-slice_fusion.2
  70.2 5.4 %collective-permute-done.4 = bf16[8,4224]{1,0:T(8,128)(2,1)S(1)} collective-permute-done((bf16[8,4224]{1,0:T(8,128)(2,1)S(1)}, bf16[8,4224]{1,0:T(8,128)(2,1)S(1)}, u32[]{:S(2)}, u32[]{:S(2)}) %collective-permute-start.4) | collective-permute-done | bytes 67616 | tf_op jit(solution)/shard_map/ppermute | solution.py:89
  75.6 1.1 collective-permute-start.5
  77.4 3.2 %collective-permute-done.5 = bf16[8,4224]{1,0:T(8,128)(2,1)S(1)} collective-permute-done((bf16[8,4224]{1,0:T(8,128)(2,1)S(1)}, bf16[8,4224]{1,0:T(8,128)(2,1)S(1)}, u32[]{:S(2)}, u32[]{:S(2)}) %collective-permute-start.5) | collective-permute-done | bytes 67616 | tf_op jit(solution)/shard_map/ppermute | solution.py:90
  80.6 3.6 %collective-permute-start.10 = (s32[2,128]{1,0:T(2,128)S(1)}, s32[2,128]{1,0:T(2,128)S(1)}, u32[]{:S(2)}, u32[]{:S(2)}) collective-permute-start(s32[2,128]{1,0:T(2,128)S(1)} %get-tuple-element.396), channel_id=1, source_target_pairs={{0,1},{1,0},{2,3},{3,2},{16,17},{17,16},{18,19},{19,18},{4,5},{5,4... | collective-permute-start | bytes 3080 | tf_op jit(solution)/shard_map/ppermute | solution.py:104
  84.2 0.7 constant_dynamic-update-slice_fusion
  85.1 2.6 %collective-permute-start.7 = (bf16[64,4224]{1,0:T(8,128)(2,1)}, bf16[64,4224]{1,0:T(8,128)(2,1)S(1)}, u32[]{:S(2)}, u32[]{:S(2)}) collective-permute-start(bf16[64,4224]{1,0:T(8,128)(2,1)} %get-tuple-element.311), channel_id=1, source_target_pairs={{0,96},{32,0},{64,32},{96,64},{1,97},{33,1},{65,33},{97,65},{2,98}... | collective-permute-start | bytes 1622024 | tf_op jit(solution)/shard_map/ppermute | solution.py:87
  87.7 10.0 %collective-permute-done.6 = bf16[64,4224]{1,0:T(8,128)(2,1)S(1)} collective-permute-done((bf16[64,4224]{1,0:T(8,128)(2,1)}, bf16[64,4224]{1,0:T(8,128)(2,1)S(1)}, u32[]{:S(2)}, u32[]{:S(2)}) %collective-permute-start.6) | collective-permute-done | bytes 540704 | tf_op jit(solution)/shard_map/ppermute | solution.py:86
  97.8 2.9 %collective-permute-start.9 = (bf16[32,4224]{1,0:T(8,128)(2,1)S(1)}, bf16[32,4224]{1,0:T(8,128)(2,1)S(1)}, u32[]{:S(2)}, u32[]{:S(2)}) collective-permute-start(bf16[32,4224]{1,0:T(8,128)(2,1)S(1)} %slice.1284), channel_id=1, source_target_pairs={{0,96},{32,0},{64,32},{96,64},{1,97},{33,1},{65,33},{97,65},{2,98}... | collective-permute-start | bytes 811016 | tf_op jit(solution)/shard_map/ppermute | solution.py:90
  100.7 0.8 constant_dynamic-update-slice_fusion.8
  101.5 0.8 constant_dynamic-update-slice_fusion.7
  102.9 3.2 %slice.1300 = bf16[512,4080]{1,0:T(8,128)(2,1)S(1)} slice(bf16[512,4096]{1,0:T(8,128)(2,1)S(1)} %pad_maximum_fusion), slice={[0:512], [16:4096]} | slice | bytes 8355840 | tf_op jit(solution)/shard_map/slice | solution.py:44
  106.1 3.2 %slice.1299 = bf16[512,4064]{1,0:T(8,128)(2,1)S(1)} slice(bf16[512,4096]{1,0:T(8,128)(2,1)S(1)} %pad_maximum_fusion), slice={[0:512], [32:4096]} | slice | bytes 8323072 | tf_op jit(solution)/shard_map/slice | solution.py:44
  109.5 3.3 %select_dynamic-update-slice_fusion = bf16[1024,4096]{1,0:T(8,128)(2,1)S(1)} fusion(bf16[1024,4096]{1,0:T(8,128)(2,1)S(1)} %constant_dynamic-update-slice_fusion.14, bf16[512,4080]{1,0:T(8,128)(2,1)S(1)} %slice.1300, bf16[512,4064]{1,0:T(8,128)(2,1)S(1)} %slice.1299, pred[512]{0:T(512)(128)(4,1)S(1)} %get-tuple-element.394, ...), kind=kLoop, calls=%fused_computation.5 | loop fusion | flops 4194304 | bytes 12583936 | tf_op jit(solution)/shard_map/concatenate | solution.py:151
  113.1 3.1 %copy-done.1 = bf16[1024,4096]{1,0:T(8,128)(2,1)} copy-done((bf16[1024,4096]{1,0:T(8,128)(2,1)}, bf16[1024,4096]{1,0:T(8,128)(2,1)S(1)}, u32[]{:S(2)}) %copy-start.1) | copy-done | bytes 8388632
  116.2 2.4 %fusion.4 = f32[256,1024]{1,0:T(8,128)S(1)} fusion(bf16[1024,4096]{1,0:T(8,128)(2,1)S(1)} %select_dynamic-update-slice_fusion, bf16[256,4224]{1,0:T(8,128)(2,1)S(1)} %constant_dynamic-update-slice_fusion.5), kind=kOutput, calls=%fused_computation.11 | convolution fusion | flops 2147483648 | bytes 11534336 | tf_op jit(solution)/shard_map/dot_general | solution.py:154
  118.6 6.5 %fusion.2 = f32[256,1024]{1,0:T(8,128)S(1)} fusion(bf16[1024,4096]{1,0:T(8,128)(2,1)} %copy-done.1, bf16[768,4096]{1,0:T(8,128)(2,1)} %all-gather.2.cloned.1.call-done), kind=kOutput, calls=%fused_computation.9 | convolution fusion | flops 2147483648 | bytes 11534336 | tf_op jit(solution)/shard_map/dot_general | solution.py:154
  127.3 0.7 slice-done.6
  128.0 1.4 slice-done.3
  129.4 4.6 %fusion = f32[512,1024]{1,0:T(8,128)S(1)} fusion(bf16[1024,4096]{1,0:T(8,128)(2,1)S(1)} %bitcast.61, bf16[768,4096]{1,0:T(8,128)(2,1)S(1)} %bitcast.79), kind=kOutput, calls=%fused_computation.2 | convolution fusion | flops 4294967296 | bytes 14680064 | tf_op jit(solution)/shard_map/dot_general | solution.py:154
  136.0 4.0 %collective-permute-start.18 = (f32[8,128]{1,0:T(8,128)S(1)}, f32[8,128]{1,0:T(8,128)S(1)}, u32[]{:S(2)}, u32[]{:S(2)}) collective-permute-start(f32[8,128]{1,0:T(8,128)S(1)} %get-tuple-element.358), channel_id=1, source_target_pairs={{2,1},{16,3},{18,17},{0,19},{19,0},{1,2},{3,16},{17,18},{6,5},{20,... | collective-permute-start | bytes 12296 | tf_op jit(solution)/shard_map/ppermute | solution.py:104
  139.9 1.8 %collective-permute-start.17 = (f32[8,128]{1,0:T(8,128)S(1)}, f32[8,128]{1,0:T(8,128)S(1)}, u32[]{:S(2)}, u32[]{:S(2)}) collective-permute-start(f32[8,128]{1,0:T(8,128)S(1)} %get-tuple-element.359), channel_id=1, source_target_pairs={{2,0},{16,2},{18,16},{0,18},{19,1},{1,3},{3,17},{17,19},{6,4},{20,... | collective-permute-start | bytes 12296 | tf_op jit(solution)/shard_map/ppermute | solution.py:104
  141.8 1.1 collective-permute-start.16
  142.9 1.0 collective-permute-done.17
  144.0 0.7 gather_fusion
  144.9 0.7 copy.27
  (165 shorter events, 7.9 us)
Async XLA Ops:
  6.5 14.3 %copy-start = (bf16[256,4096]{1,0:T(8,128)(2,1)S(1)}, bf16[256,4096]{1,0:T(8,128)(2,1)}, u32[]{:S(2)}) copy-start(bf16[256,4096]{1,0:T(8,128)(2,1)} %param.6) | copy-start | bytes 6291460
  6.5 112.1 %all-gather.2.cloned.1.call-start = ((), (), s32[]{:S(2)}) async-start(), calls=%async_computation | async-start | bytes 6684672 | tf_op jit(solution)/shard_map/all_gather | solution.py:120
  6.5 12.9 %collective-permute-start = (bf16[32,4096]{1,0:T(8,128)(2,1)}, bf16[32,4096]{1,0:T(8,128)(2,1)S(1)}, u32[]{:S(2)}, u32[]{:S(2)}) collective-permute-start(bf16[32,4096]{1,0:T(8,128)(2,1)} %bitcast.57), channel_id=1, source_target_pairs={{0,16},{16,0},{1,17},{17,1},{2,18},{18,2},{3,19},{19,3},{4,20},{20... | collective-permute-start | bytes 786440 | tf_op jit(solution)/shard_map/ppermute | solution.py:114
  22.8 4.5 %copy-start.6 = (s32[1,32]{1,0:T(1,128)S(1)}, s32[1,32]{1,0:T(1,128)}, u32[]{:S(2)}) copy-start(s32[1,32]{1,0:T(1,128)} %param.11) | copy-start | bytes 388
  22.8 5.9 %copy-start.4 = (s32[256]{0:T(256)S(1)}, s32[256]{0:T(256)}, u32[]{:S(2)}) copy-start(s32[256]{0:T(256)} %param.8) | copy-start | bytes 3076
  22.8 5.9 %copy-start.5 = (s32[256]{0:T(256)S(1)}, s32[256]{0:T(256)}, u32[]{:S(2)}) copy-start(s32[256]{0:T(256)} %param.9) | copy-start | bytes 3076
  22.8 24.2 %copy-start.7 = (u32[128]{0:T(128)S(1)}, u32[128]{0:T(128)}, u32[]{:S(2)}) copy-start(u32[128]{0:T(128)} %constant.96) | copy-start | bytes 1540
  25.2 77.2 %collective-permute-start.13 = (bf16[128,4096]{1,0:T(8,128)(2,1)}, bf16[128,4096]{1,0:T(8,128)(2,1)S(1)}, u32[]{:S(2)}, u32[]{:S(2)}) collective-permute-start(bf16[128,4096]{1,0:T(8,128)(2,1)} %get-tuple-element.247), channel_id=1, source_target_pairs={{0,1},{1,0},{2,3},{3,2},{16,17},{17,16},{18,19},{19,18},{4,5},{5,4... | collective-permute-start | bytes 3145736 | tf_op jit(solution)/shard_map/ppermute | solution.py:104
  26.1 76.3 %collective-permute-start.14 = (bf16[128,4096]{1,0:T(8,128)(2,1)}, bf16[128,4096]{1,0:T(8,128)(2,1)S(1)}, u32[]{:S(2)}, u32[]{:S(2)}) collective-permute-start(bf16[128,4096]{1,0:T(8,128)(2,1)} %get-tuple-element.246), channel_id=1, source_target_pairs={{0,2},{2,16},{16,18},{18,0},{1,19},{3,1},{17,3},{19,17},{4,6},{6,2... | collective-permute-start | bytes 3145736 | tf_op jit(solution)/shard_map/ppermute | solution.py:104
  27.3 3.9 %collective-permute-start.1 = (s32[32]{0:T(128)S(1)}, s32[32]{0:T(128)S(1)}, u32[]{:S(2)}, u32[]{:S(2)}) collective-permute-start(s32[32]{0:T(128)S(1)} %bitcast.75), channel_id=1, source_target_pairs={{0,16},{16,0},{1,17},{17,1},{2,18},{18,2},{3,19},{19,3},{4,20},{20... | collective-permute-start | bytes 392 | tf_op jit(solution)/shard_map/ppermute | solution.py:115
  32.1 29.3 %collective-permute-start.2 = (bf16[16,4224]{1,0:T(8,128)(2,1)S(1)}, bf16[16,4224]{1,0:T(8,128)(2,1)S(1)}, u32[]{:S(2)}, u32[]{:S(2)}) collective-permute-start(bf16[16,4224]{1,0:T(8,128)(2,1)S(1)} %get-tuple-element.290), channel_id=1, source_target_pairs={{0,4},{4,8},{8,12},{12,0},{1,5},{5,9},{9,13},{13,1},{2,6},{6,10},{... | collective-permute-start | bytes 405512 | tf_op jit(solution)/shard_map/ppermute | solution.py:86
  33.4 51.5 %collective-permute-start.12 = (s32[2,128]{1,0:T(2,128)S(1)}, s32[2,128]{1,0:T(2,128)S(1)}, u32[]{:S(2)}, u32[]{:S(2)}) collective-permute-start(s32[2,128]{1,0:T(2,128)S(1)} %get-tuple-element.397), channel_id=1, source_target_pairs={{1,2},{3,16},{17,18},{19,0},{0,19},{2,1},{16,3},{18,17},{5,6},{7,2... | collective-permute-start | bytes 3080 | tf_op jit(solution)/shard_map/ppermute | solution.py:104
  34.6 50.3 %collective-permute-start.11 = (s32[2,128]{1,0:T(2,128)S(1)}, s32[2,128]{1,0:T(2,128)S(1)}, u32[]{:S(2)}, u32[]{:S(2)}) collective-permute-start(s32[2,128]{1,0:T(2,128)S(1)} %get-tuple-element.398), channel_id=1, source_target_pairs={{0,2},{2,16},{16,18},{18,0},{1,19},{3,1},{17,3},{19,17},{4,6},{6,2... | collective-permute-start | bytes 3080 | tf_op jit(solution)/shard_map/ppermute | solution.py:104
  61.4 41.5 %copy-start.3 = (s32[768]{0:T(1024)}, s32[768]{0:T(1024)S(1)}, u32[]{:S(2)}) copy-start(s32[768]{0:T(1024)S(1)} %all-reduce.3) | copy-start | bytes 9220
  61.4 8.0 %collective-permute-start.3 = (bf16[16,4224]{1,0:T(8,128)(2,1)S(1)}, bf16[16,4224]{1,0:T(8,128)(2,1)S(1)}, u32[]{:S(2)}, u32[]{:S(2)}) collective-permute-start(bf16[16,4224]{1,0:T(8,128)(2,1)S(1)} %get-tuple-element.290), channel_id=1, source_target_pairs={{0,12},{4,0},{8,4},{12,8},{1,13},{5,1},{9,5},{13,9},{2,14},{6,2},{... | collective-permute-start | bytes 405512 | tf_op jit(solution)/shard_map/ppermute | solution.py:87
  69.5 6.2 %collective-permute-start.4 = (bf16[8,4224]{1,0:T(8,128)(2,1)S(1)}, bf16[8,4224]{1,0:T(8,128)(2,1)S(1)}, u32[]{:S(2)}, u32[]{:S(2)}) collective-permute-start(bf16[8,4224]{1,0:T(8,128)(2,1)S(1)} %slice.1281), channel_id=1, source_target_pairs={{0,4},{4,8},{8,12},{12,0},{1,5},{5,9},{9,13},{13,1},{2,6},{6,10},{... | collective-permute-start | bytes 202760 | tf_op jit(solution)/shard_map/ppermute | solution.py:89
  75.6 5.0 %collective-permute-start.5 = (bf16[8,4224]{1,0:T(8,128)(2,1)S(1)}, bf16[8,4224]{1,0:T(8,128)(2,1)S(1)}, u32[]{:S(2)}, u32[]{:S(2)}) collective-permute-start(bf16[8,4224]{1,0:T(8,128)(2,1)S(1)} %slice.1282), channel_id=1, source_target_pairs={{0,12},{4,0},{8,4},{12,8},{1,13},{5,1},{9,5},{13,9},{2,14},{6,2},{... | collective-permute-start | bytes 202760 | tf_op jit(solution)/shard_map/ppermute | solution.py:90
  80.6 4.5 %collective-permute-start.10 = (s32[2,128]{1,0:T(2,128)S(1)}, s32[2,128]{1,0:T(2,128)S(1)}, u32[]{:S(2)}, u32[]{:S(2)}) collective-permute-start(s32[2,128]{1,0:T(2,128)S(1)} %get-tuple-element.396), channel_id=1, source_target_pairs={{0,1},{1,0},{2,3},{3,2},{16,17},{17,16},{18,19},{19,18},{4,5},{5,4... | collective-permute-start | bytes 3080 | tf_op jit(solution)/shard_map/ppermute | solution.py:104
  84.9 17.5 %collective-permute-start.15 = (bf16[128,4096]{1,0:T(8,128)(2,1)}, bf16[128,4096]{1,0:T(8,128)(2,1)S(1)}, u32[]{:S(2)}, u32[]{:S(2)}) collective-permute-start(bf16[128,4096]{1,0:T(8,128)(2,1)} %get-tuple-element.245), channel_id=1, source_target_pairs={{1,2},{3,16},{17,18},{19,0},{0,19},{2,1},{16,3},{18,17},{5,6},{7,2... | collective-permute-start | bytes 3145736 | tf_op jit(solution)/shard_map/ppermute | solution.py:104
  84.9 12.8 %collective-permute-start.6 = (bf16[64,4224]{1,0:T(8,128)(2,1)}, bf16[64,4224]{1,0:T(8,128)(2,1)S(1)}, u32[]{:S(2)}, u32[]{:S(2)}) collective-permute-start(bf16[64,4224]{1,0:T(8,128)(2,1)} %get-tuple-element.311), channel_id=1, source_target_pairs={{0,32},{32,64},{64,96},{96,0},{1,33},{33,65},{65,97},{97,1},{2,34}... | collective-permute-start | bytes 1622024 | tf_op jit(solution)/shard_map/ppermute | solution.py:86
  85.1 12.7 %collective-permute-start.7 = (bf16[64,4224]{1,0:T(8,128)(2,1)}, bf16[64,4224]{1,0:T(8,128)(2,1)S(1)}, u32[]{:S(2)}, u32[]{:S(2)}) collective-permute-start(bf16[64,4224]{1,0:T(8,128)(2,1)} %get-tuple-element.311), channel_id=1, source_target_pairs={{0,96},{32,0},{64,32},{96,64},{1,97},{33,1},{65,33},{97,65},{2,98}... | collective-permute-start | bytes 1622024 | tf_op jit(solution)/shard_map/ppermute | solution.py:87
  97.7 15.2 %collective-permute-start.8 = (bf16[32,4224]{1,0:T(8,128)(2,1)S(1)}, bf16[32,4224]{1,0:T(8,128)(2,1)S(1)}, u32[]{:S(2)}, u32[]{:S(2)}) collective-permute-start(bf16[32,4224]{1,0:T(8,128)(2,1)S(1)} %slice.1283), channel_id=1, source_target_pairs={{0,32},{32,64},{64,96},{96,0},{1,33},{33,65},{65,97},{97,1},{2,34}... | collective-permute-start | bytes 811016 | tf_op jit(solution)/shard_map/ppermute | solution.py:89
  97.8 15.1 %collective-permute-start.9 = (bf16[32,4224]{1,0:T(8,128)(2,1)S(1)}, bf16[32,4224]{1,0:T(8,128)(2,1)S(1)}, u32[]{:S(2)}, u32[]{:S(2)}) collective-permute-start(bf16[32,4224]{1,0:T(8,128)(2,1)S(1)} %slice.1284), channel_id=1, source_target_pairs={{0,96},{32,0},{64,32},{96,64},{1,97},{33,1},{65,33},{97,65},{2,98}... | collective-permute-start | bytes 811016 | tf_op jit(solution)/shard_map/ppermute | solution.py:90
  102.9 6.4 %slice-start = ((s8[8388608]{0:T(1024)(128)(4,1)}), s8[4194304]{0:T(1024)(128)(4,1)S(1)}, s32[]{:S(2)}) async-start(s8[8388608]{0:T(1024)(128)(4,1)} %bitcast.58), calls=%async_computation.1 | async-start | bytes 8388608
  106.0 3.2 %slice-start.1 = ((s8[8388608]{0:T(1024)(128)(4,1)}), s8[4194304]{0:T(1024)(128)(4,1)S(1)}, s32[]{:S(2)}) async-start(s8[8388608]{0:T(1024)(128)(4,1)} %bitcast.58), calls=%async_computation.2 | async-start | bytes 8388608
  109.5 3.4 %copy-start.2 = (bf16[256,4224]{1,0:T(8,128)(2,1)S(1)}, bf16[256,4224]{1,0:T(8,128)(2,1)}, u32[]{:S(2)}) copy-start(bf16[256,4224]{1,0:T(8,128)(2,1)} %constant_dynamic-update-slice_fusion.7) | copy-start | bytes 6488068
  112.9 3.3 %copy-start.1 = (bf16[1024,4096]{1,0:T(8,128)(2,1)}, bf16[1024,4096]{1,0:T(8,128)(2,1)S(1)}, u32[]{:S(2)}) copy-start(bf16[1024,4096]{1,0:T(8,128)(2,1)S(1)} %select_dynamic-update-slice_fusion) | copy-start | bytes 25165828
  118.6 8.1 %slice-start.5 = ((s8[6291456]{0:T(1024)(128)(4,1)}), s8[4194304]{0:T(1024)(128)(4,1)S(1)}, s32[]{:S(2)}) async-start(s8[6291456]{0:T(1024)(128)(4,1)} %bitcast.78), calls=%async_computation.6 | async-start | bytes 8388608
  125.1 2.2 %slice-start.2 = ((s8[8388608]{0:T(1024)(128)(4,1)}), s8[4194304]{0:T(1024)(128)(4,1)S(1)}, s32[]{:S(2)}) async-start(s8[8388608]{0:T(1024)(128)(4,1)} %bitcast.60), calls=%async_computation.3 | async-start | bytes 8388608
  125.2 2.9 %slice-start.6 = ((s8[6291456]{0:T(1024)(128)(4,1)}), s8[2097152]{0:T(1024)(128)(4,1)S(1)}, s32[]{:S(2)}) async-start(s8[6291456]{0:T(1024)(128)(4,1)} %bitcast.78), calls=%async_computation.7 | async-start | bytes 4194304
  125.8 3.6 %slice-start.3 = ((s8[8388608]{0:T(1024)(128)(4,1)}), s8[4194304]{0:T(1024)(128)(4,1)S(1)}, s32[]{:S(2)}) async-start(s8[8388608]{0:T(1024)(128)(4,1)} %bitcast.60), calls=%async_computation.4 | async-start | bytes 8388608
  129.4 4.6 %slice-start.4 = ((s32[768]{0:T(1024)}), s32[512]{0:T(512)S(1)}, s32[]{:S(2)}) async-start(s32[768]{0:T(1024)} %copy-done.3), calls=%async_computation.5 | async-start | bytes 4096 | tf_op jit(solution)/shard_map/slice | solution.py:160
  136.0 6.9 %collective-permute-start.18 = (f32[8,128]{1,0:T(8,128)S(1)}, f32[8,128]{1,0:T(8,128)S(1)}, u32[]{:S(2)}, u32[]{:S(2)}) collective-permute-start(f32[8,128]{1,0:T(8,128)S(1)} %get-tuple-element.358), channel_id=1, source_target_pairs={{2,1},{16,3},{18,17},{0,19},{19,0},{1,2},{3,16},{17,18},{6,5},{20,... | collective-permute-start | bytes 12296 | tf_op jit(solution)/shard_map/ppermute | solution.py:104
  139.9 3.9 %collective-permute-start.17 = (f32[8,128]{1,0:T(8,128)S(1)}, f32[8,128]{1,0:T(8,128)S(1)}, u32[]{:S(2)}, u32[]{:S(2)}) collective-permute-start(f32[8,128]{1,0:T(8,128)S(1)} %get-tuple-element.359), channel_id=1, source_target_pairs={{2,0},{16,2},{18,16},{0,18},{19,1},{1,3},{3,17},{17,19},{6,4},{20,... | collective-permute-start | bytes 12296 | tf_op jit(solution)/shard_map/ppermute | solution.py:104
  141.8 2.1 %collective-permute-start.16 = (f32[8,128]{1,0:T(8,128)S(1)}, f32[8,128]{1,0:T(8,128)S(1)}, u32[]{:S(2)}, u32[]{:S(2)}) collective-permute-start(f32[8,128]{1,0:T(8,128)S(1)} %get-tuple-element.360), channel_id=1, source_target_pairs={{1,0},{0,1},{3,2},{2,3},{17,16},{16,17},{19,18},{18,19},{5,4},{4,5... | collective-permute-start | bytes 12296 | tf_op jit(solution)/shard_map/ppermute | solution.py:104
Sparse Core Ops, SparseCore 0:
  20.9 64.7 all-gather.1

commit v13 on v11

--- a/solution.py
+++ b/solution.py
@@ -113,6 +113,7 @@
     send_shift = jnp.sum(placed_int * query_shift[:, None], axis=0).reshape(roles, CAP)
     send_meta = jnp.stack([send_bin, send_shift], axis=1)
 
+    lib_bins, send_q, send_meta = lax.optimization_barrier((lib_bins, send_q, send_meta))
     perms = (SIBLING, UP, CROSS)
     rows = jnp.concatenate(route([send_q[i] for i in range(roles)], perms), axis=0)
     meta = jnp.stack(route([send_meta[i] for i in range(roles)], perms), axis=0)

time: 123 us -> 126 us (1.024)
  waiting for transfers between devices: 32.3 us -> 26.6 us
  starting transfers between devices: 14.2 us -> 18.7 us
  local copies, waits for them, and re-layouts: 15.5 us -> 17.8 us
  matrix products: 14.9 us -> 16.8 us
    ppermute x1, waiting for transfers between devices: 21.2 us -> 0.01 us  [on_device(): partner_bin = lax.ppermute(library_bin[0], 'blk_1', [(0, 1), (1, 0)])]
    ppermute x9, waiting for transfers between devices: 3.64 us -> 22.7 us  [route(): lax.ppermute(b, ZRING, p)]
    unnamed x1 -> x0, blocking collectives: 13.8 us -> none
    optimization_barrier x0 -> x1, blocking collectives: none -> 13.5 us  [on_device(): lax.optimization_barrier((lib_bins, send_q, send_meta))]
    all_gather x1, waiting for transfers between devices: 3.6 us -> 0.01 us  [on_device(): lax.all_gather((chunk, chunk_bin), ('blk_0', 'blk_2'), axis=0, tiled=True)]
    ppermute x9, starting transfers between devices: 8.8 us -> 11.5 us  [route(): lax.ppermute(b, ZRING, p)]
    squeeze x0 -> x1, local copies, waits for them, and re-layouts: none -> 2.71 us  [on_device(): send_q[i]]
    slice x3, local copies, waits for them, and re-layouts: 2.41 us -> 0.18 us  [the longest x1 2.23 us: on_device(): send_q[i]]
  transfers between devices with their start and end apart: 12 -> 12, of which waited for: 5 -> 6; matrix products, arithmetic and copies ran while one was open for 24% -> 27% of each run, Pallas kernels for 0% -> 0%
where the time goes in v13:
time: 126 us
  waiting for transfers between devices  26.6 us (21%)
  starting transfers between devices  18.7 us (15%)
  other arithmetic  18 us (14%)
  local copies, waits for them, and re-layouts  17.8 us (14%)
  matrix products  16.8 us (13%)
  between operations  14.5 us (12%)
  blocking collectives  13.5 us (11%)
    ppermute x9, waiting for transfers between devices, route(): lax.ppermute(b, ZRING, p)  22.7 us
    optimization_barrier x1, blocking collectives, on_device(): lax.optimization_barrier((lib_bins, send_q, send_meta))  13.5 us
    dot_general x1, matrix products, on_device(): lax.dot_general(full, both, (((1,), (1,)), ((), ())), preferred_element_t...  12.9 us
    ppermute x9, starting transfers between devices, route(): lax.ppermute(b, ZRING, p)  11.5 us
    unnamed x10, local copies, waits for them, and re-layouts  6.82 us
    slice x2, local copies, waits for them, and re-layouts, lower_bins(): return jnp.concatenate([rows[..., amount:], tail], axis=-1)  6.43 us
    reduce_sum x3, other arithmetic, unit_rows(): total = jnp.sum(values * values, axis=-1, keepdims=True)  4.56 us
    ppermute x1, starting transfers between devices, on_device(): partner = lax.ppermute(library[0], 'blk_1', [(0, 1), (1, 0)])  4.43 us
  transfers between devices with their start and end apart: 12, of which 6 were waited for; matrix products, arithmetic and copies ran while one was open for 27% of the time, Pallas kernels for 0%

profile of v13, /device:TPU:1, one launch (start us, length us, event | category | flops | bytes accessed | tf_op | source)
XLA Modules:
  0.0 125.9 jit_solution(13867960097267347275)
XLA Ops:
  6.5 4.4 %collective-permute-start.4 = (bf16[32,4096]{1,0:T(8,128)(2,1)}, bf16[32,4096]{1,0:T(8,128)(2,1)S(1)}, u32[]{:S(2)}, u32[]{:S(2)}) collective-permute-start(bf16[32,4096]{1,0:T(8,128)(2,1)} %bitcast.66), channel_id=1, source_target_pairs={{0,16},{16,0},{1,17},{17,1},{2,18},{18,2},{3,19},{19,3},{4,20},{20... | collective-permute-start | bytes 786440 | tf_op jit(solution)/shard_map/ppermute | solution.py:95
  11.0 1.3 %multiply_reduce_fusion.2 = f32[32]{0:T(128)S(1)} fusion(bf16[1,32,4096]{2,1,0:T(8,128)(2,1)} %param.10), kind=kLoop, calls=%fused_computation.20 | loop fusion | flops 393184 | bytes 262272 | tf_op jit(solution)/shard_map/reduce_sum | solution.py:37
  12.2 1.1 multiply_convert_fusion.3
  13.4 3.8 %collective-permute-done.4 = bf16[32,4096]{1,0:T(8,128)(2,1)S(1)} collective-permute-done((bf16[32,4096]{1,0:T(8,128)(2,1)}, bf16[32,4096]{1,0:T(8,128)(2,1)S(1)}, u32[]{:S(2)}, u32[]{:S(2)}) %collective-permute-start.4) | collective-permute-done | bytes 262176 | tf_op jit(solution)/shard_map/ppermute | solution.py:95
  17.2 0.3 multiply_reduce_fusion.1
  17.5 0.2 multiply_convert_fusion.2
  17.7 0.8 pad_maximum_fusion.1
  18.5 2.7 %collective-permute-start = (s32[32]{0:T(128)}, s32[32]{0:T(128)S(1)}, u32[]{:S(2)}, u32[]{:S(2)}) collective-permute-start(s32[32]{0:T(128)} %bitcast.80), channel_id=1, source_target_pairs={{0,16},{16,0},{1,17},{17,1},{2,18},{18,2},{3,19},{19,3},{4,20},{20... | collective-permute-start | bytes 392 | tf_op jit(solution)/shard_map/ppermute | solution.py:96
  21.3 0.7 fusion.46
  22.0 1.2 reduce-window.6
  23.3 0.1 copy.18
  23.5 1.2 dynamic-slice
  24.9 0.7 and_reduce_fusion
  25.6 0.9 select_reduce_fusion.1
  26.5 3.0 %multiply_reduce_fusion = f32[256]{0:T(256)S(1)} fusion(bf16[256,4096]{1,0:T(8,128)(2,1)} %param.6), kind=kLoop, calls=%fused_computation.5 | loop fusion | flops 3145472 | bytes 2098176 | tf_op jit(solution)/shard_map/reduce_sum | solution.py:37
  29.5 3.9 %convolution_convert_fusion = bf16[512,4096]{1,0:T(8,128)(2,1)} fusion(bf16[256,4096]{1,0:T(8,128)(2,1)S(1)} %copy-done, f32[256]{0:T(256)S(1)} %add_rsqrt_fusion, s32[256]{0:T(256)S(1)} %bitcast.68), kind=kOutput, calls=%fused_computation.1 | convolution fusion | flops 1079115776 | bytes 6293504 | tf_op jit(solution)/shard_map/dot_general | solution.py:108
  34.1 0.2 add_dynamic-update-slice_fusion
  34.3 13.5 %all-reduce.2 = s32[1024]{0:T(1024)S(1)} all-reduce(s32[1024]{0:T(1024)S(1)} %add_dynamic-update-slice_fusion), channel_id=1, replica_groups=mesh['blk_0'=4,'blk_1'=2,'blk_2'=4,'rep'=4] {'blk_0','blk_2'}, use_global_device_ids=true, to_apply=%add.2 | all-reduce | flops 1024 | bytes 8192 | tf_op jit(solution)/shard_map/optimization_barrier | solution.py:116
  47.9 4.8 %collective-permute-start.1 = (s32[2,128]{1,0:T(2,128)S(1)}, s32[2,128]{1,0:T(2,128)S(1)}, u32[]{:S(2)}, u32[]{:S(2)}) collective-permute-start(s32[2,128]{1,0:T(2,128)S(1)} %get-tuple-element.170), channel_id=1, source_target_pairs={{0,1},{1,0},{2,3},{3,2},{16,17},{17,16},{18,19},{19,18},{4,5},{5,4... | collective-permute-start | bytes 3080 | tf_op jit(solution)/shard_map/ppermute | solution.py:85
  52.7 2.7 %slice_bitcast_fusion.3 = (bf16[128,4096]{1,0:T(8,128)(2,1)S(1)}, bf16[128,4096]{1,0:T(8,128)(2,1)S(1)}, bf16[128,4096]{1,0:T(8,128)(2,1)S(1)}, bf16[128,4096]{1,0:T(8,128)(2,1)S(1)}) fusion(bf16[4,128,4096]{2,1,0:T(8,128)(2,1)} %bitcast.64), kind=kLoop, calls=%fused_computation.14 | loop fusion | bytes 8388608 | tf_op jit(solution)/shard_map/squeeze | solution.py:118
  55.5 0.5 collective-permute-start.6
  56.0 0.6 collective-permute-start.7
  56.6 2.9 %collective-permute-start.2 = (s32[2,128]{1,0:T(2,128)S(1)}, s32[2,128]{1,0:T(2,128)S(1)}, u32[]{:S(2)}, u32[]{:S(2)}) collective-permute-start(s32[2,128]{1,0:T(2,128)S(1)} %get-tuple-element.169), channel_id=1, source_target_pairs={{0,2},{2,16},{16,18},{18,0},{1,19},{3,1},{17,3},{19,17},{4,6},{6,2... | collective-permute-start | bytes 3080 | tf_op jit(solution)/shard_map/ppermute | solution.py:85
  59.5 2.4 %constant_dynamic-update-slice_fusion.3 = bf16[1024,4096]{1,0:T(8,128)(2,1)} fusion(bf16[4,128,4096]{2,1,0:T(8,128)(2,1)} %bitcast.65), kind=kLoop, calls=%fused_computation.133 | loop fusion | bytes 2097152
  61.9 18.0 %collective-permute-done.2 = s32[2,128]{1,0:T(2,128)S(1)} collective-permute-done((s32[2,128]{1,0:T(2,128)S(1)}, s32[2,128]{1,0:T(2,128)S(1)}, u32[]{:S(2)}, u32[]{:S(2)}) %collective-permute-start.2) | collective-permute-done | bytes 1056 | tf_op jit(solution)/shard_map/ppermute | solution.py:85
  79.9 1.0 collective-permute-done.3
  80.9 0.3 pad_maximum_fusion
  81.3 3.2 %slice.565 = bf16[512,4064]{1,0:T(8,128)(2,1)S(1)} slice(bf16[512,4096]{1,0:T(8,128)(2,1)S(1)} %pad_maximum_fusion), slice={[0:512], [32:4096]} | slice | bytes 8323072 | tf_op jit(solution)/shard_map/slice | solution.py:43
  84.5 3.2 %slice.566 = bf16[512,4080]{1,0:T(8,128)(2,1)S(1)} slice(bf16[512,4096]{1,0:T(8,128)(2,1)S(1)} %pad_maximum_fusion), slice={[0:512], [16:4096]} | slice | bytes 8355840 | tf_op jit(solution)/shard_map/slice | solution.py:43
  87.7 1.1 constant_dynamic-update-slice_fusion.2
  88.8 1.1 constant_dynamic-update-slice_fusion.1
  89.9 1.1 constant_dynamic-update-slice_fusion
  90.9 4.1 %select_dynamic-update-slice_fusion = bf16[1024,4096]{1,0:T(8,128)(2,1)} fusion(bf16[1024,4096]{1,0:T(8,128)(2,1)} %constant_dynamic-update-slice_fusion, bf16[512,4080]{1,0:T(8,128)(2,1)S(1)} %slice.566, bf16[512,4064]{1,0:T(8,128)(2,1)S(1)} %slice.565, pred[512]{0:T(512)(128)(4,1)S(1)} %get-tuple-element.166, pred[512]{0:T(512)(128)(4,1)S(1)} %get-tuple-element.165), kind=kLoop, calls=%fused_computation.3 | loop fusion | flops 4194304 | bytes 12534784 | tf_op jit(solution)/shard_map/concatenate | solution.py:127
  95.1 12.9 %fusion.121 = f32[1024,1024]{1,0:T(8,128)S(1)} fusion(bf16[1024,4096]{1,0:T(8,128)(2,1)} %all-gather.2.cloned.1.call-done, bf16[1024,4096]{1,0:T(8,128)(2,1)} %select_dynamic-update-slice_fusion), kind=kOutput, calls=%fused_computation.255 | convolution fusion | flops 8589934592 | bytes 20971520 | tf_op jit(solution)/shard_map/dot_general | solution.py:128
  108.0 0.5 fusion
  108.5 0.3 minimum_minimum_fusion.4
  108.9 0.4 minimum_maximum_fusion.1
  109.3 0.3 minimum_maximum_fusion
  109.6 0.2 minimum_minimum_fusion.6
  109.8 0.2 maximum_maximum_fusion.3
  111.1 1.3 %collective-permute-start.10 = (f32[8,128]{1,0:T(8,128)S(1)}, f32[8,128]{1,0:T(8,128)S(1)}, u32[]{:S(2)}, u32[]{:S(2)}) collective-permute-start(f32[8,128]{1,0:T(8,128)S(1)} %get-tuple-element.150), channel_id=1, source_target_pairs={{2,1},{16,3},{18,17},{0,19},{19,0},{1,2},{3,16},{17,18},{6,5},{20,... | collective-permute-start | bytes 12296 | tf_op jit(solution)/shard_map/ppermute | solution.py:85
  112.4 1.3 collective-permute-start.8
  113.7 0.5 collective-permute-done.10
  114.2 0.3 collective-permute-done.8
  114.5 2.9 %collective-permute-done.9 = f32[8,128]{1,0:T(8,128)S(1)} collective-permute-done((f32[8,128]{1,0:T(8,128)S(1)}, f32[8,128]{1,0:T(8,128)S(1)}, u32[]{:S(2)}, u32[]{:S(2)}) %collective-permute-start.9) | collective-permute-done | bytes 4128 | tf_op jit(solution)/shard_map/ppermute | solution.py:85
  117.4 0.1 copy.23
  117.5 0.7 gather_fusion
  118.4 0.7 copy.24
  (62 shorter events, 1.4 us)
Async XLA Ops:
  6.5 23.0 %copy-start = (bf16[256,4096]{1,0:T(8,128)(2,1)S(1)}, bf16[256,4096]{1,0:T(8,128)(2,1)}, u32[]{:S(2)}) copy-start(bf16[256,4096]{1,0:T(8,128)(2,1)} %param.6) | copy-start | bytes 6291460
  6.5 88.5 %all-gather.2.cloned.1.call-start = ((), (), s32[]{:S(2)}) async-start(), calls=%async_computation | async-start | bytes 8912896 | tf_op jit(solution)/shard_map/all_gather | solution.py:99
  6.5 10.7 %collective-permute-start.4 = (bf16[32,4096]{1,0:T(8,128)(2,1)}, bf16[32,4096]{1,0:T(8,128)(2,1)S(1)}, u32[]{:S(2)}, u32[]{:S(2)}) collective-permute-start(bf16[32,4096]{1,0:T(8,128)(2,1)} %bitcast.66), channel_id=1, source_target_pairs={{0,16},{16,0},{1,17},{17,1},{2,18},{18,2},{3,19},{19,3},{4,20},{20... | collective-permute-start | bytes 786440 | tf_op jit(solution)/shard_map/ppermute | solution.py:95
  18.5 15.6 %collective-permute-start = (s32[32]{0:T(128)}, s32[32]{0:T(128)S(1)}, u32[]{:S(2)}, u32[]{:S(2)}) collective-permute-start(s32[32]{0:T(128)} %bitcast.80), channel_id=1, source_target_pairs={{0,16},{16,0},{1,17},{17,1},{2,18},{18,2},{3,19},{19,3},{4,20},{20... | collective-permute-start | bytes 392 | tf_op jit(solution)/shard_map/ppermute | solution.py:96
  29.5 4.6 %copy-start.1 = (s32[1,32]{1,0:T(1,128)S(1)}, s32[1,32]{1,0:T(1,128)}, u32[]{:S(2)}) copy-start(s32[1,32]{1,0:T(1,128)} %param.11) | copy-start | bytes 388
  47.9 11.7 %collective-permute-start.1 = (s32[2,128]{1,0:T(2,128)S(1)}, s32[2,128]{1,0:T(2,128)S(1)}, u32[]{:S(2)}, u32[]{:S(2)}) collective-permute-start(s32[2,128]{1,0:T(2,128)S(1)} %get-tuple-element.170), channel_id=1, source_target_pairs={{0,1},{1,0},{2,3},{3,2},{16,17},{17,16},{18,19},{19,18},{4,5},{5,4... | collective-permute-start | bytes 3080 | tf_op jit(solution)/shard_map/ppermute | solution.py:85
  55.4 25.5 %collective-permute-start.5 = (bf16[128,4096]{1,0:T(8,128)(2,1)S(1)}, bf16[128,4096]{1,0:T(8,128)(2,1)S(1)}, u32[]{:S(2)}, u32[]{:S(2)}) collective-permute-start(bf16[128,4096]{1,0:T(8,128)(2,1)S(1)} %get-tuple-element.108), channel_id=1, source_target_pairs={{0,1},{1,0},{2,3},{3,2},{16,17},{17,16},{18,19},{19,18},{4,5},{5,4... | collective-permute-start | bytes 3145736 | tf_op jit(solution)/shard_map/ppermute | solution.py:85
  55.5 25.4 %collective-permute-start.6 = (bf16[128,4096]{1,0:T(8,128)(2,1)S(1)}, bf16[128,4096]{1,0:T(8,128)(2,1)S(1)}, u32[]{:S(2)}, u32[]{:S(2)}) collective-permute-start(bf16[128,4096]{1,0:T(8,128)(2,1)S(1)} %get-tuple-element.107), channel_id=1, source_target_pairs={{0,2},{2,16},{16,18},{18,0},{1,19},{3,1},{17,3},{19,17},{4,6},{6,2... | collective-permute-start | bytes 3145736 | tf_op jit(solution)/shard_map/ppermute | solution.py:85
  56.0 25.0 %collective-permute-start.7 = (bf16[128,4096]{1,0:T(8,128)(2,1)S(1)}, bf16[128,4096]{1,0:T(8,128)(2,1)S(1)}, u32[]{:S(2)}, u32[]{:S(2)}) collective-permute-start(bf16[128,4096]{1,0:T(8,128)(2,1)S(1)} %get-tuple-element.106), channel_id=1, source_target_pairs={{1,2},{3,16},{17,18},{19,0},{0,19},{2,1},{16,3},{18,17},{5,6},{7,2... | collective-permute-start | bytes 3145736 | tf_op jit(solution)/shard_map/ppermute | solution.py:85
  56.6 23.3 %collective-permute-start.2 = (s32[2,128]{1,0:T(2,128)S(1)}, s32[2,128]{1,0:T(2,128)S(1)}, u32[]{:S(2)}, u32[]{:S(2)}) collective-permute-start(s32[2,128]{1,0:T(2,128)S(1)} %get-tuple-element.169), channel_id=1, source_target_pairs={{0,2},{2,16},{16,18},{18,0},{1,19},{3,1},{17,3},{19,17},{4,6},{6,2... | collective-permute-start | bytes 3080 | tf_op jit(solution)/shard_map/ppermute | solution.py:85
  59.5 21.3 %collective-permute-start.3 = (s32[2,128]{1,0:T(2,128)S(1)}, s32[2,128]{1,0:T(2,128)S(1)}, u32[]{:S(2)}, u32[]{:S(2)}) collective-permute-start(s32[2,128]{1,0:T(2,128)S(1)} %get-tuple-element.168), channel_id=1, source_target_pairs={{1,2},{3,16},{17,18},{19,0},{0,19},{2,1},{16,3},{18,17},{5,6},{7,2... | collective-permute-start | bytes 3080 | tf_op jit(solution)/shard_map/ppermute | solution.py:85
  111.1 3.1 %collective-permute-start.10 = (f32[8,128]{1,0:T(8,128)S(1)}, f32[8,128]{1,0:T(8,128)S(1)}, u32[]{:S(2)}, u32[]{:S(2)}) collective-permute-start(f32[8,128]{1,0:T(8,128)S(1)} %get-tuple-element.150), channel_id=1, source_target_pairs={{2,1},{16,3},{18,17},{0,19},{19,0},{1,2},{3,16},{17,18},{6,5},{20,... | collective-permute-start | bytes 12296 | tf_op jit(solution)/shard_map/ppermute | solution.py:85
  112.4 2.1 %collective-permute-start.8 = (f32[8,128]{1,0:T(8,128)S(1)}, f32[8,128]{1,0:T(8,128)S(1)}, u32[]{:S(2)}, u32[]{:S(2)}) collective-permute-start(f32[8,128]{1,0:T(8,128)S(1)} %get-tuple-element.152), channel_id=1, source_target_pairs={{1,0},{0,1},{3,2},{2,3},{17,16},{16,17},{19,18},{18,19},{5,4},{4,5... | collective-permute-start | bytes 12296 | tf_op jit(solution)/shard_map/ppermute | solution.py:85
  113.7 3.8 %collective-permute-start.9 = (f32[8,128]{1,0:T(8,128)S(1)}, f32[8,128]{1,0:T(8,128)S(1)}, u32[]{:S(2)}, u32[]{:S(2)}) collective-permute-start(f32[8,128]{1,0:T(8,128)S(1)} %get-tuple-element.151), channel_id=1, source_target_pairs={{2,0},{16,2},{18,16},{0,18},{19,1},{1,3},{3,17},{17,19},{6,4},{20,... | collective-permute-start | bytes 12296 | tf_op jit(solution)/shard_map/ppermute | solution.py:85
Sparse Core Ops, SparseCore 0:
  18.7 73.1 all-gather.1

commit v14 on v11

--- a/solution.py
+++ b/solution.py
@@ -130,7 +130,10 @@
     best = top_rows(scores)
     home = route([best[:, i * CAP:(i + 1) * CAP] for i in range(roles)], tuple(inverse(p) for p in perms))
     home = jnp.concatenate(home, axis=1)
-    return jnp.take(home, slot, axis=1).T
+    return lax.dot_general(
+        placed.astype(jnp.float32), home, (((1,), (1,)), ((), ())),
+        preferred_element_type=jnp.float32, precision=lax.Precision.HIGHEST,
+    )
 
 
 def solution(mesh):

time: 123 us -> 123 us (level)
  local copies, waits for them, and re-layouts: 15.5 us -> 14 us
where the time goes in v14:
time: 123 us; the launch traced here: 122 us
  waiting for transfers between devices  32.5 us (26%)
  other arithmetic  17.5 us (14%)
  matrix products  15.8 us (13%)
  between operations  14.5 us (12%)
  starting transfers between devices  14.2 us (12%)
  local copies, waits for them, and re-layouts  14 us (11%)
  blocking collectives  13.8 us (11%)
    ppermute x1, waiting for transfers between devices, on_device(): partner_bin = lax.ppermute(library_bin[0], 'blk_1', [(0, 1), (1, 0)])  21.2 us
    unnamed x1, blocking collectives  13.8 us
    dot_general x1, matrix products, on_device(): lax.dot_general(full, both, (((1,), (1,)), ((), ())), preferred_element_t...  12.9 us
    ppermute x9, starting transfers between devices, route(): lax.ppermute(b, ZRING, p)  8.82 us
    slice x2, local copies, waits for them, and re-layouts, lower_bins(): return jnp.concatenate([rows[..., amount:], tail], axis=-1)  6.32 us
    unnamed x17, local copies, waits for them, and re-layouts  5.08 us
    reduce_sum x3, other arithmetic, unit_rows(): total = jnp.sum(values * values, axis=-1, keepdims=True)  4.56 us
    ppermute x1, starting transfers between devices, on_device(): partner = lax.ppermute(library[0], 'blk_1', [(0, 1), (1, 0)])  4.43 us
  transfers between devices with their start and end apart: 12, of which 5 were waited for; matrix products, arithmetic and copies ran while one was open for 24% of the time, Pallas kernels for 0%

profile of v14, /device:TPU:1, one launch (start us, length us, event | category | flops | bytes accessed | tf_op | source)
XLA Modules:
  0.0 122.3 jit_solution(17424423997017000671)
XLA Ops:
  6.5 4.4 %collective-permute-start.4 = (bf16[32,4096]{1,0:T(8,128)(2,1)}, bf16[32,4096]{1,0:T(8,128)(2,1)S(1)}, u32[]{:S(2)}, u32[]{:S(2)}) collective-permute-start(bf16[32,4096]{1,0:T(8,128)(2,1)} %bitcast.52), channel_id=1, source_target_pairs={{0,16},{16,0},{1,17},{17,1},{2,18},{18,2},{3,19},{19,3},{4,20},{20... | collective-permute-start | bytes 786440 | tf_op jit(solution)/shard_map/ppermute | solution.py:95
  11.0 1.3 %multiply_reduce_fusion.2 = f32[32]{0:T(128)S(1)} fusion(bf16[1,32,4096]{2,1,0:T(8,128)(2,1)} %param.10), kind=kLoop, calls=%fused_computation.15 | loop fusion | flops 393184 | bytes 262272 | tf_op jit(solution)/shard_map/reduce_sum | solution.py:37
  12.2 1.1 multiply_convert_fusion.3
  13.4 3.8 %collective-permute-done.4 = bf16[32,4096]{1,0:T(8,128)(2,1)S(1)} collective-permute-done((bf16[32,4096]{1,0:T(8,128)(2,1)}, bf16[32,4096]{1,0:T(8,128)(2,1)S(1)}, u32[]{:S(2)}, u32[]{:S(2)}) %collective-permute-start.4) | collective-permute-done | bytes 262176 | tf_op jit(solution)/shard_map/ppermute | solution.py:95
  17.2 0.3 multiply_reduce_fusion.1
  17.5 0.2 multiply_convert_fusion.2
  17.7 0.8 pad_maximum_fusion.1
  18.6 0.7 fusion.58
  19.3 1.2 %reduce-window.6 = s32[4,2,128]{2,1,0:T(2,128)S(1)} reduce-window(s32[4,2,128]{2,1,0:T(2,128)S(1)} %compare_convert_fusion, s32[]{:T(128)} %constant.60.clone.1), window={size=1x1x128 pad=0_0x0_0x127_0}, to_apply=%region_0.1 | reduce-window | flops 130048 | bytes 8196 | tf_op jit(solution)/shard_map/reduce-window
  20.5 0.1 slice.564
  20.6 0.1 copy.14
  20.7 0.1 copy.15
  20.8 0.1 add_bitcast_fusion
  20.9 3.0 %multiply_reduce_fusion = f32[256]{0:T(256)S(1)} fusion(bf16[256,4096]{1,0:T(8,128)(2,1)} %param.6), kind=kLoop, calls=%fused_computation.4 | loop fusion | flops 3145472 | bytes 2098176 | tf_op jit(solution)/shard_map/reduce_sum | solution.py:37
  24.0 2.0 %convolution_convert_fusion = bf16[512,4096]{1,0:T(8,128)(2,1)S(1)} fusion(bf16[256,4096]{1,0:T(8,128)(2,1)S(1)} %copy-done, f32[256]{0:T(256)S(1)} %add_rsqrt_fusion, s32[256]{0:T(256)S(1)} %bitcast.53), kind=kOutput, calls=%fused_computation | convolution fusion | flops 1079115776 | bytes 6293504 | tf_op jit(solution)/shard_map/dot_general | solution.py:108
  26.0 2.3 %fusion.135 = (bf16[128,4096]{1,0:T(8,128)(2,1)S(1)}, bf16[1024,4096]{1,0:T(8,128)(2,1)}, bf16[128,4096]{1,0:T(8,128)(2,1)}, bf16[128,4096]{1,0:T(8,128)(2,1)}, bf16[128,4096]{1,0:T(8,128)(2,1)}) fusion(bf16[512,4096]{1,0:T(8,128)(2,1)S(1)} %convolution_convert_fusion), kind=kLoop, calls=%fused_computation.262 | loop fusion | bytes 9437184 | tf_op jit(solution)/shard_map/slice | solution.py:117
  28.3 1.2 %collective-permute-start.5 = (bf16[128,4096]{1,0:T(8,128)(2,1)}, bf16[128,4096]{1,0:T(8,128)(2,1)S(1)}, u32[]{:S(2)}, u32[]{:S(2)}) collective-permute-start(bf16[128,4096]{1,0:T(8,128)(2,1)} %get-tuple-element.100), channel_id=1, source_target_pairs={{0,1},{1,0},{2,3},{3,2},{16,17},{17,16},{18,19},{19,18},{4,5},{5,4... | collective-permute-start | bytes 3145736 | tf_op jit(solution)/shard_map/ppermute | solution.py:85
  29.5 3.1 %collective-permute-start.6 = (bf16[128,4096]{1,0:T(8,128)(2,1)}, bf16[128,4096]{1,0:T(8,128)(2,1)S(1)}, u32[]{:S(2)}, u32[]{:S(2)}) collective-permute-start(bf16[128,4096]{1,0:T(8,128)(2,1)} %get-tuple-element.99), channel_id=1, source_target_pairs={{0,2},{2,16},{16,18},{18,0},{1,19},{3,1},{17,3},{19,17},{4,6},{6,2... | collective-permute-start | bytes 3145736 | tf_op jit(solution)/shard_map/ppermute | solution.py:85
  32.6 0.2 select_reduce_fusion.1
  32.8 0.6 collective-permute-start.1
  33.4 1.0 collective-permute-start
  34.4 0.6 dynamic-slice
  35.6 21.2 %collective-permute-done = s32[32]{0:T(128)S(1)} collective-permute-done((s32[32]{0:T(128)S(1)}, s32[32]{0:T(128)S(1)}, u32[]{:S(2)}, u32[]{:S(2)}) %collective-permute-start) | collective-permute-done | bytes 160 | tf_op jit(solution)/shard_map/ppermute | solution.py:96
  56.9 0.2 add_dynamic-update-slice_fusion
  57.0 0.7 collective-permute-start.3
  57.7 13.8 %all-reduce.2 = s32[1024]{0:T(1024)S(1)} all-reduce(s32[1024]{0:T(1024)S(1)} %add_dynamic-update-slice_fusion), channel_id=1, replica_groups=mesh['blk_0'=4,'blk_1'=2,'blk_2'=4,'rep'=4] {'blk_0','blk_2'}, use_global_device_ids=true, to_apply=%add.2 | all-reduce | flops 1024 | bytes 8192
  71.6 1.5 %pad_maximum_fusion = bf16[512,4096]{1,0:T(8,128)(2,1)S(1)} fusion(bf16[128,4096]{1,0:T(8,128)(2,1)} %collective-permute-done.7, bf16[128,4096]{1,0:T(8,128)(2,1)S(1)} %collective-permute-done.6, bf16[128,4096]{1,0:T(8,128)(2,1)S(1)} %collective-permute-done.5, bf16[128,4096]{1,0:T(8,128)(2,1)S(1)} %get-tuple-element.96), kind=kLoop, calls=%fused_computation.1 | loop fusion | flops 16777216 | bytes 8388608 | tf_op jit(solution)/shard_map/concatenate | solution.py:117
  73.1 3.2 %slice.577 = bf16[512,4064]{1,0:T(8,128)(2,1)S(1)} slice(bf16[512,4096]{1,0:T(8,128)(2,1)S(1)} %pad_maximum_fusion), slice={[0:512], [32:4096]} | slice | bytes 8323072 | tf_op jit(solution)/shard_map/slice | solution.py:43
  76.2 3.2 %slice.578 = bf16[512,4080]{1,0:T(8,128)(2,1)S(1)} slice(bf16[512,4096]{1,0:T(8,128)(2,1)S(1)} %pad_maximum_fusion), slice={[0:512], [16:4096]} | slice | bytes 8355840 | tf_op jit(solution)/shard_map/slice | solution.py:43
  79.4 1.1 constant_dynamic-update-slice_fusion.2
  80.5 1.0 constant_dynamic-update-slice_fusion.1
  81.5 2.4 %constant_dynamic-update-slice_fusion = bf16[1024,4096]{1,0:T(8,128)(2,1)} fusion(bf16[1024,4096]{1,0:T(8,128)(2,1)} %constant_dynamic-update-slice_fusion.1, bf16[128,4096]{1,0:T(8,128)(2,1)} %collective-permute-done.7), kind=kLoop, calls=%fused_computation.124 | loop fusion | bytes 2097152
  83.9 4.1 %select_dynamic-update-slice_fusion = bf16[1024,4096]{1,0:T(8,128)(2,1)} fusion(bf16[1024,4096]{1,0:T(8,128)(2,1)} %constant_dynamic-update-slice_fusion, bf16[512,4080]{1,0:T(8,128)(2,1)S(1)} %slice.578, bf16[512,4064]{1,0:T(8,128)(2,1)S(1)} %slice.577, pred[512]{0:T(512)(128)(4,1)S(1)} %get-tuple-element.158, pred[512]{0:T(512)(128)(4,1)S(1)} %get-tuple-element.157), kind=kLoop, calls=%fused_computation.2 | loop fusion | flops 4194304 | bytes 12534784 | tf_op jit(solution)/shard_map/concatenate | solution.py:126
  87.9 3.8 %all-gather.2.cloned.1.call-done = bf16[1024,4096]{1,0:T(8,128)(2,1)} async-done(((bf16[64,4096]{1,0:T(8,128)(2,1)}), bf16[1024,4096]{1,0:T(8,128)(2,1)}) %all-gather.2.cloned.1.call-update) | async-done | bytes 8388624 | tf_op jit(solution)/shard_map/all_gather | solution.py:99
  91.7 12.9 %fusion.137 = f32[1024,1024]{1,0:T(8,128)S(1)} fusion(bf16[1024,4096]{1,0:T(8,128)(2,1)} %all-gather.2.cloned.1.call-done, bf16[1024,4096]{1,0:T(8,128)(2,1)} %select_dynamic-update-slice_fusion), kind=kOutput, calls=%fused_computation.264 | convolution fusion | flops 8589934592 | bytes 20971520 | tf_op jit(solution)/shard_map/dot_general | solution.py:127
  104.6 0.5 fusion
  105.1 0.3 minimum_minimum_fusion.4
  105.5 0.4 minimum_maximum_fusion.1
  105.9 0.3 minimum_maximum_fusion
  106.2 0.2 minimum_minimum_fusion.6
  106.4 0.2 maximum_maximum_fusion.3
  106.8 0.1 minimum_minimum_fusion.8
  106.9 0.1 maximum_maximum_fusion.5
  107.7 1.9 %collective-permute-start.10 = (f32[8,128]{1,0:T(8,128)S(1)}, f32[8,128]{1,0:T(8,128)S(1)}, u32[]{:S(2)}, u32[]{:S(2)}) collective-permute-start(f32[8,128]{1,0:T(8,128)S(1)} %get-tuple-element.142), channel_id=1, source_target_pairs={{2,1},{16,3},{18,17},{0,19},{19,0},{1,2},{3,16},{17,18},{6,5},{20,... | collective-permute-start | bytes 12296 | tf_op jit(solution)/shard_map/ppermute | solution.py:85
  109.6 1.2 %collective-permute-start.8 = (f32[8,128]{1,0:T(8,128)S(1)}, f32[8,128]{1,0:T(8,128)S(1)}, u32[]{:S(2)}, u32[]{:S(2)}) collective-permute-start(f32[8,128]{1,0:T(8,128)S(1)} %get-tuple-element.144), channel_id=1, source_target_pairs={{1,0},{0,1},{3,2},{2,3},{17,16},{16,17},{19,18},{18,19},{5,4},{4,5... | collective-permute-start | bytes 12296 | tf_op jit(solution)/shard_map/ppermute | solution.py:85
  110.9 0.8 collective-permute-done.8
  111.6 2.8 %collective-permute-done.9 = f32[8,128]{1,0:T(8,128)S(1)} collective-permute-done((f32[8,128]{1,0:T(8,128)S(1)}, f32[8,128]{1,0:T(8,128)S(1)}, u32[]{:S(2)}, u32[]{:S(2)}) %collective-permute-start.9) | collective-permute-done | bytes 4128 | tf_op jit(solution)/shard_map/ppermute | solution.py:85
  114.5 1.0 fusion.2
  (63 shorter events, 0.9 us)
Async XLA Ops:
  6.5 17.4 %copy-start.1 = (s32[256,1]{0,1:T(1,128)S(1)}, s32[256,1]{0,1:T(1,128)}, u32[]{:S(2)}) copy-start(s32[256,1]{0,1:T(1,128)} %param.7) | copy-start | bytes 3076
  6.5 17.4 %copy-start = (bf16[256,4096]{1,0:T(8,128)(2,1)S(1)}, bf16[256,4096]{1,0:T(8,128)(2,1)}, u32[]{:S(2)}) copy-start(bf16[256,4096]{1,0:T(8,128)(2,1)} %param.6) | copy-start | bytes 6291460
  6.5 85.2 %all-gather.2.cloned.1.call-start = ((), (), s32[]{:S(2)}) async-start(), calls=%async_computation | async-start | bytes 8912896 | tf_op jit(solution)/shard_map/all_gather | solution.py:99
  6.5 10.7 %collective-permute-start.4 = (bf16[32,4096]{1,0:T(8,128)(2,1)}, bf16[32,4096]{1,0:T(8,128)(2,1)S(1)}, u32[]{:S(2)}, u32[]{:S(2)}) collective-permute-start(bf16[32,4096]{1,0:T(8,128)(2,1)} %bitcast.52), channel_id=1, source_target_pairs={{0,16},{16,0},{1,17},{17,1},{2,18},{18,2},{3,19},{19,3},{4,20},{20... | collective-permute-start | bytes 786440 | tf_op jit(solution)/shard_map/ppermute | solution.py:95
  26.0 6.7 %copy-start.2 = (s32[256]{0:T(256)S(1)}, s32[256]{0:T(256)}, u32[]{:S(2)}) copy-start(s32[256]{0:T(256)} %param.8) | copy-start | bytes 3076
  26.0 6.7 %copy-start.3 = (s32[256]{0:T(256)S(1)}, s32[256]{0:T(256)}, u32[]{:S(2)}) copy-start(s32[256]{0:T(256)} %param.9) | copy-start | bytes 3076
  26.0 7.4 %copy-start.4 = (s32[1,32]{1,0:T(1,128)S(1)}, s32[1,32]{1,0:T(1,128)}, u32[]{:S(2)}) copy-start(s32[1,32]{1,0:T(1,128)} %param.11) | copy-start | bytes 388
  26.0 8.4 %copy-start.5 = (u32[128]{0:T(128)S(1)}, u32[128]{0:T(128)}, u32[]{:S(2)}) copy-start(u32[128]{0:T(128)} %constant.77) | copy-start | bytes 1540
  28.3 43.3 %collective-permute-start.5 = (bf16[128,4096]{1,0:T(8,128)(2,1)}, bf16[128,4096]{1,0:T(8,128)(2,1)S(1)}, u32[]{:S(2)}, u32[]{:S(2)}) collective-permute-start(bf16[128,4096]{1,0:T(8,128)(2,1)} %get-tuple-element.100), channel_id=1, source_target_pairs={{0,1},{1,0},{2,3},{3,2},{16,17},{17,16},{18,19},{19,18},{4,5},{5,4... | collective-permute-start | bytes 3145736 | tf_op jit(solution)/shard_map/ppermute | solution.py:85
  29.5 42.1 %collective-permute-start.6 = (bf16[128,4096]{1,0:T(8,128)(2,1)}, bf16[128,4096]{1,0:T(8,128)(2,1)S(1)}, u32[]{:S(2)}, u32[]{:S(2)}) collective-permute-start(bf16[128,4096]{1,0:T(8,128)(2,1)} %get-tuple-element.99), channel_id=1, source_target_pairs={{0,2},{2,16},{16,18},{18,0},{1,19},{3,1},{17,3},{19,17},{4,6},{6,2... | collective-permute-start | bytes 3145736 | tf_op jit(solution)/shard_map/ppermute | solution.py:85
  32.6 39.0 %collective-permute-start.7 = (bf16[128,4096]{1,0:T(8,128)(2,1)}, bf16[128,4096]{1,0:T(8,128)(2,1)}, u32[]{:S(2)}, u32[]{:S(2)}) collective-permute-start(bf16[128,4096]{1,0:T(8,128)(2,1)} %get-tuple-element.98), channel_id=1, source_target_pairs={{1,2},{3,16},{17,18},{19,0},{0,19},{2,1},{16,3},{18,17},{5,6},{7,2... | collective-permute-start | bytes 3145736 | tf_op jit(solution)/shard_map/ppermute | solution.py:85
  32.8 24.2 %collective-permute-start.1 = (s32[2,128]{1,0:T(2,128)S(1)}, s32[2,128]{1,0:T(2,128)S(1)}, u32[]{:S(2)}, u32[]{:S(2)}) collective-permute-start(s32[2,128]{1,0:T(2,128)S(1)} %get-tuple-element.160), channel_id=1, source_target_pairs={{0,1},{1,0},{2,3},{3,2},{16,17},{17,16},{18,19},{19,18},{4,5},{5,4... | collective-permute-start | bytes 3080 | tf_op jit(solution)/shard_map/ppermute | solution.py:85
  33.4 23.4 %collective-permute-start = (s32[32]{0:T(128)S(1)}, s32[32]{0:T(128)S(1)}, u32[]{:S(2)}, u32[]{:S(2)}) collective-permute-start(s32[32]{0:T(128)S(1)} %bitcast.66), channel_id=1, source_target_pairs={{0,16},{16,0},{1,17},{17,1},{2,18},{18,2},{3,19},{19,3},{4,20},{20... | collective-permute-start | bytes 392 | tf_op jit(solution)/shard_map/ppermute | solution.py:96
  56.9 14.7 %collective-permute-start.2 = (s32[2,128]{1,0:T(2,128)S(1)}, s32[2,128]{1,0:T(2,128)S(1)}, u32[]{:S(2)}, u32[]{:S(2)}) collective-permute-start(s32[2,128]{1,0:T(2,128)S(1)} %get-tuple-element.162), channel_id=1, source_target_pairs={{0,2},{2,16},{16,18},{18,0},{1,19},{3,1},{17,3},{19,17},{4,6},{6,2... | collective-permute-start | bytes 3080 | tf_op jit(solution)/shard_map/ppermute | solution.py:85
  57.0 14.5 %collective-permute-start.3 = (s32[2,128]{1,0:T(2,128)S(1)}, s32[2,128]{1,0:T(2,128)S(1)}, u32[]{:S(2)}, u32[]{:S(2)}) collective-permute-start(s32[2,128]{1,0:T(2,128)S(1)} %get-tuple-element.161), channel_id=1, source_target_pairs={{1,2},{3,16},{17,18},{19,0},{0,19},{2,1},{16,3},{18,17},{5,6},{7,2... | collective-permute-start | bytes 3080 | tf_op jit(solution)/shard_map/ppermute | solution.py:85
  107.7 3.2 %collective-permute-start.10 = (f32[8,128]{1,0:T(8,128)S(1)}, f32[8,128]{1,0:T(8,128)S(1)}, u32[]{:S(2)}, u32[]{:S(2)}) collective-permute-start(f32[8,128]{1,0:T(8,128)S(1)} %get-tuple-element.142), channel_id=1, source_target_pairs={{2,1},{16,3},{18,17},{0,19},{19,0},{1,2},{3,16},{17,18},{6,5},{20,... | collective-permute-start | bytes 12296 | tf_op jit(solution)/shard_map/ppermute | solution.py:85
  109.6 2.1 %collective-permute-start.8 = (f32[8,128]{1,0:T(8,128)S(1)}, f32[8,128]{1,0:T(8,128)S(1)}, u32[]{:S(2)}, u32[]{:S(2)}) collective-permute-start(f32[8,128]{1,0:T(8,128)S(1)} %get-tuple-element.144), channel_id=1, source_target_pairs={{1,0},{0,1},{3,2},{2,3},{17,16},{16,17},{19,18},{18,19},{5,4},{4,5... | collective-permute-start | bytes 12296 | tf_op jit(solution)/shard_map/ppermute | solution.py:85
  110.8 3.7 %collective-permute-start.9 = (f32[8,128]{1,0:T(8,128)S(1)}, f32[8,128]{1,0:T(8,128)S(1)}, u32[]{:S(2)}, u32[]{:S(2)}) collective-permute-start(f32[8,128]{1,0:T(8,128)S(1)} %get-tuple-element.143), channel_id=1, source_target_pairs={{2,0},{16,2},{18,16},{0,18},{19,1},{1,3},{3,17},{17,19},{6,4},{20,... | collective-permute-start | bytes 12296 | tf_op jit(solution)/shard_map/ppermute | solution.py:85
Sparse Core Ops, SparseCore 0:
  18.7 73.0 all-gather.1
